TPU v7x, 32 devices: a whole 2x2x4 slice. The times are simulated.
32 devices in a mesh: fsdp: 8 (over y, x, core), rep: 4 (over z).
Axes of the slice: x: 2, y: 2, z: 4, core: 2. Of those that a mesh axis runs over, the one named last changes fastest.
Arguments:
- tokens: bfloat16 [12288, 2048], P(('fsdp', 'rep')), may hold values from -6 to 6
- lengths: int32 [32], replicated, may hold values from 96 to 384, as said below
- placement: int32 [32], replicated, may hold values from 0 to 31, each once
- attention_gain: bfloat16 [2048], P('fsdp'), may hold values from 0.5 to 1.5
- query_weight: bfloat16 [2048, 2048], P('fsdp'), may hold values from -0.125 to 0.125
- key_weight: bfloat16 [2048, 1024], P('fsdp'), may hold values from -0.125 to 0.125
- value_weight: bfloat16 [2048, 1024], P('fsdp'), may hold values from -0.125 to 0.125
- query_gain: bfloat16 [128], replicated, may hold values from 0.5 to 1.5
- key_gain: bfloat16 [128], replicated, may hold values from 0.5 to 1.5
- output_weight: bfloat16 [2048, 2048], P('fsdp'), may hold values from -1 to 1
- feed_gain: bfloat16 [2048], P('fsdp'), may hold values from 0.5 to 1.5
- gate_weight: bfloat16 [2048, 6144], P('fsdp'), may hold values from -0.125 to 0.125
- up_weight: bfloat16 [2048, 6144], P('fsdp'), may hold values from -0.125 to 0.125
- down_weight: bfloat16 [6144, 2048], P('fsdp'), may hold values from -0.078125 to 0.078125
- cotangent: bfloat16 [12288, 2048], P(('fsdp', 'rep')), may hold values from -6 to 6
Outputs:
- layer_out: bfloat16 [12288, 2048], P(('fsdp', 'rep'))
- input_grad: float32 [12288, 2048], P(('fsdp', 'rep'))
- attention_gain_grad: float32 [2048], P('fsdp')
- query_weight_grad: float32 [2048, 2048], P('fsdp')
- key_weight_grad: float32 [2048, 1024], P('fsdp')
- value_weight_grad: float32 [2048, 1024], P('fsdp')
- query_gain_grad: float32 [128], replicated
- key_gain_grad: float32 [128], replicated
- output_weight_grad: float32 [2048, 2048], P('fsdp')
- feed_gain_grad: float32 [2048], P('fsdp')
- gate_weight_grad: float32 [2048, 6144], P('fsdp')
- up_weight_grad: float32 [2048, 6144], P('fsdp')
- down_weight_grad: float32 [6144, 2048], P('fsdp')
Inputs may be any that keep to these rules, and one draw needn't show every extreme that they name: lengths[s] is the number of valid leading positions of sequence s; some sequence has exactly 384 and some exactly 96. `placement`: each sequence stands in exactly one slot.
All inputs are finite; a program needn't handle non-finite values.
Results may differ from a plain program's by a relative error of at most 0.018.
Values may be sent and summed in bfloat16 or wider, within the bound.
No kernel may reach another device: no remote copies, remote signals or barrier semaphores. Data moves between devices by JAX's collectives and lax.ppermute only.
A program may use at most 448 MiB of HBM per device.

v0:
```python
import jax
import jax.numpy as jnp
from jax import lax
from jax.sharding import PartitionSpec as P

EPSILON = 1e-06
ROPE_BASE = 1000000.0


def angle_tables(length, width):
    exponent = jnp.arange(width // 2).astype(jnp.float32) * (2.0 / width)
    frequency = ROPE_BASE ** (-exponent)
    position = jnp.arange(length).astype(jnp.float32)
    phase = position[:, None] * frequency[None, :]
    phase = jnp.concatenate([phase, phase], axis=-1)
    return (jnp.cos(phase), jnp.sin(phase))


def turn_half(values):
    half_width = values.shape[-1] // 2
    return jnp.concatenate([-values[..., half_width:], values[..., :half_width]], axis=-1)


def rotate(values, cosine, sine):
    return values * cosine + turn_half(values) * sine


def unrotate(grads_out, cosine, sine):
    return grads_out * cosine - turn_half(grads_out * sine)


def rms_forward(values, norm_gain):
    inverse = lax.rsqrt(jnp.mean(values * values, axis=-1, keepdims=True) + EPSILON)
    normal = values * inverse
    return (normal * norm_gain, normal, inverse)


def rms_backward(grads_out, normal, inverse, norm_gain):
    scaled = grads_out * norm_gain
    grads_in = inverse * (scaled - normal * jnp.mean(scaled * normal, axis=-1, keepdims=True))
    return (grads_in, grads_out * normal)


def inner_rows(left, right):
    return lax.dot_general(
        left, right, (((0,), (0,)), ((), ())), preferred_element_type=jnp.float32
    )


def times_transposed(left, right):
    return lax.dot_general(
        left, right, (((1,), (1,)), ((), ())), preferred_element_type=jnp.float32
    )


def masked_scores(query_low, key_low):
    scores = jnp.einsum("qkgd,skd->kgqs", query_low, key_low, preferred_element_type=jnp.float32)
    length = query_low.shape[0]
    causal = jnp.arange(length)[:, None] >= jnp.arange(length)[None, :]
    return jnp.where(causal, scores, -1000000000.0)


def per_device(
    tokens,
    lengths,
    placement,
    attention_gain,
    query_weight,
    key_weight,
    value_weight,
    query_gain,
    key_gain,
    output_weight,
    feed_gain,
    gate_weight,
    up_weight,
    down_weight,
    cotangent,
):
    row_count = tokens.shape[0]
    head_width = query_gain.shape[0]
    value_heads = key_weight.shape[1] // head_width
    query_heads = query_weight.shape[1] // head_width
    group_size = query_heads // value_heads
    slot_index = lax.axis_index("fsdp") * lax.axis_size("rep") + lax.axis_index("rep")
    slot_length = lengths[placement[slot_index]]
    valid_rows = (jnp.arange(row_count) < slot_length).astype(jnp.float32)[:, None]
    cosine, sine = angle_tables(row_count, head_width)
    cosine = cosine[:, None, :]
    sine = sine[:, None, :]
    scale = head_width ** (-0.5)
    gain_query = query_gain.astype(jnp.float32)
    gain_key = key_gain.astype(jnp.float32)
    attention_set = (
        lax.all_gather(attention_gain, "fsdp", axis=0, tiled=True),
        lax.all_gather(query_weight, "fsdp", axis=0, tiled=True),
        lax.all_gather(key_weight, "fsdp", axis=0, tiled=True),
        lax.all_gather(value_weight, "fsdp", axis=0, tiled=True),
        lax.all_gather(output_weight, "fsdp", axis=0, tiled=True),
    )
    feed_set = (
        lax.all_gather(feed_gain, "fsdp", axis=0, tiled=True),
        lax.all_gather(gate_weight, "fsdp", axis=0, tiled=True),
        lax.all_gather(up_weight, "fsdp", axis=0, tiled=True),
        lax.all_gather(down_weight, "fsdp", axis=0, tiled=True),
    )
    inputs_wide = tokens.astype(jnp.float32)
    gain_one = attention_set[0].astype(jnp.float32)
    normed_one, normal_one, inverse_one = rms_forward(inputs_wide, gain_one)
    normed_one_low = normed_one.astype(jnp.bfloat16)
    query_raw = jnp.dot(
        normed_one_low, attention_set[1], preferred_element_type=jnp.float32
    ).reshape(row_count, query_heads, head_width)
    key_raw = jnp.dot(normed_one_low, attention_set[2], preferred_element_type=jnp.float32).reshape(
        row_count, value_heads, head_width
    )
    value_low = (
        jnp.dot(normed_one_low, attention_set[3], preferred_element_type=jnp.float32)
        .astype(jnp.bfloat16)
        .reshape(row_count, value_heads, head_width)
    )
    query_normed, query_normal, query_inverse = rms_forward(query_raw, gain_query)
    key_normed, key_normal, key_inverse = rms_forward(key_raw, gain_key)
    query_low = (
        (rotate(query_normed, cosine, sine) * scale)
        .astype(jnp.bfloat16)
        .reshape(row_count, value_heads, group_size, head_width)
    )
    key_low = rotate(key_normed, cosine, sine).astype(jnp.bfloat16)
    scores = masked_scores(query_low, key_low)
    row_top = jnp.max(scores, axis=-1, keepdims=True)
    exp_scores = jnp.exp(scores - row_top)
    row_total = jnp.sum(exp_scores, axis=-1, keepdims=True)
    probs_low = (exp_scores / row_total).astype(jnp.bfloat16)
    log_total = row_top + jnp.log(row_total)
    mixed = jnp.einsum("kgqs,skd->qkgd", probs_low, value_low, preferred_element_type=jnp.float32)
    mixed_low = mixed.reshape(row_count, query_heads * head_width).astype(jnp.bfloat16)
    branch = jnp.dot(mixed_low, attention_set[4], preferred_element_type=jnp.float32)
    middle = inputs_wide + branch
    gain_two = feed_set[0].astype(jnp.float32)
    normed_two, normal_two, inverse_two = rms_forward(middle, gain_two)
    normed_two_low = normed_two.astype(jnp.bfloat16)
    gate_value = jnp.dot(normed_two_low, feed_set[1], preferred_element_type=jnp.float32)
    up_value = jnp.dot(normed_two_low, feed_set[2], preferred_element_type=jnp.float32)
    hidden_low = (jax.nn.silu(gate_value) * up_value).astype(jnp.bfloat16)
    down_value = jnp.dot(hidden_low, feed_set[3], preferred_element_type=jnp.float32)
    layer_out = ((middle + down_value) * valid_rows).astype(jnp.bfloat16)
    feed_set = (
        lax.all_gather(feed_gain, "fsdp", axis=0, tiled=True),
        lax.all_gather(gate_weight, "fsdp", axis=0, tiled=True),
        lax.all_gather(up_weight, "fsdp", axis=0, tiled=True),
        lax.all_gather(down_weight, "fsdp", axis=0, tiled=True),
    )
    grad_top = cotangent.astype(jnp.float32) * valid_rows
    grad_down_low = grad_top.astype(jnp.bfloat16)
    down_grad = inner_rows(hidden_low, grad_down_low)
    grad_hidden = times_transposed(grad_down_low, feed_set[3])
    sigmoid_gate = jax.nn.sigmoid(gate_value)
    grad_gate_low = (
        grad_hidden * up_value * sigmoid_gate * (1.0 + gate_value * (1.0 - sigmoid_gate))
    ).astype(jnp.bfloat16)
    grad_up_low = (grad_hidden * (gate_value * sigmoid_gate)).astype(jnp.bfloat16)
    gate_grad = inner_rows(normed_two_low, grad_gate_low)
    up_grad = inner_rows(normed_two_low, grad_up_low)
    grad_normed_two = times_transposed(grad_gate_low, feed_set[1]) + times_transposed(
        grad_up_low, feed_set[2]
    )
    grad_from_two, gain_two_terms = rms_backward(grad_normed_two, normal_two, inverse_two, gain_two)
    feed_gain_grad = jnp.sum(gain_two_terms, axis=0)
    grad_middle = grad_top + grad_from_two
    feed_parts = (
        lax.psum_scatter(
            feed_gain_grad.astype(jnp.bfloat16), "fsdp", scatter_dimension=0, tiled=True
        ).astype(jnp.float32),
        lax.psum_scatter(
            gate_grad.astype(jnp.bfloat16), "fsdp", scatter_dimension=0, tiled=True
        ).astype(jnp.float32),
        lax.psum_scatter(
            up_grad.astype(jnp.bfloat16), "fsdp", scatter_dimension=0, tiled=True
        ).astype(jnp.float32),
        lax.psum_scatter(
            down_grad.astype(jnp.bfloat16), "fsdp", scatter_dimension=0, tiled=True
        ).astype(jnp.float32),
    )
    attention_set = (
        lax.all_gather(attention_gain, "fsdp", axis=0, tiled=True),
        lax.all_gather(query_weight, "fsdp", axis=0, tiled=True),
        lax.all_gather(key_weight, "fsdp", axis=0, tiled=True),
        lax.all_gather(value_weight, "fsdp", axis=0, tiled=True),
        lax.all_gather(output_weight, "fsdp", axis=0, tiled=True),
    )
    grad_branch_low = grad_middle.astype(jnp.bfloat16)
    output_grad = inner_rows(mixed_low, grad_branch_low)
    grad_mixed_low = (
        times_transposed(grad_branch_low, attention_set[4])
        .astype(jnp.bfloat16)
        .reshape(row_count, value_heads, group_size, head_width)
    )
    scores_again = masked_scores(query_low, key_low)
    probs_again = jnp.exp(scores_again - log_total)
    probs_again_low = probs_again.astype(jnp.bfloat16)
    grad_probs = jnp.einsum(
        "qkgd,skd->kgqs", grad_mixed_low, value_low, preferred_element_type=jnp.float32
    )
    row_term = jnp.sum(probs_again * grad_probs, axis=-1, keepdims=True)
    grad_scores_low = (probs_again * (grad_probs - row_term)).astype(jnp.bfloat16)
    grad_query_rot = (
        jnp.einsum(
            "kgqs,skd->qkgd", grad_scores_low, key_low, preferred_element_type=jnp.float32
        ).reshape(row_count, query_heads, head_width)
        * scale
    )
    grad_key_rot = jnp.einsum(
        "kgqs,qkgd->skd", grad_scores_low, query_low, preferred_element_type=jnp.float32
    )
    grad_value_low = (
        jnp.einsum(
            "kgqs,qkgd->skd", probs_again_low, grad_mixed_low, preferred_element_type=jnp.float32
        )
        .astype(jnp.bfloat16)
        .reshape(row_count, value_heads * head_width)
    )
    grad_query_raw, query_gain_terms = rms_backward(
        unrotate(grad_query_rot, cosine, sine), query_normal, query_inverse, gain_query
    )
    grad_key_raw, key_gain_terms = rms_backward(
        unrotate(grad_key_rot, cosine, sine), key_normal, key_inverse, gain_key
    )
    query_gain_grad = jnp.sum(query_gain_terms, axis=(0, 1))
    key_gain_grad = jnp.sum(key_gain_terms, axis=(0, 1))
    grad_query_low = grad_query_raw.astype(jnp.bfloat16).reshape(
        row_count, query_heads * head_width
    )
    grad_key_low = grad_key_raw.astype(jnp.bfloat16).reshape(row_count, value_heads * head_width)
    query_grad = inner_rows(normed_one_low, grad_query_low)
    key_grad = inner_rows(normed_one_low, grad_key_low)
    value_grad = inner_rows(normed_one_low, grad_value_low)
    grad_normed_one = (
        times_transposed(grad_query_low, attention_set[1])
        + times_transposed(grad_key_low, attention_set[2])
        + times_transposed(grad_value_low, attention_set[3])
    )
    grad_from_one, gain_one_terms = rms_backward(grad_normed_one, normal_one, inverse_one, gain_one)
    attention_gain_grad = jnp.sum(gain_one_terms, axis=0)
    input_grad = grad_middle + grad_from_one
    head_terms = jnp.concatenate([query_gain_grad, key_gain_grad])
    head_tiles = jnp.broadcast_to(head_terms[None, :], (lax.axis_size("fsdp"), head_terms.shape[0]))
    attention_parts = (
        lax.psum_scatter(attention_gain_grad, "fsdp", scatter_dimension=0, tiled=True),
        lax.psum_scatter(query_grad, "fsdp", scatter_dimension=0, tiled=True),
        lax.psum_scatter(key_grad, "fsdp", scatter_dimension=0, tiled=True),
        lax.psum_scatter(value_grad, "fsdp", scatter_dimension=0, tiled=True),
        lax.psum_scatter(output_grad, "fsdp", scatter_dimension=0, tiled=True),
        lax.psum_scatter(head_tiles, "fsdp", scatter_dimension=0, tiled=True),
    )
    finals = (
        lax.psum(feed_parts[0].astype(jnp.bfloat16), "rep").astype(jnp.float32),
        lax.psum(feed_parts[1].astype(jnp.bfloat16), "rep").astype(jnp.float32),
        lax.psum(feed_parts[2].astype(jnp.bfloat16), "rep").astype(jnp.float32),
        lax.psum(feed_parts[3].astype(jnp.bfloat16), "rep").astype(jnp.float32),
        lax.psum(attention_parts[0].astype(jnp.bfloat16), "rep").astype(jnp.float32),
        lax.psum(attention_parts[1].astype(jnp.bfloat16), "rep").astype(jnp.float32),
        lax.psum(attention_parts[2].astype(jnp.bfloat16), "rep").astype(jnp.float32),
        lax.psum(attention_parts[3].astype(jnp.bfloat16), "rep").astype(jnp.float32),
        lax.psum(attention_parts[4].astype(jnp.bfloat16), "rep").astype(jnp.float32),
        lax.psum(attention_parts[5].astype(jnp.bfloat16), "rep").astype(jnp.float32),
    )
    head_sum = finals[9]
    return (
        layer_out,
        input_grad,
        finals[4],
        finals[5],
        finals[6],
        finals[7],
        head_sum[0, :head_width],
        head_sum[0, head_width:],
        finals[8],
        finals[0],
        finals[1],
        finals[2],
        finals[3],
    )


def solution(mesh):
    return jax.shard_map(
        per_device,
        mesh=mesh,
        in_specs=(
            P(("fsdp", "rep"), None),
            P(),
            P(),
            P("fsdp"),
            P("fsdp", None),
            P("fsdp", None),
            P("fsdp", None),
            P(),
            P(),
            P("fsdp", None),
            P("fsdp"),
            P("fsdp", None),
            P("fsdp", None),
            P("fsdp", None),
            P(("fsdp", "rep"), None),
        ),
        out_specs=(
            P(("fsdp", "rep"), None),
            P(("fsdp", "rep"), None),
            P("fsdp"),
            P("fsdp", None),
            P("fsdp", None),
            P("fsdp", None),
            P(),
            P(),
            P("fsdp", None),
            P("fsdp"),
            P("fsdp", None),
            P("fsdp", None),
            P("fsdp", None),
        ),
        check_vma=False,
    )
```

profile of v0, /device:TPU:0, one launch (start us, length us, event | category | flops | bytes accessed | tf_op | source)
XLA Modules:
  0.0 2013.2 jit_solution(7309984929366544705)
XLA Ops:
  13.9 10.4 all-gather
  24.5 9.1 all-gather.1
  37.5 11.7 all-gather.12.cloned.1.call-done
  60.8 26.9 %all-gather.10.cloned.1.call-done = bf16[2048,1024]{1,0:T(8,128)(2,1)} async-done(((bf16[256,1024]{1,0:T(8,128)(2,1)}), bf16[2048,1024]{1,0:T(8,128)(2,1)}) %all-gather.10.cloned.1.call-update) | async-done | bytes 4194320 | tf_op jit(solution)/shard_map/all_gather | solution.py:98
  95.1 48.8 %all-gather.14.cloned.1.call-done = bf16[2048,2048]{1,0:T(8,128)(2,1)} async-done(((bf16[256,2048]{1,0:T(8,128)(2,1)}), bf16[2048,2048]{1,0:T(8,128)(2,1)}) %all-gather.14.cloned.1.call-update) | async-done | bytes 8388624 | tf_op jit(solution)/shard_map/all_gather | solution.py:96
  143.9 8.5 fusion.59
  166.7 33.3 %all-gather.16.cloned.1.call-done = bf16[2048,2048]{1,0:T(8,128)(2,1)} async-done(((bf16[256,2048]{1,0:T(8,128)(2,1)}), bf16[2048,2048]{1,0:T(8,128)(2,1)}) %all-gather.16.cloned.1.call-update) | async-done | bytes 8388624 | tf_op jit(solution)/shard_map/all_gather | solution.py:99
  208.0 118.9 %all-gather.18.cloned.1.call-done = bf16[2048,6144]{1,0:T(8,128)(2,1)} async-done(((bf16[256,6144]{1,0:T(8,128)(2,1)}), bf16[2048,6144]{1,0:T(8,128)(2,1)}) %all-gather.18.cloned.1.call-update) | async-done | bytes 25165840 | tf_op jit(solution)/shard_map/all_gather | solution.py:103
  326.9 17.2 fusion.63
  344.1 109.8 %all-gather.20.cloned.1.call-done = bf16[2048,6144]{1,0:T(8,128)(2,1)} async-done(((bf16[256,6144]{1,0:T(8,128)(2,1)}), bf16[2048,6144]{1,0:T(8,128)(2,1)}) %all-gather.20.cloned.1.call-update) | async-done | bytes 25165840 | tf_op jit(solution)/shard_map/all_gather | solution.py:104
  453.9 16.9 fusion.64
  470.8 110.2 %all-gather.22.cloned.1.call-done = bf16[6144,2048]{1,0:T(8,128)(2,1)} async-done(((bf16[768,2048]{1,0:T(8,128)(2,1)}), bf16[6144,2048]{1,0:T(8,128)(2,1)}) %all-gather.22.cloned.1.call-update) | async-done | bytes 25165840 | tf_op jit(solution)/shard_map/all_gather | solution.py:105
  581.0 25.0 %multiply_convert_fusion = (bf16[384,6144]{1,0:T(8,128)(2,1)}, bf16[384,6144]{1,0:T(8,128)(2,1)}, bf16[384,6144]{1,0:T(8,128)(2,1)}) fusion(f32[384,6144]{1,0:T(8,128)} %fusion.63, f32[384,6144]{1,0:T(8,128)} %fusion.64, bf16[6144,2048]{1,0:T(8,128)(2,1)} %all-gather.22.cloned.1.call-done, bf16[384,2048]{1,0:T(8,128)(2,1)S(1)} %copy-done.41, f32[384]{0:T(512)S(1)} %fusion.50), kind=kOutput, calls=%fused_computation.10 | convolution fusion | flops 9701425152 | bytes 59770368 | tf_op jit(solution)/shard_map/dot_general | solution.py:51
  606.0 17.4 fusion.65
  623.4 19.4 multiply_reduce_fusion
  647.3 10.1 convolution_convert_fusion.3
  666.9 11.1 fusion.2
  756.3 8.5 fusion.57
  766.2 12.0 fusion.39
  780.0 19.7 convolution_convert_fusion.2
  799.7 19.1 convolution_convert_fusion.1
  820.2 19.4 convolution_convert_fusion
  844.0 114.1 %reduce-scatter.8.cloned.1.call-done = f32[256,2048]{1,0:T(8,128)} async-done(((f32[2048,2048]{1,0:T(8,128)}), f32[256,2048]{1,0:T(8,128)}) %reduce-scatter.8.cloned.1.call-update) | async-done | bytes 2097168 | tf_op jit(solution)/shard_map/reduce_scatter | solution.py:250
  960.8 117.1 %reduce-scatter.14.cloned.1.call-done = f32[256,2048]{1,0:T(8,128)} async-done(((f32[2048,2048]{1,0:T(8,128)}), f32[256,2048]{1,0:T(8,128)}) %reduce-scatter.14.cloned.1.call-update) | async-done | bytes 2097168 | tf_op jit(solution)/shard_map/reduce_scatter | solution.py:253
  1080.6 157.1 %reduce-scatter.16.cloned.1.call-done = bf16[256,6144]{1,0:T(8,128)(2,1)} async-done(((bf16[2048,6144]{1,0:T(8,128)(2,1)}), bf16[256,6144]{1,0:T(8,128)(2,1)}) %reduce-scatter.16.cloned.1.call-update) | async-done | bytes 3145744 | tf_op jit(solution)/shard_map/reduce_scatter | solution.py:175
  1237.7 160.0 %reduce-scatter.18.cloned.1.call-done = bf16[256,6144]{1,0:T(8,128)(2,1)} async-done(((bf16[2048,6144]{1,0:T(8,128)(2,1)}), bf16[256,6144]{1,0:T(8,128)(2,1)}) %reduce-scatter.18.cloned.1.call-update) | async-done | bytes 3145744 | tf_op jit(solution)/shard_map/reduce_scatter | solution.py:178
  1397.6 159.8 %reduce-scatter.20.cloned.1.call-done = bf16[768,2048]{1,0:T(8,128)(2,1)} async-done(((bf16[6144,2048]{1,0:T(8,128)(2,1)}), bf16[768,2048]{1,0:T(8,128)(2,1)}) %reduce-scatter.20.cloned.1.call-update) | async-done | bytes 3145744 | tf_op jit(solution)/shard_map/reduce_scatter | solution.py:181
  1573.8 24.5 %all-reduce.3 = (bf16[2048]{0:T(1024)(128)(2,1)S(1)}, bf16[8,256]{1,0:T(8,128)(2,1)S(1)}) all-reduce(f32[2048]{0:T(1024)S(1)} %get-tuple-element.17, f32[8,256]{1,0:T(8,128)S(1)} %broadcast_in_dim.12), channel_id=2, replica_groups=mesh['fsdp'=8,'rep'=4] {'fsdp'}, use_global_device_ids=true, to_apply=%region_12.13.clone | all-reduce | flops 4096 | bytes 24576
  1598.4 12.6 all-reduce.2
  1611.7 12.9 all-reduce.4
  1631.9 17.1 multiply_convert_fusion.3
  1649.0 339.5 %all-reduce.8.cloned.1.call-done = (bf16[256,2048]{1,0:T(8,128)(2,1)}, bf16[256,1024]{1,0:T(8,128)(2,1)}, bf16[256,1024]{1,0:T(8,128)(2,1)}, bf16[256,2048]{1,0:...) async-done(((bf16[256,2048]{1,0:T(8,128)(2,1)}, bf16[256,1024]{1,0:T(8,128)(2,1)}, bf16[256,1024]{1,0:T(8,128)(2,1)}, ...) | async-done | bytes 12582928 | tf_op jit(solution)/shard_map/psum | solution.py:262
  (285 shorter events, 197.4 us)
Async XLA Ops:
  7.2 42.0 %all-gather.12.cloned.1.call-start = ((), (), s32[]{:S(2)}) async-start(), calls=%async_computation.8 | async-start | bytes 4718592 | tf_op jit(solution)/shard_map/all_gather | solution.py:97
  7.9 79.8 %all-gather.10.cloned.1.call-start = ((), (), s32[]{:S(2)}) async-start(), calls=%async_computation.7 | async-start | bytes 4718592 | tf_op jit(solution)/shard_map/all_gather | solution.py:98
  8.7 135.2 %all-gather.14.cloned.1.call-start = ((), (), s32[]{:S(2)}) async-start(), calls=%async_computation.9 | async-start | bytes 9437184 | tf_op jit(solution)/shard_map/all_gather | solution.py:96
  9.4 190.5 %all-gather.16.cloned.1.call-start = ((), (), s32[]{:S(2)}) async-start(), calls=%async_computation.10 | async-start | bytes 9437184 | tf_op jit(solution)/shard_map/all_gather | solution.py:99
  10.0 316.9 %all-gather.18.cloned.1.call-start = ((), (), s32[]{:S(2)}) async-start(), calls=%async_computation.11 | async-start | bytes 28311552 | tf_op jit(solution)/shard_map/all_gather | solution.py:103
  10.6 13.8 copy-start.74
  10.6 23.6 %copy-start.75 = (s32[32]{0:T(128)S(1)}, s32[32]{0:T(128)}, u32[]{:S(2)}) copy-start(s32[32]{0:T(128)} %param.16) | copy-start | bytes 388
  10.6 26.5 %copy-start.3 = (bf16[384,2048]{1,0:T(8,128)(2,1)S(1)}, bf16[384,2048]{1,0:T(8,128)(2,1)}, u32[]{:S(2)}) copy-start(bf16[384,2048]{1,0:T(8,128)(2,1)} %param.15) | copy-start | bytes 4718596
  10.6 443.2 %all-gather.20.cloned.1.call-start = ((), (), s32[]{:S(2)}) async-start(), calls=%async_computation.12 | async-start | bytes 28311552 | tf_op jit(solution)/shard_map/all_gather | solution.py:104
  11.2 569.8 %all-gather.22.cloned.1.call-start = ((), (), s32[]{:S(2)}) async-start(), calls=%async_computation.13 | async-start | bytes 28311552 | tf_op jit(solution)/shard_map/all_gather | solution.py:105
  12.0 827.8 %reduce-scatter.10.cloned.1.call-start = ((), (), s32[]{:S(2)}) async-start(), calls=%async_computation.15 | async-start | bytes 9437184 | tf_op jit(solution)/shard_map/reduce_scatter | solution.py:251
  24.4 119.5 %copy-start.46 = (f32[8,1,256]{2,1,0:T(1,128)}, f32[8,1,256]{2,1,0:T(1,128)S(1)}, u32[]{:S(2)}) copy-start(f32[8,1,256]{2,1,0:T(1,128)S(1)} %convert_element_type.230) | copy-start | bytes 24580
  24.4 132.5 %copy-start.62 = (f32[128]{0:T(128)}, f32[128]{0:T(128)S(1)}, u32[]{:S(2)}) copy-start(f32[128]{0:T(128)S(1)} %convert_element_type.187) | copy-start | bytes 1540
  24.4 68.9 %copy-start.66 = (f32[128]{0:T(128)}, f32[128]{0:T(128)S(1)}, u32[]{:S(2)}) copy-start(f32[128]{0:T(128)S(1)} %convert_element_type.183) | copy-start | bytes 1540
  35.5 607.3 %copy-start.64 = (f32[384]{0:T(512)}, f32[384]{0:T(512)S(1)}, u32[]{:S(2)}) copy-start(f32[384]{0:T(512)S(1)} %fusion.50) | copy-start | bytes 4612
  37.1 119.8 %copy-start.31 = (f32[384,128]{0,1:T(8,128)}, f32[384,128]{0,1:T(8,128)S(1)}, u32[]{:S(2)}) copy-start(f32[384,128]{0,1:T(8,128)S(1)} %get-tuple-element.48) | copy-start | bytes 589828
  37.5 106.4 %copy-start.55 = (f32[384]{0:T(512)}, f32[384]{0:T(512)S(1)}, u32[]{:S(2)}) copy-start(f32[384]{0:T(512)S(1)} %add_rsqrt_fusion.3) | copy-start | bytes 4612
  56.6 36.7 %copy-start.8 = (f32[384,8,128]{0,2,1:T(8,128)}, f32[384,8,128]{0,2,1:T(8,128)S(1)}, u32[]{:S(2)}) copy-start(f32[384,8,128]{0,2,1:T(8,128)S(1)} %copy.120) | copy-start | bytes 4718596
  163.9 36.1 %copy-start.4 = (bf16[384,2048]{1,0:T(8,128)(2,1)S(1)}, bf16[384,2048]{1,0:T(8,128)(2,1)}, u32[]{:S(2)}) copy-start(bf16[384,2048]{1,0:T(8,128)(2,1)} %param.15) | copy-start | bytes 4718596
  166.7 39.3 %copy-start.22 = (bf16[8,128,2,384]{3,1,2,0:T(8,128)(2,1)}, bf16[8,128,2,384]{3,1,2,0:T(8,128)(2,1)S(1)}, u32[]{:S(2)}) copy-start(bf16[8,128,2,384]{3,1,2,0:T(8,128)(2,1)S(1)} %fusion.32) | copy-start | bytes 4718596
  208.0 245.9 %copy-start.44 = (bf16[384,2048]{1,0:T(8,128)(2,1)}, bf16[384,2048]{1,0:T(8,128)(2,1)S(1)}, u32[]{:S(2)}) copy-start(bf16[384,2048]{1,0:T(8,128)(2,1)S(1)} %multiply_convert_fusion.4) | copy-start | bytes 4718596
  344.1 236.9 %copy-start.41 = (bf16[384,2048]{1,0:T(8,128)(2,1)S(1)}, bf16[384,2048]{1,0:T(8,128)(2,1)}, u32[]{:S(2)}) copy-start(bf16[384,2048]{1,0:T(8,128)(2,1)} %param.29) | copy-start | bytes 4718596
  606.0 17.4 copy-start.11
  623.4 19.4 copy-start.42
  691.7 150.1 %reduce-scatter.12.cloned.1.call-start = ((), (), s32[]{:S(2)}) async-start(), calls=%async_computation.16 | async-start | bytes 9437184 | tf_op jit(solution)/shard_map/reduce_scatter | solution.py:252
  705.4 252.7 %reduce-scatter.8.cloned.1.call-start = ((), (), s32[]{:S(2)}) async-start(), calls=%async_computation.14 | async-start | bytes 18874368 | tf_op jit(solution)/shard_map/reduce_scatter | solution.py:250
  764.8 313.0 %reduce-scatter.14.cloned.1.call-start = ((), (), s32[]{:S(2)}) async-start(), calls=%async_computation.17 | async-start | bytes 18874368 | tf_op jit(solution)/shard_map/reduce_scatter | solution.py:253
  778.3 459.4 %reduce-scatter.16.cloned.1.call-start = ((), (), s32[]{:S(2)}) async-start(), calls=%async_computation.18 | async-start | bytes 28311552 | tf_op jit(solution)/shard_map/reduce_scatter | solution.py:175
  799.7 597.9 %reduce-scatter.18.cloned.1.call-start = ((), (), s32[]{:S(2)}) async-start(), calls=%async_computation.19 | async-start | bytes 28311552 | tf_op jit(solution)/shard_map/reduce_scatter | solution.py:178
  818.8 738.6 %reduce-scatter.20.cloned.1.call-start = ((), (), s32[]{:S(2)}) async-start(), calls=%async_computation.20 | async-start | bytes 28311552 | tf_op jit(solution)/shard_map/reduce_scatter | solution.py:181
  839.7 1148.8 %all-reduce.8.cloned.1.call-start = ((), (), s32[]{:S(2)}) async-start(), calls=%async_computation.21 | async-start | bytes 25165824 | tf_op jit(solution)/shard_map/psum | solution.py:262
  1569.6 28.8 %copy-start.68 = (bf16[2048]{0:T(1024)(128)(2,1)S(1)}, bf16[2048]{0:T(1024)(128)(2,1)}, u32[]{:S(2)}) copy-start(bf16[2048]{0:T(1024)(128)(2,1)} %get-tuple-element.15) | copy-start | bytes 12292
  (60 other events, 201.7 us)
Sparse Core Ops, SparseCore 0:
  9.9 39.2 all-gather.11
  51.1 36.5 all-gather.9
  89.6 54.2 all-gather.13
  145.6 54.2 all-gather.15
  201.7 125.1 all-gather.17
  328.6 125.1 all-gather.19
  455.7 125.1 all-gather.21
  691.9 71.4 reduce-scatter.9
  766.9 71.5 reduce-scatter.11
  841.8 116.1 reduce-scatter.7
  961.6 116.1 reduce-scatter.13
  1081.3 156.2 reduce-scatter.15
  1241.3 156.3 reduce-scatter.17
  1401.1 156.3 reduce-scatter.19
  1561.9 426.5 all-reduce.7
where the time goes:
time: 2020 us; the launch traced here: 2010 us
  waiting for transfers between devices  1510 us (75%)
  matrix products  276 us (14%)
  other arithmetic  83.4 us (4%)
  blocking collectives  69.5 us (3%)
  local copies, waits for them, and re-layouts  54 us (3%)
    psum x1, waiting for transfers between devices, per_device(): lax.psum(attention_parts[1].astype(jnp.bfloat16), 'rep').astype(jnp.float32)  339 us
    reduce_scatter x1, waiting for transfers between devices, per_device(): lax.psum_scatter(up_grad.astype(jnp.bfloat16), 'fsdp', scatter_dimension=...  160 us
    reduce_scatter x1, waiting for transfers between devices, per_device(): lax.psum_scatter(down_grad.astype(jnp.bfloat16), 'fsdp', scatter_dimensio...  160 us
    reduce_scatter x1, waiting for transfers between devices, per_device(): lax.psum_scatter(gate_grad.astype(jnp.bfloat16), 'fsdp', scatter_dimensio...  157 us
    all_gather x1, waiting for transfers between devices, per_device(): lax.all_gather(gate_weight, 'fsdp', axis=0, tiled=True)  119 us
    reduce_scatter x1, waiting for transfers between devices, per_device(): lax.psum_scatter(output_grad, 'fsdp', scatter_dimension=0, tiled=True)  117 us
    reduce_scatter x1, waiting for transfers between devices, per_device(): lax.psum_scatter(query_grad, 'fsdp', scatter_dimension=0, tiled=True)  114 us
    all_gather x1, waiting for transfers between devices, per_device(): lax.all_gather(down_weight, 'fsdp', axis=0, tiled=True)  110 us
  transfers between devices with their start and end apart: 15, of which 13 were waited for; matrix products, arithmetic and copies ran while one was open for 13% of the time, Pallas kernels for 0%

commit v1 on v0

--- a/solution.py
+++ b/solution.py
@@ -98,12 +98,8 @@
         lax.all_gather(value_weight, "fsdp", axis=0, tiled=True),
         lax.all_gather(output_weight, "fsdp", axis=0, tiled=True),
     )
-    feed_set = (
-        lax.all_gather(feed_gain, "fsdp", axis=0, tiled=True),
-        lax.all_gather(gate_weight, "fsdp", axis=0, tiled=True),
-        lax.all_gather(up_weight, "fsdp", axis=0, tiled=True),
-        lax.all_gather(down_weight, "fsdp", axis=0, tiled=True),
-    )
+    gate_block = lax.all_to_all(gate_weight, "fsdp", 1, 0, tiled=True)
+    up_block = lax.all_to_all(up_weight, "fsdp", 1, 0, tiled=True)
     inputs_wide = tokens.astype(jnp.float32)
     gain_one = attention_set[0].astype(jnp.float32)
     normed_one, normal_one, inverse_one = rms_forward(inputs_wide, gain_one)
@@ -137,34 +133,32 @@
     mixed_low = mixed.reshape(row_count, query_heads * head_width).astype(jnp.bfloat16)
     branch = jnp.dot(mixed_low, attention_set[4], preferred_element_type=jnp.float32)
     middle = inputs_wide + branch
-    gain_two = feed_set[0].astype(jnp.float32)
+    gain_two = lax.all_gather(feed_gain, "fsdp", axis=0, tiled=True).astype(jnp.float32)
     normed_two, normal_two, inverse_two = rms_forward(middle, gain_two)
     normed_two_low = normed_two.astype(jnp.bfloat16)
-    gate_value = jnp.dot(normed_two_low, feed_set[1], preferred_element_type=jnp.float32)
-    up_value = jnp.dot(normed_two_low, feed_set[2], preferred_element_type=jnp.float32)
+    normed_two_group = lax.all_gather(normed_two_low, "fsdp", axis=0, tiled=True)
+    gate_value = jnp.dot(normed_two_group, gate_block, preferred_element_type=jnp.float32)
+    up_value = jnp.dot(normed_two_group, up_block, preferred_element_type=jnp.float32)
     hidden_low = (jax.nn.silu(gate_value) * up_value).astype(jnp.bfloat16)
-    down_value = jnp.dot(hidden_low, feed_set[3], preferred_element_type=jnp.float32)
+    down_part = jnp.dot(hidden_low, down_weight, preferred_element_type=jnp.float32)
+    down_value = lax.psum_scatter(down_part, "fsdp", scatter_dimension=0, tiled=True)
     layer_out = ((middle + down_value) * valid_rows).astype(jnp.bfloat16)
-    feed_set = (
-        lax.all_gather(feed_gain, "fsdp", axis=0, tiled=True),
-        lax.all_gather(gate_weight, "fsdp", axis=0, tiled=True),
-        lax.all_gather(up_weight, "fsdp", axis=0, tiled=True),
-        lax.all_gather(down_weight, "fsdp", axis=0, tiled=True),
-    )
     grad_top = cotangent.astype(jnp.float32) * valid_rows
     grad_down_low = grad_top.astype(jnp.bfloat16)
-    down_grad = inner_rows(hidden_low, grad_down_low)
-    grad_hidden = times_transposed(grad_down_low, feed_set[3])
+    grad_down_group = lax.all_gather(grad_down_low, "fsdp", axis=0, tiled=True)
+    down_grad = inner_rows(hidden_low, grad_down_group)
+    grad_hidden = times_transposed(grad_down_group, down_weight)
     sigmoid_gate = jax.nn.sigmoid(gate_value)
     grad_gate_low = (
         grad_hidden * up_value * sigmoid_gate * (1.0 + gate_value * (1.0 - sigmoid_gate))
     ).astype(jnp.bfloat16)
     grad_up_low = (grad_hidden * (gate_value * sigmoid_gate)).astype(jnp.bfloat16)
-    gate_grad = inner_rows(normed_two_low, grad_gate_low)
-    up_grad = inner_rows(normed_two_low, grad_up_low)
-    grad_normed_two = times_transposed(grad_gate_low, feed_set[1]) + times_transposed(
-        grad_up_low, feed_set[2]
-    )
+    gate_grad_block = inner_rows(normed_two_group, grad_gate_low)
+    up_grad_block = inner_rows(normed_two_group, grad_up_low)
+    grad_normed_part = times_transposed(grad_gate_low, gate_block) + times_transposed(
+        grad_up_low, up_block
+    )
+    grad_normed_two = lax.psum_scatter(grad_normed_part, "fsdp", scatter_dimension=0, tiled=True)
     grad_from_two, gain_two_terms = rms_backward(grad_normed_two, normal_two, inverse_two, gain_two)
     feed_gain_grad = jnp.sum(gain_two_terms, axis=0)
     grad_middle = grad_top + grad_from_two
@@ -172,22 +166,13 @@
         lax.psum_scatter(
             feed_gain_grad.astype(jnp.bfloat16), "fsdp", scatter_dimension=0, tiled=True
         ).astype(jnp.float32),
-        lax.psum_scatter(
-            gate_grad.astype(jnp.bfloat16), "fsdp", scatter_dimension=0, tiled=True
-        ).astype(jnp.float32),
-        lax.psum_scatter(
-            up_grad.astype(jnp.bfloat16), "fsdp", scatter_dimension=0, tiled=True
-        ).astype(jnp.float32),
-        lax.psum_scatter(
-            down_grad.astype(jnp.bfloat16), "fsdp", scatter_dimension=0, tiled=True
-        ).astype(jnp.float32),
-    )
-    attention_set = (
-        lax.all_gather(attention_gain, "fsdp", axis=0, tiled=True),
-        lax.all_gather(query_weight, "fsdp", axis=0, tiled=True),
-        lax.all_gather(key_weight, "fsdp", axis=0, tiled=True),
-        lax.all_gather(value_weight, "fsdp", axis=0, tiled=True),
-        lax.all_gather(output_weight, "fsdp", axis=0, tiled=True),
+        lax.all_to_all(gate_grad_block.astype(jnp.bfloat16), "fsdp", 0, 1, tiled=True).astype(
+            jnp.float32
+        ),
+        lax.all_to_all(up_grad_block.astype(jnp.bfloat16), "fsdp", 0, 1, tiled=True).astype(
+            jnp.float32
+        ),
+        down_grad,
     )
     grad_branch_low = grad_middle.astype(jnp.bfloat16)
     output_grad = inner_rows(mixed_low, grad_branch_low)
@@ -245,12 +230,15 @@
     input_grad = grad_middle + grad_from_one
     head_terms = jnp.concatenate([query_gain_grad, key_gain_grad])
     head_tiles = jnp.broadcast_to(head_terms[None, :], (lax.axis_size("fsdp"), head_terms.shape[0]))
+    low_sum = lambda v: lax.psum_scatter(
+        v.astype(jnp.bfloat16), "fsdp", scatter_dimension=0, tiled=True
+    )
     attention_parts = (
         lax.psum_scatter(attention_gain_grad, "fsdp", scatter_dimension=0, tiled=True),
-        lax.psum_scatter(query_grad, "fsdp", scatter_dimension=0, tiled=True),
-        lax.psum_scatter(key_grad, "fsdp", scatter_dimension=0, tiled=True),
-        lax.psum_scatter(value_grad, "fsdp", scatter_dimension=0, tiled=True),
-        lax.psum_scatter(output_grad, "fsdp", scatter_dimension=0, tiled=True),
+        low_sum(query_grad),
+        low_sum(key_grad),
+        low_sum(value_grad),
+        low_sum(output_grad),
         lax.psum_scatter(head_tiles, "fsdp", scatter_dimension=0, tiled=True),
     )
     finals = (

time: 2020 us -> 1590 us (0.79)
  waiting for transfers between devices: 1510 us -> 1050 us
  local copies, waits for them, and re-layouts: 54 us -> 78.4 us
    reduce_scatter x7 -> x6, waiting for transfers between devices: 708 us -> 359 us  [the longest x1 157 us: per_device(): lax.psum_scatter(down_part, 'fsdp', scatter_dimension=0, tiled=True)]
    all_gather x3 -> x2, waiting for transfers between devices: 339 us -> 42.5 us  [the longest x1 42.5 us: per_device(): grad_down_group = lax.all_gather(grad_down_low, 'fsdp', axis=0, tiled=True)]
    all_to_all x0 -> x4, waiting for transfers between devices: none -> 172 us  [the longest x1 58.2 us: per_device(): up_block = lax.all_to_all(up_weight, 'fsdp', 1, 0, tiled=True)]
    all_gather x1, waiting for transfers between devices: 11.7 us -> 32.9 us  [per_device(): lax.all_gather(key_weight, 'fsdp', axis=0, tiled=True)]
  transfers between devices with their start and end apart: 15 -> 17, of which waited for: 13 -> 13; matrix products, arithmetic and copies ran while one was open for 13% -> 19% of each run, Pallas kernels for 0% -> 0%
where the time goes in v1:
time: 1590 us; the launch traced here: 1580 us
  waiting for transfers between devices  1050 us (66%)
  matrix products  257 us (16%)
  other arithmetic  93 us (6%)
  local copies, waits for them, and re-layouts  78.4 us (5%)
  blocking collectives  68.8 us (4%)
  starting transfers between devices  19.4 us (1%)
  between operations  17.6 us (1%)
    psum x1, waiting for transfers between devices, per_device(): lax.psum(attention_parts[1].astype(jnp.bfloat16), 'rep').astype(jnp.float32)  357 us
    reduce_scatter x1, waiting for transfers between devices, per_device(): lax.psum_scatter(down_part, 'fsdp', scatter_dimension=0, tiled=True)  157 us
    reduce_scatter x1, waiting for transfers between devices, per_device(): lax.psum_scatter(grad_normed_part, 'fsdp', scatter_dimension=0, tiled=True)  136 us
    dot_general x7, matrix products, times_transposed(): lax.dot_general(left, right, (((1,), (1,)), ((), ())), preferred_element_...  83.8 us
    dot_general x7, matrix products, inner_rows(): lax.dot_general(left, right, (((0,), (0,)), ((), ())), preferred_element_...  73.1 us
    reduce_scatter x4, waiting for transfers between devices, per_device(): lax.psum_scatter(v.astype(jnp.bfloat16), 'fsdp', scatter_dimension=0, til...  65.4 us
    all_to_all x1, waiting for transfers between devices, per_device(): up_block = lax.all_to_all(up_weight, 'fsdp', 1, 0, tiled=True)  58.2 us
    all_to_all x1, waiting for transfers between devices, per_device(): lax.all_to_all(up_grad_block.astype(jnp.bfloat16), 'fsdp', 0, 1, tiled=True)  43.7 us
  transfers between devices with their start and end apart: 17, of which 13 were waited for; matrix products, arithmetic and copies ran while one was open for 19% of the time, Pallas kernels for 0%

profile of v1, /device:TPU:0, one launch (start us, length us, event | category | flops | bytes accessed | tf_op | source)
XLA Modules:
  0.0 1582.2 jit_solution(11391256627915958565)
XLA Ops:
  10.8 10.4 all-gather.1
  21.2 9.1 all-gather
  33.9 15.4 all-gather.9.cloned.1.call-done
  54.9 32.9 %all-gather.11.cloned.1.call-done = bf16[2048,1024]{1,0:T(8,128)(2,1)} async-done(((bf16[256,1024]{1,0:T(8,128)(2,1)}), bf16[2048,1024]{1,0:T(8,128)(2,1)}) %all-gather.11.cloned.1.call-update) | async-done | bytes 4194320 | tf_op jit(solution)/shard_map/all_gather | solution.py:97
  103.9 40.1 %all-gather.13.cloned.1.call-done = bf16[2048,2048]{1,0:T(8,128)(2,1)} async-done(((bf16[256,2048]{1,0:T(8,128)(2,1)}), bf16[2048,2048]{1,0:T(8,128)(2,1)}) %all-gather.13.cloned.1.call-update) | async-done | bytes 8388624 | tf_op jit(solution)/shard_map/all_gather | solution.py:96
  144.0 9.0 fusion.52
  173.7 26.3 %all-gather.15.cloned.1.call-done = bf16[2048,2048]{1,0:T(8,128)(2,1)} async-done(((bf16[256,2048]{1,0:T(8,128)(2,1)}), bf16[2048,2048]{1,0:T(8,128)(2,1)}) %all-gather.15.cloned.1.call-update) | async-done | bytes 8388624 | tf_op jit(solution)/shard_map/all_gather | solution.py:99
  200.0 8.0 multiply_reduce_fusion.4
  232.5 41.5 %all-to-all-done = bf16[256,8,768]{0,2,1:T(8,128)(2,1)} async-done(((bf16[256,8,768]{0,2,1:T(8,128)(2,1)}), bf16[256,8,768]{0,2,1:T(8,128)(2,1)}, u32[]{:S(2)}, u32[]{:S(2)}) %all-to-all-start) | async-done | bytes 3145760 | tf_op jit(solution)/shard_map/all_to_all | solution.py:101
  283.4 58.2 %all-to-all-done.1 = bf16[256,8,768]{0,2,1:T(8,128)(2,1)} async-done(((bf16[256,8,768]{0,2,1:T(8,128)(2,1)}), bf16[256,8,768]{0,2,1:T(8,128)(2,1)}, u32[]{:S(2)}, u32[]{:S(2)}) %all-to-all-start.1) | async-done | bytes 3145760 | tf_op jit(solution)/shard_map/all_to_all | solution.py:102
  346.2 16.1 %fusion.57 = f32[3072,768]{1,0:T(8,128)} fusion(bf16[3072,2048]{1,0:T(8,128)(2,1)} %all-gather.17.cloned.1.call-done, bf16[2048,768]{1,0:T(8,128)(2,1)} %bitcast.206), kind=kOutput, calls=%fused_computation.129 | convolution fusion | flops 9663676416 | bytes 25165824 | tf_op jit(solution)/shard_map/dot_general | solution.py:141
  362.4 12.5 fusion.56
  374.9 42.5 %all-gather.19.cloned.1.call-done = bf16[3072,2048]{1,0:T(8,128)(2,1)} async-done(((bf16[384,2048]{1,0:T(8,128)(2,1)}), bf16[3072,2048]{1,0:T(8,128)(2,1)}) %all-gather.19.cloned.1.call-update) | async-done | bytes 12582928 | tf_op jit(solution)/shard_map/all_gather | solution.py:148
  417.4 23.3 %multiply_convert_fusion = (bf16[3072,768]{1,0:T(8,128)(2,1)}, bf16[3072,768]{1,0:T(8,128)(2,1)}, bf16[3072,768]{1,0:T(8,128)(2,1)}) fusion(f32[3072,768]{1,0:T(8,128)} %fusion.56, f32[3072,768]{1,0:T(8,128)} %fusion.57, bf16[3072,2048]{1,0:T(8,128)(2,1)} %all-gather.19.cloned.1.call-done, bf16[768,2048]{1,0:T(8,128)(2,1)S(1)} %copy-done), kind=kOutput, calls=%fused_computation.8 | convolution fusion | flops 9699065856 | bytes 48758784 | tf_op jit(solution)/shard_map/dot_general | solution.py:51
  440.7 17.6 %fusion.59 = f32[3072,2048]{1,0:T(8,128)} fusion(bf16[3072,768]{1,0:T(8,128)(2,1)} %get-tuple-element.35, bf16[2048,768]{1,0:T(8,128)(2,1)} %bitcast.204), kind=kOutput, calls=%fused_computation.131 | convolution fusion | flops 9663676416 | bytes 33030144 | tf_op jit(solution)/shard_map/dot_general | solution.py:51
  458.3 21.4 %convolution_add_fusion = f32[3072,2048]{1,0:T(8,128)} fusion(f32[3072,2048]{1,0:T(8,128)} %fusion.59, bf16[3072,768]{1,0:T(8,128)(2,1)} %get-tuple-element.34, bf16[2048,768]{1,0:T(8,128)(2,1)} %bitcast.207), kind=kOutput, calls=%fused_computation | convolution fusion | flops 9669967872 | bytes 58195968 | tf_op jit(solution)/shard_map/dot_general | solution.py:51
  479.7 19.1 %fusion.58 = f32[3072,2048]{1,0:T(8,128)} fusion(bf16[3072,768]{1,0:T(8,128)(2,1)} %get-tuple-element.36, bf16[768,2048]{1,0:T(8,128)(2,1)S(1)} %copy-done), kind=kOutput, calls=%fused_computation.130 | convolution fusion | flops 9663676416 | bytes 33030144 | tf_op jit(solution)/shard_map/dot_general | solution.py:143
  499.7 136.5 %reduce-scatter.9.cloned.1.call-done = f32[384,2048]{1,0:T(8,128)} async-done(((f32[3072,2048]{1,0:T(8,128)}), f32[384,2048]{1,0:T(8,128)}) %reduce-scatter.9.cloned.1.call-update) | async-done | bytes 3145744 | tf_op jit(solution)/shard_map/reduce_scatter | solution.py:161
  638.8 157.2 %reduce-scatter.7.cloned.1.call-done = f32[384,2048]{1,0:T(8,128)} async-done(((f32[3072,2048]{1,0:T(8,128)}), f32[384,2048]{1,0:T(8,128)}) %reduce-scatter.7.cloned.1.call-update) | async-done | bytes 3145744 | tf_op jit(solution)/shard_map/reduce_scatter | solution.py:144
  830.6 12.4 fusion.2
  857.7 8.2 convolution_convert_fusion
  909.3 7.9 fusion.26
  924.6 15.8 %convolution_convert_fusion.4 = bf16[2048,768]{1,0:T(8,128)(2,1)} fusion(bf16[3072,2048]{1,0:T(8,128)(2,1)} %all-gather.17.cloned.1.call-done, bf16[3072,768]{1,0:T(8,128)(2,1)} %get-tuple-element.34), kind=kOutput, calls=%fused_computation.34 | convolution fusion | flops 9665249280 | bytes 20447232 | tf_op jit(solution)/shard_map/dot_general | solution.py:45
  945.0 16.6 %convolution_convert_fusion.5 = bf16[2048,768]{1,0:T(8,128)(2,1)} fusion(bf16[3072,2048]{1,0:T(8,128)(2,1)} %all-gather.17.cloned.1.call-done, bf16[3072,768]{1,0:T(8,128)(2,1)} %get-tuple-element.35), kind=kOutput, calls=%fused_computation.35 | convolution fusion | flops 9665249280 | bytes 20447232 | tf_op jit(solution)/shard_map/dot_general | solution.py:45
  961.7 43.7 %all-to-all-done.3 = bf16[8,256,768]{2,1,0:T(8,128)(2,1)} async-done(((bf16[8,256,768]{2,1,0:T(8,128)(2,1)}), bf16[8,256,768]{2,1,0:T(8,128)(2,1)}, u32[]{:S(2)}, u32[]{:S(2)}) %all-to-all-start.3) | async-done | bytes 3145760 | tf_op jit(solution)/shard_map/all_to_all | solution.py:172
  1009.9 16.0 %convolution_convert_fusion.6 = bf16[768,2048]{1,0:T(8,128)(2,1)} fusion(bf16[3072,768]{1,0:T(8,128)(2,1)} %get-tuple-element.36, bf16[3072,2048]{1,0:T(8,128)(2,1)} %all-gather.19.cloned.1.call-done), kind=kOutput, calls=%fused_computation.36 | convolution fusion | flops 9665249280 | bytes 20447232 | tf_op jit(solution)/shard_map/dot_general | solution.py:45
  1029.8 28.5 %all-to-all-done.2 = bf16[8,256,768]{2,1,0:T(8,128)(2,1)} async-done(((bf16[8,256,768]{2,1,0:T(8,128)(2,1)}), bf16[8,256,768]{2,1,0:T(8,128)(2,1)}, u32[]{:S(2)}, u32[]{:S(2)}) %all-to-all-start.2) | async-done | bytes 3145760 | tf_op jit(solution)/shard_map/all_to_all | solution.py:169
  1062.4 65.3 %reduce-scatter.11.cloned.1.call-done = bf16[256,2048]{1,0:T(8,128)(2,1)} async-done(((bf16[2048,2048]{1,0:T(8,128)(2,1)}), bf16[256,2048]{1,0:T(8,128)(2,1)}) %reduce-scatter.11.cloned.1.call-update) | async-done | bytes 1048592 | tf_op jit(solution)/shard_map/reduce_scatter | solution.py:233
  1129.6 12.6 all-reduce.2
  1157.0 23.9 %all-reduce.3 = (bf16[2048]{0:T(1024)(128)(2,1)S(1)}, bf16[8,256]{1,0:T(8,128)(2,1)S(1)}) all-reduce(f32[2048]{0:T(1024)S(1)} %get-tuple-element.17, f32[8,256]{1,0:T(8,128)S(1)} %broadcast_in_dim.12), channel_id=4, replica_groups=mesh['fsdp'=8,'rep'=4] {'fsdp'}, use_global_device_ids=true, to_apply=%region_14.15.clone | all-reduce | flops 4096 | bytes 24576
  1181.6 12.9 all-reduce.4
  1201.7 356.6 %all-reduce.8.cloned.1.call-done = (bf16[256,2048]{1,0:T(8,128)(2,1)}, bf16[256,1024]{1,0:T(8,128)(2,1)}, bf16[256,1024]{1,0:T(8,128)(2,1)}, bf16[256,2048]{1,0:...) async-done(((bf16[256,2048]{1,0:T(8,128)(2,1)}, bf16[256,1024]{1,0:T(8,128)(2,1)}, bf16[256,1024]{1,0:T(8,128)(2,1)}, ...) | async-done | bytes 12582928 | tf_op jit(solution)/shard_map/psum | solution.py:250
  (287 shorter events, 247.0 us)
Async XLA Ops:
  7.2 410.2 %copy-start = (bf16[768,2048]{1,0:T(8,128)(2,1)S(1)}, bf16[768,2048]{1,0:T(8,128)(2,1)}, u32[]{:S(2)}) copy-start(bf16[768,2048]{1,0:T(8,128)(2,1)} %param.28) | copy-start | bytes 9437188
  7.2 42.1 %all-gather.9.cloned.1.call-start = ((), (), s32[]{:S(2)}) async-start(), calls=%async_computation.10 | async-start | bytes 4718592 | tf_op jit(solution)/shard_map/all_gather | solution.py:98
  8.0 79.8 %all-gather.11.cloned.1.call-start = ((), (), s32[]{:S(2)}) async-start(), calls=%async_computation.11 | async-start | bytes 4718592 | tf_op jit(solution)/shard_map/all_gather | solution.py:97
  8.7 135.3 %all-gather.13.cloned.1.call-start = ((), (), s32[]{:S(2)}) async-start(), calls=%async_computation.12 | async-start | bytes 9437184 | tf_op jit(solution)/shard_map/all_gather | solution.py:96
  9.4 190.6 %all-gather.15.cloned.1.call-start = ((), (), s32[]{:S(2)}) async-start(), calls=%async_computation.13 | async-start | bytes 9437184 | tf_op jit(solution)/shard_map/all_gather | solution.py:99
  10.0 336.2 %all-gather.17.cloned.1.call-start = ((), (), s32[]{:S(2)}) async-start(), calls=%async_computation.14 | async-start | bytes 14155776 | tf_op jit(solution)/shard_map/all_gather | solution.py:139
  10.7 151.3 %copy-start.62 = (f32[128]{0:T(128)}, f32[128]{0:T(128)S(1)}, u32[]{:S(2)}) copy-start(f32[128]{0:T(128)S(1)} %convert_element_type.185) | copy-start | bytes 1540
  10.7 91.8 %copy-start.65 = (f32[128]{0:T(128)}, f32[128]{0:T(128)S(1)}, u32[]{:S(2)}) copy-start(f32[128]{0:T(128)S(1)} %convert_element_type.181) | copy-start | bytes 1540
  21.2 186.8 %copy-start.49 = (f32[8,1,256]{2,1,0:T(1,128)}, f32[8,1,256]{2,1,0:T(1,128)S(1)}, u32[]{:S(2)}) copy-start(f32[8,1,256]{2,1,0:T(1,128)S(1)} %convert_element_type.229) | copy-start | bytes 24580
  30.3 113.7 %copy-start.51 = (f32[8,1,256]{2,1,0:T(1,128)}, f32[8,1,256]{2,1,0:T(1,128)S(1)}, u32[]{:S(2)}) copy-start(f32[8,1,256]{2,1,0:T(1,128)S(1)} %convert_element_type.228) | copy-start | bytes 24580
  30.4 137.6 %copy-start.20 = (pred[384,384]{0,1:T(8,128)(4,1)}, pred[384,384]{0,1:T(8,128)(4,1)S(1)}, u32[]{:S(2)}) copy-start(pred[384,384]{0,1:T(8,128)(4,1)S(1)} %iota_compare_fusion) | copy-start | bytes 442372
  32.0 130.1 %copy-start.27 = (f32[384,128]{0,1:T(8,128)}, f32[384,128]{0,1:T(8,128)S(1)}, u32[]{:S(2)}) copy-start(f32[384,128]{0,1:T(8,128)S(1)} %get-tuple-element.50) | copy-start | bytes 589828
  33.8 110.1 %copy-start.55 = (f32[384]{0:T(512)}, f32[384]{0:T(512)S(1)}, u32[]{:S(2)}) copy-start(f32[384]{0:T(512)S(1)} %add_rsqrt_fusion.3) | copy-start | bytes 4612
  211.1 206.3 %all-gather.19.cloned.1.call-start = ((), (), s32[]{:S(2)}) async-start(), calls=%async_computation.16 | async-start | bytes 14155776 | tf_op jit(solution)/shard_map/all_gather | solution.py:148
  223.4 50.6 %all-to-all-start = ((bf16[256,8,768]{0,2,1:T(8,128)(2,1)}), bf16[256,8,768]{0,2,1:T(8,128)(2,1)}, u32[]{:S(2)}, u32[]{:S(2)}) async-start(bf16[256,8,768]{0,2,1:T(8,128)(2,1)} %bitcast.194), calls=%async_computation | async-start | bytes 6291456 | tf_op jit(solution)/shard_map/all_to_all | solution.py:101
  274.0 67.6 %all-to-all-start.1 = ((bf16[256,8,768]{0,2,1:T(8,128)(2,1)}), bf16[256,8,768]{0,2,1:T(8,128)(2,1)}, u32[]{:S(2)}, u32[]{:S(2)}) async-start(bf16[256,8,768]{0,2,1:T(8,128)(2,1)} %bitcast.192), calls=%async_computation.1 | async-start | bytes 6291456 | tf_op jit(solution)/shard_map/all_to_all | solution.py:102
  278.5 357.7 %reduce-scatter.9.cloned.1.call-start = ((), (), s32[]{:S(2)}) async-start(), calls=%async_computation.17 | async-start | bytes 28311552 | tf_op jit(solution)/shard_map/reduce_scatter | solution.py:161
  346.2 16.2 %copy-start.23 = (bf16[8,256,768]{2,1,0:T(8,128)(2,1)S(1)}, bf16[8,256,768]{2,1,0:T(8,128)(2,1)}, u32[]{:S(2)}) copy-start(bf16[8,256,768]{2,1,0:T(8,128)(2,1)} %copy.172) | copy-start | bytes 9437188
  346.2 16.2 %copy-start.68 = (bf16[3072,2048]{1,0:T(8,128)(2,1)S(1)}, bf16[3072,2048]{1,0:T(8,128)(2,1)}, u32[]{:S(2)}) copy-start(bf16[3072,2048]{1,0:T(8,128)(2,1)} %all-gather.17.cloned.1.call-done) | copy-start | bytes 37748740
  479.7 316.4 %reduce-scatter.7.cloned.1.call-start = ((), (), s32[]{:S(2)}) async-start(), calls=%async_computation.15 | async-start | bytes 28311552 | tf_op jit(solution)/shard_map/reduce_scatter | solution.py:144
  498.8 137.3 %copy-start.7 = (f32[384,2048]{1,0:T(8,128)S(1)}, f32[384,2048]{1,0:T(8,128)}, u32[]{:S(2)}) copy-start(f32[384,2048]{1,0:T(8,128)} %copy-done.6) | copy-start | bytes 9437188
  498.8 137.3 %copy-start.50 = (f32[8,1,256]{2,1,0:T(1,128)S(1)}, f32[8,1,256]{2,1,0:T(1,128)}, u32[]{:S(2)}) copy-start(f32[8,1,256]{2,1,0:T(1,128)} %copy-done.49) | copy-start | bytes 24580
  498.8 137.3 %copy-start.58 = (f32[384]{0:T(512)S(1)}, f32[384]{0:T(512)}, u32[]{:S(2)}) copy-start(f32[384]{0:T(512)} %copy-done.57) | copy-start | bytes 4612
  498.9 563.5 %reduce-scatter.15.cloned.1.call-start = ((), (), s32[]{:S(2)}) async-start(), calls=%async_computation.20 | async-start | bytes 4718592 | tf_op jit(solution)/shard_map/reduce_scatter | solution.py:233
  499.6 296.4 %copy-start.61 = (f32[384]{0:T(512)S(1)}, f32[384]{0:T(512)}, u32[]{:S(2)}) copy-start(f32[384]{0:T(512)} %copy-done.60) | copy-start | bytes 4612
  822.6 239.8 %reduce-scatter.13.cloned.1.call-start = ((), (), s32[]{:S(2)}) async-start(), calls=%async_computation.19 | async-start | bytes 4718592 | tf_op jit(solution)/shard_map/reduce_scatter | solution.py:233
  855.8 206.6 %reduce-scatter.17.cloned.1.call-start = ((), (), s32[]{:S(2)}) async-start(), calls=%async_computation.21 | async-start | bytes 9437184 | tf_op jit(solution)/shard_map/reduce_scatter | solution.py:233
  865.9 261.8 %reduce-scatter.11.cloned.1.call-start = ((), (), s32[]{:S(2)}) async-start(), calls=%async_computation.18 | async-start | bytes 9437184 | tf_op jit(solution)/shard_map/reduce_scatter | solution.py:233
  940.4 65.0 %all-to-all-start.3 = ((bf16[8,256,768]{2,1,0:T(8,128)(2,1)}), bf16[8,256,768]{2,1,0:T(8,128)(2,1)}, u32[]{:S(2)}, u32[]{:S(2)}) async-start(bf16[8,256,768]{2,1,0:T(8,128)(2,1)} %bitcast.209), calls=%async_computation.9 | async-start | bytes 6291456 | tf_op jit(solution)/shard_map/all_to_all | solution.py:172
  1005.4 53.0 %all-to-all-start.2 = ((bf16[8,256,768]{2,1,0:T(8,128)(2,1)}), bf16[8,256,768]{2,1,0:T(8,128)(2,1)}, u32[]{:S(2)}, u32[]{:S(2)}) async-start(bf16[8,256,768]{2,1,0:T(8,128)(2,1)} %bitcast.208), calls=%async_computation.8 | async-start | bytes 6291456 | tf_op jit(solution)/shard_map/all_to_all | solution.py:169
  1009.9 548.4 %all-reduce.8.cloned.1.call-start = ((), (), s32[]{:S(2)}) async-start(), calls=%async_computation.22 | async-start | bytes 25165824 | tf_op jit(solution)/shard_map/psum | solution.py:250
  1127.7 14.5 copy-start.67
  (60 other events, 207.9 us)
Sparse Core Ops, SparseCore 0:
  9.9 39.3 all-gather.8
  51.2 36.5 all-gather.10
  89.7 54.2 all-gather.12
  145.7 54.2 all-gather.14
  211.2 123.8 all-gather.16
  337.4 79.9 all-gather.18
  479.8 156.2 reduce-scatter.8
  639.8 156.2 reduce-scatter.6
  822.7 51.1 reduce-scatter.14
  877.1 51.1 reduce-scatter.12
  931.7 112.7 reduce-scatter.16
  1047.9 79.7 reduce-scatter.10
  1131.7 426.5 all-reduce.7

commit v2 on v1

--- a/solution.py
+++ b/solution.py
@@ -58,6 +58,49 @@
     length = query_low.shape[0]
     causal = jnp.arange(length)[:, None] >= jnp.arange(length)[None, :]
     return jnp.where(causal, scores, -1000000000.0)
+
+
+def ring_sum(parts, axis):
+    n = lax.axis_size(axis)
+    me = lax.axis_index(axis)
+    forward = [(i, (i + 1) % n) for i in range(n)]
+    backward = [(i, (i - 1) % n) for i in range(n)]
+    pieces = [p.reshape((2, n, p.shape[0] // (2 * n)) + p.shape[1:]) for p in parts]
+    ahead = [q[0] for q in pieces]
+    behind = [q[1] for q in pieces]
+    take = lambda q, i: lax.dynamic_index_in_dim(q, i % n, axis=0, keepdims=False)
+    run_a = [take(q, me) for q in ahead]
+    run_b = [take(q, me) for q in behind]
+    for step in range(n - 1):
+        got_a = lax.ppermute([r.astype(jnp.bfloat16) for r in run_a], axis, forward)
+        got_b = lax.ppermute([r.astype(jnp.bfloat16) for r in run_b], axis, backward)
+        run_a = [g.astype(jnp.float32) + take(q, me - 1 - step) for g, q in zip(got_a, ahead)]
+        run_b = [g.astype(jnp.float32) + take(q, me + 1 + step) for g, q in zip(got_b, behind)]
+    own_a = [r.astype(jnp.bfloat16) for r in run_a]
+    own_b = [r.astype(jnp.bfloat16) for r in run_b]
+    out_a = [
+        lax.dynamic_update_index_in_dim(jnp.zeros(q.shape, jnp.bfloat16), o, (me + 1) % n, 0)
+        for q, o in zip(ahead, own_a)
+    ]
+    out_b = [
+        lax.dynamic_update_index_in_dim(jnp.zeros(q.shape, jnp.bfloat16), o, (me - 1) % n, 0)
+        for q, o in zip(behind, own_b)
+    ]
+    for step in range(n - 1):
+        own_a = lax.ppermute(own_a, axis, forward)
+        own_b = lax.ppermute(own_b, axis, backward)
+        out_a = [
+            lax.dynamic_update_index_in_dim(t, o, (me - step) % n, 0)
+            for t, o in zip(out_a, own_a)
+        ]
+        out_b = [
+            lax.dynamic_update_index_in_dim(t, o, (me + step) % n, 0)
+            for t, o in zip(out_b, own_b)
+        ]
+    return [
+        jnp.stack([a, b]).reshape(p.shape).astype(jnp.float32)
+        for a, b, p in zip(out_a, out_b, parts)
+    ]
 
 
 def per_device(
@@ -141,8 +184,6 @@
     up_value = jnp.dot(normed_two_group, up_block, preferred_element_type=jnp.float32)
     hidden_low = (jax.nn.silu(gate_value) * up_value).astype(jnp.bfloat16)
     down_part = jnp.dot(hidden_low, down_weight, preferred_element_type=jnp.float32)
-    down_value = lax.psum_scatter(down_part, "fsdp", scatter_dimension=0, tiled=True)
-    layer_out = ((middle + down_value) * valid_rows).astype(jnp.bfloat16)
     grad_top = cotangent.astype(jnp.float32) * valid_rows
     grad_down_low = grad_top.astype(jnp.bfloat16)
     grad_down_group = lax.all_gather(grad_down_low, "fsdp", axis=0, tiled=True)
@@ -159,6 +200,9 @@
         grad_up_low, up_block
     )
     grad_normed_two = lax.psum_scatter(grad_normed_part, "fsdp", scatter_dimension=0, tiled=True)
+    grad_normed_two, down_part = lax.optimization_barrier((grad_normed_two, down_part))
+    down_value = lax.psum_scatter(down_part, "fsdp", scatter_dimension=0, tiled=True)
+    layer_out = ((middle + down_value) * valid_rows).astype(jnp.bfloat16)
     grad_from_two, gain_two_terms = rms_backward(grad_normed_two, normal_two, inverse_two, gain_two)
     feed_gain_grad = jnp.sum(gain_two_terms, axis=0)
     grad_middle = grad_top + grad_from_two
@@ -174,6 +218,7 @@
         ),
         down_grad,
     )
+    feed_rep = ring_sum(list(feed_parts[1:]), "rep")
     grad_branch_low = grad_middle.astype(jnp.bfloat16)
     output_grad = inner_rows(mixed_low, grad_branch_low)
     grad_mixed_low = (
@@ -243,9 +288,9 @@
     )
     finals = (
         lax.psum(feed_parts[0].astype(jnp.bfloat16), "rep").astype(jnp.float32),
-        lax.psum(feed_parts[1].astype(jnp.bfloat16), "rep").astype(jnp.float32),
-        lax.psum(feed_parts[2].astype(jnp.bfloat16), "rep").astype(jnp.float32),
-        lax.psum(feed_parts[3].astype(jnp.bfloat16), "rep").astype(jnp.float32),
+        feed_rep[0],
+        feed_rep[1],
+        feed_rep[2],
         lax.psum(attention_parts[0].astype(jnp.bfloat16), "rep").astype(jnp.float32),
         lax.psum(attention_parts[1].astype(jnp.bfloat16), "rep").astype(jnp.float32),
         lax.psum(attention_parts[2].astype(jnp.bfloat16), "rep").astype(jnp.float32),

time: 1590 us -> 1330 us (0.84)
  waiting for transfers between devices: 1050 us -> 638 us
  starting transfers between devices: 19.4 us -> 71.7 us
  local copies, waits for them, and re-layouts: 78.4 us -> 130 us
  other arithmetic: 93 us -> 130 us
    psum x1, waiting for transfers between devices: 357 us -> 64.3 us  [per_device(): lax.psum(attention_parts[1].astype(jnp.bfloat16), 'rep').astype(jnp.float32)]
    reduce_scatter x1, waiting for transfers between devices: 157 us -> 0.02 us  [per_device(): lax.psum_scatter(down_part, 'fsdp', scatter_dimension=0, tiled=True)]
    ppermute x0 -> x36, waiting for transfers between devices: none -> 99.1 us  [the longest x9 45 us: ring_sum(): own_b = lax.ppermute(own_b, axis, backward)]
    all_gather x1, waiting for transfers between devices: 0.01 us -> 55.1 us  [per_device(): lax.all_gather(normed_two_low, 'fsdp', axis=0, tiled=True)]
    ppermute x0 -> x36, starting transfers between devices: none -> 54.1 us  [the longest x9 28.3 us: ring_sum(): lax.ppermute([r.astype(jnp.bfloat16) for r in run_b], axis, backward)]
    all_to_all x1, waiting for transfers between devices: 43.7 us -> 0.01 us  [per_device(): lax.all_to_all(up_grad_block.astype(jnp.bfloat16), 'fsdp', 0, 1, tiled=True)]
    all_gather x1, waiting for transfers between devices: 42.5 us -> 0.01 us  [per_device(): grad_down_group = lax.all_gather(grad_down_low, 'fsdp', axis=0, tiled=True)]
    convert_element_type x3 -> x17, other arithmetic: 10.4 us -> 36 us  [the longest x3 11.9 us: ring_sum(): jnp.stack([a, b]).reshape(p.shape).astype(jnp.float32)]
  transfers between devices with their start and end apart: 17 -> 53, of which waited for: 13 -> 28; matrix products, arithmetic and copies ran while one was open for 19% -> 32% of each run, Pallas kernels for 0% -> 0%
where the time goes in v2:
time: 1330 us; the launch traced here: 1320 us
  waiting for transfers between devices  638 us (48%)
  matrix products  263 us (20%)
  local copies, waits for them, and re-layouts  130 us (10%)
  other arithmetic  130 us (10%)
  starting transfers between devices  71.7 us (5%)
  blocking collectives  68.2 us (5%)
  between operations  18.5 us (1%)
    reduce_scatter x1, waiting for transfers between devices, per_device(): lax.psum_scatter(grad_normed_part, 'fsdp', scatter_dimension=0, tiled=True)  138 us
    dot_general x7, matrix products, times_transposed(): lax.dot_general(left, right, (((1,), (1,)), ((), ())), preferred_element_...  78.9 us
    dot_general x7, matrix products, inner_rows(): lax.dot_general(left, right, (((0,), (0,)), ((), ())), preferred_element_...  72.7 us
    psum x1, waiting for transfers between devices, per_device(): lax.psum(attention_parts[1].astype(jnp.bfloat16), 'rep').astype(jnp.float32)  64.3 us
    all_gather x1, waiting for transfers between devices, per_device(): lax.all_gather(normed_two_low, 'fsdp', axis=0, tiled=True)  55.1 us
    all_to_all x1, waiting for transfers between devices, per_device(): gate_block = lax.all_to_all(gate_weight, 'fsdp', 1, 0, tiled=True)  49.9 us
    reduce_scatter x4, waiting for transfers between devices, per_device(): lax.psum_scatter(v.astype(jnp.bfloat16), 'fsdp', scatter_dimension=0, til...  48.6 us
    all_gather x1, waiting for transfers between devices, per_device(): lax.all_gather(query_weight, 'fsdp', axis=0, tiled=True)  48.2 us
  transfers between devices with their start and end apart: 53, of which 28 were waited for; matrix products, arithmetic and copies ran while one was open for 32% of the time, Pallas kernels for 0%

profile of v2, /device:TPU:0, one launch (start us, length us, event | category | flops | bytes accessed | tf_op | source)
XLA Modules:
  0.0 1319.4 jit_solution(5274312940598464426)
XLA Ops:
  17.4 10.6 all-gather
  28.1 9.0 all-gather.1
  61.9 25.9 %all-gather.9.cloned.1.call-done = bf16[2048,1024]{1,0:T(8,128)(2,1)} async-done(((bf16[256,1024]{1,0:T(8,128)(2,1)}), bf16[2048,1024]{1,0:T(8,128)(2,1)}) %all-gather.9.cloned.1.call-update) | async-done | bytes 4194320 | tf_op jit(solution)/shard_map/all_gather | solution.py:141
  95.7 48.2 %all-gather.13.cloned.1.call-done = bf16[2048,2048]{1,0:T(8,128)(2,1)} async-done(((bf16[256,2048]{1,0:T(8,128)(2,1)}), bf16[2048,2048]{1,0:T(8,128)(2,1)}) %all-gather.13.cloned.1.call-update) | async-done | bytes 8388624 | tf_op jit(solution)/shard_map/all_gather | solution.py:139
  144.0 9.0 fusion.76
  173.4 26.6 %all-gather.15.cloned.1.call-done = bf16[2048,2048]{1,0:T(8,128)(2,1)} async-done(((bf16[256,2048]{1,0:T(8,128)(2,1)}), bf16[2048,2048]{1,0:T(8,128)(2,1)}) %all-gather.15.cloned.1.call-update) | async-done | bytes 8388624 | tf_op jit(solution)/shard_map/all_gather | solution.py:142
  224.9 49.9 %all-to-all-done.1 = bf16[256,8,768]{0,2,1:T(8,128)(2,1)} async-done(((bf16[256,8,768]{0,2,1:T(8,128)(2,1)}), bf16[256,8,768]{0,2,1:T(8,128)(2,1)}, u32[]{:S(2)}, u32[]{:S(2)}) %all-to-all-start.1) | async-done | bytes 3145760 | tf_op jit(solution)/shard_map/all_to_all | solution.py:144
  284.4 48.0 %all-to-all-done = bf16[256,8,768]{0,2,1:T(8,128)(2,1)} async-done(((bf16[256,8,768]{0,2,1:T(8,128)(2,1)}), bf16[256,8,768]{0,2,1:T(8,128)(2,1)}, u32[]{:S(2)}, u32[]{:S(2)}) %all-to-all-start) | async-done | bytes 3145760 | tf_op jit(solution)/shard_map/all_to_all | solution.py:145
  337.1 15.1 %fusion.89 = f32[3072,768]{1,0:T(8,128)} fusion(bf16[3072,2048]{1,0:T(8,128)(2,1)} %all-gather.17.cloned.1.call-done, bf16[768,2048]{1,0:T(8,128)(2,1)S(1)} %copy-done), kind=kOutput, calls=%fused_computation.210 | convolution fusion | flops 9663676416 | bytes 25165824 | tf_op jit(solution)/shard_map/dot_general | solution.py:51
  352.2 55.1 %all-gather.19.cloned.1.call-done = bf16[3072,2048]{1,0:T(8,128)(2,1)} async-done(((bf16[384,2048]{1,0:T(8,128)(2,1)}), bf16[3072,2048]{1,0:T(8,128)(2,1)}) %all-gather.19.cloned.1.call-update) | async-done | bytes 12582928 | tf_op jit(solution)/shard_map/all_gather | solution.py:182
  407.3 16.1 %fusion.90 = f32[3072,768]{1,0:T(8,128)} fusion(bf16[3072,2048]{1,0:T(8,128)(2,1)} %all-gather.19.cloned.1.call-done, bf16[2048,768]{1,0:T(8,128)(2,1)} %bitcast.359), kind=kOutput, calls=%fused_computation.211 | convolution fusion | flops 9663676416 | bytes 25165824 | tf_op jit(solution)/shard_map/dot_general | solution.py:183
  423.5 24.7 %multiply_convert_fusion = (bf16[3072,768]{1,0:T(8,128)(2,1)}, bf16[3072,768]{1,0:T(8,128)(2,1)}, bf16[3072,768]{1,0:T(8,128)(2,1)}) fusion(f32[3072,768]{1,0:T(8,128)} %fusion.90, f32[3072,768]{1,0:T(8,128)} %fusion.89, bf16[3072,2048]{1,0:T(8,128)(2,1)} %all-gather.19.cloned.1.call-done, bf16[2048,768]{1,0:T(8,128)(2,1)} %bitcast.361), kind=kOutput, calls=%fused_computation.8 | convolution fusion | flops 9699065856 | bytes 48758784 | tf_op jit(solution)/shard_map/dot_general | solution.py:184
  448.2 17.5 %fusion.91 = f32[3072,2048]{1,0:T(8,128)} fusion(bf16[3072,768]{1,0:T(8,128)(2,1)} %get-tuple-element.48, bf16[2048,768]{1,0:T(8,128)(2,1)} %bitcast.360), kind=kOutput, calls=%fused_computation.212 | convolution fusion | flops 9663676416 | bytes 33030144 | tf_op jit(solution)/shard_map/dot_general | solution.py:51
  465.6 21.3 %convolution_add_fusion = f32[3072,2048]{1,0:T(8,128)} fusion(f32[3072,2048]{1,0:T(8,128)} %fusion.91, bf16[3072,768]{1,0:T(8,128)(2,1)} %get-tuple-element.49, bf16[2048,768]{1,0:T(8,128)(2,1)} %bitcast.362), kind=kOutput, calls=%fused_computation | convolution fusion | flops 9669967872 | bytes 58195968 | tf_op jit(solution)/shard_map/dot_general | solution.py:51
  487.0 18.7 %fusion.92 = f32[3072,2048]{1,0:T(8,128)} fusion(bf16[3072,768]{1,0:T(8,128)(2,1)} %get-tuple-element.47, bf16[768,2048]{1,0:T(8,128)(2,1)S(1)} %copy-done), kind=kOutput, calls=%fused_computation.213 | convolution fusion | flops 9663676416 | bytes 33030144 | tf_op jit(solution)/shard_map/dot_general | solution.py:186
  505.8 137.7 %reduce-scatter.7.cloned.1.call-done = f32[384,2048]{1,0:T(8,128)} async-done(((f32[3072,2048]{1,0:T(8,128)}), f32[384,2048]{1,0:T(8,128)}) %reduce-scatter.7.cloned.1.call-update) | async-done | bytes 3145744 | tf_op jit(solution)/shard_map/reduce_scatter | solution.py:202
  650.3 15.8 %fusion.96 = f32[768,2048]{1,0:T(8,128)S(1)} fusion(bf16[3072,768]{1,0:T(8,128)(2,1)} %get-tuple-element.47, bf16[3072,2048]{1,0:T(8,128)(2,1)} %all-gather.17.cloned.1.call-done), kind=kOutput, calls=%fused_computation.217 | convolution fusion | flops 9663676416 | bytes 23592960 | tf_op jit(solution)/shard_map/dot_general | solution.py:45
  674.1 18.1 %convolution_convert_fusion.4 = bf16[2048,768]{1,0:T(8,128)(2,1)} fusion(bf16[3072,2048]{1,0:T(8,128)(2,1)} %all-gather.19.cloned.1.call-done, bf16[3072,768]{1,0:T(8,128)(2,1)} %get-tuple-element.49), kind=kOutput, calls=%fused_computation.36 | convolution fusion | flops 9665249280 | bytes 20447232 | tf_op jit(solution)/shard_map/dot_general | solution.py:45
  702.5 8.7 collective-permute-done.25
  737.4 15.7 %convolution_convert_fusion.5 = bf16[2048,768]{1,0:T(8,128)(2,1)} fusion(bf16[3072,2048]{1,0:T(8,128)(2,1)} %all-gather.19.cloned.1.call-done, bf16[3072,768]{1,0:T(8,128)(2,1)} %get-tuple-element.48), kind=kOutput, calls=%fused_computation.37 | convolution fusion | flops 9665249280 | bytes 20447232 | tf_op jit(solution)/shard_map/dot_general | solution.py:45
  757.8 9.1 collective-permute-done.28
  816.5 23.5 %all-to-all-done.2 = bf16[8,256,768]{2,1,0:T(8,128)(2,1)} async-done(((bf16[8,256,768]{2,1,0:T(8,128)(2,1)}), bf16[8,256,768]{2,1,0:T(8,128)(2,1)}, u32[]{:S(2)}, u32[]{:S(2)}) %all-to-all-start.2) | async-done | bytes 3145760 | tf_op jit(solution)/shard_map/all_to_all | solution.py:213
  882.5 10.1 convolution_convert_fusion.6
  902.6 11.3 fusion.2
  1044.2 10.3 collective-permute-done.9
  1061.2 10.2 collective-permute-done.22
  1078.1 10.0 collective-permute-done.10
  1121.3 11.8 all-reduce.2
  1133.2 48.6 %reduce-scatter.17.cloned.1.call-done = bf16[256,2048]{1,0:T(8,128)(2,1)} async-done(((bf16[2048,2048]{1,0:T(8,128)(2,1)}), bf16[256,2048]{1,0:T(8,128)(2,1)}) %reduce-scatter.17.cloned.1.call-update) | async-done | bytes 1048592 | tf_op jit(solution)/shard_map/reduce_scatter | solution.py:278
  1196.8 24.5 %all-reduce.3 = (bf16[2048]{0:T(1024)(128)(2,1)S(1)}, bf16[8,256]{1,0:T(8,128)(2,1)S(1)}) all-reduce(f32[2048]{0:T(1024)S(1)} %get-tuple-element.21, f32[8,256]{1,0:T(8,128)S(1)} %broadcast_in_dim.72), channel_id=4, replica_groups=mesh['fsdp'=8,'rep'=4] {'fsdp'}, use_global_device_ids=true, to_apply=%region_14.15.clone | all-reduce | flops 4096 | bytes 24576
  1222.0 12.4 all-reduce.4
  1241.4 64.3 %all-reduce.8.cloned.1.call-done = (bf16[256,2048]{1,0:T(8,128)(2,1)}, bf16[256,1024]{1,0:T(8,128)(2,1)}, bf16[256,1024]{1,0:T(8,128)(2,1)}, bf16[256,2048]{1,0:T(8,128)(2,1)}) async-done(((bf16[256,2048]{1,0:T(8,128)(2,1)}, bf16[256,1024]{1,0:T(8,128)(2,1)}, bf16[256,1024]{1,0:T(8,128)(2,1)}, bf16[256,2048]{1,0:T(8,128)(2,1)}), (bf16[256,2048]{1,0:T(8,128)(2,1)}, bf16[256,1024]{1,0:T(8,128)(2,1)}, ...) | async-done | bytes 3145744 | tf_op jit(solution)/shard_map/psum | solution.py:295
  (455 shorter events, 463.0 us)
Async XLA Ops:
  7.2 42.1 %all-gather.11.cloned.1.call-start = ((), (), s32[]{:S(2)}) async-start(), calls=%async_computation.11 | async-start | bytes 4718592 | tf_op jit(solution)/shard_map/all_gather | solution.py:140
  8.0 79.8 %all-gather.9.cloned.1.call-start = ((), (), s32[]{:S(2)}) async-start(), calls=%async_computation.10 | async-start | bytes 4718592 | tf_op jit(solution)/shard_map/all_gather | solution.py:141
  8.7 135.3 %all-gather.13.cloned.1.call-start = ((), (), s32[]{:S(2)}) async-start(), calls=%async_computation.12 | async-start | bytes 9437184 | tf_op jit(solution)/shard_map/all_gather | solution.py:139
  9.5 190.5 %all-gather.15.cloned.1.call-start = ((), (), s32[]{:S(2)}) async-start(), calls=%async_computation.13 | async-start | bytes 9437184 | tf_op jit(solution)/shard_map/all_gather | solution.py:142
  10.1 327.1 %all-gather.17.cloned.1.call-start = ((), (), s32[]{:S(2)}) async-start(), calls=%async_computation.14 | async-start | bytes 14155776 | tf_op jit(solution)/shard_map/all_gather | solution.py:189
  17.4 390.0 %all-gather.19.cloned.1.call-start = ((), (), s32[]{:S(2)}) async-start(), calls=%async_computation.15 | async-start | bytes 14155776 | tf_op jit(solution)/shard_map/all_gather | solution.py:182
  215.8 59.0 %all-to-all-start.1 = ((bf16[256,8,768]{0,2,1:T(8,128)(2,1)}), bf16[256,8,768]{0,2,1:T(8,128)(2,1)}, u32[]{:S(2)}, u32[]{:S(2)}) async-start(bf16[256,8,768]{0,2,1:T(8,128)(2,1)} %bitcast.341), calls=%async_computation.1 | async-start | bytes 6291456 | tf_op jit(solution)/shard_map/all_to_all | solution.py:144
  274.8 57.6 %all-to-all-start = ((bf16[256,8,768]{0,2,1:T(8,128)(2,1)}), bf16[256,8,768]{0,2,1:T(8,128)(2,1)}, u32[]{:S(2)}, u32[]{:S(2)}) async-start(bf16[256,8,768]{0,2,1:T(8,128)(2,1)} %bitcast.339), calls=%async_computation | async-start | bytes 6291456 | tf_op jit(solution)/shard_map/all_to_all | solution.py:145
  279.3 364.2 %reduce-scatter.7.cloned.1.call-start = ((), (), s32[]{:S(2)}) async-start(), calls=%async_computation.16 | async-start | bytes 28311552 | tf_op jit(solution)/shard_map/reduce_scatter | solution.py:202
  487.0 388.2 %reduce-scatter.9.cloned.1.call-start = ((), (), s32[]{:S(2)}) async-start(), calls=%async_computation.17 | async-start | bytes 28311552 | tf_op jit(solution)/shard_map/reduce_scatter | solution.py:204
  692.2 92.4 %all-to-all-start.3 = ((bf16[8,256,768]{2,1,0:T(8,128)(2,1)}), bf16[8,256,768]{2,1,0:T(8,128)(2,1)S(1)}, u32[]{:S(2)}, u32[]{:S(2)}) async-start(bf16[8,256,768]{2,1,0:T(8,128)(2,1)} %bitcast.357), calls=%async_computation.9 | async-start | bytes 6291456 | tf_op jit(solution)/shard_map/all_to_all | solution.py:216
  784.6 55.4 %all-to-all-start.2 = ((bf16[8,256,768]{2,1,0:T(8,128)(2,1)}), bf16[8,256,768]{2,1,0:T(8,128)(2,1)}, u32[]{:S(2)}, u32[]{:S(2)}) async-start(bf16[8,256,768]{2,1,0:T(8,128)(2,1)} %bitcast.358), calls=%async_computation.8 | async-start | bytes 6291456 | tf_op jit(solution)/shard_map/all_to_all | solution.py:213
  789.1 344.1 %reduce-scatter.13.cloned.1.call-start = ((), (), s32[]{:S(2)}) async-start(), calls=%async_computation.19 | async-start | bytes 4718592 | tf_op jit(solution)/shard_map/reduce_scatter | solution.py:278
  805.0 57.6 %collective-permute-start.12 = (bf16[32,6144]{1,0:T(8,128)(2,1)}, bf16[32,6144]{1,0:T(8,128)(2,1)S(1)}, u32[]{:S(2)}, u32[]{:S(2)}) collective-permute-start(bf16[32,6144]{1,0:T(8,128)(2,1)} %fusion.64), channel_id=1, source_target_pairs={{0,1},{1,2},{2,3},{3,0},{4,5},{5,6},{6,7},{7,4},{8,9},{9,10},{10,1... | collective-permute-start | bytes 1179656 | tf_op jit(solution)/shard_map/ppermute | solution.py:75
  813.3 51.2 %collective-permute-start.18 = (bf16[32,6144]{1,0:T(8,128)(2,1)}, bf16[32,6144]{1,0:T(8,128)(2,1)}, u32[]{:S(2)}, u32[]{:S(2)}) collective-permute-start(bf16[32,6144]{1,0:T(8,128)(2,1)} %fusion.65), channel_id=1, source_target_pairs={{0,3},{1,0},{2,1},{3,2},{4,7},{5,4},{6,5},{7,6},{8,11},{9,8},{10,9... | collective-permute-start | bytes 1179656 | tf_op jit(solution)/shard_map/ppermute | solution.py:76
  859.9 66.8 %collective-permute-start.6 = (bf16[32,6144]{1,0:T(8,128)(2,1)}, bf16[32,6144]{1,0:T(8,128)(2,1)}, u32[]{:S(2)}, u32[]{:S(2)}) collective-permute-start(bf16[32,6144]{1,0:T(8,128)(2,1)} %fusion.63), channel_id=1, source_target_pairs={{0,3},{1,0},{2,1},{3,2},{4,7},{5,4},{6,5},{7,6},{8,11},{9,8},{10,9... | collective-permute-start | bytes 1179656 | tf_op jit(solution)/shard_map/ppermute | solution.py:76
  864.5 68.2 %collective-permute-start.13 = (bf16[32,6144]{1,0:T(8,128)(2,1)}, bf16[32,6144]{1,0:T(8,128)(2,1)}, u32[]{:S(2)}, u32[]{:S(2)}) collective-permute-start(bf16[32,6144]{1,0:T(8,128)(2,1)} %fusion.50), channel_id=1, source_target_pairs={{0,1},{1,2},{2,3},{3,0},{4,5},{5,6},{6,7},{7,4},{8,9},{9,10},{10,1... | collective-permute-start | bytes 1179656 | tf_op jit(solution)/shard_map/ppermute | solution.py:75
  866.5 68.3 %collective-permute-start.19 = (bf16[32,6144]{1,0:T(8,128)(2,1)}, bf16[32,6144]{1,0:T(8,128)(2,1)}, u32[]{:S(2)}, u32[]{:S(2)}) collective-permute-start(bf16[32,6144]{1,0:T(8,128)(2,1)} %fusion.47), channel_id=1, source_target_pairs={{0,3},{1,0},{2,1},{3,2},{4,7},{5,4},{6,5},{7,6},{8,11},{9,8},{10,9... | collective-permute-start | bytes 1179656 | tf_op jit(solution)/shard_map/ppermute | solution.py:76
  872.4 68.4 %collective-permute-start.1 = (bf16[32,6144]{1,0:T(8,128)(2,1)}, bf16[32,6144]{1,0:T(8,128)(2,1)}, u32[]{:S(2)}, u32[]{:S(2)}) collective-permute-start(bf16[32,6144]{1,0:T(8,128)(2,1)} %fusion.56), channel_id=1, source_target_pairs={{0,1},{1,2},{2,3},{3,0},{4,5},{5,6},{6,7},{7,4},{8,9},{9,10},{10,1... | collective-permute-start | bytes 1179656 | tf_op jit(solution)/shard_map/ppermute | solution.py:75
  926.6 206.5 %reduce-scatter.15.cloned.1.call-start = ((), (), s32[]{:S(2)}) async-start(), calls=%async_computation.20 | async-start | bytes 4718592 | tf_op jit(solution)/shard_map/reduce_scatter | solution.py:278
  937.0 79.5 %collective-permute-start.20 = (bf16[32,6144]{1,0:T(8,128)(2,1)}, bf16[32,6144]{1,0:T(8,128)(2,1)}, u32[]{:S(2)}, u32[]{:S(2)}) collective-permute-start(bf16[32,6144]{1,0:T(8,128)(2,1)} %fusion.46), channel_id=1, source_target_pairs={{0,3},{1,0},{2,1},{3,2},{4,7},{5,4},{6,5},{7,6},{8,11},{9,8},{10,9... | collective-permute-start | bytes 1179656 | tf_op jit(solution)/shard_map/ppermute | solution.py:76
  942.9 80.8 %collective-permute-start.2 = (bf16[32,6144]{1,0:T(8,128)(2,1)}, bf16[32,6144]{1,0:T(8,128)(2,1)}, u32[]{:S(2)}, u32[]{:S(2)}) collective-permute-start(bf16[32,6144]{1,0:T(8,128)(2,1)} %fusion.55), channel_id=1, source_target_pairs={{0,1},{1,2},{2,3},{3,0},{4,5},{5,6},{6,7},{7,4},{8,9},{9,10},{10,1... | collective-permute-start | bytes 1179656 | tf_op jit(solution)/shard_map/ppermute | solution.py:75
  954.1 179.0 %reduce-scatter.11.cloned.1.call-start = ((), (), s32[]{:S(2)}) async-start(), calls=%async_computation.18 | async-start | bytes 9437184 | tf_op jit(solution)/shard_map/reduce_scatter | solution.py:278
  956.4 69.1 %collective-permute-start.8 = (bf16[32,6144]{1,0:T(8,128)(2,1)}, bf16[32,6144]{1,0:T(8,128)(2,1)}, u32[]{:S(2)}, u32[]{:S(2)}) collective-permute-start(bf16[32,6144]{1,0:T(8,128)(2,1)} %fusion.52), channel_id=1, source_target_pairs={{0,3},{1,0},{2,1},{3,2},{4,7},{5,4},{6,5},{7,6},{8,11},{9,8},{10,9... | collective-permute-start | bytes 1179656 | tf_op jit(solution)/shard_map/ppermute | solution.py:76
  963.8 70.8 %collective-permute-start.15 = (bf16[32,6144]{1,0:T(8,128)(2,1)}, bf16[32,6144]{1,0:T(8,128)(2,1)}, u32[]{:S(2)}, u32[]{:S(2)}) collective-permute-start(bf16[32,6144]{1,0:T(8,128)(2,1)} %get-tuple-element.39), channel_id=1, source_target_pairs={{0,1},{1,2},{2,3},{3,0},{4,5},{5,6},{6,7},{7,4},{8,9},{9,10},{10,1... | collective-permute-start | bytes 1179656 | tf_op jit(solution)/shard_map/ppermute | solution.py:90
  1016.5 165.3 %reduce-scatter.17.cloned.1.call-start = ((), (), s32[]{:S(2)}) async-start(), calls=%async_computation.21 | async-start | bytes 9437184 | tf_op jit(solution)/shard_map/reduce_scatter | solution.py:278
  1037.7 33.8 %collective-permute-start.22 = (bf16[32,6144]{1,0:T(8,128)(2,1)S(1)}, bf16[32,6144]{1,0:T(8,128)(2,1)}, u32[]{:S(2)}, u32[]{:S(2)}) collective-permute-start(bf16[32,6144]{1,0:T(8,128)(2,1)S(1)} %collective-permute-done.21), channel_id=1, source_target_pairs={{0,3},{1,0},{2,1},{3,2},{4,7},{5,4},{6,5},{7,6},{8,11},{9,8},{10,9... | collective-permute-start | bytes 1179656 | tf_op jit(solution)/shard_map/ppermute | solution.py:91
  1042.3 33.9 %collective-permute-start.4 = (bf16[32,6144]{1,0:T(8,128)(2,1)S(1)}, bf16[32,6144]{1,0:T(8,128)(2,1)}, u32[]{:S(2)}, u32[]{:S(2)}) collective-permute-start(bf16[32,6144]{1,0:T(8,128)(2,1)S(1)} %collective-permute-done.3), channel_id=1, source_target_pairs={{0,1},{1,2},{2,3},{3,0},{4,5},{5,6},{6,7},{7,4},{8,9},{9,10},{10,1... | collective-permute-start | bytes 1179656 | tf_op jit(solution)/shard_map/ppermute | solution.py:90
  1054.6 33.6 %collective-permute-start.10 = (bf16[32,6144]{1,0:T(8,128)(2,1)S(1)}, bf16[32,6144]{1,0:T(8,128)(2,1)S(1)}, u32[]{:S(2)}, u32[]{:S(2)}) collective-permute-start(bf16[32,6144]{1,0:T(8,128)(2,1)S(1)} %collective-permute-done.9), channel_id=1, source_target_pairs={{0,3},{1,0},{2,1},{3,2},{4,7},{5,4},{6,5},{7,6},{8,11},{9,8},{10,9... | collective-permute-start | bytes 1179656 | tf_op jit(solution)/shard_map/ppermute | solution.py:91
  1059.3 41.3 %collective-permute-start.17 = (bf16[32,6144]{1,0:T(8,128)(2,1)}, bf16[32,6144]{1,0:T(8,128)(2,1)}, u32[]{:S(2)}, u32[]{:S(2)}) collective-permute-start(bf16[32,6144]{1,0:T(8,128)(2,1)} %collective-permute-done.16), channel_id=1, source_target_pairs={{0,1},{1,2},{2,3},{3,0},{4,5},{5,6},{6,7},{7,4},{8,9},{9,10},{10,1... | collective-permute-start | bytes 1179656 | tf_op jit(solution)/shard_map/ppermute | solution.py:90
  1071.5 32.9 %collective-permute-start.23 = (bf16[32,6144]{1,0:T(8,128)(2,1)}, bf16[32,6144]{1,0:T(8,128)(2,1)}, u32[]{:S(2)}, u32[]{:S(2)}) collective-permute-start(bf16[32,6144]{1,0:T(8,128)(2,1)} %collective-permute-done.22), channel_id=1, source_target_pairs={{0,3},{1,0},{2,1},{3,2},{4,7},{5,4},{6,5},{7,6},{8,11},{9,8},{10,9... | collective-permute-start | bytes 1179656 | tf_op jit(solution)/shard_map/ppermute | solution.py:91
  1098.7 207.1 %all-reduce.8.cloned.1.call-start = ((), (), s32[]{:S(2)}) async-start(), calls=%async_computation.22 | async-start | bytes 6291456 | tf_op jit(solution)/shard_map/psum | solution.py:295
  (113 other events, 2836.9 us)
Sparse Core Ops, SparseCore 0:
  9.9 39.3 all-gather.10
  51.2 36.5 all-gather.8
  89.7 54.2 all-gather.12
  145.7 54.2 all-gather.14
  202.3 122.1 all-gather.16
  326.8 80.4 all-gather.18
  487.1 156.3 reduce-scatter.6
  647.1 214.6 reduce-scatter.8
  926.8 50.7 reduce-scatter.12
  980.8 51.1 reduce-scatter.14
  1035.4 71.4 reduce-scatter.10
  1110.3 71.4 reduce-scatter.16
  1184.4 121.3 all-reduce.7

commit v3 on v2

--- a/solution.py
+++ b/solution.py
@@ -68,7 +68,9 @@
     pieces = [p.reshape((2, n, p.shape[0] // (2 * n)) + p.shape[1:]) for p in parts]
     ahead = [q[0] for q in pieces]
     behind = [q[1] for q in pieces]
-    take = lambda q, i: lax.dynamic_index_in_dim(q, i % n, axis=0, keepdims=False)
+    take = lambda q, i: lax.dynamic_index_in_dim(q, i % n, axis=0, keepdims=False).astype(
+        jnp.float32
+    )
     run_a = [take(q, me) for q in ahead]
     run_b = [take(q, me) for q in behind]
     for step in range(n - 1):
@@ -143,6 +145,7 @@
     )
     gate_block = lax.all_to_all(gate_weight, "fsdp", 1, 0, tiled=True)
     up_block = lax.all_to_all(up_weight, "fsdp", 1, 0, tiled=True)
+    tokens, gate_block, up_block = lax.optimization_barrier((tokens, gate_block, up_block))
     inputs_wide = tokens.astype(jnp.float32)
     gain_one = attention_set[0].astype(jnp.float32)
     normed_one, normal_one, inverse_one = rms_forward(inputs_wide, gain_one)
@@ -199,9 +202,13 @@
     grad_normed_part = times_transposed(grad_gate_low, gate_block) + times_transposed(
         grad_up_low, up_block
     )
-    grad_normed_two = lax.psum_scatter(grad_normed_part, "fsdp", scatter_dimension=0, tiled=True)
+    grad_normed_two = lax.psum_scatter(
+        grad_normed_part.astype(jnp.bfloat16), "fsdp", scatter_dimension=0, tiled=True
+    ).astype(jnp.float32)
     grad_normed_two, down_part = lax.optimization_barrier((grad_normed_two, down_part))
-    down_value = lax.psum_scatter(down_part, "fsdp", scatter_dimension=0, tiled=True)
+    down_value = lax.psum_scatter(
+        down_part.astype(jnp.bfloat16), "fsdp", scatter_dimension=0, tiled=True
+    ).astype(jnp.float32)
     layer_out = ((middle + down_value) * valid_rows).astype(jnp.bfloat16)
     grad_from_two, gain_two_terms = rms_backward(grad_normed_two, normal_two, inverse_two, gain_two)
     feed_gain_grad = jnp.sum(gain_two_terms, axis=0)
@@ -210,15 +217,21 @@
         lax.psum_scatter(
             feed_gain_grad.astype(jnp.bfloat16), "fsdp", scatter_dimension=0, tiled=True
         ).astype(jnp.float32),
-        lax.all_to_all(gate_grad_block.astype(jnp.bfloat16), "fsdp", 0, 1, tiled=True).astype(
-            jnp.float32
-        ),
-        lax.all_to_all(up_grad_block.astype(jnp.bfloat16), "fsdp", 0, 1, tiled=True).astype(
-            jnp.float32
-        ),
-        down_grad,
-    )
-    feed_rep = ring_sum(list(feed_parts[1:]), "rep")
+        lax.all_to_all(gate_grad_block.astype(jnp.bfloat16), "fsdp", 0, 1, tiled=True),
+        lax.all_to_all(up_grad_block.astype(jnp.bfloat16), "fsdp", 0, 1, tiled=True),
+        down_grad.astype(jnp.bfloat16),
+    )
+    feed_width = feed_parts[1].shape[1]
+    feed_rows = [feed_parts[1].shape[0], feed_parts[2].shape[0]]
+    feed_stack = jnp.concatenate(
+        [feed_parts[1], feed_parts[2], feed_parts[3].reshape(-1, feed_width)], axis=0
+    )
+    (feed_sum,) = ring_sum([feed_stack], "rep")
+    feed_rep = (
+        feed_sum[: feed_rows[0]],
+        feed_sum[feed_rows[0] : feed_rows[0] + feed_rows[1]],
+        feed_sum[feed_rows[0] + feed_rows[1] :].reshape(feed_parts[3].shape),
+    )
     grad_branch_low = grad_middle.astype(jnp.bfloat16)
     output_grad = inner_rows(mixed_low, grad_branch_low)
     grad_mixed_low = (

time: 1330 us -> 1390 us (1.045)
  starting transfers between devices: 71.7 us -> 127 us
  blocking collectives: 68.2 us -> 115 us
  waiting for transfers between devices: 638 us -> 605 us
  other arithmetic: 130 us -> 116 us
    all_gather x1, waiting for transfers between devices: 0.01 us -> 63.2 us  [per_device(): grad_down_group = lax.all_gather(grad_down_low, 'fsdp', axis=0, tiled=True)]
    ppermute x9 -> x3, starting transfers between devices: 7.57 us -> 56.8 us  [ring_sum(): own_a = lax.ppermute(own_a, axis, forward)]
    ppermute x9 -> x3, waiting for transfers between devices: 16.5 us -> 65.6 us  [ring_sum(): got_a = lax.ppermute([r.astype(jnp.bfloat16) for r in run_a], axis, forward)]
    reduce_scatter x4, waiting for transfers between devices: 48.6 us -> 0.03 us  [per_device(): lax.psum_scatter(v.astype(jnp.bfloat16), 'fsdp', scatter_dimension=0, til...]
    all_to_all x1, waiting for transfers between devices: 48 us -> 0.01 us  [per_device(): up_block = lax.all_to_all(up_weight, 'fsdp', 1, 0, tiled=True)]
    all_gather x1, blocking collectives: 10.6 us -> 56.5 us  [per_device(): lax.all_gather(attention_gain, 'fsdp', axis=0, tiled=True)]
    all_gather x1, waiting for transfers between devices: 48.2 us -> 12.7 us  [per_device(): lax.all_gather(query_weight, 'fsdp', axis=0, tiled=True)]
    ppermute x9 -> x3, starting transfers between devices: 4.3 us -> 39.4 us  [ring_sum(): got_a = lax.ppermute([r.astype(jnp.bfloat16) for r in run_a], axis, forward)]
  transfers between devices with their start and end apart: 53 -> 29, of which waited for: 28 -> 20; matrix products, arithmetic and copies ran while one was open for 32% -> 26% of each run, Pallas kernels for 0% -> 0%
where the time goes in v3:
time: 1390 us; the launch traced here: 1380 us
  waiting for transfers between devices  605 us (44%)
  matrix products  255 us (18%)
  local copies, waits for them, and re-layouts  143 us (10%)
  starting transfers between devices  127 us (9%)
  other arithmetic  116 us (8%)
  blocking collectives  115 us (8%)
  between operations  18 us (1%)
    reduce_scatter x1, waiting for transfers between devices, per_device(): lax.psum_scatter(down_part.astype(jnp.bfloat16), 'fsdp', scatter_dimensio...  87.3 us
    dot_general x7, matrix products, times_transposed(): lax.dot_general(left, right, (((1,), (1,)), ((), ())), preferred_element_...  77.7 us
    reduce_scatter x1, waiting for transfers between devices, per_device(): lax.psum_scatter(grad_normed_part.astype(jnp.bfloat16), 'fsdp', scatter_d...  77.5 us
    dot_general x7, matrix products, inner_rows(): lax.dot_general(left, right, (((0,), (0,)), ((), ())), preferred_element_...  68.7 us
    ppermute x3, waiting for transfers between devices, ring_sum(): got_a = lax.ppermute([r.astype(jnp.bfloat16) for r in run_a], axis, forward)  65.6 us
    all_gather x1, waiting for transfers between devices, per_device(): grad_down_group = lax.all_gather(grad_down_low, 'fsdp', axis=0, tiled=True)  63.2 us
    psum x1, waiting for transfers between devices, per_device(): lax.psum(attention_parts[1].astype(jnp.bfloat16), 'rep').astype(jnp.float32)  61.9 us
    all_gather x1, waiting for transfers between devices, per_device(): lax.all_gather(normed_two_low, 'fsdp', axis=0, tiled=True)  59 us
  transfers between devices with their start and end apart: 29, of which 20 were waited for; matrix products, arithmetic and copies ran while one was open for 26% of the time, Pallas kernels for 0%

profile of v3, /device:TPU:0, one launch (start us, length us, event | category | flops | bytes accessed | tf_op | source)
XLA Modules:
  0.0 1378.8 jit_solution(4307889181917074829)
XLA Ops:
  31.9 44.5 %all-to-all-done = bf16[256,8,768]{0,2,1:T(8,128)(2,1)} async-done(((bf16[256,8,768]{0,2,1:T(8,128)(2,1)}), bf16[256,8,768]{0,2,1:T(8,128)(2,1)}, u32[]{:S(2)}, u32[]{:S(2)}) %all-to-all-start) | async-done | bytes 3145760 | tf_op jit(solution)/shard_map/all_to_all | solution.py:146
  81.1 56.5 %all-gather = bf16[8,1,256]{2,1,0:T(2,128)(2,1)S(1)} all-gather(bf16[1,1,256]{2,1,0:T(2,128)(2,1)S(1)} %reshape.301), channel_id=1, replica_groups=mesh['fsdp'=8,'rep'=4] {'fsdp'}, dimensions={0}, use_global_device_ids=true | all-gather | bytes 4608 | tf_op jit(solution)/shard_map/all_gather | solution.py:140
  222.9 26.4 %all-gather.15.cloned.1.call-done = bf16[2048,2048]{1,0:T(8,128)(2,1)} async-done(((bf16[256,2048]{1,0:T(8,128)(2,1)}), bf16[2048,2048]{1,0:T(8,128)(2,1)}) %all-gather.15.cloned.1.call-update) | async-done | bytes 8388624 | tf_op jit(solution)/shard_map/all_gather | solution.py:144
  260.5 63.2 %all-gather.17.cloned.1.call-done = bf16[3072,2048]{1,0:T(8,128)(2,1)} async-done(((bf16[384,2048]{1,0:T(8,128)(2,1)}), bf16[3072,2048]{1,0:T(8,128)(2,1)}) %all-gather.17.cloned.1.call-update) | async-done | bytes 12582928 | tf_op jit(solution)/shard_map/all_gather | solution.py:192
  323.7 15.4 %fusion.65 = f32[3072,768]{1,0:T(8,128)} fusion(bf16[3072,2048]{1,0:T(8,128)(2,1)} %all-gather.17.cloned.1.call-done, bf16[768,2048]{1,0:T(8,128)(2,1)S(1)} %copy-done), kind=kOutput, calls=%fused_computation.155 | convolution fusion | flops 9663676416 | bytes 25165824 | tf_op jit(solution)/shard_map/dot_general | solution.py:51
  339.0 59.0 %all-gather.19.cloned.1.call-done = bf16[3072,2048]{1,0:T(8,128)(2,1)} async-done(((bf16[384,2048]{1,0:T(8,128)(2,1)}), bf16[3072,2048]{1,0:T(8,128)(2,1)}) %all-gather.19.cloned.1.call-update) | async-done | bytes 12582928 | tf_op jit(solution)/shard_map/all_gather | solution.py:185
  398.0 16.1 %fusion.66 = f32[3072,768]{1,0:T(8,128)} fusion(bf16[3072,2048]{1,0:T(8,128)(2,1)} %all-gather.19.cloned.1.call-done, bf16[2048,768]{1,0:T(8,128)(2,1)} %bitcast.255), kind=kOutput, calls=%fused_computation.156 | convolution fusion | flops 9663676416 | bytes 25165824 | tf_op jit(solution)/shard_map/dot_general | solution.py:186
  414.1 24.7 %multiply_convert_fusion = (bf16[3072,768]{1,0:T(8,128)(2,1)}, bf16[3072,768]{1,0:T(8,128)(2,1)}, bf16[3072,768]{1,0:T(8,128)(2,1)}) fusion(f32[3072,768]{1,0:T(8,128)} %fusion.66, f32[3072,768]{1,0:T(8,128)} %fusion.65, bf16[3072,2048]{1,0:T(8,128)(2,1)} %all-gather.19.cloned.1.call-done, bf16[2048,768]{1,0:T(8,128)(2,1)} %bitcast.257), kind=kOutput, calls=%fused_computation.10 | convolution fusion | flops 9699065856 | bytes 48758784 | tf_op jit(solution)/shard_map/dot_general | solution.py:187
  438.8 17.6 %fusion.67 = f32[3072,2048]{1,0:T(8,128)} fusion(bf16[3072,768]{1,0:T(8,128)(2,1)} %get-tuple-element.49, bf16[2048,768]{1,0:T(8,128)(2,1)} %bitcast.256), kind=kOutput, calls=%fused_computation.157 | convolution fusion | flops 9663676416 | bytes 33030144 | tf_op jit(solution)/shard_map/dot_general | solution.py:51
  456.4 19.7 %add_convert_fusion = bf16[3072,2048]{1,0:T(8,128)(2,1)} fusion(f32[3072,2048]{1,0:T(8,128)} %fusion.67, bf16[3072,768]{1,0:T(8,128)(2,1)} %get-tuple-element.50, bf16[2048,768]{1,0:T(8,128)(2,1)} %bitcast.258), kind=kOutput, calls=%fused_computation | convolution fusion | flops 9676259328 | bytes 45613056 | tf_op jit(solution)/shard_map/dot_general | solution.py:51
  476.2 14.9 %fusion.68 = bf16[3072,2048]{1,0:T(8,128)(2,1)} fusion(bf16[3072,768]{1,0:T(8,128)(2,1)} %get-tuple-element.48, bf16[768,2048]{1,0:T(8,128)(2,1)S(1)} %copy-done), kind=kOutput, calls=%fused_computation.158 | convolution fusion | flops 9663676416 | bytes 20447232 | tf_op jit(solution)/shard_map/dot_general | solution.py:189
  491.1 77.5 %reduce-scatter.7.cloned.1.call-done = bf16[384,2048]{1,0:T(8,128)(2,1)} async-done(((bf16[3072,2048]{1,0:T(8,128)(2,1)}), bf16[384,2048]{1,0:T(8,128)(2,1)}) %reduce-scatter.7.cloned.1.call-update) | async-done | bytes 1572880 | tf_op jit(solution)/shard_map/reduce_scatter | solution.py:205
  577.2 87.3 %reduce-scatter.9.cloned.1.call-done = bf16[384,2048]{1,0:T(8,128)(2,1)} async-done(((bf16[3072,2048]{1,0:T(8,128)(2,1)}), bf16[384,2048]{1,0:T(8,128)(2,1)}) %reduce-scatter.9.cloned.1.call-update) | async-done | bytes 1572880 | tf_op jit(solution)/shard_map/reduce_scatter | solution.py:209
  736.2 15.3 %convolution_convert_fusion.5 = bf16[2048,768]{1,0:T(8,128)(2,1)S(1)} fusion(bf16[3072,2048]{1,0:T(8,128)(2,1)} %all-gather.19.cloned.1.call-done, bf16[3072,768]{1,0:T(8,128)(2,1)} %get-tuple-element.49), kind=kOutput, calls=%fused_computation.39 | convolution fusion | flops 9665249280 | bytes 20447232 | tf_op jit(solution)/shard_map/dot_general | solution.py:45
  759.1 14.6 %convolution_convert_fusion.4 = bf16[2048,768]{1,0:T(8,128)(2,1)S(1)} fusion(bf16[3072,2048]{1,0:T(8,128)(2,1)} %all-gather.19.cloned.1.call-done, bf16[3072,768]{1,0:T(8,128)(2,1)} %get-tuple-element.50), kind=kOutput, calls=%fused_computation.38 | convolution fusion | flops 9665249280 | bytes 20447232 | tf_op jit(solution)/shard_map/dot_general | solution.py:45
  832.4 15.8 %convolution_convert_fusion.6 = bf16[768,2048]{1,0:T(8,128)(2,1)} fusion(bf16[3072,768]{1,0:T(8,128)(2,1)} %get-tuple-element.48, bf16[3072,2048]{1,0:T(8,128)(2,1)} %all-gather.17.cloned.1.call-done), kind=kOutput, calls=%fused_computation.40 | convolution fusion | flops 9665249280 | bytes 20447232 | tf_op jit(solution)/shard_map/dot_general | solution.py:45
  896.2 17.5 %collective-permute-done = bf16[96,6144]{1,0:T(8,128)(2,1)} collective-permute-done((bf16[96,6144]{1,0:T(8,128)(2,1)S(1)}, bf16[96,6144]{1,0:T(8,128)(2,1)}, u32[]{:S(2)}, u32[]{:S(2)}) %collective-permute-start) | collective-permute-done | bytes 1179680 | tf_op jit(solution)/shard_map/ppermute | solution.py:77
  915.6 18.4 %collective-permute-start.1 = (bf16[96,6144]{1,0:T(8,128)(2,1)S(1)}, bf16[96,6144]{1,0:T(8,128)(2,1)S(1)}, u32[]{:S(2)}, u32[]{:S(2)}) collective-permute-start(bf16[96,6144]{1,0:T(8,128)(2,1)S(1)} %fusion.37), channel_id=1, source_target_pairs={{0,1},{1,2},{2,3},{3,0},{4,5},{5,6},{6,7},{7,4},{8,9},{9,10},{10,1... | collective-permute-start | bytes 3538952 | tf_op jit(solution)/shard_map/ppermute | solution.py:77
  940.7 23.7 %collective-permute-done.1 = bf16[96,6144]{1,0:T(8,128)(2,1)S(1)} collective-permute-done((bf16[96,6144]{1,0:T(8,128)(2,1)S(1)}, bf16[96,6144]{1,0:T(8,128)(2,1)S(1)}, u32[]{:S(2)}, u32[]{:S(2)}) %collective-permute-start.1) | collective-permute-done | bytes 1179680 | tf_op jit(solution)/shard_map/ppermute | solution.py:77
  966.0 19.5 %collective-permute-start.2 = (bf16[96,6144]{1,0:T(8,128)(2,1)S(1)}, bf16[96,6144]{1,0:T(8,128)(2,1)S(1)}, u32[]{:S(2)}, u32[]{:S(2)}) collective-permute-start(bf16[96,6144]{1,0:T(8,128)(2,1)S(1)} %fusion.36), channel_id=1, source_target_pairs={{0,1},{1,2},{2,3},{3,0},{4,5},{5,6},{6,7},{7,4},{8,9},{9,10},{10,1... | collective-permute-start | bytes 3538952 | tf_op jit(solution)/shard_map/ppermute | solution.py:77
  991.3 24.4 %collective-permute-done.2 = bf16[96,6144]{1,0:T(8,128)(2,1)S(1)} collective-permute-done((bf16[96,6144]{1,0:T(8,128)(2,1)S(1)}, bf16[96,6144]{1,0:T(8,128)(2,1)S(1)}, u32[]{:S(2)}, u32[]{:S(2)}) %collective-permute-start.2) | collective-permute-done | bytes 1179680 | tf_op jit(solution)/shard_map/ppermute | solution.py:77
  1017.9 18.4 %collective-permute-start.3 = (bf16[96,6144]{1,0:T(8,128)(2,1)S(1)}, bf16[96,6144]{1,0:T(8,128)(2,1)}, u32[]{:S(2)}, u32[]{:S(2)}) collective-permute-start(bf16[96,6144]{1,0:T(8,128)(2,1)S(1)} %get-tuple-element.41), channel_id=1, source_target_pairs={{0,1},{1,2},{2,3},{3,0},{4,5},{5,6},{6,7},{7,4},{8,9},{9,10},{10,1... | collective-permute-start | bytes 3538952 | tf_op jit(solution)/shard_map/ppermute | solution.py:92
  1046.4 20.7 %collective-permute-done.3 = bf16[96,6144]{1,0:T(8,128)(2,1)} collective-permute-done((bf16[96,6144]{1,0:T(8,128)(2,1)S(1)}, bf16[96,6144]{1,0:T(8,128)(2,1)}, u32[]{:S(2)}, u32[]{:S(2)}) %collective-permute-start.3) | collective-permute-done | bytes 1179680 | tf_op jit(solution)/shard_map/ppermute | solution.py:92
  1067.1 19.5 %collective-permute-start.4 = (bf16[96,6144]{1,0:T(8,128)(2,1)}, bf16[96,6144]{1,0:T(8,128)(2,1)}, u32[]{:S(2)}, u32[]{:S(2)}) collective-permute-start(bf16[96,6144]{1,0:T(8,128)(2,1)} %collective-permute-done.3), channel_id=1, source_target_pairs={{0,1},{1,2},{2,3},{3,0},{4,5},{5,6},{6,7},{7,4},{8,9},{9,10},{10,1... | collective-permute-start | bytes 3538952 | tf_op jit(solution)/shard_map/ppermute | solution.py:92
  1102.9 15.5 %collective-permute-done.4 = bf16[96,6144]{1,0:T(8,128)(2,1)} collective-permute-done((bf16[96,6144]{1,0:T(8,128)(2,1)}, bf16[96,6144]{1,0:T(8,128)(2,1)}, u32[]{:S(2)}, u32[]{:S(2)}) %collective-permute-start.4) | collective-permute-done | bytes 1179680 | tf_op jit(solution)/shard_map/ppermute | solution.py:92
  1118.3 18.8 %collective-permute-start.5 = (bf16[96,6144]{1,0:T(8,128)(2,1)}, bf16[96,6144]{1,0:T(8,128)(2,1)S(1)}, u32[]{:S(2)}, u32[]{:S(2)}) collective-permute-start(bf16[96,6144]{1,0:T(8,128)(2,1)} %collective-permute-done.4), channel_id=1, source_target_pairs={{0,1},{1,2},{2,3},{3,0},{4,5},{5,6},{6,7},{7,4},{8,9},{9,10},{10,1... | collective-permute-start | bytes 3538952 | tf_op jit(solution)/shard_map/ppermute | solution.py:92
  1146.9 22.5 %collective-permute-done.5 = bf16[96,6144]{1,0:T(8,128)(2,1)S(1)} collective-permute-done((bf16[96,6144]{1,0:T(8,128)(2,1)}, bf16[96,6144]{1,0:T(8,128)(2,1)S(1)}, u32[]{:S(2)}, u32[]{:S(2)}) %collective-permute-start.5) | collective-permute-done | bytes 1179680 | tf_op jit(solution)/shard_map/ppermute | solution.py:92
  1170.4 17.8 %collective-permute-done.11 = bf16[96,6144]{1,0:T(8,128)(2,1)S(1)} collective-permute-done((bf16[96,6144]{1,0:T(8,128)(2,1)S(1)}, bf16[96,6144]{1,0:T(8,128)(2,1)S(1)}, u32[]{:S(2)}, u32[]{:S(2)}) %collective-permute-start.11) | collective-permute-done | bytes 1179680 | tf_op jit(solution)/shard_map/ppermute | solution.py:93
  1210.2 13.8 %fusion.64 = (f32[256,6144]{1,0:T(8,128)}, f32[256,6144]{1,0:T(8,128)}, f32[256,6144]{1,0:T(8,128)}) fusion(f32[768,6144]{1,0:T(8,128)} %bitcast_convert_fusion), kind=kLoop, calls=%fused_computation.154 | loop fusion | bytes 37748736 | tf_op jit(solution)/shard_map/slice | solution.py:233
  1231.5 14.9 %all-reduce.2 = bf16[2048]{0:T(1024)(128)(2,1)S(1)} all-reduce(bf16[2048]{0:T(1024)(128)(2,1)S(1)} %copy-done.61), channel_id=10, replica_groups=mesh['fsdp'=8,'rep'=4] {'fsdp'}, use_global_device_ids=true, to_apply=%region_29.30.clone | all-reduce | flops 2048 | bytes 8192
  1261.3 23.9 %all-reduce.3 = (bf16[2048]{0:T(1024)(128)(2,1)S(1)}, bf16[8,256]{1,0:T(8,128)(2,1)S(1)}) all-reduce(f32[2048]{0:T(1024)S(1)} %get-tuple-element.27, f32[8,256]{1,0:T(8,128)S(1)} %broadcast_in_dim.22), channel_id=4, replica_groups=mesh['fsdp'=8,'rep'=4] {'fsdp'}, use_global_device_ids=true, to_apply=%region_14.15.clone | all-reduce | flops 4096 | bytes 24576
  1303.3 61.9 %all-reduce.8.cloned.1.call-done = (bf16[256,2048]{1,0:T(8,128)(2,1)}, bf16[256,1024]{1,0:T(8,128)(2,1)}, bf16[256,1024]{1,0:T(8,128)(2,1)}, bf16[256,2048]{1,0:T(8,128)(2,1)}) async-done(((bf16[256,2048]{1,0:T(8,128)(2,1)}, bf16[256,1024]{1,0:T(8,128)(2,1)}, bf16[256,1024]{1,0:T(8,128)(2,1)}, bf16[256,2048]{1,0:T(8,128)(2,1)}), (bf16[256,2048]{1,0:T(8,128)(2,1)}, bf16[256,1024]{1,0:T(8,128)(2,1)}, ...) | async-done | bytes 3145744 | tf_op jit(solution)/shard_map/psum | solution.py:308
  (332 shorter events, 441.1 us)
Async XLA Ops:
  7.2 316.5 %copy-start = (bf16[768,2048]{1,0:T(8,128)(2,1)S(1)}, bf16[768,2048]{1,0:T(8,128)(2,1)}, u32[]{:S(2)}) copy-start(bf16[768,2048]{1,0:T(8,128)(2,1)} %param.28) | copy-start | bytes 9437188
  7.2 152.5 %all-gather.11.cloned.1.call-start = ((), (), s32[]{:S(2)}) async-start(), calls=%async_computation.11 | async-start | bytes 4718592 | tf_op jit(solution)/shard_map/all_gather | solution.py:142
  7.9 164.7 %all-gather.9.cloned.1.call-start = ((), (), s32[]{:S(2)}) async-start(), calls=%async_computation.10 | async-start | bytes 4718592 | tf_op jit(solution)/shard_map/all_gather | solution.py:143
  8.7 184.6 %all-gather.13.cloned.1.call-start = ((), (), s32[]{:S(2)}) async-start(), calls=%async_computation.12 | async-start | bytes 9437184 | tf_op jit(solution)/shard_map/all_gather | solution.py:141
  9.4 239.9 %all-gather.15.cloned.1.call-start = ((), (), s32[]{:S(2)}) async-start(), calls=%async_computation.13 | async-start | bytes 9437184 | tf_op jit(solution)/shard_map/all_gather | solution.py:144
  10.0 313.6 %all-gather.17.cloned.1.call-start = ((), (), s32[]{:S(2)}) async-start(), calls=%async_computation.14 | async-start | bytes 14155776 | tf_op jit(solution)/shard_map/all_gather | solution.py:192
  22.0 54.4 %all-to-all-start = ((bf16[256,8,768]{0,2,1:T(8,128)(2,1)}), bf16[256,8,768]{0,2,1:T(8,128)(2,1)}, u32[]{:S(2)}, u32[]{:S(2)}) async-start(bf16[256,8,768]{0,2,1:T(8,128)(2,1)} %bitcast.247), calls=%async_computation | async-start | bytes 6291456 | tf_op jit(solution)/shard_map/all_to_all | solution.py:146
  76.4 76.8 %all-to-all-start.1 = ((bf16[256,8,768]{0,2,1:T(8,128)(2,1)}), bf16[256,8,768]{0,2,1:T(8,128)(2,1)}, u32[]{:S(2)}, u32[]{:S(2)}) async-start(bf16[256,8,768]{0,2,1:T(8,128)(2,1)} %bitcast.245), calls=%async_computation.1 | async-start | bytes 6291456 | tf_op jit(solution)/shard_map/all_to_all | solution.py:147
  81.0 317.0 %all-gather.19.cloned.1.call-start = ((), (), s32[]{:S(2)}) async-start(), calls=%async_computation.15 | async-start | bytes 14155776 | tf_op jit(solution)/shard_map/all_gather | solution.py:185
  137.7 73.7 %copy-start.62 = (f32[128]{0:T(128)}, f32[128]{0:T(128)S(1)}, u32[]{:S(2)}) copy-start(f32[128]{0:T(128)S(1)} %convert_element_type.266) | copy-start | bytes 1540
  260.4 308.2 %reduce-scatter.7.cloned.1.call-start = ((), (), s32[]{:S(2)}) async-start(), calls=%async_computation.16 | async-start | bytes 14155776 | tf_op jit(solution)/shard_map/reduce_scatter | solution.py:205
  476.2 188.4 %reduce-scatter.9.cloned.1.call-start = ((), (), s32[]{:S(2)}) async-start(), calls=%async_computation.17 | async-start | bytes 14155776 | tf_op jit(solution)/shard_map/reduce_scatter | solution.py:209
  572.1 674.4 %reduce-scatter.13.cloned.1.call-start = ((), (), s32[]{:S(2)}) async-start(), calls=%async_computation.19 | async-start | bytes 4718592 | tf_op jit(solution)/shard_map/reduce_scatter | solution.py:291
  574.0 90.6 %copy-start.60 = (f32[384]{0:T(512)S(1)}, f32[384]{0:T(512)}, u32[]{:S(2)}) copy-start(f32[384]{0:T(512)} %copy-done.59) | copy-start | bytes 4612
  715.3 531.2 %reduce-scatter.15.cloned.1.call-start = ((), (), s32[]{:S(2)}) async-start(), calls=%async_computation.20 | async-start | bytes 4718592 | tf_op jit(solution)/shard_map/reduce_scatter | solution.py:291
  754.2 66.2 %all-to-all-start.2 = ((bf16[8,256,768]{1,2,0:T(8,128)(2,1)}), bf16[8,256,768]{1,2,0:T(8,128)(2,1)}, u32[]{:S(2)}, u32[]{:S(2)}) async-start(bf16[8,256,768]{1,2,0:T(8,128)(2,1)} %copy.210), calls=%async_computation.8 | async-start | bytes 6291456 | tf_op jit(solution)/shard_map/all_to_all | solution.py:220
  820.4 45.9 %all-to-all-start.3 = ((bf16[8,256,768]{1,2,0:T(8,128)(2,1)}), bf16[8,256,768]{1,2,0:T(8,128)(2,1)}, u32[]{:S(2)}, u32[]{:S(2)}) async-start(bf16[8,256,768]{1,2,0:T(8,128)(2,1)} %copy.211), calls=%async_computation.9 | async-start | bytes 6291456 | tf_op jit(solution)/shard_map/all_to_all | solution.py:221
  825.2 421.4 %reduce-scatter.11.cloned.1.call-start = ((), (), s32[]{:S(2)}) async-start(), calls=%async_computation.18 | async-start | bytes 9437184 | tf_op jit(solution)/shard_map/reduce_scatter | solution.py:291
  832.3 414.3 %reduce-scatter.17.cloned.1.call-start = ((), (), s32[]{:S(2)}) async-start(), calls=%async_computation.21 | async-start | bytes 9437184 | tf_op jit(solution)/shard_map/reduce_scatter | solution.py:291
  882.8 30.8 %collective-permute-start = (bf16[96,6144]{1,0:T(8,128)(2,1)S(1)}, bf16[96,6144]{1,0:T(8,128)(2,1)}, u32[]{:S(2)}, u32[]{:S(2)}) collective-permute-start(bf16[96,6144]{1,0:T(8,128)(2,1)S(1)} %dynamic-slice_bitcast_fusion.1), channel_id=1, source_target_pairs={{0,1},{1,2},{2,3},{3,0},{4,5},{5,6},{6,7},{7,4},{8,9},{9,10},{10,1... | collective-permute-start | bytes 3538952 | tf_op jit(solution)/shard_map/ppermute | solution.py:77
  893.8 45.0 %collective-permute-start.6 = (bf16[96,6144]{1,0:T(8,128)(2,1)S(1)}, bf16[96,6144]{1,0:T(8,128)(2,1)S(1)}, u32[]{:S(2)}, u32[]{:S(2)}) collective-permute-start(bf16[96,6144]{1,0:T(8,128)(2,1)S(1)} %dynamic-slice_bitcast_fusion), channel_id=1, source_target_pairs={{0,3},{1,0},{2,1},{3,2},{4,7},{5,4},{6,5},{7,6},{8,11},{9,8},{10,9... | collective-permute-start | bytes 3538952 | tf_op jit(solution)/shard_map/ppermute | solution.py:78
  915.6 48.7 %collective-permute-start.1 = (bf16[96,6144]{1,0:T(8,128)(2,1)S(1)}, bf16[96,6144]{1,0:T(8,128)(2,1)S(1)}, u32[]{:S(2)}, u32[]{:S(2)}) collective-permute-start(bf16[96,6144]{1,0:T(8,128)(2,1)S(1)} %fusion.37), channel_id=1, source_target_pairs={{0,1},{1,2},{2,3},{3,0},{4,5},{5,6},{6,7},{7,4},{8,9},{9,10},{10,1... | collective-permute-start | bytes 3538952 | tf_op jit(solution)/shard_map/ppermute | solution.py:77
  939.1 50.5 %collective-permute-start.7 = (bf16[96,6144]{1,0:T(8,128)(2,1)S(1)}, bf16[96,6144]{1,0:T(8,128)(2,1)S(1)}, u32[]{:S(2)}, u32[]{:S(2)}) collective-permute-start(bf16[96,6144]{1,0:T(8,128)(2,1)S(1)} %fusion.34), channel_id=1, source_target_pairs={{0,3},{1,0},{2,1},{3,2},{4,7},{5,4},{6,5},{7,6},{8,11},{9,8},{10,9... | collective-permute-start | bytes 3538952 | tf_op jit(solution)/shard_map/ppermute | solution.py:78
  966.0 49.8 %collective-permute-start.2 = (bf16[96,6144]{1,0:T(8,128)(2,1)S(1)}, bf16[96,6144]{1,0:T(8,128)(2,1)S(1)}, u32[]{:S(2)}, u32[]{:S(2)}) collective-permute-start(bf16[96,6144]{1,0:T(8,128)(2,1)S(1)} %fusion.36), channel_id=1, source_target_pairs={{0,1},{1,2},{2,3},{3,0},{4,5},{5,6},{6,7},{7,4},{8,9},{9,10},{10,1... | collective-permute-start | bytes 3538952 | tf_op jit(solution)/shard_map/ppermute | solution.py:77
  989.9 51.1 %collective-permute-start.8 = (bf16[96,6144]{1,0:T(8,128)(2,1)S(1)}, bf16[96,6144]{1,0:T(8,128)(2,1)S(1)}, u32[]{:S(2)}, u32[]{:S(2)}) collective-permute-start(bf16[96,6144]{1,0:T(8,128)(2,1)S(1)} %fusion.33), channel_id=1, source_target_pairs={{0,3},{1,0},{2,1},{3,2},{4,7},{5,4},{6,5},{7,6},{8,11},{9,8},{10,9... | collective-permute-start | bytes 3538952 | tf_op jit(solution)/shard_map/ppermute | solution.py:78
  1017.9 49.2 %collective-permute-start.3 = (bf16[96,6144]{1,0:T(8,128)(2,1)S(1)}, bf16[96,6144]{1,0:T(8,128)(2,1)}, u32[]{:S(2)}, u32[]{:S(2)}) collective-permute-start(bf16[96,6144]{1,0:T(8,128)(2,1)S(1)} %get-tuple-element.41), channel_id=1, source_target_pairs={{0,1},{1,2},{2,3},{3,0},{4,5},{5,6},{6,7},{7,4},{8,9},{9,10},{10,1... | collective-permute-start | bytes 3538952 | tf_op jit(solution)/shard_map/ppermute | solution.py:92
  1045.1 50.9 %collective-permute-start.9 = (bf16[96,6144]{1,0:T(8,128)(2,1)}, bf16[96,6144]{1,0:T(8,128)(2,1)}, u32[]{:S(2)}, u32[]{:S(2)}) collective-permute-start(bf16[96,6144]{1,0:T(8,128)(2,1)} %get-tuple-element.43), channel_id=1, source_target_pairs={{0,3},{1,0},{2,1},{3,2},{4,7},{5,4},{6,5},{7,6},{8,11},{9,8},{10,9... | collective-permute-start | bytes 3538952 | tf_op jit(solution)/shard_map/ppermute | solution.py:93
  1067.1 51.2 %collective-permute-start.4 = (bf16[96,6144]{1,0:T(8,128)(2,1)}, bf16[96,6144]{1,0:T(8,128)(2,1)}, u32[]{:S(2)}, u32[]{:S(2)}) collective-permute-start(bf16[96,6144]{1,0:T(8,128)(2,1)} %collective-permute-done.3), channel_id=1, source_target_pairs={{0,1},{1,2},{2,3},{3,0},{4,5},{5,6},{6,7},{7,4},{8,9},{9,10},{10,1... | collective-permute-start | bytes 3538952 | tf_op jit(solution)/shard_map/ppermute | solution.py:92
  1093.5 271.6 %all-reduce.8.cloned.1.call-start = ((), (), s32[]{:S(2)}) async-start(), calls=%async_computation.22 | async-start | bytes 6291456 | tf_op jit(solution)/shard_map/psum | solution.py:308
  1095.9 47.5 %collective-permute-start.10 = (bf16[96,6144]{1,0:T(8,128)(2,1)}, bf16[96,6144]{1,0:T(8,128)(2,1)S(1)}, u32[]{:S(2)}, u32[]{:S(2)}) collective-permute-start(bf16[96,6144]{1,0:T(8,128)(2,1)} %collective-permute-done.9), channel_id=1, source_target_pairs={{0,3},{1,0},{2,1},{3,2},{4,7},{5,4},{6,5},{7,6},{8,11},{9,8},{10,9... | collective-permute-start | bytes 3538952 | tf_op jit(solution)/shard_map/ppermute | solution.py:93
  1118.3 51.0 %collective-permute-start.5 = (bf16[96,6144]{1,0:T(8,128)(2,1)}, bf16[96,6144]{1,0:T(8,128)(2,1)S(1)}, u32[]{:S(2)}, u32[]{:S(2)}) collective-permute-start(bf16[96,6144]{1,0:T(8,128)(2,1)} %collective-permute-done.4), channel_id=1, source_target_pairs={{0,1},{1,2},{2,3},{3,0},{4,5},{5,6},{6,7},{7,4},{8,9},{9,10},{10,1... | collective-permute-start | bytes 3538952 | tf_op jit(solution)/shard_map/ppermute | solution.py:92
  1143.4 44.8 %collective-permute-start.11 = (bf16[96,6144]{1,0:T(8,128)(2,1)S(1)}, bf16[96,6144]{1,0:T(8,128)(2,1)S(1)}, u32[]{:S(2)}, u32[]{:S(2)}) collective-permute-start(bf16[96,6144]{1,0:T(8,128)(2,1)S(1)} %collective-permute-done.10), channel_id=1, source_target_pairs={{0,3},{1,0},{2,1},{3,2},{4,7},{5,4},{6,5},{7,6},{8,11},{9,8},{10,9... | collective-permute-start | bytes 3538952 | tf_op jit(solution)/shard_map/ppermute | solution.py:93
  (71 other events, 800.4 us)
Sparse Core Ops, SparseCore 0:
  9.9 58.4 all-gather.10
  70.3 65.5 all-gather.8
  137.8 55.3 all-gather.12
  195.0 54.2 all-gather.14
  251.6 71.9 all-gather.16
  326.0 71.9 all-gather.18
  476.3 92.2 reduce-scatter.6
  572.2 92.2 reduce-scatter.8
  715.5 54.3 reduce-scatter.12
  773.0 63.1 reduce-scatter.14
  839.7 79.7 reduce-scatter.10
  1093.6 72.4 reduce-scatter.16
  1246.7 118.4 all-reduce.7

commit v4 on v1

--- a/solution.py
+++ b/solution.py
@@ -2,6 +2,7 @@
 import jax.numpy as jnp
 from jax import lax
 from jax.sharding import PartitionSpec as P
+
 
 EPSILON = 1e-06
 ROPE_BASE = 1000000.0
@@ -58,6 +59,66 @@
     length = query_low.shape[0]
     causal = jnp.arange(length)[:, None] >= jnp.arange(length)[None, :]
     return jnp.where(causal, scores, -1000000000.0)
+
+
+class RepRing:
+    def __init__(self, part, axis):
+        n = lax.axis_size(axis)
+        self.n, self.axis, self.shape = n, axis, part.shape
+        self.me = lax.axis_index(axis)
+        self.forward = [(i, (i + 1) % n) for i in range(n)]
+        self.backward = [(i, (i - 1) % n) for i in range(n)]
+        pieces = part.reshape((2, n, part.shape[0] // (2 * n)) + part.shape[1:])
+        self.ahead, self.behind = pieces[0], pieces[1]
+        self.run_a = self.take(self.ahead, self.me)
+        self.run_b = self.take(self.behind, self.me)
+        self.step = 0
+        self.steps = 2 * (n - 1)
+
+    def take(self, q, i):
+        return lax.dynamic_index_in_dim(q, i % self.n, axis=0, keepdims=False).astype(
+            jnp.float32
+        )
+
+    def issue(self):
+        if self.step >= self.steps:
+            return
+        if self.step < self.n - 1:
+            sends = (self.run_a.astype(jnp.bfloat16), self.run_b.astype(jnp.bfloat16))
+        else:
+            sends = (self.own_a, self.own_b)
+        self.pending = (
+            lax.ppermute(sends[0], self.axis, self.forward),
+            lax.ppermute(sends[1], self.axis, self.backward),
+        )
+
+    def land(self, carry):
+        if self.step >= self.steps:
+            return carry
+        (got_a, got_b), carry = lax.optimization_barrier((self.pending, carry))
+        n, me, s = self.n, self.me, self.step
+        if s < n - 1:
+            self.run_a = got_a.astype(jnp.float32) + self.take(self.ahead, me - 1 - s)
+            self.run_b = got_b.astype(jnp.float32) + self.take(self.behind, me + 1 + s)
+            if s == n - 2:
+                self.own_a = self.run_a.astype(jnp.bfloat16)
+                self.own_b = self.run_b.astype(jnp.bfloat16)
+                zeros = jnp.zeros(self.ahead.shape, jnp.bfloat16)
+                self.out_a = lax.dynamic_update_index_in_dim(zeros, self.own_a, (me + 1) % n, 0)
+                self.out_b = lax.dynamic_update_index_in_dim(zeros, self.own_b, (me - 1) % n, 0)
+        else:
+            t = s - (n - 1)
+            self.own_a, self.own_b = got_a, got_b
+            self.out_a = lax.dynamic_update_index_in_dim(self.out_a, got_a, (me - t) % n, 0)
+            self.out_b = lax.dynamic_update_index_in_dim(self.out_b, got_b, (me + t) % n, 0)
+        self.step += 1
+        return carry
+
+    def result(self):
+        while self.step < self.steps:
+            self.issue()
+            self.land(())
+        return jnp.stack([self.out_a, self.out_b]).reshape(self.shape).astype(jnp.float32)
 
 
 def per_device(
@@ -100,6 +161,7 @@
     )
     gate_block = lax.all_to_all(gate_weight, "fsdp", 1, 0, tiled=True)
     up_block = lax.all_to_all(up_weight, "fsdp", 1, 0, tiled=True)
+    tokens, gate_block, up_block = lax.optimization_barrier((tokens, gate_block, up_block))
     inputs_wide = tokens.astype(jnp.float32)
     gain_one = attention_set[0].astype(jnp.float32)
     normed_one, normal_one, inverse_one = rms_forward(inputs_wide, gain_one)
@@ -141,8 +203,6 @@
     up_value = jnp.dot(normed_two_group, up_block, preferred_element_type=jnp.float32)
     hidden_low = (jax.nn.silu(gate_value) * up_value).astype(jnp.bfloat16)
     down_part = jnp.dot(hidden_low, down_weight, preferred_element_type=jnp.float32)
-    down_value = lax.psum_scatter(down_part, "fsdp", scatter_dimension=0, tiled=True)
-    layer_out = ((middle + down_value) * valid_rows).astype(jnp.bfloat16)
     grad_top = cotangent.astype(jnp.float32) * valid_rows
     grad_down_low = grad_top.astype(jnp.bfloat16)
     grad_down_group = lax.all_gather(grad_down_low, "fsdp", axis=0, tiled=True)
@@ -158,7 +218,13 @@
     grad_normed_part = times_transposed(grad_gate_low, gate_block) + times_transposed(
         grad_up_low, up_block
     )
-    grad_normed_two = lax.psum_scatter(grad_normed_part, "fsdp", scatter_dimension=0, tiled=True)
+    grad_normed_two = lax.psum_scatter(
+        grad_normed_part.astype(jnp.bfloat16), "fsdp", scatter_dimension=0, tiled=True
+    ).astype(jnp.float32)
+    grad_normed_two, down_part = lax.optimization_barrier((grad_normed_two, down_part))
+    down_value = lax.psum_scatter(
+        down_part.astype(jnp.bfloat16), "fsdp", scatter_dimension=0, tiled=True
+    ).astype(jnp.float32)
     grad_from_two, gain_two_terms = rms_backward(grad_normed_two, normal_two, inverse_two, gain_two)
     feed_gain_grad = jnp.sum(gain_two_terms, axis=0)
     grad_middle = grad_top + grad_from_two
@@ -166,14 +232,17 @@
         lax.psum_scatter(
             feed_gain_grad.astype(jnp.bfloat16), "fsdp", scatter_dimension=0, tiled=True
         ).astype(jnp.float32),
-        lax.all_to_all(gate_grad_block.astype(jnp.bfloat16), "fsdp", 0, 1, tiled=True).astype(
-            jnp.float32
-        ),
-        lax.all_to_all(up_grad_block.astype(jnp.bfloat16), "fsdp", 0, 1, tiled=True).astype(
-            jnp.float32
-        ),
-        down_grad,
-    )
+        lax.all_to_all(gate_grad_block.astype(jnp.bfloat16), "fsdp", 0, 1, tiled=True),
+        lax.all_to_all(up_grad_block.astype(jnp.bfloat16), "fsdp", 0, 1, tiled=True),
+        down_grad.astype(jnp.bfloat16),
+    )
+    feed_width = feed_parts[1].shape[1]
+    feed_rows = [feed_parts[1].shape[0], feed_parts[2].shape[0]]
+    feed_stack = jnp.concatenate(
+        [feed_parts[1], feed_parts[2], feed_parts[3].reshape(-1, feed_width)], axis=0
+    )
+    ring = RepRing(feed_stack, "rep")
+    ring.issue()
     grad_branch_low = grad_middle.astype(jnp.bfloat16)
     output_grad = inner_rows(mixed_low, grad_branch_low)
     grad_mixed_low = (
@@ -181,6 +250,8 @@
         .astype(jnp.bfloat16)
         .reshape(row_count, value_heads, group_size, head_width)
     )
+    grad_mixed_low, output_grad = ring.land((grad_mixed_low, output_grad))
+    ring.issue()
     scores_again = masked_scores(query_low, key_low)
     probs_again = jnp.exp(scores_again - log_total)
     probs_again_low = probs_again.astype(jnp.bfloat16)
@@ -189,6 +260,8 @@
     )
     row_term = jnp.sum(probs_again * grad_probs, axis=-1, keepdims=True)
     grad_scores_low = (probs_again * (grad_probs - row_term)).astype(jnp.bfloat16)
+    grad_scores_low, probs_again_low = ring.land((grad_scores_low, probs_again_low))
+    ring.issue()
     grad_query_rot = (
         jnp.einsum(
             "kgqs,skd->qkgd", grad_scores_low, key_low, preferred_element_type=jnp.float32
@@ -205,6 +278,10 @@
         .astype(jnp.bfloat16)
         .reshape(row_count, value_heads * head_width)
     )
+    grad_query_rot, grad_key_rot, grad_value_low = ring.land(
+        (grad_query_rot, grad_key_rot, grad_value_low)
+    )
+    ring.issue()
     grad_query_raw, query_gain_terms = rms_backward(
         unrotate(grad_query_rot, cosine, sine), query_normal, query_inverse, gain_query
     )
@@ -217,17 +294,30 @@
         row_count, query_heads * head_width
     )
     grad_key_low = grad_key_raw.astype(jnp.bfloat16).reshape(row_count, value_heads * head_width)
+    value_grad = inner_rows(normed_one_low, grad_value_low)
+    grad_query_low, grad_key_low = ring.land((grad_query_low, grad_key_low))
+    ring.issue()
     query_grad = inner_rows(normed_one_low, grad_query_low)
     key_grad = inner_rows(normed_one_low, grad_key_low)
-    value_grad = inner_rows(normed_one_low, grad_value_low)
+    grad_normed_one = times_transposed(grad_query_low, attention_set[1])
+    grad_normed_one, down_value = ring.land((grad_normed_one, down_value))
+    ring.issue()
+    layer_out = ((middle + down_value) * valid_rows).astype(jnp.bfloat16)
     grad_normed_one = (
-        times_transposed(grad_query_low, attention_set[1])
+        grad_normed_one
         + times_transposed(grad_key_low, attention_set[2])
         + times_transposed(grad_value_low, attention_set[3])
     )
     grad_from_one, gain_one_terms = rms_backward(grad_normed_one, normal_one, inverse_one, gain_one)
     attention_gain_grad = jnp.sum(gain_one_terms, axis=0)
     input_grad = grad_middle + grad_from_one
+    input_grad = ring.land(input_grad)
+    feed_sum = ring.result()
+    feed_rep = (
+        feed_sum[: feed_rows[0]],
+        feed_sum[feed_rows[0] : feed_rows[0] + feed_rows[1]],
+        feed_sum[feed_rows[0] + feed_rows[1] :].reshape(feed_parts[3].shape),
+    )
     head_terms = jnp.concatenate([query_gain_grad, key_gain_grad])
     head_tiles = jnp.broadcast_to(head_terms[None, :], (lax.axis_size("fsdp"), head_terms.shape[0]))
     low_sum = lambda v: lax.psum_scatter(
@@ -243,9 +333,9 @@
     )
     finals = (
         lax.psum(feed_parts[0].astype(jnp.bfloat16), "rep").astype(jnp.float32),
-        lax.psum(feed_parts[1].astype(jnp.bfloat16), "rep").astype(jnp.float32),
-        lax.psum(feed_parts[2].astype(jnp.bfloat16), "rep").astype(jnp.float32),
-        lax.psum(feed_parts[3].astype(jnp.bfloat16), "rep").astype(jnp.float32),
+        feed_rep[0],
+        feed_rep[1],
+        feed_rep[2],
         lax.psum(attention_parts[0].astype(jnp.bfloat16), "rep").astype(jnp.float32),
         lax.psum(attention_parts[1].astype(jnp.bfloat16), "rep").astype(jnp.float32),
         lax.psum(attention_parts[2].astype(jnp.bfloat16), "rep").astype(jnp.float32),

time: 1590 us -> 1420 us (0.89)
  waiting for transfers between devices: 1050 us -> 698 us
  blocking collectives: 68.8 us -> 174 us
  local copies, waits for them, and re-layouts: 78.4 us -> 126 us
  starting transfers between devices: 19.4 us -> 43.6 us
    psum x1, waiting for transfers between devices: 357 us -> 53.9 us  [per_device(): lax.psum(attention_parts[1].astype(jnp.bfloat16), 'rep').astype(jnp.float32)]
    reduce_scatter x2, waiting for transfers between devices: 294 us -> 95.6 us  [the longest x1 95.6 us: per_device(): lax.psum_scatter(down_part.astype(jnp.bfloat16), 'fsdp', scatter_dimensio...]
    ppermute x0 -> x12, waiting for transfers between devices: none -> 130 us  [the longest x6 89 us: issue(): lax.ppermute(sends[1], self.axis, self.backward)]
    reduce_scatter x4, waiting for transfers between devices: 65.4 us -> 154 us  [per_device(): lax.psum_scatter(v.astype(jnp.bfloat16), 'fsdp', scatter_dimension=0, til...]
    all_gather x1, waiting for transfers between devices: 0.01 us -> 58.9 us  [per_device(): lax.all_gather(normed_two_low, 'fsdp', axis=0, tiled=True)]
    all_to_all x1, waiting for transfers between devices: 58.2 us -> 0.01 us  [per_device(): up_block = lax.all_to_all(up_weight, 'fsdp', 1, 0, tiled=True)]
    psum x1, blocking collectives: 12.9 us -> 69.5 us  [per_device(): lax.psum(attention_parts[0].astype(jnp.bfloat16), 'rep').astype(jnp.float32)]
    all_gather x1, blocking collectives: 9.05 us -> 56.5 us  [per_device(): lax.all_gather(attention_gain, 'fsdp', axis=0, tiled=True)]
  transfers between devices with their start and end apart: 17 -> 29, of which waited for: 13 -> 19; matrix products, arithmetic and copies ran while one was open for 19% -> 23% of each run, Pallas kernels for 0% -> 0%
where the time goes in v4:
time: 1420 us; the launch traced here: 1410 us
  waiting for transfers between devices  698 us (49%)
  matrix products  257 us (18%)
  blocking collectives  174 us (12%)
  local copies, waits for them, and re-layouts  126 us (9%)
  other arithmetic  95.3 us (7%)
  starting transfers between devices  43.6 us (3%)
  between operations  17.7 us (1%)
    reduce_scatter x4, waiting for transfers between devices, per_device(): lax.psum_scatter(v.astype(jnp.bfloat16), 'fsdp', scatter_dimension=0, til...  154 us
    reduce_scatter x1, waiting for transfers between devices, per_device(): lax.psum_scatter(down_part.astype(jnp.bfloat16), 'fsdp', scatter_dimensio...  95.6 us
    ppermute x6, waiting for transfers between devices, issue(): lax.ppermute(sends[1], self.axis, self.backward)  89 us
    dot_general x7, matrix products, times_transposed(): lax.dot_general(left, right, (((1,), (1,)), ((), ())), preferred_element_...  76.9 us
    dot_general x7, matrix products, inner_rows(): lax.dot_general(left, right, (((0,), (0,)), ((), ())), preferred_element_...  73.3 us
    psum x1, blocking collectives, per_device(): lax.psum(attention_parts[0].astype(jnp.bfloat16), 'rep').astype(jnp.float32)  69.5 us
    all_gather x1, waiting for transfers between devices, per_device(): grad_down_group = lax.all_gather(grad_down_low, 'fsdp', axis=0, tiled=True)  63.2 us
    all_gather x1, waiting for transfers between devices, per_device(): lax.all_gather(normed_two_low, 'fsdp', axis=0, tiled=True)  58.9 us
  transfers between devices with their start and end apart: 29, of which 19 were waited for; matrix products, arithmetic and copies ran while one was open for 23% of the time, Pallas kernels for 0%

profile of v4, /device:TPU:0, one launch (start us, length us, event | category | flops | bytes accessed | tf_op | source)
XLA Modules:
  0.0 1412.1 jit_solution(10123755991666828975)
XLA Ops:
  31.8 44.5 %all-to-all-done = bf16[256,8,768]{0,2,1:T(8,128)(2,1)} async-done(((bf16[256,8,768]{0,2,1:T(8,128)(2,1)}), bf16[256,8,768]{0,2,1:T(8,128)(2,1)}, u32[]{:S(2)}, u32[]{:S(2)}) %all-to-all-start) | async-done | bytes 3145760 | tf_op jit(solution)/shard_map/all_to_all | solution.py:162
  81.0 56.5 %all-gather = bf16[8,1,256]{2,1,0:T(2,128)(2,1)S(1)} all-gather(bf16[1,1,256]{2,1,0:T(2,128)(2,1)S(1)} %reshape.275), channel_id=1, replica_groups=mesh['fsdp'=8,'rep'=4] {'fsdp'}, dimensions={0}, use_global_device_ids=true | all-gather | bytes 4608 | tf_op jit(solution)/shard_map/all_gather | solution.py:156
  219.9 29.4 %all-gather.15.cloned.1.call-done = bf16[2048,2048]{1,0:T(8,128)(2,1)} async-done(((bf16[256,2048]{1,0:T(8,128)(2,1)}), bf16[2048,2048]{1,0:T(8,128)(2,1)}) %all-gather.15.cloned.1.call-update) | async-done | bytes 8388624 | tf_op jit(solution)/shard_map/all_gather | solution.py:160
  260.4 63.2 %all-gather.19.cloned.1.call-done = bf16[3072,2048]{1,0:T(8,128)(2,1)} async-done(((bf16[384,2048]{1,0:T(8,128)(2,1)}), bf16[3072,2048]{1,0:T(8,128)(2,1)}) %all-gather.19.cloned.1.call-update) | async-done | bytes 12582928 | tf_op jit(solution)/shard_map/all_gather | solution.py:208
  323.6 15.4 %fusion.63 = f32[3072,768]{1,0:T(8,128)} fusion(bf16[3072,2048]{1,0:T(8,128)(2,1)} %all-gather.19.cloned.1.call-done, bf16[768,2048]{1,0:T(8,128)(2,1)S(1)} %copy-done), kind=kOutput, calls=%fused_computation.144 | convolution fusion | flops 9663676416 | bytes 25165824 | tf_op jit(solution)/shard_map/dot_general | solution.py:52
  339.0 58.9 %all-gather.17.cloned.1.call-done = bf16[3072,2048]{1,0:T(8,128)(2,1)} async-done(((bf16[384,2048]{1,0:T(8,128)(2,1)}), bf16[3072,2048]{1,0:T(8,128)(2,1)}) %all-gather.17.cloned.1.call-update) | async-done | bytes 12582928 | tf_op jit(solution)/shard_map/all_gather | solution.py:201
  397.9 16.1 %fusion.64 = f32[3072,768]{1,0:T(8,128)} fusion(bf16[3072,2048]{1,0:T(8,128)(2,1)} %all-gather.17.cloned.1.call-done, bf16[2048,768]{1,0:T(8,128)(2,1)} %bitcast.216), kind=kOutput, calls=%fused_computation.145 | convolution fusion | flops 9663676416 | bytes 25165824 | tf_op jit(solution)/shard_map/dot_general | solution.py:202
  414.1 24.9 %multiply_convert_fusion = (bf16[3072,768]{1,0:T(8,128)(2,1)}, bf16[3072,768]{1,0:T(8,128)(2,1)}, bf16[3072,768]{1,0:T(8,128)(2,1)}) fusion(f32[3072,768]{1,0:T(8,128)} %fusion.64, f32[3072,768]{1,0:T(8,128)} %fusion.63, bf16[3072,2048]{1,0:T(8,128)(2,1)} %all-gather.17.cloned.1.call-done, bf16[2048,768]{1,0:T(8,128)(2,1)} %bitcast.218), kind=kOutput, calls=%fused_computation.10 | convolution fusion | flops 9699065856 | bytes 48758784 | tf_op jit(solution)/shard_map/dot_general | solution.py:203
  439.0 17.5 %fusion.65 = f32[3072,2048]{1,0:T(8,128)} fusion(bf16[3072,768]{1,0:T(8,128)(2,1)} %get-tuple-element.99, bf16[2048,768]{1,0:T(8,128)(2,1)} %bitcast.217), kind=kOutput, calls=%fused_computation.146 | convolution fusion | flops 9663676416 | bytes 33030144 | tf_op jit(solution)/shard_map/dot_general | solution.py:52
  456.5 19.5 %add_convert_fusion = bf16[3072,2048]{1,0:T(8,128)(2,1)} fusion(f32[3072,2048]{1,0:T(8,128)} %fusion.65, bf16[3072,768]{1,0:T(8,128)(2,1)} %get-tuple-element.100, bf16[2048,768]{1,0:T(8,128)(2,1)} %bitcast.219), kind=kOutput, calls=%fused_computation.1 | convolution fusion | flops 9676259328 | bytes 45613056 | tf_op jit(solution)/shard_map/dot_general | solution.py:52
  476.1 15.8 %convolution_convert_fusion.3 = bf16[2048,768]{1,0:T(8,128)(2,1)} fusion(bf16[3072,2048]{1,0:T(8,128)(2,1)} %all-gather.17.cloned.1.call-done, bf16[3072,768]{1,0:T(8,128)(2,1)} %get-tuple-element.100), kind=kOutput, calls=%fused_computation.33 | convolution fusion | flops 9665249280 | bytes 20447232 | tf_op jit(solution)/shard_map/dot_general | solution.py:46
  509.4 15.8 %convolution_convert_fusion.4 = bf16[2048,768]{1,0:T(8,128)(2,1)} fusion(bf16[3072,2048]{1,0:T(8,128)(2,1)} %all-gather.17.cloned.1.call-done, bf16[3072,768]{1,0:T(8,128)(2,1)} %get-tuple-element.99), kind=kOutput, calls=%fused_computation.34 | convolution fusion | flops 9665249280 | bytes 20447232 | tf_op jit(solution)/shard_map/dot_general | solution.py:46
  529.8 41.5 %all-to-all-done.3 = bf16[8,256,768]{1,2,0:T(8,128)(2,1)} async-done(((bf16[8,256,768]{1,2,0:T(8,128)(2,1)}), bf16[8,256,768]{1,2,0:T(8,128)(2,1)}, u32[]{:S(2)}, u32[]{:S(2)}) %all-to-all-start.3) | async-done | bytes 3145760 | tf_op jit(solution)/shard_map/all_to_all | solution.py:236
  575.9 17.0 %convolution_convert_fusion.5 = bf16[768,2048]{1,0:T(8,128)(2,1)} fusion(bf16[3072,768]{1,0:T(8,128)(2,1)} %get-tuple-element.98, bf16[3072,2048]{1,0:T(8,128)(2,1)} %all-gather.19.cloned.1.call-done), kind=kOutput, calls=%fused_computation.35 | convolution fusion | flops 9665249280 | bytes 20447232 | tf_op jit(solution)/shard_map/dot_general | solution.py:46
  603.2 14.7 %fusion.66 = bf16[3072,2048]{1,0:T(8,128)(2,1)} fusion(bf16[3072,768]{1,0:T(8,128)(2,1)} %get-tuple-element.98, bf16[768,2048]{1,0:T(8,128)(2,1)S(1)} %copy-done), kind=kOutput, calls=%fused_computation.147 | convolution fusion | flops 9663676416 | bytes 20447232 | tf_op jit(solution)/shard_map/dot_general | solution.py:205
  617.9 12.6 all-to-all-done.2
  684.1 16.1 %collective-permute-done.1 = bf16[96,6144]{1,0:T(8,128)(2,1)} collective-permute-done((bf16[96,6144]{1,0:T(8,128)(2,1)}, bf16[96,6144]{1,0:T(8,128)(2,1)}, u32[]{:S(2)}, u32[]{:S(2)}) %collective-permute-start.1) | collective-permute-done | bytes 1179680 | tf_op jit(solution)/shard_map/ppermute | solution.py:92
  711.4 13.6 fusion.2
  734.1 24.3 %collective-permute-done.3 = bf16[96,6144]{1,0:T(8,128)(2,1)} collective-permute-done((bf16[96,6144]{1,0:T(8,128)(2,1)}, bf16[96,6144]{1,0:T(8,128)(2,1)}, u32[]{:S(2)}, u32[]{:S(2)}) %collective-permute-start.3) | collective-permute-done | bytes 1179680 | tf_op jit(solution)/shard_map/ppermute | solution.py:92
  771.6 19.5 %collective-permute-done.4 = bf16[96,6144]{1,0:T(8,128)(2,1)} collective-permute-done((bf16[96,6144]{1,0:T(8,128)(2,1)S(1)}, bf16[96,6144]{1,0:T(8,128)(2,1)}, u32[]{:S(2)}, u32[]{:S(2)}) %collective-permute-start.4) | collective-permute-done | bytes 1179680 | tf_op jit(solution)/shard_map/ppermute | solution.py:91
  791.2 24.3 %collective-permute-done.5 = bf16[96,6144]{1,0:T(8,128)(2,1)} collective-permute-done((bf16[96,6144]{1,0:T(8,128)(2,1)S(1)}, bf16[96,6144]{1,0:T(8,128)(2,1)}, u32[]{:S(2)}, u32[]{:S(2)}) %collective-permute-start.5) | collective-permute-done | bytes 1179680 | tf_op jit(solution)/shard_map/ppermute | solution.py:92
  843.8 12.8 collective-permute-done.6
  856.5 24.3 %collective-permute-done.7 = bf16[96,6144]{1,0:T(8,128)(2,1)} collective-permute-done((bf16[96,6144]{1,0:T(8,128)(2,1)S(1)}, bf16[96,6144]{1,0:T(8,128)(2,1)}, u32[]{:S(2)}, u32[]{:S(2)}) %collective-permute-start.7) | collective-permute-done | bytes 1179680 | tf_op jit(solution)/shard_map/ppermute | solution.py:92
  895.1 15.0 %all-reduce.2 = bf16[2048]{0:T(1024)(128)(2,1)S(1)} all-reduce(bf16[2048]{0:T(1024)(128)(2,1)S(1)} %get-tuple-element.71), channel_id=10, replica_groups=mesh['fsdp'=8,'rep'=4] {'fsdp'}, use_global_device_ids=true, to_apply=%region_29.30.clone | all-reduce | flops 2048 | bytes 8192
  936.2 74.8 %reduce-scatter.17.cloned.1.call-done = bf16[256,2048]{1,0:T(8,128)(2,1)} async-done(((bf16[2048,2048]{1,0:T(8,128)(2,1)}), bf16[256,2048]{1,0:T(8,128)(2,1)}) %reduce-scatter.17.cloned.1.call-update) | async-done | bytes 1048592 | tf_op jit(solution)/shard_map/reduce_scatter | solution.py:323
  1011.1 75.0 %reduce-scatter.11.cloned.1.call-done = bf16[256,2048]{1,0:T(8,128)(2,1)} async-done(((bf16[2048,2048]{1,0:T(8,128)(2,1)}), bf16[256,2048]{1,0:T(8,128)(2,1)}) %reduce-scatter.11.cloned.1.call-update) | async-done | bytes 1048592 | tf_op jit(solution)/shard_map/reduce_scatter | solution.py:323
  1086.1 95.6 %reduce-scatter.9.cloned.1.call-done = bf16[384,2048]{1,0:T(8,128)(2,1)} async-done(((bf16[3072,2048]{1,0:T(8,128)(2,1)}), bf16[384,2048]{1,0:T(8,128)(2,1)}) %reduce-scatter.9.cloned.1.call-update) | async-done | bytes 1572880 | tf_op jit(solution)/shard_map/reduce_scatter | solution.py:225
  1197.1 23.9 %all-reduce.3 = (bf16[2048]{0:T(1024)(128)(2,1)S(1)}, bf16[8,256]{1,0:T(8,128)(2,1)S(1)}) all-reduce(f32[2048]{0:T(1024)S(1)} %get-tuple-element.73, f32[8,256]{1,0:T(8,128)S(1)} %broadcast_in_dim.22), channel_id=4, replica_groups=mesh['fsdp'=8,'rep'=4] {'fsdp'}, use_global_device_ids=true, to_apply=%region_14.15.clone | all-reduce | flops 4096 | bytes 24576
  1221.7 69.5 %all-reduce.4 = (bf16[256]{0:T(256)(128)(2,1)S(1)}, bf16[1,256]{1,0:T(2,128)(2,1)S(1)}, bf16[256]{0:T(256)(128)(2,1)S(1)}) all-reduce(bf16[256]{0:T(256)(128)(2,1)S(1)} %dynamic-slice.8, bf16[1,256]{1,0:T(2,128)(2,1)S(1)} %dynamic-slice_convert_fusion, bf16[256]{0:T(256)(128)(2,1)S(1)} %dynamic-slice.5), channel_id=1, replica_groups=mesh['fsdp'=8,'rep'=4] {'rep'}, use_global_device_ids=true, to_apply=%region_15.16 | all-reduce | flops 768 | bytes 3072 | tf_op jit(solution)/shard_map/psum | solution.py:339
  1297.7 53.9 %all-reduce.8.cloned.1.call-done = (bf16[256,2048]{1,0:T(8,128)(2,1)}, bf16[256,1024]{1,0:T(8,128)(2,1)}, bf16[256,1024]{1,0:T(8,128)(2,1)}, bf16[256,2048]{1,0:T(8,128)(2,1)}) async-done(((bf16[256,2048]{1,0:T(8,128)(2,1)}, bf16[256,1024]{1,0:T(8,128)(2,1)}, bf16[256,1024]{1,0:T(8,128)(2,1)}, bf16[256,2048]{1,0:T(8,128)(2,1)}), (bf16[256,2048]{1,0:T(8,128)(2,1)}, bf16[256,1024]{1,0:T(8,128)(2,1)}, ...) | async-done | bytes 3145744 | tf_op jit(solution)/shard_map/psum | solution.py:340
  1371.2 12.7 bitcast_convert_fusion
  1383.9 13.8 fusion.62
  (313 shorter events, 361.9 us)
Async XLA Ops:
  7.2 316.4 %copy-start = (bf16[768,2048]{1,0:T(8,128)(2,1)S(1)}, bf16[768,2048]{1,0:T(8,128)(2,1)}, u32[]{:S(2)}) copy-start(bf16[768,2048]{1,0:T(8,128)(2,1)} %param.28) | copy-start | bytes 9437188
  7.2 154.4 %all-gather.11.cloned.1.call-start = ((), (), s32[]{:S(2)}) async-start(), calls=%async_computation.11 | async-start | bytes 4718592 | tf_op jit(solution)/shard_map/all_gather | solution.py:158
  8.0 167.1 %all-gather.9.cloned.1.call-start = ((), (), s32[]{:S(2)}) async-start(), calls=%async_computation.10 | async-start | bytes 4718592 | tf_op jit(solution)/shard_map/all_gather | solution.py:159
  8.7 184.5 %all-gather.13.cloned.1.call-start = ((), (), s32[]{:S(2)}) async-start(), calls=%async_computation.12 | async-start | bytes 9437184 | tf_op jit(solution)/shard_map/all_gather | solution.py:157
  9.4 239.8 %all-gather.15.cloned.1.call-start = ((), (), s32[]{:S(2)}) async-start(), calls=%async_computation.13 | async-start | bytes 9437184 | tf_op jit(solution)/shard_map/all_gather | solution.py:160
  10.0 313.6 %all-gather.19.cloned.1.call-start = ((), (), s32[]{:S(2)}) async-start(), calls=%async_computation.15 | async-start | bytes 14155776 | tf_op jit(solution)/shard_map/all_gather | solution.py:208
  22.0 54.4 %all-to-all-start = ((bf16[256,8,768]{0,2,1:T(8,128)(2,1)}), bf16[256,8,768]{0,2,1:T(8,128)(2,1)}, u32[]{:S(2)}, u32[]{:S(2)}) async-start(bf16[256,8,768]{0,2,1:T(8,128)(2,1)} %bitcast.209), calls=%async_computation | async-start | bytes 6291456 | tf_op jit(solution)/shard_map/all_to_all | solution.py:162
  76.4 77.7 %all-to-all-start.1 = ((bf16[256,8,768]{0,2,1:T(8,128)(2,1)}), bf16[256,8,768]{0,2,1:T(8,128)(2,1)}, u32[]{:S(2)}, u32[]{:S(2)}) async-start(bf16[256,8,768]{0,2,1:T(8,128)(2,1)} %bitcast.208), calls=%async_computation.1 | async-start | bytes 6291456 | tf_op jit(solution)/shard_map/all_to_all | solution.py:163
  81.0 317.0 %all-gather.17.cloned.1.call-start = ((), (), s32[]{:S(2)}) async-start(), calls=%async_computation.14 | async-start | bytes 14155776 | tf_op jit(solution)/shard_map/all_gather | solution.py:201
  147.7 109.5 %copy-start.44 = (f32[8,1,256]{2,1,0:T(1,128)}, f32[8,1,256]{2,1,0:T(1,128)S(1)}, u32[]{:S(2)}) copy-start(f32[8,1,256]{2,1,0:T(1,128)S(1)} %convert_element_type.343) | copy-start | bytes 24580
  260.4 400.6 %reduce-scatter.7.cloned.1.call-start = ((), (), s32[]{:S(2)}) async-start(), calls=%async_computation.16 | async-start | bytes 14155776 | tf_op jit(solution)/shard_map/reduce_scatter | solution.py:221
  496.7 74.6 %all-to-all-start.3 = ((bf16[8,256,768]{1,2,0:T(8,128)(2,1)}), bf16[8,256,768]{1,2,0:T(8,128)(2,1)}, u32[]{:S(2)}, u32[]{:S(2)}) async-start(bf16[8,256,768]{1,2,0:T(8,128)(2,1)} %copy.182), calls=%async_computation.3 | async-start | bytes 6291456 | tf_op jit(solution)/shard_map/all_to_all | solution.py:236
  571.3 59.2 %all-to-all-start.2 = ((bf16[8,256,768]{1,2,0:T(8,128)(2,1)}), bf16[8,256,768]{1,2,0:T(8,128)(2,1)}, u32[]{:S(2)}, u32[]{:S(2)}) async-start(bf16[8,256,768]{1,2,0:T(8,128)(2,1)} %copy.181), calls=%async_computation.2 | async-start | bytes 6291456 | tf_op jit(solution)/shard_map/all_to_all | solution.py:235
  575.8 356.2 %reduce-scatter.15.cloned.1.call-start = ((), (), s32[]{:S(2)}) async-start(), calls=%async_computation.20 | async-start | bytes 4718592 | tf_op jit(solution)/shard_map/reduce_scatter | solution.py:323
  648.0 36.1 %collective-permute-start = (bf16[96,6144]{1,0:T(8,128)(2,1)}, bf16[96,6144]{1,0:T(8,128)(2,1)}, u32[]{:S(2)}, u32[]{:S(2)}) collective-permute-start(bf16[96,6144]{1,0:T(8,128)(2,1)} %dynamic-slice_bitcast_fusion.1), channel_id=1, source_target_pairs={{0,1},{1,2},{2,3},{3,0},{4,5},{5,6},{6,7},{7,4},{8,9},{9,10},{10,1... | collective-permute-start | bytes 3538952 | tf_op jit(solution)/shard_map/ppermute | solution.py:91
  658.8 41.3 %collective-permute-start.1 = (bf16[96,6144]{1,0:T(8,128)(2,1)}, bf16[96,6144]{1,0:T(8,128)(2,1)}, u32[]{:S(2)}, u32[]{:S(2)}) collective-permute-start(bf16[96,6144]{1,0:T(8,128)(2,1)} %dynamic-slice_bitcast_fusion), channel_id=1, source_target_pairs={{0,3},{1,0},{2,1},{3,2},{4,7},{5,4},{6,5},{7,6},{8,11},{9,8},{10,9... | collective-permute-start | bytes 3538952 | tf_op jit(solution)/shard_map/ppermute | solution.py:92
  703.1 31.0 %collective-permute-start.2 = (bf16[96,6144]{1,0:T(8,128)(2,1)}, bf16[96,6144]{1,0:T(8,128)(2,1)}, u32[]{:S(2)}, u32[]{:S(2)}) collective-permute-start(bf16[96,6144]{1,0:T(8,128)(2,1)} %fusion.29), channel_id=1, source_target_pairs={{0,1},{1,2},{2,3},{3,0},{4,5},{5,6},{6,7},{7,4},{8,9},{9,10},{10,1... | collective-permute-start | bytes 3538952 | tf_op jit(solution)/shard_map/ppermute | solution.py:91
  706.6 51.8 %collective-permute-start.3 = (bf16[96,6144]{1,0:T(8,128)(2,1)}, bf16[96,6144]{1,0:T(8,128)(2,1)}, u32[]{:S(2)}, u32[]{:S(2)}) collective-permute-start(bf16[96,6144]{1,0:T(8,128)(2,1)} %fusion.28), channel_id=1, source_target_pairs={{0,3},{1,0},{2,1},{3,2},{4,7},{5,4},{6,5},{7,6},{8,11},{9,8},{10,9... | collective-permute-start | bytes 3538952 | tf_op jit(solution)/shard_map/ppermute | solution.py:92
  760.3 30.8 %collective-permute-start.4 = (bf16[96,6144]{1,0:T(8,128)(2,1)S(1)}, bf16[96,6144]{1,0:T(8,128)(2,1)}, u32[]{:S(2)}, u32[]{:S(2)}) collective-permute-start(bf16[96,6144]{1,0:T(8,128)(2,1)S(1)} %fusion.27), channel_id=1, source_target_pairs={{0,1},{1,2},{2,3},{3,0},{4,5},{5,6},{6,7},{7,4},{8,9},{9,10},{10,1... | collective-permute-start | bytes 3538952 | tf_op jit(solution)/shard_map/ppermute | solution.py:91
  763.0 52.5 %collective-permute-start.5 = (bf16[96,6144]{1,0:T(8,128)(2,1)S(1)}, bf16[96,6144]{1,0:T(8,128)(2,1)}, u32[]{:S(2)}, u32[]{:S(2)}) collective-permute-start(bf16[96,6144]{1,0:T(8,128)(2,1)S(1)} %fusion.26), channel_id=1, source_target_pairs={{0,3},{1,0},{2,1},{3,2},{4,7},{5,4},{6,5},{7,6},{8,11},{9,8},{10,9... | collective-permute-start | bytes 3538952 | tf_op jit(solution)/shard_map/ppermute | solution.py:92
  820.0 116.2 %reduce-scatter.13.cloned.1.call-start = ((), (), s32[]{:S(2)}) async-start(), calls=%async_computation.19 | async-start | bytes 4718592 | tf_op jit(solution)/shard_map/reduce_scatter | solution.py:323
  825.7 30.8 %collective-permute-start.6 = (bf16[96,6144]{1,0:T(8,128)(2,1)S(1)}, bf16[96,6144]{1,0:T(8,128)(2,1)}, u32[]{:S(2)}, u32[]{:S(2)}) collective-permute-start(bf16[96,6144]{1,0:T(8,128)(2,1)S(1)} %get-tuple-element.89), channel_id=1, source_target_pairs={{0,1},{1,2},{2,3},{3,0},{4,5},{5,6},{6,7},{7,4},{8,9},{9,10},{10,1... | collective-permute-start | bytes 3538952 | tf_op jit(solution)/shard_map/ppermute | solution.py:91
  832.3 48.5 %collective-permute-start.7 = (bf16[96,6144]{1,0:T(8,128)(2,1)S(1)}, bf16[96,6144]{1,0:T(8,128)(2,1)}, u32[]{:S(2)}, u32[]{:S(2)}) collective-permute-start(bf16[96,6144]{1,0:T(8,128)(2,1)S(1)} %get-tuple-element.91), channel_id=1, source_target_pairs={{0,3},{1,0},{2,1},{3,2},{4,7},{5,4},{6,5},{7,6},{8,11},{9,8},{10,9... | collective-permute-start | bytes 3538952 | tf_op jit(solution)/shard_map/ppermute | solution.py:92
  885.4 125.7 %reduce-scatter.17.cloned.1.call-start = ((), (), s32[]{:S(2)}) async-start(), calls=%async_computation.21 | async-start | bytes 9437184 | tf_op jit(solution)/shard_map/reduce_scatter | solution.py:323
  886.0 200.1 %reduce-scatter.11.cloned.1.call-start = ((), (), s32[]{:S(2)}) async-start(), calls=%async_computation.18 | async-start | bytes 9437184 | tf_op jit(solution)/shard_map/reduce_scatter | solution.py:323
  893.2 288.5 %reduce-scatter.9.cloned.1.call-start = ((), (), s32[]{:S(2)}) async-start(), calls=%async_computation.17 | async-start | bytes 14155776 | tf_op jit(solution)/shard_map/reduce_scatter | solution.py:225
  893.8 457.7 %all-reduce.8.cloned.1.call-start = ((), (), s32[]{:S(2)}) async-start(), calls=%async_computation.22 | async-start | bytes 6291456 | tf_op jit(solution)/shard_map/psum | solution.py:340
  910.2 273.4 %collective-permute-start.8 = (bf16[96,6144]{1,0:T(8,128)(2,1)}, bf16[96,6144]{1,0:T(8,128)(2,1)}, u32[]{:S(2)}, u32[]{:S(2)}) collective-permute-start(bf16[96,6144]{1,0:T(8,128)(2,1)} %collective-permute-done.6), channel_id=1, source_target_pairs={{0,1},{1,2},{2,3},{3,0},{4,5},{5,6},{6,7},{7,4},{8,9},{9,10},{10,1... | collective-permute-start | bytes 3538952 | tf_op jit(solution)/shard_map/ppermute | solution.py:91
  910.6 273.0 %collective-permute-start.9 = (bf16[96,6144]{1,0:T(8,128)(2,1)}, bf16[96,6144]{1,0:T(8,128)(2,1)}, u32[]{:S(2)}, u32[]{:S(2)}) collective-permute-start(bf16[96,6144]{1,0:T(8,128)(2,1)} %collective-permute-done.7), channel_id=1, source_target_pairs={{0,3},{1,0},{2,1},{3,2},{4,7},{5,4},{6,5},{7,6},{8,11},{9,8},{10,9... | collective-permute-start | bytes 3538952 | tf_op jit(solution)/shard_map/ppermute | solution.py:92
  1086.1 97.6 %copy-start.7 = (f32[384,2048]{1,0:T(8,128)S(1)}, f32[384,2048]{1,0:T(8,128)}, u32[]{:S(2)}) copy-start(f32[384,2048]{1,0:T(8,128)} %copy-done.5) | copy-start | bytes 9437188
  1185.1 173.2 %collective-permute-start.10 = (bf16[96,6144]{1,0:T(8,128)(2,1)}, bf16[96,6144]{1,0:T(8,128)(2,1)}, u32[]{:S(2)}, u32[]{:S(2)}) collective-permute-start(bf16[96,6144]{1,0:T(8,128)(2,1)} %collective-permute-done.8), channel_id=1, source_target_pairs={{0,1},{1,2},{2,3},{3,0},{4,5},{5,6},{6,7},{7,4},{8,9},{9,10},{10,1... | collective-permute-start | bytes 3538952 | tf_op jit(solution)/shard_map/ppermute | solution.py:91
  1186.6 171.7 %collective-permute-start.11 = (bf16[96,6144]{1,0:T(8,128)(2,1)}, bf16[96,6144]{1,0:T(8,128)(2,1)}, u32[]{:S(2)}, u32[]{:S(2)}) collective-permute-start(bf16[96,6144]{1,0:T(8,128)(2,1)} %collective-permute-done.9), channel_id=1, source_target_pairs={{0,3},{1,0},{2,1},{3,2},{4,7},{5,4},{6,5},{7,6},{8,11},{9,8},{10,9... | collective-permute-start | bytes 3538952 | tf_op jit(solution)/shard_map/ppermute | solution.py:92
  (67 other events, 981.1 us)
Sparse Core Ops, SparseCore 0:
  9.9 58.4 all-gather.10
  70.3 65.5 all-gather.8
  137.8 55.3 all-gather.12
  195.0 54.2 all-gather.14
  251.6 71.9 all-gather.18
  325.9 71.9 all-gather.16
  476.1 146.6 reduce-scatter.6
  820.1 50.5 reduce-scatter.14
  885.5 50.6 reduce-scatter.12
  939.5 71.4 reduce-scatter.16
  1014.5 71.4 reduce-scatter.10
  1089.4 92.2 reduce-scatter.8
  1184.3 167.2 all-reduce.7

commit v5 on v4

--- a/solution.py
+++ b/solution.py
@@ -320,9 +320,10 @@
     )
     head_terms = jnp.concatenate([query_gain_grad, key_gain_grad])
     head_tiles = jnp.broadcast_to(head_terms[None, :], (lax.axis_size("fsdp"), head_terms.shape[0]))
-    low_sum = lambda v: lax.psum_scatter(
-        v.astype(jnp.bfloat16), "fsdp", scatter_dimension=0, tiled=True
-    )
+
+    def low_sum(v):
+        return lax.psum_scatter(v.astype(jnp.bfloat16), "fsdp", scatter_dimension=0, tiled=True)
+
     attention_parts = (
         lax.psum_scatter(attention_gain_grad, "fsdp", scatter_dimension=0, tiled=True),
         low_sum(query_grad),

time: 1420 us -> 1420 us (level)
  no operation moved by 1% of the time
where the time goes in v5:
time: 1420 us; the launch traced here: 1410 us
  waiting for transfers between devices  698 us (49%)
  matrix products  257 us (18%)
  blocking collectives  174 us (12%)
  local copies, waits for them, and re-layouts  126 us (9%)
  other arithmetic  95.3 us (7%)
  starting transfers between devices  43.6 us (3%)
  between operations  17.7 us (1%)
    reduce_scatter x4, waiting for transfers between devices, low_sum(): lax.psum_scatter(v.astype(jnp.bfloat16), 'fsdp', scatter_dimension=0, til...  154 us
    reduce_scatter x1, waiting for transfers between devices, per_device(): lax.psum_scatter(down_part.astype(jnp.bfloat16), 'fsdp', scatter_dimensio...  95.6 us
    ppermute x6, waiting for transfers between devices, issue(): lax.ppermute(sends[1], self.axis, self.backward)  89 us
    dot_general x7, matrix products, times_transposed(): lax.dot_general(left, right, (((1,), (1,)), ((), ())), preferred_element_...  76.9 us
    dot_general x7, matrix products, inner_rows(): lax.dot_general(left, right, (((0,), (0,)), ((), ())), preferred_element_...  73.3 us
    psum x1, blocking collectives, per_device(): lax.psum(attention_parts[0].astype(jnp.bfloat16), 'rep').astype(jnp.float32)  69.5 us
    all_gather x1, waiting for transfers between devices, per_device(): grad_down_group = lax.all_gather(grad_down_low, 'fsdp', axis=0, tiled=True)  63.2 us
    all_gather x1, waiting for transfers between devices, per_device(): lax.all_gather(normed_two_low, 'fsdp', axis=0, tiled=True)  58.9 us
  transfers between devices with their start and end apart: 29, of which 19 were waited for; matrix products, arithmetic and copies ran while one was open for 23% of the time, Pallas kernels for 0%

profile of v5, /device:TPU:0, one launch (start us, length us, event | category | flops | bytes accessed | tf_op | source)
XLA Modules:
  0.0 1412.1 jit_solution(10123755991666828975)
XLA Ops:
  31.8 44.5 %all-to-all-done = bf16[256,8,768]{0,2,1:T(8,128)(2,1)} async-done(((bf16[256,8,768]{0,2,1:T(8,128)(2,1)}), bf16[256,8,768]{0,2,1:T(8,128)(2,1)}, u32[]{:S(2)}, u32[]{:S(2)}) %all-to-all-start) | async-done | bytes 3145760 | tf_op jit(solution)/shard_map/all_to_all | solution.py:162
  81.0 56.5 %all-gather = bf16[8,1,256]{2,1,0:T(2,128)(2,1)S(1)} all-gather(bf16[1,1,256]{2,1,0:T(2,128)(2,1)S(1)} %reshape.275), channel_id=1, replica_groups=mesh['fsdp'=8,'rep'=4] {'fsdp'}, dimensions={0}, use_global_device_ids=true | all-gather | bytes 4608 | tf_op jit(solution)/shard_map/all_gather | solution.py:156
  219.9 29.4 %all-gather.15.cloned.1.call-done = bf16[2048,2048]{1,0:T(8,128)(2,1)} async-done(((bf16[256,2048]{1,0:T(8,128)(2,1)}), bf16[2048,2048]{1,0:T(8,128)(2,1)}) %all-gather.15.cloned.1.call-update) | async-done | bytes 8388624 | tf_op jit(solution)/shard_map/all_gather | solution.py:160
  260.4 63.2 %all-gather.19.cloned.1.call-done = bf16[3072,2048]{1,0:T(8,128)(2,1)} async-done(((bf16[384,2048]{1,0:T(8,128)(2,1)}), bf16[3072,2048]{1,0:T(8,128)(2,1)}) %all-gather.19.cloned.1.call-update) | async-done | bytes 12582928 | tf_op jit(solution)/shard_map/all_gather | solution.py:208
  323.6 15.4 %fusion.63 = f32[3072,768]{1,0:T(8,128)} fusion(bf16[3072,2048]{1,0:T(8,128)(2,1)} %all-gather.19.cloned.1.call-done, bf16[768,2048]{1,0:T(8,128)(2,1)S(1)} %copy-done), kind=kOutput, calls=%fused_computation.144 | convolution fusion | flops 9663676416 | bytes 25165824 | tf_op jit(solution)/shard_map/dot_general | solution.py:52
  339.0 58.9 %all-gather.17.cloned.1.call-done = bf16[3072,2048]{1,0:T(8,128)(2,1)} async-done(((bf16[384,2048]{1,0:T(8,128)(2,1)}), bf16[3072,2048]{1,0:T(8,128)(2,1)}) %all-gather.17.cloned.1.call-update) | async-done | bytes 12582928 | tf_op jit(solution)/shard_map/all_gather | solution.py:201
  397.9 16.1 %fusion.64 = f32[3072,768]{1,0:T(8,128)} fusion(bf16[3072,2048]{1,0:T(8,128)(2,1)} %all-gather.17.cloned.1.call-done, bf16[2048,768]{1,0:T(8,128)(2,1)} %bitcast.216), kind=kOutput, calls=%fused_computation.145 | convolution fusion | flops 9663676416 | bytes 25165824 | tf_op jit(solution)/shard_map/dot_general | solution.py:202
  414.1 24.9 %multiply_convert_fusion = (bf16[3072,768]{1,0:T(8,128)(2,1)}, bf16[3072,768]{1,0:T(8,128)(2,1)}, bf16[3072,768]{1,0:T(8,128)(2,1)}) fusion(f32[3072,768]{1,0:T(8,128)} %fusion.64, f32[3072,768]{1,0:T(8,128)} %fusion.63, bf16[3072,2048]{1,0:T(8,128)(2,1)} %all-gather.17.cloned.1.call-done, bf16[2048,768]{1,0:T(8,128)(2,1)} %bitcast.218), kind=kOutput, calls=%fused_computation.10 | convolution fusion | flops 9699065856 | bytes 48758784 | tf_op jit(solution)/shard_map/dot_general | solution.py:203
  439.0 17.5 %fusion.65 = f32[3072,2048]{1,0:T(8,128)} fusion(bf16[3072,768]{1,0:T(8,128)(2,1)} %get-tuple-element.99, bf16[2048,768]{1,0:T(8,128)(2,1)} %bitcast.217), kind=kOutput, calls=%fused_computation.146 | convolution fusion | flops 9663676416 | bytes 33030144 | tf_op jit(solution)/shard_map/dot_general | solution.py:52
  456.5 19.5 %add_convert_fusion = bf16[3072,2048]{1,0:T(8,128)(2,1)} fusion(f32[3072,2048]{1,0:T(8,128)} %fusion.65, bf16[3072,768]{1,0:T(8,128)(2,1)} %get-tuple-element.100, bf16[2048,768]{1,0:T(8,128)(2,1)} %bitcast.219), kind=kOutput, calls=%fused_computation.1 | convolution fusion | flops 9676259328 | bytes 45613056 | tf_op jit(solution)/shard_map/dot_general | solution.py:52
  476.1 15.8 %convolution_convert_fusion.3 = bf16[2048,768]{1,0:T(8,128)(2,1)} fusion(bf16[3072,2048]{1,0:T(8,128)(2,1)} %all-gather.17.cloned.1.call-done, bf16[3072,768]{1,0:T(8,128)(2,1)} %get-tuple-element.100), kind=kOutput, calls=%fused_computation.33 | convolution fusion | flops 9665249280 | bytes 20447232 | tf_op jit(solution)/shard_map/dot_general | solution.py:46
  509.4 15.8 %convolution_convert_fusion.4 = bf16[2048,768]{1,0:T(8,128)(2,1)} fusion(bf16[3072,2048]{1,0:T(8,128)(2,1)} %all-gather.17.cloned.1.call-done, bf16[3072,768]{1,0:T(8,128)(2,1)} %get-tuple-element.99), kind=kOutput, calls=%fused_computation.34 | convolution fusion | flops 9665249280 | bytes 20447232 | tf_op jit(solution)/shard_map/dot_general | solution.py:46
  529.8 41.5 %all-to-all-done.3 = bf16[8,256,768]{1,2,0:T(8,128)(2,1)} async-done(((bf16[8,256,768]{1,2,0:T(8,128)(2,1)}), bf16[8,256,768]{1,2,0:T(8,128)(2,1)}, u32[]{:S(2)}, u32[]{:S(2)}) %all-to-all-start.3) | async-done | bytes 3145760 | tf_op jit(solution)/shard_map/all_to_all | solution.py:236
  575.9 17.0 %convolution_convert_fusion.5 = bf16[768,2048]{1,0:T(8,128)(2,1)} fusion(bf16[3072,768]{1,0:T(8,128)(2,1)} %get-tuple-element.98, bf16[3072,2048]{1,0:T(8,128)(2,1)} %all-gather.19.cloned.1.call-done), kind=kOutput, calls=%fused_computation.35 | convolution fusion | flops 9665249280 | bytes 20447232 | tf_op jit(solution)/shard_map/dot_general | solution.py:46
  603.2 14.7 %fusion.66 = bf16[3072,2048]{1,0:T(8,128)(2,1)} fusion(bf16[3072,768]{1,0:T(8,128)(2,1)} %get-tuple-element.98, bf16[768,2048]{1,0:T(8,128)(2,1)S(1)} %copy-done), kind=kOutput, calls=%fused_computation.147 | convolution fusion | flops 9663676416 | bytes 20447232 | tf_op jit(solution)/shard_map/dot_general | solution.py:205
  617.9 12.6 all-to-all-done.2
  684.1 16.1 %collective-permute-done.1 = bf16[96,6144]{1,0:T(8,128)(2,1)} collective-permute-done((bf16[96,6144]{1,0:T(8,128)(2,1)}, bf16[96,6144]{1,0:T(8,128)(2,1)}, u32[]{:S(2)}, u32[]{:S(2)}) %collective-permute-start.1) | collective-permute-done | bytes 1179680 | tf_op jit(solution)/shard_map/ppermute | solution.py:92
  711.4 13.6 fusion.2
  734.1 24.3 %collective-permute-done.3 = bf16[96,6144]{1,0:T(8,128)(2,1)} collective-permute-done((bf16[96,6144]{1,0:T(8,128)(2,1)}, bf16[96,6144]{1,0:T(8,128)(2,1)}, u32[]{:S(2)}, u32[]{:S(2)}) %collective-permute-start.3) | collective-permute-done | bytes 1179680 | tf_op jit(solution)/shard_map/ppermute | solution.py:92
  771.6 19.5 %collective-permute-done.4 = bf16[96,6144]{1,0:T(8,128)(2,1)} collective-permute-done((bf16[96,6144]{1,0:T(8,128)(2,1)S(1)}, bf16[96,6144]{1,0:T(8,128)(2,1)}, u32[]{:S(2)}, u32[]{:S(2)}) %collective-permute-start.4) | collective-permute-done | bytes 1179680 | tf_op jit(solution)/shard_map/ppermute | solution.py:91
  791.2 24.3 %collective-permute-done.5 = bf16[96,6144]{1,0:T(8,128)(2,1)} collective-permute-done((bf16[96,6144]{1,0:T(8,128)(2,1)S(1)}, bf16[96,6144]{1,0:T(8,128)(2,1)}, u32[]{:S(2)}, u32[]{:S(2)}) %collective-permute-start.5) | collective-permute-done | bytes 1179680 | tf_op jit(solution)/shard_map/ppermute | solution.py:92
  843.8 12.8 collective-permute-done.6
  856.5 24.3 %collective-permute-done.7 = bf16[96,6144]{1,0:T(8,128)(2,1)} collective-permute-done((bf16[96,6144]{1,0:T(8,128)(2,1)S(1)}, bf16[96,6144]{1,0:T(8,128)(2,1)}, u32[]{:S(2)}, u32[]{:S(2)}) %collective-permute-start.7) | collective-permute-done | bytes 1179680 | tf_op jit(solution)/shard_map/ppermute | solution.py:92
  895.1 15.0 %all-reduce.2 = bf16[2048]{0:T(1024)(128)(2,1)S(1)} all-reduce(bf16[2048]{0:T(1024)(128)(2,1)S(1)} %get-tuple-element.71), channel_id=10, replica_groups=mesh['fsdp'=8,'rep'=4] {'fsdp'}, use_global_device_ids=true, to_apply=%region_29.30.clone | all-reduce | flops 2048 | bytes 8192
  936.2 74.8 %reduce-scatter.17.cloned.1.call-done = bf16[256,2048]{1,0:T(8,128)(2,1)} async-done(((bf16[2048,2048]{1,0:T(8,128)(2,1)}), bf16[256,2048]{1,0:T(8,128)(2,1)}) %reduce-scatter.17.cloned.1.call-update) | async-done | bytes 1048592 | tf_op jit(solution)/shard_map/reduce_scatter | solution.py:325
  1011.1 75.0 %reduce-scatter.11.cloned.1.call-done = bf16[256,2048]{1,0:T(8,128)(2,1)} async-done(((bf16[2048,2048]{1,0:T(8,128)(2,1)}), bf16[256,2048]{1,0:T(8,128)(2,1)}) %reduce-scatter.11.cloned.1.call-update) | async-done | bytes 1048592 | tf_op jit(solution)/shard_map/reduce_scatter | solution.py:325
  1086.1 95.6 %reduce-scatter.9.cloned.1.call-done = bf16[384,2048]{1,0:T(8,128)(2,1)} async-done(((bf16[3072,2048]{1,0:T(8,128)(2,1)}), bf16[384,2048]{1,0:T(8,128)(2,1)}) %reduce-scatter.9.cloned.1.call-update) | async-done | bytes 1572880 | tf_op jit(solution)/shard_map/reduce_scatter | solution.py:225
  1197.1 23.9 %all-reduce.3 = (bf16[2048]{0:T(1024)(128)(2,1)S(1)}, bf16[8,256]{1,0:T(8,128)(2,1)S(1)}) all-reduce(f32[2048]{0:T(1024)S(1)} %get-tuple-element.73, f32[8,256]{1,0:T(8,128)S(1)} %broadcast_in_dim.22), channel_id=4, replica_groups=mesh['fsdp'=8,'rep'=4] {'fsdp'}, use_global_device_ids=true, to_apply=%region_14.15.clone | all-reduce | flops 4096 | bytes 24576
  1221.7 69.5 %all-reduce.4 = (bf16[256]{0:T(256)(128)(2,1)S(1)}, bf16[1,256]{1,0:T(2,128)(2,1)S(1)}, bf16[256]{0:T(256)(128)(2,1)S(1)}) all-reduce(bf16[256]{0:T(256)(128)(2,1)S(1)} %dynamic-slice.8, bf16[1,256]{1,0:T(2,128)(2,1)S(1)} %dynamic-slice_convert_fusion, bf16[256]{0:T(256)(128)(2,1)S(1)} %dynamic-slice.5), channel_id=1, replica_groups=mesh['fsdp'=8,'rep'=4] {'rep'}, use_global_device_ids=true, to_apply=%region_15.16 | all-reduce | flops 768 | bytes 3072 | tf_op jit(solution)/shard_map/psum | solution.py:340
  1297.7 53.9 %all-reduce.8.cloned.1.call-done = (bf16[256,2048]{1,0:T(8,128)(2,1)}, bf16[256,1024]{1,0:T(8,128)(2,1)}, bf16[256,1024]{1,0:T(8,128)(2,1)}, bf16[256,2048]{1,0:T(8,128)(2,1)}) async-done(((bf16[256,2048]{1,0:T(8,128)(2,1)}, bf16[256,1024]{1,0:T(8,128)(2,1)}, bf16[256,1024]{1,0:T(8,128)(2,1)}, bf16[256,2048]{1,0:T(8,128)(2,1)}), (bf16[256,2048]{1,0:T(8,128)(2,1)}, bf16[256,1024]{1,0:T(8,128)(2,1)}, ...) | async-done | bytes 3145744 | tf_op jit(solution)/shard_map/psum | solution.py:341
  1371.2 12.7 bitcast_convert_fusion
  1383.9 13.8 fusion.62
  (313 shorter events, 361.9 us)
Async XLA Ops:
  7.2 316.4 %copy-start = (bf16[768,2048]{1,0:T(8,128)(2,1)S(1)}, bf16[768,2048]{1,0:T(8,128)(2,1)}, u32[]{:S(2)}) copy-start(bf16[768,2048]{1,0:T(8,128)(2,1)} %param.28) | copy-start | bytes 9437188
  7.2 154.4 %all-gather.11.cloned.1.call-start = ((), (), s32[]{:S(2)}) async-start(), calls=%async_computation.11 | async-start | bytes 4718592 | tf_op jit(solution)/shard_map/all_gather | solution.py:158
  8.0 167.1 %all-gather.9.cloned.1.call-start = ((), (), s32[]{:S(2)}) async-start(), calls=%async_computation.10 | async-start | bytes 4718592 | tf_op jit(solution)/shard_map/all_gather | solution.py:159
  8.7 184.5 %all-gather.13.cloned.1.call-start = ((), (), s32[]{:S(2)}) async-start(), calls=%async_computation.12 | async-start | bytes 9437184 | tf_op jit(solution)/shard_map/all_gather | solution.py:157
  9.4 239.8 %all-gather.15.cloned.1.call-start = ((), (), s32[]{:S(2)}) async-start(), calls=%async_computation.13 | async-start | bytes 9437184 | tf_op jit(solution)/shard_map/all_gather | solution.py:160
  10.0 313.6 %all-gather.19.cloned.1.call-start = ((), (), s32[]{:S(2)}) async-start(), calls=%async_computation.15 | async-start | bytes 14155776 | tf_op jit(solution)/shard_map/all_gather | solution.py:208
  22.0 54.4 %all-to-all-start = ((bf16[256,8,768]{0,2,1:T(8,128)(2,1)}), bf16[256,8,768]{0,2,1:T(8,128)(2,1)}, u32[]{:S(2)}, u32[]{:S(2)}) async-start(bf16[256,8,768]{0,2,1:T(8,128)(2,1)} %bitcast.209), calls=%async_computation | async-start | bytes 6291456 | tf_op jit(solution)/shard_map/all_to_all | solution.py:162
  76.4 77.7 %all-to-all-start.1 = ((bf16[256,8,768]{0,2,1:T(8,128)(2,1)}), bf16[256,8,768]{0,2,1:T(8,128)(2,1)}, u32[]{:S(2)}, u32[]{:S(2)}) async-start(bf16[256,8,768]{0,2,1:T(8,128)(2,1)} %bitcast.208), calls=%async_computation.1 | async-start | bytes 6291456 | tf_op jit(solution)/shard_map/all_to_all | solution.py:163
  81.0 317.0 %all-gather.17.cloned.1.call-start = ((), (), s32[]{:S(2)}) async-start(), calls=%async_computation.14 | async-start | bytes 14155776 | tf_op jit(solution)/shard_map/all_gather | solution.py:201
  147.7 109.5 %copy-start.44 = (f32[8,1,256]{2,1,0:T(1,128)}, f32[8,1,256]{2,1,0:T(1,128)S(1)}, u32[]{:S(2)}) copy-start(f32[8,1,256]{2,1,0:T(1,128)S(1)} %convert_element_type.343) | copy-start | bytes 24580
  260.4 400.6 %reduce-scatter.7.cloned.1.call-start = ((), (), s32[]{:S(2)}) async-start(), calls=%async_computation.16 | async-start | bytes 14155776 | tf_op jit(solution)/shard_map/reduce_scatter | solution.py:221
  496.7 74.6 %all-to-all-start.3 = ((bf16[8,256,768]{1,2,0:T(8,128)(2,1)}), bf16[8,256,768]{1,2,0:T(8,128)(2,1)}, u32[]{:S(2)}, u32[]{:S(2)}) async-start(bf16[8,256,768]{1,2,0:T(8,128)(2,1)} %copy.182), calls=%async_computation.3 | async-start | bytes 6291456 | tf_op jit(solution)/shard_map/all_to_all | solution.py:236
  571.3 59.2 %all-to-all-start.2 = ((bf16[8,256,768]{1,2,0:T(8,128)(2,1)}), bf16[8,256,768]{1,2,0:T(8,128)(2,1)}, u32[]{:S(2)}, u32[]{:S(2)}) async-start(bf16[8,256,768]{1,2,0:T(8,128)(2,1)} %copy.181), calls=%async_computation.2 | async-start | bytes 6291456 | tf_op jit(solution)/shard_map/all_to_all | solution.py:235
  575.8 356.2 %reduce-scatter.15.cloned.1.call-start = ((), (), s32[]{:S(2)}) async-start(), calls=%async_computation.20 | async-start | bytes 4718592 | tf_op jit(solution)/shard_map/reduce_scatter | solution.py:325
  648.0 36.1 %collective-permute-start = (bf16[96,6144]{1,0:T(8,128)(2,1)}, bf16[96,6144]{1,0:T(8,128)(2,1)}, u32[]{:S(2)}, u32[]{:S(2)}) collective-permute-start(bf16[96,6144]{1,0:T(8,128)(2,1)} %dynamic-slice_bitcast_fusion.1), channel_id=1, source_target_pairs={{0,1},{1,2},{2,3},{3,0},{4,5},{5,6},{6,7},{7,4},{8,9},{9,10},{10,1... | collective-permute-start | bytes 3538952 | tf_op jit(solution)/shard_map/ppermute | solution.py:91
  658.8 41.3 %collective-permute-start.1 = (bf16[96,6144]{1,0:T(8,128)(2,1)}, bf16[96,6144]{1,0:T(8,128)(2,1)}, u32[]{:S(2)}, u32[]{:S(2)}) collective-permute-start(bf16[96,6144]{1,0:T(8,128)(2,1)} %dynamic-slice_bitcast_fusion), channel_id=1, source_target_pairs={{0,3},{1,0},{2,1},{3,2},{4,7},{5,4},{6,5},{7,6},{8,11},{9,8},{10,9... | collective-permute-start | bytes 3538952 | tf_op jit(solution)/shard_map/ppermute | solution.py:92
  703.1 31.0 %collective-permute-start.2 = (bf16[96,6144]{1,0:T(8,128)(2,1)}, bf16[96,6144]{1,0:T(8,128)(2,1)}, u32[]{:S(2)}, u32[]{:S(2)}) collective-permute-start(bf16[96,6144]{1,0:T(8,128)(2,1)} %fusion.29), channel_id=1, source_target_pairs={{0,1},{1,2},{2,3},{3,0},{4,5},{5,6},{6,7},{7,4},{8,9},{9,10},{10,1... | collective-permute-start | bytes 3538952 | tf_op jit(solution)/shard_map/ppermute | solution.py:91
  706.6 51.8 %collective-permute-start.3 = (bf16[96,6144]{1,0:T(8,128)(2,1)}, bf16[96,6144]{1,0:T(8,128)(2,1)}, u32[]{:S(2)}, u32[]{:S(2)}) collective-permute-start(bf16[96,6144]{1,0:T(8,128)(2,1)} %fusion.28), channel_id=1, source_target_pairs={{0,3},{1,0},{2,1},{3,2},{4,7},{5,4},{6,5},{7,6},{8,11},{9,8},{10,9... | collective-permute-start | bytes 3538952 | tf_op jit(solution)/shard_map/ppermute | solution.py:92
  760.3 30.8 %collective-permute-start.4 = (bf16[96,6144]{1,0:T(8,128)(2,1)S(1)}, bf16[96,6144]{1,0:T(8,128)(2,1)}, u32[]{:S(2)}, u32[]{:S(2)}) collective-permute-start(bf16[96,6144]{1,0:T(8,128)(2,1)S(1)} %fusion.27), channel_id=1, source_target_pairs={{0,1},{1,2},{2,3},{3,0},{4,5},{5,6},{6,7},{7,4},{8,9},{9,10},{10,1... | collective-permute-start | bytes 3538952 | tf_op jit(solution)/shard_map/ppermute | solution.py:91
  763.0 52.5 %collective-permute-start.5 = (bf16[96,6144]{1,0:T(8,128)(2,1)S(1)}, bf16[96,6144]{1,0:T(8,128)(2,1)}, u32[]{:S(2)}, u32[]{:S(2)}) collective-permute-start(bf16[96,6144]{1,0:T(8,128)(2,1)S(1)} %fusion.26), channel_id=1, source_target_pairs={{0,3},{1,0},{2,1},{3,2},{4,7},{5,4},{6,5},{7,6},{8,11},{9,8},{10,9... | collective-permute-start | bytes 3538952 | tf_op jit(solution)/shard_map/ppermute | solution.py:92
  820.0 116.2 %reduce-scatter.13.cloned.1.call-start = ((), (), s32[]{:S(2)}) async-start(), calls=%async_computation.19 | async-start | bytes 4718592 | tf_op jit(solution)/shard_map/reduce_scatter | solution.py:325
  825.7 30.8 %collective-permute-start.6 = (bf16[96,6144]{1,0:T(8,128)(2,1)S(1)}, bf16[96,6144]{1,0:T(8,128)(2,1)}, u32[]{:S(2)}, u32[]{:S(2)}) collective-permute-start(bf16[96,6144]{1,0:T(8,128)(2,1)S(1)} %get-tuple-element.89), channel_id=1, source_target_pairs={{0,1},{1,2},{2,3},{3,0},{4,5},{5,6},{6,7},{7,4},{8,9},{9,10},{10,1... | collective-permute-start | bytes 3538952 | tf_op jit(solution)/shard_map/ppermute | solution.py:91
  832.3 48.5 %collective-permute-start.7 = (bf16[96,6144]{1,0:T(8,128)(2,1)S(1)}, bf16[96,6144]{1,0:T(8,128)(2,1)}, u32[]{:S(2)}, u32[]{:S(2)}) collective-permute-start(bf16[96,6144]{1,0:T(8,128)(2,1)S(1)} %get-tuple-element.91), channel_id=1, source_target_pairs={{0,3},{1,0},{2,1},{3,2},{4,7},{5,4},{6,5},{7,6},{8,11},{9,8},{10,9... | collective-permute-start | bytes 3538952 | tf_op jit(solution)/shard_map/ppermute | solution.py:92
  885.4 125.7 %reduce-scatter.17.cloned.1.call-start = ((), (), s32[]{:S(2)}) async-start(), calls=%async_computation.21 | async-start | bytes 9437184 | tf_op jit(solution)/shard_map/reduce_scatter | solution.py:325
  886.0 200.1 %reduce-scatter.11.cloned.1.call-start = ((), (), s32[]{:S(2)}) async-start(), calls=%async_computation.18 | async-start | bytes 9437184 | tf_op jit(solution)/shard_map/reduce_scatter | solution.py:325
  893.2 288.5 %reduce-scatter.9.cloned.1.call-start = ((), (), s32[]{:S(2)}) async-start(), calls=%async_computation.17 | async-start | bytes 14155776 | tf_op jit(solution)/shard_map/reduce_scatter | solution.py:225
  893.8 457.7 %all-reduce.8.cloned.1.call-start = ((), (), s32[]{:S(2)}) async-start(), calls=%async_computation.22 | async-start | bytes 6291456 | tf_op jit(solution)/shard_map/psum | solution.py:341
  910.2 273.4 %collective-permute-start.8 = (bf16[96,6144]{1,0:T(8,128)(2,1)}, bf16[96,6144]{1,0:T(8,128)(2,1)}, u32[]{:S(2)}, u32[]{:S(2)}) collective-permute-start(bf16[96,6144]{1,0:T(8,128)(2,1)} %collective-permute-done.6), channel_id=1, source_target_pairs={{0,1},{1,2},{2,3},{3,0},{4,5},{5,6},{6,7},{7,4},{8,9},{9,10},{10,1... | collective-permute-start | bytes 3538952 | tf_op jit(solution)/shard_map/ppermute | solution.py:91
  910.6 273.0 %collective-permute-start.9 = (bf16[96,6144]{1,0:T(8,128)(2,1)}, bf16[96,6144]{1,0:T(8,128)(2,1)}, u32[]{:S(2)}, u32[]{:S(2)}) collective-permute-start(bf16[96,6144]{1,0:T(8,128)(2,1)} %collective-permute-done.7), channel_id=1, source_target_pairs={{0,3},{1,0},{2,1},{3,2},{4,7},{5,4},{6,5},{7,6},{8,11},{9,8},{10,9... | collective-permute-start | bytes 3538952 | tf_op jit(solution)/shard_map/ppermute | solution.py:92
  1086.1 97.6 %copy-start.7 = (f32[384,2048]{1,0:T(8,128)S(1)}, f32[384,2048]{1,0:T(8,128)}, u32[]{:S(2)}) copy-start(f32[384,2048]{1,0:T(8,128)} %copy-done.5) | copy-start | bytes 9437188
  1185.1 173.2 %collective-permute-start.10 = (bf16[96,6144]{1,0:T(8,128)(2,1)}, bf16[96,6144]{1,0:T(8,128)(2,1)}, u32[]{:S(2)}, u32[]{:S(2)}) collective-permute-start(bf16[96,6144]{1,0:T(8,128)(2,1)} %collective-permute-done.8), channel_id=1, source_target_pairs={{0,1},{1,2},{2,3},{3,0},{4,5},{5,6},{6,7},{7,4},{8,9},{9,10},{10,1... | collective-permute-start | bytes 3538952 | tf_op jit(solution)/shard_map/ppermute | solution.py:91
  1186.6 171.7 %collective-permute-start.11 = (bf16[96,6144]{1,0:T(8,128)(2,1)}, bf16[96,6144]{1,0:T(8,128)(2,1)}, u32[]{:S(2)}, u32[]{:S(2)}) collective-permute-start(bf16[96,6144]{1,0:T(8,128)(2,1)} %collective-permute-done.9), channel_id=1, source_target_pairs={{0,3},{1,0},{2,1},{3,2},{4,7},{5,4},{6,5},{7,6},{8,11},{9,8},{10,9... | collective-permute-start | bytes 3538952 | tf_op jit(solution)/shard_map/ppermute | solution.py:92
  (67 other events, 981.1 us)
Sparse Core Ops, SparseCore 0:
  9.9 58.4 all-gather.10
  70.3 65.5 all-gather.8
  137.8 55.3 all-gather.12
  195.0 54.2 all-gather.14
  251.6 71.9 all-gather.18
  325.9 71.9 all-gather.16
  476.1 146.6 reduce-scatter.6
  820.1 50.5 reduce-scatter.14
  885.5 50.6 reduce-scatter.12
  939.5 71.4 reduce-scatter.16
  1014.5 71.4 reduce-scatter.10
  1089.4 92.2 reduce-scatter.8
  1184.3 167.2 all-reduce.7

commit v6 on v5

--- a/solution.py
+++ b/solution.py
@@ -152,8 +152,9 @@
     scale = head_width ** (-0.5)
     gain_query = query_gain.astype(jnp.float32)
     gain_key = key_gain.astype(jnp.float32)
+    gains = lax.all_gather(jnp.stack([attention_gain, feed_gain]), "fsdp", axis=1, tiled=True)
     attention_set = (
-        lax.all_gather(attention_gain, "fsdp", axis=0, tiled=True),
+        gains[0],
         lax.all_gather(query_weight, "fsdp", axis=0, tiled=True),
         lax.all_gather(key_weight, "fsdp", axis=0, tiled=True),
         lax.all_gather(value_weight, "fsdp", axis=0, tiled=True),
@@ -195,7 +196,7 @@
     mixed_low = mixed.reshape(row_count, query_heads * head_width).astype(jnp.bfloat16)
     branch = jnp.dot(mixed_low, attention_set[4], preferred_element_type=jnp.float32)
     middle = inputs_wide + branch
-    gain_two = lax.all_gather(feed_gain, "fsdp", axis=0, tiled=True).astype(jnp.float32)
+    gain_two = gains[1].astype(jnp.float32)
     normed_two, normal_two, inverse_two = rms_forward(middle, gain_two)
     normed_two_low = normed_two.astype(jnp.bfloat16)
     normed_two_group = lax.all_gather(normed_two_low, "fsdp", axis=0, tiled=True)
@@ -213,14 +214,14 @@
         grad_hidden * up_value * sigmoid_gate * (1.0 + gate_value * (1.0 - sigmoid_gate))
     ).astype(jnp.bfloat16)
     grad_up_low = (grad_hidden * (gate_value * sigmoid_gate)).astype(jnp.bfloat16)
-    gate_grad_block = inner_rows(normed_two_group, grad_gate_low)
-    up_grad_block = inner_rows(normed_two_group, grad_up_low)
     grad_normed_part = times_transposed(grad_gate_low, gate_block) + times_transposed(
         grad_up_low, up_block
     )
     grad_normed_two = lax.psum_scatter(
         grad_normed_part.astype(jnp.bfloat16), "fsdp", scatter_dimension=0, tiled=True
     ).astype(jnp.float32)
+    gate_grad_block = inner_rows(normed_two_group, grad_gate_low)
+    up_grad_block = inner_rows(normed_two_group, grad_up_low)
     grad_normed_two, down_part = lax.optimization_barrier((grad_normed_two, down_part))
     down_value = lax.psum_scatter(
         down_part.astype(jnp.bfloat16), "fsdp", scatter_dimension=0, tiled=True
@@ -229,9 +230,7 @@
     feed_gain_grad = jnp.sum(gain_two_terms, axis=0)
     grad_middle = grad_top + grad_from_two
     feed_parts = (
-        lax.psum_scatter(
-            feed_gain_grad.astype(jnp.bfloat16), "fsdp", scatter_dimension=0, tiled=True
-        ).astype(jnp.float32),
+        None,
         lax.all_to_all(gate_grad_block.astype(jnp.bfloat16), "fsdp", 0, 1, tiled=True),
         lax.all_to_all(up_grad_block.astype(jnp.bfloat16), "fsdp", 0, 1, tiled=True),
         down_grad.astype(jnp.bfloat16),
@@ -318,33 +317,35 @@
         feed_sum[feed_rows[0] : feed_rows[0] + feed_rows[1]],
         feed_sum[feed_rows[0] + feed_rows[1] :].reshape(feed_parts[3].shape),
     )
-    head_terms = jnp.concatenate([query_gain_grad, key_gain_grad])
-    head_tiles = jnp.broadcast_to(head_terms[None, :], (lax.axis_size("fsdp"), head_terms.shape[0]))
+    model_width = attention_gain_grad.shape[0]
+    gain_share = model_width // lax.axis_size("fsdp")
+    gain_sums = lax.psum(
+        jnp.concatenate([attention_gain_grad, feed_gain_grad, query_gain_grad, key_gain_grad]),
+        ("fsdp", "rep"),
+    )
+    gain_start = lax.axis_index("fsdp") * gain_share
+    attention_gain_out = lax.dynamic_slice_in_dim(gain_sums, gain_start, gain_share)
+    feed_gain_out = lax.dynamic_slice_in_dim(gain_sums, model_width + gain_start, gain_share)
+    query_gain_out = gain_sums[2 * model_width : 2 * model_width + head_width]
+    key_gain_out = gain_sums[2 * model_width + head_width :]
 
     def low_sum(v):
         return lax.psum_scatter(v.astype(jnp.bfloat16), "fsdp", scatter_dimension=0, tiled=True)
 
     attention_parts = (
-        lax.psum_scatter(attention_gain_grad, "fsdp", scatter_dimension=0, tiled=True),
-        low_sum(query_grad),
-        low_sum(key_grad),
-        low_sum(value_grad),
-        low_sum(output_grad),
-        lax.psum_scatter(head_tiles, "fsdp", scatter_dimension=0, tiled=True),
+        None, low_sum(query_grad), low_sum(key_grad), low_sum(value_grad), low_sum(output_grad)
     )
     finals = (
-        lax.psum(feed_parts[0].astype(jnp.bfloat16), "rep").astype(jnp.float32),
+        feed_gain_out,
         feed_rep[0],
         feed_rep[1],
         feed_rep[2],
-        lax.psum(attention_parts[0].astype(jnp.bfloat16), "rep").astype(jnp.float32),
+        attention_gain_out,
         lax.psum(attention_parts[1].astype(jnp.bfloat16), "rep").astype(jnp.float32),
         lax.psum(attention_parts[2].astype(jnp.bfloat16), "rep").astype(jnp.float32),
         lax.psum(attention_parts[3].astype(jnp.bfloat16), "rep").astype(jnp.float32),
         lax.psum(attention_parts[4].astype(jnp.bfloat16), "rep").astype(jnp.float32),
-        lax.psum(attention_parts[5].astype(jnp.bfloat16), "rep").astype(jnp.float32),
-    )
-    head_sum = finals[9]
+    )
     return (
         layer_out,
         input_grad,
@@ -352,8 +353,8 @@
         finals[5],
         finals[6],
         finals[7],
-        head_sum[0, :head_width],
-        head_sum[0, head_width:],
+        query_gain_out,
+        key_gain_out,
         finals[8],
         finals[0],
         finals[1],

time: 1420 us -> 1420 us (level)
    psum x1, blocking collectives: 69.5 us -> 113 us  [per_device(): lax.psum(jnp.concatenate([attention_gain_grad, feed_gain_grad, query_gain...]
    unnamed x2 -> x0, blocking collectives: 38.9 us -> none
    psum x1, waiting for transfers between devices: 53.9 us -> 35.2 us  [per_device(): lax.psum(attention_parts[1].astype(jnp.bfloat16), 'rep').astype(jnp.float32)]
    reduce_scatter x4, waiting for transfers between devices: 154 us -> 170 us  [low_sum(): lax.psum_scatter(v.astype(jnp.bfloat16), 'fsdp', scatter_dimension=0, til...]
    all_gather x2 -> x1, blocking collectives: 65.6 us -> 55.5 us  [per_device(): lax.all_gather(jnp.stack([attention_gain, feed_gain]), 'fsdp', axis=1, ti...]
where the time goes in v6:
time: 1420 us; the launch traced here: 1410 us
  waiting for transfers between devices  705 us (50%)
  matrix products  258 us (18%)
  blocking collectives  169 us (12%)
  local copies, waits for them, and re-layouts  125 us (9%)
  other arithmetic  94.2 us (7%)
  starting transfers between devices  43.6 us (3%)
  between operations  17.1 us (1%)
    reduce_scatter x4, waiting for transfers between devices, low_sum(): lax.psum_scatter(v.astype(jnp.bfloat16), 'fsdp', scatter_dimension=0, til...  170 us
    psum x1, blocking collectives, per_device(): lax.psum(jnp.concatenate([attention_gain_grad, feed_gain_grad, query_gain...  113 us
    reduce_scatter x1, waiting for transfers between devices, per_device(): lax.psum_scatter(down_part.astype(jnp.bfloat16), 'fsdp', scatter_dimensio...  95.6 us
    ppermute x6, waiting for transfers between devices, issue(): lax.ppermute(sends[1], self.axis, self.backward)  89 us
    dot_general x7, matrix products, times_transposed(): lax.dot_general(left, right, (((1,), (1,)), ((), ())), preferred_element_...  77.2 us
    dot_general x7, matrix products, inner_rows(): lax.dot_general(left, right, (((0,), (0,)), ((), ())), preferred_element_...  73.3 us
    all_gather x1, waiting for transfers between devices, per_device(): grad_down_group = lax.all_gather(grad_down_low, 'fsdp', axis=0, tiled=True)  63.2 us
    all_gather x1, waiting for transfers between devices, per_device(): lax.all_gather(normed_two_low, 'fsdp', axis=0, tiled=True)  58.9 us
  transfers between devices with their start and end apart: 29, of which 19 were waited for; matrix products, arithmetic and copies ran while one was open for 23% of the time, Pallas kernels for 0%

profile of v6, /device:TPU:0, one launch (start us, length us, event | category | flops | bytes accessed | tf_op | source)
XLA Modules:
  0.0 1412.4 jit_solution(18314636358808842571)
XLA Ops:
  31.8 44.5 %all-to-all-done = bf16[256,8,768]{0,2,1:T(8,128)(2,1)} async-done(((bf16[256,8,768]{0,2,1:T(8,128)(2,1)}), bf16[256,8,768]{0,2,1:T(8,128)(2,1)}, u32[]{:S(2)}, u32[]{:S(2)}) %all-to-all-start) | async-done | bytes 3145760 | tf_op jit(solution)/shard_map/all_to_all | solution.py:163
  82.1 55.5 %all_gather.21 = bf16[2,2048]{1,0:T(2,128)(2,1)S(1)} all-gather(bf16[2,256]{1,0:T(2,128)(2,1)S(1)} %pad_maximum_fusion.5), channel_id=1, replica_groups=mesh['fsdp'=8,'rep'=4] {'fsdp'}, dimensions={1}, use_global_device_ids=true | all-gather | bytes 9216 | tf_op jit(solution)/shard_map/all_gather | solution.py:155
  173.1 20.2 %all-gather.11.cloned.1.call-done = bf16[2048,2048]{1,0:T(8,128)(2,1)} async-done(((bf16[256,2048]{1,0:T(8,128)(2,1)}), bf16[2048,2048]{1,0:T(8,128)(2,1)}) %all-gather.11.cloned.1.call-update) | async-done | bytes 8388624 | tf_op jit(solution)/shard_map/all_gather | solution.py:158
  219.9 29.4 %all-gather.13.cloned.1.call-done = bf16[2048,2048]{1,0:T(8,128)(2,1)} async-done(((bf16[256,2048]{1,0:T(8,128)(2,1)}), bf16[2048,2048]{1,0:T(8,128)(2,1)}) %all-gather.13.cloned.1.call-update) | async-done | bytes 8388624 | tf_op jit(solution)/shard_map/all_gather | solution.py:161
  260.4 63.2 %all-gather.17.cloned.1.call-done = bf16[3072,2048]{1,0:T(8,128)(2,1)} async-done(((bf16[384,2048]{1,0:T(8,128)(2,1)}), bf16[3072,2048]{1,0:T(8,128)(2,1)}) %all-gather.17.cloned.1.call-update) | async-done | bytes 12582928 | tf_op jit(solution)/shard_map/all_gather | solution.py:209
  323.6 15.4 %fusion.65 = f32[3072,768]{1,0:T(8,128)} fusion(bf16[3072,2048]{1,0:T(8,128)(2,1)} %all-gather.17.cloned.1.call-done, bf16[768,2048]{1,0:T(8,128)(2,1)S(1)} %copy-done), kind=kOutput, calls=%fused_computation.145 | convolution fusion | flops 9663676416 | bytes 25165824 | tf_op jit(solution)/shard_map/dot_general | solution.py:52
  339.0 58.9 %all-gather.15.cloned.1.call-done = bf16[3072,2048]{1,0:T(8,128)(2,1)} async-done(((bf16[384,2048]{1,0:T(8,128)(2,1)}), bf16[3072,2048]{1,0:T(8,128)(2,1)}) %all-gather.15.cloned.1.call-update) | async-done | bytes 12582928 | tf_op jit(solution)/shard_map/all_gather | solution.py:202
  397.9 16.1 %fusion.66 = f32[3072,768]{1,0:T(8,128)} fusion(bf16[3072,2048]{1,0:T(8,128)(2,1)} %all-gather.15.cloned.1.call-done, bf16[2048,768]{1,0:T(8,128)(2,1)} %bitcast.211), kind=kOutput, calls=%fused_computation.146 | convolution fusion | flops 9663676416 | bytes 25165824 | tf_op jit(solution)/shard_map/dot_general | solution.py:203
  414.1 24.9 %multiply_convert_fusion = (bf16[3072,768]{1,0:T(8,128)(2,1)}, bf16[3072,768]{1,0:T(8,128)(2,1)}, bf16[3072,768]{1,0:T(8,128)(2,1)}) fusion(f32[3072,768]{1,0:T(8,128)} %fusion.66, f32[3072,768]{1,0:T(8,128)} %fusion.65, bf16[3072,2048]{1,0:T(8,128)(2,1)} %all-gather.15.cloned.1.call-done, bf16[2048,768]{1,0:T(8,128)(2,1)} %bitcast.213), kind=kOutput, calls=%fused_computation.10 | convolution fusion | flops 9699065856 | bytes 48758784 | tf_op jit(solution)/shard_map/dot_general | solution.py:204
  439.0 17.7 %fusion.67 = f32[3072,2048]{1,0:T(8,128)} fusion(bf16[3072,768]{1,0:T(8,128)(2,1)} %get-tuple-element.94, bf16[2048,768]{1,0:T(8,128)(2,1)} %bitcast.212), kind=kOutput, calls=%fused_computation.147 | convolution fusion | flops 9663676416 | bytes 33030144 | tf_op jit(solution)/shard_map/dot_general | solution.py:52
  456.6 19.5 %add_convert_fusion = bf16[3072,2048]{1,0:T(8,128)(2,1)} fusion(f32[3072,2048]{1,0:T(8,128)} %fusion.67, bf16[3072,768]{1,0:T(8,128)(2,1)} %get-tuple-element.95, bf16[2048,768]{1,0:T(8,128)(2,1)} %bitcast.214), kind=kOutput, calls=%fused_computation.1 | convolution fusion | flops 9676259328 | bytes 45613056 | tf_op jit(solution)/shard_map/dot_general | solution.py:52
  476.3 15.8 %convolution_convert_fusion.3 = bf16[2048,768]{1,0:T(8,128)(2,1)} fusion(bf16[3072,2048]{1,0:T(8,128)(2,1)} %all-gather.15.cloned.1.call-done, bf16[3072,768]{1,0:T(8,128)(2,1)} %get-tuple-element.95), kind=kOutput, calls=%fused_computation.33 | convolution fusion | flops 9665249280 | bytes 20447232 | tf_op jit(solution)/shard_map/dot_general | solution.py:46
  509.6 15.8 %convolution_convert_fusion.4 = bf16[2048,768]{1,0:T(8,128)(2,1)} fusion(bf16[3072,2048]{1,0:T(8,128)(2,1)} %all-gather.15.cloned.1.call-done, bf16[3072,768]{1,0:T(8,128)(2,1)} %get-tuple-element.94), kind=kOutput, calls=%fused_computation.34 | convolution fusion | flops 9665249280 | bytes 20447232 | tf_op jit(solution)/shard_map/dot_general | solution.py:46
  530.0 41.5 %all-to-all-done.3 = bf16[8,256,768]{1,2,0:T(8,128)(2,1)} async-done(((bf16[8,256,768]{1,2,0:T(8,128)(2,1)}), bf16[8,256,768]{1,2,0:T(8,128)(2,1)}, u32[]{:S(2)}, u32[]{:S(2)}) %all-to-all-start.3) | async-done | bytes 3145760 | tf_op jit(solution)/shard_map/all_to_all | solution.py:235
  576.1 17.0 %convolution_convert_fusion.5 = bf16[768,2048]{1,0:T(8,128)(2,1)} fusion(bf16[3072,768]{1,0:T(8,128)(2,1)} %get-tuple-element.93, bf16[3072,2048]{1,0:T(8,128)(2,1)} %all-gather.17.cloned.1.call-done), kind=kOutput, calls=%fused_computation.35 | convolution fusion | flops 9665249280 | bytes 20447232 | tf_op jit(solution)/shard_map/dot_general | solution.py:46
  603.4 14.7 %fusion.68 = bf16[3072,2048]{1,0:T(8,128)(2,1)} fusion(bf16[3072,768]{1,0:T(8,128)(2,1)} %get-tuple-element.93, bf16[768,2048]{1,0:T(8,128)(2,1)S(1)} %copy-done), kind=kOutput, calls=%fused_computation.148 | convolution fusion | flops 9663676416 | bytes 20447232 | tf_op jit(solution)/shard_map/dot_general | solution.py:206
  618.1 12.6 all-to-all-done.2
  684.3 16.1 %collective-permute-done.1 = bf16[96,6144]{1,0:T(8,128)(2,1)} collective-permute-done((bf16[96,6144]{1,0:T(8,128)(2,1)}, bf16[96,6144]{1,0:T(8,128)(2,1)}, u32[]{:S(2)}, u32[]{:S(2)}) %collective-permute-start.1) | collective-permute-done | bytes 1179680 | tf_op jit(solution)/shard_map/ppermute | solution.py:92
  711.6 13.5 fusion.2
  734.3 24.3 %collective-permute-done.3 = bf16[96,6144]{1,0:T(8,128)(2,1)} collective-permute-done((bf16[96,6144]{1,0:T(8,128)(2,1)}, bf16[96,6144]{1,0:T(8,128)(2,1)}, u32[]{:S(2)}, u32[]{:S(2)}) %collective-permute-start.3) | collective-permute-done | bytes 1179680 | tf_op jit(solution)/shard_map/ppermute | solution.py:92
  771.8 19.5 %collective-permute-done.4 = bf16[96,6144]{1,0:T(8,128)(2,1)} collective-permute-done((bf16[96,6144]{1,0:T(8,128)(2,1)S(1)}, bf16[96,6144]{1,0:T(8,128)(2,1)}, u32[]{:S(2)}, u32[]{:S(2)}) %collective-permute-start.4) | collective-permute-done | bytes 1179680 | tf_op jit(solution)/shard_map/ppermute | solution.py:91
  791.4 24.3 %collective-permute-done.5 = bf16[96,6144]{1,0:T(8,128)(2,1)} collective-permute-done((bf16[96,6144]{1,0:T(8,128)(2,1)S(1)}, bf16[96,6144]{1,0:T(8,128)(2,1)}, u32[]{:S(2)}, u32[]{:S(2)}) %collective-permute-start.5) | collective-permute-done | bytes 1179680 | tf_op jit(solution)/shard_map/ppermute | solution.py:92
  843.9 12.8 collective-permute-done.6
  856.7 24.3 %collective-permute-done.7 = bf16[96,6144]{1,0:T(8,128)(2,1)} collective-permute-done((bf16[96,6144]{1,0:T(8,128)(2,1)S(1)}, bf16[96,6144]{1,0:T(8,128)(2,1)}, u32[]{:S(2)}, u32[]{:S(2)}) %collective-permute-start.7) | collective-permute-done | bytes 1179680 | tf_op jit(solution)/shard_map/ppermute | solution.py:92
  916.1 20.4 %reduce-scatter.13.cloned.1.call-done = bf16[256,1024]{1,0:T(8,128)(2,1)} async-done(((bf16[2048,1024]{1,0:T(8,128)(2,1)}), bf16[256,1024]{1,0:T(8,128)(2,1)}) %reduce-scatter.13.cloned.1.call-update) | async-done | bytes 524304 | tf_op jit(solution)/shard_map/reduce_scatter | solution.py:333
  936.4 74.8 %reduce-scatter.17.cloned.1.call-done = bf16[256,2048]{1,0:T(8,128)(2,1)} async-done(((bf16[2048,2048]{1,0:T(8,128)(2,1)}), bf16[256,2048]{1,0:T(8,128)(2,1)}) %reduce-scatter.17.cloned.1.call-update) | async-done | bytes 1048592 | tf_op jit(solution)/shard_map/reduce_scatter | solution.py:333
  1011.2 75.0 %reduce-scatter.11.cloned.1.call-done = bf16[256,2048]{1,0:T(8,128)(2,1)} async-done(((bf16[2048,2048]{1,0:T(8,128)(2,1)}), bf16[256,2048]{1,0:T(8,128)(2,1)}) %reduce-scatter.11.cloned.1.call-update) | async-done | bytes 1048592 | tf_op jit(solution)/shard_map/reduce_scatter | solution.py:333
  1086.3 95.6 %reduce-scatter.9.cloned.1.call-done = bf16[384,2048]{1,0:T(8,128)(2,1)} async-done(((bf16[3072,2048]{1,0:T(8,128)(2,1)}), bf16[384,2048]{1,0:T(8,128)(2,1)}) %reduce-scatter.9.cloned.1.call-update) | async-done | bytes 1572880 | tf_op jit(solution)/shard_map/reduce_scatter | solution.py:226
  1197.3 113.5 %psum.35 = f32[4352]{0:T(1024)S(1)} all-reduce(f32[4352]{0:T(1024)S(1)} %pad_maximum_fusion.4), channel_id=1, replica_groups=mesh['fsdp'=8,'rep'=4] {'fsdp','rep'}, use_global_device_ids=true, to_apply=%region_17.18 | all-reduce | flops 4352 | bytes 34816 | tf_op jit(solution)/shard_map/psum | solution.py:322
  1316.7 35.2 %all-reduce.3.cloned.1.call-done = (bf16[256,2048]{1,0:T(8,128)(2,1)}, bf16[256,1024]{1,0:T(8,128)(2,1)}, bf16[256,1024]{1,0:T(8,128)(2,1)}, bf16[256,2048]{1,0:T(8,128)(2,1)}) async-done(((bf16[256,2048]{1,0:T(8,128)(2,1)}, bf16[256,1024]{1,0:T(8,128)(2,1)}, bf16[256,1024]{1,0:T(8,128)(2,1)}, bf16[256,2048]{1,0:T(8,128)(2,1)}), (bf16[256,2048]{1,0:T(8,128)(2,1)}, bf16[256,1024]{1,0:T(8,128)(2,1)}, ...) | async-done | bytes 3145744 | tf_op jit(solution)/shard_map/psum | solution.py:344
  1371.5 12.8 bitcast_convert_fusion
  1384.2 13.8 fusion.62
  (301 shorter events, 337.0 us)
Async XLA Ops:
  7.2 316.4 %copy-start = (bf16[768,2048]{1,0:T(8,128)(2,1)S(1)}, bf16[768,2048]{1,0:T(8,128)(2,1)}, u32[]{:S(2)}) copy-start(bf16[768,2048]{1,0:T(8,128)(2,1)} %param.28) | copy-start | bytes 9437188
  7.2 144.3 %all-gather.9.cloned.1.call-start = ((), (), s32[]{:S(2)}) async-start(), calls=%async_computation.11 | async-start | bytes 4718592 | tf_op jit(solution)/shard_map/all_gather | solution.py:159
  8.0 156.8 %all-gather.7.cloned.1.call-start = ((), (), s32[]{:S(2)}) async-start(), calls=%async_computation.10 | async-start | bytes 4718592 | tf_op jit(solution)/shard_map/all_gather | solution.py:160
  8.7 184.5 %all-gather.11.cloned.1.call-start = ((), (), s32[]{:S(2)}) async-start(), calls=%async_computation.12 | async-start | bytes 9437184 | tf_op jit(solution)/shard_map/all_gather | solution.py:158
  9.4 239.8 %all-gather.13.cloned.1.call-start = ((), (), s32[]{:S(2)}) async-start(), calls=%async_computation.13 | async-start | bytes 9437184 | tf_op jit(solution)/shard_map/all_gather | solution.py:161
  10.0 313.6 %all-gather.17.cloned.1.call-start = ((), (), s32[]{:S(2)}) async-start(), calls=%async_computation.15 | async-start | bytes 14155776 | tf_op jit(solution)/shard_map/all_gather | solution.py:209
  22.0 54.4 %all-to-all-start = ((bf16[256,8,768]{0,2,1:T(8,128)(2,1)}), bf16[256,8,768]{0,2,1:T(8,128)(2,1)}, u32[]{:S(2)}, u32[]{:S(2)}) async-start(bf16[256,8,768]{0,2,1:T(8,128)(2,1)} %bitcast.204), calls=%async_computation | async-start | bytes 6291456 | tf_op jit(solution)/shard_map/all_to_all | solution.py:163
  76.4 67.6 %all-to-all-start.1 = ((bf16[256,8,768]{0,2,1:T(8,128)(2,1)}), bf16[256,8,768]{0,2,1:T(8,128)(2,1)}, u32[]{:S(2)}, u32[]{:S(2)}) async-start(bf16[256,8,768]{0,2,1:T(8,128)(2,1)} %bitcast.203), calls=%async_computation.1 | async-start | bytes 6291456 | tf_op jit(solution)/shard_map/all_to_all | solution.py:164
  81.0 317.0 %all-gather.15.cloned.1.call-start = ((), (), s32[]{:S(2)}) async-start(), calls=%async_computation.14 | async-start | bytes 14155776 | tf_op jit(solution)/shard_map/all_gather | solution.py:202
  139.1 118.2 %copy-start.44 = (f32[1,2048]{1,0:T(1,128)}, f32[1,2048]{1,0:T(1,128)S(1)}, u32[]{:S(2)}) copy-start(f32[1,2048]{1,0:T(1,128)S(1)} %get-tuple-element.112) | copy-start | bytes 24580
  260.4 400.8 %reduce-scatter.7.cloned.1.call-start = ((), (), s32[]{:S(2)}) async-start(), calls=%async_computation.16 | async-start | bytes 14155776 | tf_op jit(solution)/shard_map/reduce_scatter | solution.py:220
  496.9 74.6 %all-to-all-start.3 = ((bf16[8,256,768]{1,2,0:T(8,128)(2,1)}), bf16[8,256,768]{1,2,0:T(8,128)(2,1)}, u32[]{:S(2)}, u32[]{:S(2)}) async-start(bf16[8,256,768]{1,2,0:T(8,128)(2,1)} %copy.182), calls=%async_computation.3 | async-start | bytes 6291456 | tf_op jit(solution)/shard_map/all_to_all | solution.py:235
  571.5 59.2 %all-to-all-start.2 = ((bf16[8,256,768]{1,2,0:T(8,128)(2,1)}), bf16[8,256,768]{1,2,0:T(8,128)(2,1)}, u32[]{:S(2)}, u32[]{:S(2)}) async-start(bf16[8,256,768]{1,2,0:T(8,128)(2,1)} %copy.181), calls=%async_computation.2 | async-start | bytes 6291456 | tf_op jit(solution)/shard_map/all_to_all | solution.py:234
  576.0 340.0 %reduce-scatter.15.cloned.1.call-start = ((), (), s32[]{:S(2)}) async-start(), calls=%async_computation.20 | async-start | bytes 4718592 | tf_op jit(solution)/shard_map/reduce_scatter | solution.py:333
  648.2 36.1 %collective-permute-start = (bf16[96,6144]{1,0:T(8,128)(2,1)}, bf16[96,6144]{1,0:T(8,128)(2,1)}, u32[]{:S(2)}, u32[]{:S(2)}) collective-permute-start(bf16[96,6144]{1,0:T(8,128)(2,1)} %dynamic-slice_bitcast_fusion.1), channel_id=1, source_target_pairs={{0,1},{1,2},{2,3},{3,0},{4,5},{5,6},{6,7},{7,4},{8,9},{9,10},{10,1... | collective-permute-start | bytes 3538952 | tf_op jit(solution)/shard_map/ppermute | solution.py:91
  659.0 41.3 %collective-permute-start.1 = (bf16[96,6144]{1,0:T(8,128)(2,1)}, bf16[96,6144]{1,0:T(8,128)(2,1)}, u32[]{:S(2)}, u32[]{:S(2)}) collective-permute-start(bf16[96,6144]{1,0:T(8,128)(2,1)} %dynamic-slice_bitcast_fusion), channel_id=1, source_target_pairs={{0,3},{1,0},{2,1},{3,2},{4,7},{5,4},{6,5},{7,6},{8,11},{9,8},{10,9... | collective-permute-start | bytes 3538952 | tf_op jit(solution)/shard_map/ppermute | solution.py:92
  703.3 31.0 %collective-permute-start.2 = (bf16[96,6144]{1,0:T(8,128)(2,1)}, bf16[96,6144]{1,0:T(8,128)(2,1)}, u32[]{:S(2)}, u32[]{:S(2)}) collective-permute-start(bf16[96,6144]{1,0:T(8,128)(2,1)} %fusion.29), channel_id=1, source_target_pairs={{0,1},{1,2},{2,3},{3,0},{4,5},{5,6},{6,7},{7,4},{8,9},{9,10},{10,1... | collective-permute-start | bytes 3538952 | tf_op jit(solution)/shard_map/ppermute | solution.py:91
  706.8 51.8 %collective-permute-start.3 = (bf16[96,6144]{1,0:T(8,128)(2,1)}, bf16[96,6144]{1,0:T(8,128)(2,1)}, u32[]{:S(2)}, u32[]{:S(2)}) collective-permute-start(bf16[96,6144]{1,0:T(8,128)(2,1)} %fusion.28), channel_id=1, source_target_pairs={{0,3},{1,0},{2,1},{3,2},{4,7},{5,4},{6,5},{7,6},{8,11},{9,8},{10,9... | collective-permute-start | bytes 3538952 | tf_op jit(solution)/shard_map/ppermute | solution.py:92
  760.5 30.8 %collective-permute-start.4 = (bf16[96,6144]{1,0:T(8,128)(2,1)S(1)}, bf16[96,6144]{1,0:T(8,128)(2,1)}, u32[]{:S(2)}, u32[]{:S(2)}) collective-permute-start(bf16[96,6144]{1,0:T(8,128)(2,1)S(1)} %fusion.27), channel_id=1, source_target_pairs={{0,1},{1,2},{2,3},{3,0},{4,5},{5,6},{6,7},{7,4},{8,9},{9,10},{10,1... | collective-permute-start | bytes 3538952 | tf_op jit(solution)/shard_map/ppermute | solution.py:91
  763.2 52.5 %collective-permute-start.5 = (bf16[96,6144]{1,0:T(8,128)(2,1)S(1)}, bf16[96,6144]{1,0:T(8,128)(2,1)}, u32[]{:S(2)}, u32[]{:S(2)}) collective-permute-start(bf16[96,6144]{1,0:T(8,128)(2,1)S(1)} %fusion.26), channel_id=1, source_target_pairs={{0,3},{1,0},{2,1},{3,2},{4,7},{5,4},{6,5},{7,6},{8,11},{9,8},{10,9... | collective-permute-start | bytes 3538952 | tf_op jit(solution)/shard_map/ppermute | solution.py:92
  820.2 116.2 %reduce-scatter.13.cloned.1.call-start = ((), (), s32[]{:S(2)}) async-start(), calls=%async_computation.19 | async-start | bytes 4718592 | tf_op jit(solution)/shard_map/reduce_scatter | solution.py:333
  825.9 30.8 %collective-permute-start.6 = (bf16[96,6144]{1,0:T(8,128)(2,1)S(1)}, bf16[96,6144]{1,0:T(8,128)(2,1)}, u32[]{:S(2)}, u32[]{:S(2)}) collective-permute-start(bf16[96,6144]{1,0:T(8,128)(2,1)S(1)} %get-tuple-element.84), channel_id=1, source_target_pairs={{0,1},{1,2},{2,3},{3,0},{4,5},{5,6},{6,7},{7,4},{8,9},{9,10},{10,1... | collective-permute-start | bytes 3538952 | tf_op jit(solution)/shard_map/ppermute | solution.py:91
  832.5 48.5 %collective-permute-start.7 = (bf16[96,6144]{1,0:T(8,128)(2,1)S(1)}, bf16[96,6144]{1,0:T(8,128)(2,1)}, u32[]{:S(2)}, u32[]{:S(2)}) collective-permute-start(bf16[96,6144]{1,0:T(8,128)(2,1)S(1)} %get-tuple-element.86), channel_id=1, source_target_pairs={{0,3},{1,0},{2,1},{3,2},{4,7},{5,4},{6,5},{7,6},{8,11},{9,8},{10,9... | collective-permute-start | bytes 3538952 | tf_op jit(solution)/shard_map/ppermute | solution.py:92
  885.6 125.7 %reduce-scatter.17.cloned.1.call-start = ((), (), s32[]{:S(2)}) async-start(), calls=%async_computation.21 | async-start | bytes 9437184 | tf_op jit(solution)/shard_map/reduce_scatter | solution.py:333
  886.2 200.1 %reduce-scatter.11.cloned.1.call-start = ((), (), s32[]{:S(2)}) async-start(), calls=%async_computation.18 | async-start | bytes 9437184 | tf_op jit(solution)/shard_map/reduce_scatter | solution.py:333
  893.4 288.5 %reduce-scatter.9.cloned.1.call-start = ((), (), s32[]{:S(2)}) async-start(), calls=%async_computation.17 | async-start | bytes 14155776 | tf_op jit(solution)/shard_map/reduce_scatter | solution.py:226
  894.0 457.9 %all-reduce.3.cloned.1.call-start = ((), (), s32[]{:S(2)}) async-start(), calls=%async_computation.22 | async-start | bytes 6291456 | tf_op jit(solution)/shard_map/psum | solution.py:344
  894.0 289.8 %collective-permute-start.8 = (bf16[96,6144]{1,0:T(8,128)(2,1)}, bf16[96,6144]{1,0:T(8,128)(2,1)}, u32[]{:S(2)}, u32[]{:S(2)}) collective-permute-start(bf16[96,6144]{1,0:T(8,128)(2,1)} %collective-permute-done.6), channel_id=1, source_target_pairs={{0,1},{1,2},{2,3},{3,0},{4,5},{5,6},{6,7},{7,4},{8,9},{9,10},{10,1... | collective-permute-start | bytes 3538952 | tf_op jit(solution)/shard_map/ppermute | solution.py:91
  894.6 289.2 %collective-permute-start.9 = (bf16[96,6144]{1,0:T(8,128)(2,1)}, bf16[96,6144]{1,0:T(8,128)(2,1)}, u32[]{:S(2)}, u32[]{:S(2)}) collective-permute-start(bf16[96,6144]{1,0:T(8,128)(2,1)} %collective-permute-done.7), channel_id=1, source_target_pairs={{0,3},{1,0},{2,1},{3,2},{4,7},{5,4},{6,5},{7,6},{8,11},{9,8},{10,9... | collective-permute-start | bytes 3538952 | tf_op jit(solution)/shard_map/ppermute | solution.py:92
  1086.2 97.6 %copy-start.7 = (f32[384,2048]{1,0:T(8,128)S(1)}, f32[384,2048]{1,0:T(8,128)}, u32[]{:S(2)}) copy-start(f32[384,2048]{1,0:T(8,128)} %copy-done.5) | copy-start | bytes 9437188
  1185.3 173.3 %collective-permute-start.10 = (bf16[96,6144]{1,0:T(8,128)(2,1)}, bf16[96,6144]{1,0:T(8,128)(2,1)}, u32[]{:S(2)}, u32[]{:S(2)}) collective-permute-start(bf16[96,6144]{1,0:T(8,128)(2,1)} %collective-permute-done.8), channel_id=1, source_target_pairs={{0,1},{1,2},{2,3},{3,0},{4,5},{5,6},{6,7},{7,4},{8,9},{9,10},{10,1... | collective-permute-start | bytes 3538952 | tf_op jit(solution)/shard_map/ppermute | solution.py:91
  1186.8 171.8 %collective-permute-start.11 = (bf16[96,6144]{1,0:T(8,128)(2,1)}, bf16[96,6144]{1,0:T(8,128)(2,1)}, u32[]{:S(2)}, u32[]{:S(2)}) collective-permute-start(bf16[96,6144]{1,0:T(8,128)(2,1)} %collective-permute-done.9), channel_id=1, source_target_pairs={{0,3},{1,0},{2,1},{3,2},{4,7},{5,4},{6,5},{7,6},{8,11},{9,8},{10,9... | collective-permute-start | bytes 3538952 | tf_op jit(solution)/shard_map/ppermute | solution.py:92
  (66 other events, 814.3 us)
Sparse Core Ops, SparseCore 0:
  9.9 58.4 all-gather.8
  70.3 65.5 all-gather.6
  137.8 55.3 all-gather.10
  195.0 54.2 all-gather.12
  251.6 71.9 all-gather.16
  325.9 71.9 all-gather.14
  476.2 146.7 reduce-scatter.6
  820.3 50.5 reduce-scatter.14
  885.7 50.6 reduce-scatter.12
  939.7 71.4 reduce-scatter.16
  1014.7 71.4 reduce-scatter.10
  1089.6 92.2 reduce-scatter.8
  1184.5 167.3 all-reduce.2

commit v7 on v6

--- a/solution.py
+++ b/solution.py
@@ -204,6 +204,12 @@
     up_value = jnp.dot(normed_two_group, up_block, preferred_element_type=jnp.float32)
     hidden_low = (jax.nn.silu(gate_value) * up_value).astype(jnp.bfloat16)
     down_part = jnp.dot(hidden_low, down_weight, preferred_element_type=jnp.float32)
+    gate_value, up_value, hidden_low, down_part = lax.optimization_barrier(
+        (gate_value, up_value, hidden_low, down_part)
+    )
+    down_value = lax.psum_scatter(
+        down_part.astype(jnp.bfloat16), "fsdp", scatter_dimension=0, tiled=True
+    ).astype(jnp.float32)
     grad_top = cotangent.astype(jnp.float32) * valid_rows
     grad_down_low = grad_top.astype(jnp.bfloat16)
     grad_down_group = lax.all_gather(grad_down_low, "fsdp", axis=0, tiled=True)
@@ -222,10 +228,6 @@
     ).astype(jnp.float32)
     gate_grad_block = inner_rows(normed_two_group, grad_gate_low)
     up_grad_block = inner_rows(normed_two_group, grad_up_low)
-    grad_normed_two, down_part = lax.optimization_barrier((grad_normed_two, down_part))
-    down_value = lax.psum_scatter(
-        down_part.astype(jnp.bfloat16), "fsdp", scatter_dimension=0, tiled=True
-    ).astype(jnp.float32)
     grad_from_two, gain_two_terms = rms_backward(grad_normed_two, normal_two, inverse_two, gain_two)
     feed_gain_grad = jnp.sum(gain_two_terms, axis=0)
     grad_middle = grad_top + grad_from_two
@@ -280,7 +282,6 @@
     grad_query_rot, grad_key_rot, grad_value_low = ring.land(
         (grad_query_rot, grad_key_rot, grad_value_low)
     )
-    ring.issue()
     grad_query_raw, query_gain_terms = rms_backward(
         unrotate(grad_query_rot, cosine, sine), query_normal, query_inverse, gain_query
     )
@@ -294,13 +295,10 @@
     )
     grad_key_low = grad_key_raw.astype(jnp.bfloat16).reshape(row_count, value_heads * head_width)
     value_grad = inner_rows(normed_one_low, grad_value_low)
-    grad_query_low, grad_key_low = ring.land((grad_query_low, grad_key_low))
-    ring.issue()
     query_grad = inner_rows(normed_one_low, grad_query_low)
     key_grad = inner_rows(normed_one_low, grad_key_low)
     grad_normed_one = times_transposed(grad_query_low, attention_set[1])
-    grad_normed_one, down_value = ring.land((grad_normed_one, down_value))
-    ring.issue()
+    grad_normed_one, down_value = lax.optimization_barrier((grad_normed_one, down_value))
     layer_out = ((middle + down_value) * valid_rows).astype(jnp.bfloat16)
     grad_normed_one = (
         grad_normed_one
@@ -310,7 +308,6 @@
     grad_from_one, gain_one_terms = rms_backward(grad_normed_one, normal_one, inverse_one, gain_one)
     attention_gain_grad = jnp.sum(gain_one_terms, axis=0)
     input_grad = grad_middle + grad_from_one
-    input_grad = ring.land(input_grad)
     feed_sum = ring.result()
     feed_rep = (
         feed_sum[: feed_rows[0]],

time: 1420 us -> 1200 us (0.85)
  waiting for transfers between devices: 705 us -> 564 us
  blocking collectives: 169 us -> 95 us
    reduce_scatter x4, waiting for transfers between devices: 170 us -> 33.8 us  [low_sum(): lax.psum_scatter(v.astype(jnp.bfloat16), 'fsdp', scatter_dimension=0, til...]
    reduce_scatter x1, waiting for transfers between devices: 95.6 us -> 0.02 us  [per_device(): lax.psum_scatter(down_part.astype(jnp.bfloat16), 'fsdp', scatter_dimensio...]
    psum x1, blocking collectives: 113 us -> 42.2 us  [per_device(): lax.psum(jnp.concatenate([attention_gain_grad, feed_gain_grad, query_gain...]
    ppermute x6, waiting for transfers between devices: 41.4 us -> 109 us  [issue(): lax.ppermute(sends[0], self.axis, self.forward)]
    psum x1, waiting for transfers between devices: 35.2 us -> 89.2 us  [per_device(): lax.psum(attention_parts[1].astype(jnp.bfloat16), 'rep').astype(jnp.float32)]
    all_gather x1, waiting for transfers between devices: 63.2 us -> 26 us  [per_device(): grad_down_group = lax.all_gather(grad_down_low, 'fsdp', axis=0, tiled=True)]
    all_to_all x1, waiting for transfers between devices: 12.6 us -> 44.4 us  [per_device(): lax.all_to_all(gate_grad_block.astype(jnp.bfloat16), 'fsdp', 0, 1, tiled=...]
    all_to_all x1, waiting for transfers between devices: 41.5 us -> 20.5 us  [per_device(): lax.all_to_all(up_grad_block.astype(jnp.bfloat16), 'fsdp', 0, 1, tiled=True)]
  transfers between devices with their start and end apart: 29 -> 29, of which waited for: 19 -> 18; matrix products, arithmetic and copies ran while one was open for 23% -> 32% of each run, Pallas kernels for 0% -> 0%
where the time goes in v7:
time: 1200 us; the launch traced here: 1190 us
  waiting for transfers between devices  564 us (47%)
  matrix products  252 us (21%)
  local copies, waits for them, and re-layouts  122 us (10%)
  other arithmetic  104 us (9%)
  blocking collectives  95 us (8%)
  starting transfers between devices  40.9 us (3%)
  between operations  17.3 us (1%)
    ppermute x6, waiting for transfers between devices, issue(): lax.ppermute(sends[0], self.axis, self.forward)  109 us
    psum x1, waiting for transfers between devices, per_device(): lax.psum(attention_parts[1].astype(jnp.bfloat16), 'rep').astype(jnp.float32)  89.2 us
    dot_general x7, matrix products, times_transposed(): lax.dot_general(left, right, (((1,), (1,)), ((), ())), preferred_element_...  81.2 us
    ppermute x6, waiting for transfers between devices, issue(): lax.ppermute(sends[1], self.axis, self.backward)  72 us
    dot_general x7, matrix products, inner_rows(): lax.dot_general(left, right, (((0,), (0,)), ((), ())), preferred_element_...  71.5 us
    all_gather x1, waiting for transfers between devices, per_device(): lax.all_gather(normed_two_low, 'fsdp', axis=0, tiled=True)  64.8 us
    all_gather x1, blocking collectives, per_device(): lax.all_gather(jnp.stack([attention_gain, feed_gain]), 'fsdp', axis=1, ti...  52.8 us
    all_to_all x1, waiting for transfers between devices, per_device(): gate_block = lax.all_to_all(gate_weight, 'fsdp', 1, 0, tiled=True)  50 us
  transfers between devices with their start and end apart: 29, of which 18 were waited for; matrix products, arithmetic and copies ran while one was open for 32% of the time, Pallas kernels for 0%

profile of v7, /device:TPU:0, one launch (start us, length us, event | category | flops | bytes accessed | tf_op | source)
XLA Modules:
  0.0 1194.6 jit_solution(6798050488182160920)
XLA Ops:
  24.5 50.0 %all-to-all-done = bf16[256,8,768]{0,2,1:T(8,128)(2,1)} async-done(((bf16[256,8,768]{0,2,1:T(8,128)(2,1)}), bf16[256,8,768]{0,2,1:T(8,128)(2,1)}, u32[]{:S(2)}, u32[]{:S(2)}) %all-to-all-start) | async-done | bytes 3145760 | tf_op jit(solution)/shard_map/all_to_all | solution.py:163
  80.2 52.8 %all_gather.21 = bf16[2,2048]{1,0:T(2,128)(2,1)S(1)} all-gather(bf16[2,256]{1,0:T(2,128)(2,1)S(1)} %pad_maximum_fusion.5), channel_id=1, replica_groups=mesh['fsdp'=8,'rep'=4] {'fsdp'}, dimensions={1}, use_global_device_ids=true | all-gather | bytes 9216 | tf_op jit(solution)/shard_map/all_gather | solution.py:155
  169.9 20.7 %all-gather.11.cloned.1.call-done = bf16[2048,2048]{1,0:T(8,128)(2,1)} async-done(((bf16[256,2048]{1,0:T(8,128)(2,1)}), bf16[2048,2048]{1,0:T(8,128)(2,1)}) %all-gather.11.cloned.1.call-update) | async-done | bytes 8388624 | tf_op jit(solution)/shard_map/all_gather | solution.py:158
  217.3 29.3 %all-gather.13.cloned.1.call-done = bf16[2048,2048]{1,0:T(8,128)(2,1)} async-done(((bf16[256,2048]{1,0:T(8,128)(2,1)}), bf16[2048,2048]{1,0:T(8,128)(2,1)}) %all-gather.13.cloned.1.call-update) | async-done | bytes 8388624 | tf_op jit(solution)/shard_map/all_gather | solution.py:161
  265.3 64.8 %all-gather.15.cloned.1.call-done = bf16[3072,2048]{1,0:T(8,128)(2,1)} async-done(((bf16[384,2048]{1,0:T(8,128)(2,1)}), bf16[3072,2048]{1,0:T(8,128)(2,1)}) %all-gather.15.cloned.1.call-update) | async-done | bytes 12582928 | tf_op jit(solution)/shard_map/all_gather | solution.py:202
  330.1 16.4 %fusion.70 = f32[3072,768]{1,0:T(8,128)} fusion(bf16[3072,2048]{1,0:T(8,128)(2,1)} %all-gather.15.cloned.1.call-done, bf16[2048,768]{1,0:T(8,128)(2,1)} %bitcast.210), kind=kOutput, calls=%fused_computation.149 | convolution fusion | flops 9663676416 | bytes 25165824 | tf_op jit(solution)/shard_map/dot_general | solution.py:203
  346.5 17.6 %multiply_convert_fusion.2 = (bf16[3072,768]{1,0:T(8,128)(2,1)S(1)}, f32[3072,768]{1,0:T(8,128)}) fusion(f32[3072,768]{1,0:T(8,128)} %fusion.70, bf16[3072,2048]{1,0:T(8,128)(2,1)} %all-gather.15.cloned.1.call-done, bf16[2048,768]{1,0:T(8,128)(2,1)S(1)} %bitcast.212), kind=kOutput, calls=%fused_computation.13 | convolution fusion | flops 9677832192 | bytes 39321600 | tf_op jit(solution)/shard_map/dot_general | solution.py:204
  366.2 12.2 %fusion.71 = bf16[3072,2048]{1,0:T(8,128)(2,1)} fusion(bf16[3072,768]{1,0:T(8,128)(2,1)S(1)} %get-tuple-element.46, bf16[768,2048]{1,0:T(8,128)(2,1)S(1)} %copy-done), kind=kOutput, calls=%fused_computation.150 | convolution fusion | flops 9663676416 | bytes 20447232 | tf_op jit(solution)/shard_map/dot_general | solution.py:206
  378.5 26.0 %all-gather.17.cloned.1.call-done = bf16[3072,2048]{1,0:T(8,128)(2,1)} async-done(((bf16[384,2048]{1,0:T(8,128)(2,1)}), bf16[3072,2048]{1,0:T(8,128)(2,1)}) %all-gather.17.cloned.1.call-update) | async-done | bytes 12582928 | tf_op jit(solution)/shard_map/all_gather | solution.py:215
  404.5 22.4 %multiply_convert_fusion.1 = (bf16[3072,768]{1,0:T(8,128)(2,1)}, bf16[3072,768]{1,0:T(8,128)(2,1)}) fusion(f32[3072,768]{1,0:T(8,128)} %fusion.70, f32[3072,768]{1,0:T(8,128)} %get-tuple-element.44, bf16[3072,2048]{1,0:T(8,128)(2,1)} %all-gather.17.cloned.1.call-done, bf16[768,2048]{1,0:T(8,128)(2,1)S(1)} %copy-done), kind=kOutput, calls=%fused_computation.11 | convolution fusion | flops 9694347264 | bytes 44040192 | tf_op jit(solution)/shard_map/dot_general | solution.py:52
  426.9 17.7 %fusion.72 = f32[3072,2048]{1,0:T(8,128)} fusion(bf16[3072,768]{1,0:T(8,128)(2,1)} %get-tuple-element.90, bf16[2048,768]{1,0:T(8,128)(2,1)} %bitcast.211), kind=kOutput, calls=%fused_computation.151 | convolution fusion | flops 9663676416 | bytes 33030144 | tf_op jit(solution)/shard_map/dot_general | solution.py:52
  444.6 18.5 %add_convert_fusion = bf16[3072,2048]{1,0:T(8,128)(2,1)} fusion(f32[3072,2048]{1,0:T(8,128)} %fusion.72, bf16[3072,768]{1,0:T(8,128)(2,1)} %get-tuple-element.91, bf16[2048,768]{1,0:T(8,128)(2,1)S(1)} %bitcast.213), kind=kOutput, calls=%fused_computation.1 | convolution fusion | flops 9676259328 | bytes 45613056 | tf_op jit(solution)/shard_map/dot_general | solution.py:52
  463.1 14.7 %convolution_convert_fusion.4 = bf16[2048,768]{1,0:T(8,128)(2,1)S(1)} fusion(bf16[3072,2048]{1,0:T(8,128)(2,1)} %all-gather.15.cloned.1.call-done, bf16[3072,768]{1,0:T(8,128)(2,1)} %get-tuple-element.90), kind=kOutput, calls=%fused_computation.37 | convolution fusion | flops 9665249280 | bytes 20447232 | tf_op jit(solution)/shard_map/dot_general | solution.py:46
  485.2 15.7 %convolution_convert_fusion.3 = bf16[2048,768]{1,0:T(8,128)(2,1)} fusion(bf16[3072,2048]{1,0:T(8,128)(2,1)} %all-gather.15.cloned.1.call-done, bf16[3072,768]{1,0:T(8,128)(2,1)} %get-tuple-element.91), kind=kOutput, calls=%fused_computation.36 | convolution fusion | flops 9665249280 | bytes 20447232 | tf_op jit(solution)/shard_map/dot_general | solution.py:46
  505.6 44.4 %all-to-all-done.2 = bf16[8,256,768]{1,2,0:T(8,128)(2,1)S(1)} async-done(((bf16[8,256,768]{1,2,0:T(8,128)(2,1)}), bf16[8,256,768]{1,2,0:T(8,128)(2,1)S(1)}, u32[]{:S(2)}, u32[]{:S(2)}) %all-to-all-start.2) | async-done | bytes 3145760 | tf_op jit(solution)/shard_map/all_to_all | solution.py:236
  562.4 15.9 %convolution_convert_fusion.5 = bf16[768,2048]{1,0:T(8,128)(2,1)} fusion(bf16[3072,768]{1,0:T(8,128)(2,1)} %copy-done.81, bf16[3072,2048]{1,0:T(8,128)(2,1)} %all-gather.17.cloned.1.call-done), kind=kOutput, calls=%fused_computation.38 | convolution fusion | flops 9665249280 | bytes 20447232 | tf_op jit(solution)/shard_map/dot_general | solution.py:46
  588.6 20.5 %all-to-all-done.3 = bf16[8,256,768]{1,2,0:T(8,128)(2,1)} async-done(((bf16[8,256,768]{1,2,0:T(8,128)(2,1)}), bf16[8,256,768]{1,2,0:T(8,128)(2,1)}, u32[]{:S(2)}, u32[]{:S(2)}) %all-to-all-start.3) | async-done | bytes 3145760 | tf_op jit(solution)/shard_map/all_to_all | solution.py:237
  645.4 10.2 convolution_convert_fusion.6
  667.3 10.3 collective-permute-done
  688.8 13.7 %fusion.2 = bf16[8,2,384,384]{2,3,1,0:T(8,128)(2,1)} fusion(f32[8,384,384,2]{2,1,3,0:T(8,128)} %copy-done.2, f32[8,2,384]{2,1,0:T(2,128)S(1)} %bitcast.238, pred[384,384]{0,1:T(8,128)(4,1)S(1)} %copy-done.32, bf16[384,8,2,128]{0,3,2,1:T(8,128)(2,1)S(1)} %copy.190, bf16[384,8,128,1]{2,1,0,3:T(8,128)(2,1)} %bitcast.220), kind=kOutput, calls=%fused_computation.7 | convolution fusion | flops 1226840448 | bytes 16687104 | tf_op jit(solution)/shard_map/sub | solution.py:263
  710.5 25.3 %collective-permute-done.2 = bf16[96,6144]{1,0:T(8,128)(2,1)} collective-permute-done((bf16[96,6144]{1,0:T(8,128)(2,1)}, bf16[96,6144]{1,0:T(8,128)(2,1)}, u32[]{:S(2)}, u32[]{:S(2)}) %collective-permute-start.2) | collective-permute-done | bytes 1179680 | tf_op jit(solution)/shard_map/ppermute | solution.py:91
  750.2 17.3 %collective-permute-done.5 = bf16[96,6144]{1,0:T(8,128)(2,1)S(1)} collective-permute-done((bf16[96,6144]{1,0:T(8,128)(2,1)S(1)}, bf16[96,6144]{1,0:T(8,128)(2,1)S(1)}, u32[]{:S(2)}, u32[]{:S(2)}) %collective-permute-start.5) | collective-permute-done | bytes 1179680 | tf_op jit(solution)/shard_map/ppermute | solution.py:92
  767.5 25.3 %collective-permute-done.4 = bf16[96,6144]{1,0:T(8,128)(2,1)S(1)} collective-permute-done((bf16[96,6144]{1,0:T(8,128)(2,1)S(1)}, bf16[96,6144]{1,0:T(8,128)(2,1)S(1)}, u32[]{:S(2)}, u32[]{:S(2)}) %collective-permute-start.4) | collective-permute-done | bytes 1179680 | tf_op jit(solution)/shard_map/ppermute | solution.py:91
  853.6 42.2 %psum.35 = f32[4352]{0:T(1024)S(1)} all-reduce(f32[4352]{0:T(1024)S(1)} %pad_maximum_fusion.4), channel_id=1, replica_groups=mesh['fsdp'=8,'rep'=4] {'fsdp','rep'}, use_global_device_ids=true, to_apply=%region_17.18 | all-reduce | flops 4352 | bytes 34816 | tf_op jit(solution)/shard_map/psum | solution.py:319
  911.8 23.8 %collective-permute-done.8 = bf16[96,6144]{1,0:T(8,128)(2,1)S(1)} collective-permute-done((bf16[96,6144]{1,0:T(8,128)(2,1)}, bf16[96,6144]{1,0:T(8,128)(2,1)S(1)}, u32[]{:S(2)}, u32[]{:S(2)}) %collective-permute-start.8) | collective-permute-done | bytes 1179680 | tf_op jit(solution)/shard_map/ppermute | solution.py:91
  935.6 23.1 %collective-permute-done.9 = bf16[96,6144]{1,0:T(8,128)(2,1)S(1)} collective-permute-done((bf16[96,6144]{1,0:T(8,128)(2,1)}, bf16[96,6144]{1,0:T(8,128)(2,1)S(1)}, u32[]{:S(2)}, u32[]{:S(2)}) %collective-permute-start.9) | collective-permute-done | bytes 1179680 | tf_op jit(solution)/shard_map/ppermute | solution.py:92
  965.0 24.4 %collective-permute-done.10 = bf16[96,6144]{1,0:T(8,128)(2,1)S(1)} collective-permute-done((bf16[96,6144]{1,0:T(8,128)(2,1)S(1)}, bf16[96,6144]{1,0:T(8,128)(2,1)S(1)}, u32[]{:S(2)}, u32[]{:S(2)}) %collective-permute-start.10) | collective-permute-done | bytes 1179680 | tf_op jit(solution)/shard_map/ppermute | solution.py:91
  989.4 23.5 %collective-permute-done.11 = bf16[96,6144]{1,0:T(8,128)(2,1)S(1)} collective-permute-done((bf16[96,6144]{1,0:T(8,128)(2,1)S(1)}, bf16[96,6144]{1,0:T(8,128)(2,1)S(1)}, u32[]{:S(2)}, u32[]{:S(2)}) %collective-permute-start.11) | collective-permute-done | bytes 1179680 | tf_op jit(solution)/shard_map/ppermute | solution.py:92
  1023.6 33.8 %reduce-scatter.11.cloned.1.call-done = bf16[256,2048]{1,0:T(8,128)(2,1)} async-done(((bf16[2048,2048]{1,0:T(8,128)(2,1)}), bf16[256,2048]{1,0:T(8,128)(2,1)}) %reduce-scatter.11.cloned.1.call-update) | async-done | bytes 1048592 | tf_op jit(solution)/shard_map/reduce_scatter | solution.py:330
  1057.4 13.2 %bitcast_convert_fusion = f32[768,6144]{1,0:T(8,128)} fusion(bf16[2,4,96,6144]{3,2,1,0:T(8,128)(2,1)} %pad_maximum_fusion), kind=kLoop, calls=%fused_computation.3 | loop fusion | flops 4718592 | bytes 28311552 | tf_op jit(solution)/shard_map/convert_element_type | solution.py:121
  1070.6 13.9 %fusion.67 = (f32[256,6144]{1,0:T(8,128)}, f32[256,6144]{1,0:T(8,128)}, f32[256,6144]{1,0:T(8,128)}) fusion(f32[768,6144]{1,0:T(8,128)} %bitcast_convert_fusion), kind=kLoop, calls=%fused_computation.146 | loop fusion | bytes 37748736 | tf_op jit(solution)/shard_map/slice | solution.py:315
  1092.0 89.2 %all-reduce.3.cloned.1.call-done = (bf16[256,2048]{1,0:T(8,128)(2,1)}, bf16[256,1024]{1,0:T(8,128)(2,1)}, bf16[256,1024]{1,0:T(8,128)(2,1)}, bf16[256,2048]{1,0:T(8,128)(2,1)}) async-done(((bf16[256,2048]{1,0:T(8,128)(2,1)}, bf16[256,1024]{1,0:T(8,128)(2,1)}, bf16[256,1024]{1,0:T(8,128)(2,1)}, bf16[256,2048]{1,0:T(8,128)(2,1)}), (bf16[256,2048]{1,0:T(8,128)(2,1)}, bf16[256,1024]{1,0:T(8,128)(2,1)}, ...) | async-done | bytes 3145744 | tf_op jit(solution)/shard_map/psum | solution.py:341
  (328 shorter events, 328.8 us)
Async XLA Ops:
  7.2 359.1 %copy-start = (bf16[768,2048]{1,0:T(8,128)(2,1)S(1)}, bf16[768,2048]{1,0:T(8,128)(2,1)}, u32[]{:S(2)}) copy-start(bf16[768,2048]{1,0:T(8,128)(2,1)} %param.28) | copy-start | bytes 9437188
  7.2 139.9 %all-gather.7.cloned.1.call-start = ((), (), s32[]{:S(2)}) async-start(), calls=%async_computation.10 | async-start | bytes 4718592 | tf_op jit(solution)/shard_map/all_gather | solution.py:160
  7.9 144.7 %all-gather.9.cloned.1.call-start = ((), (), s32[]{:S(2)}) async-start(), calls=%async_computation.11 | async-start | bytes 4718592 | tf_op jit(solution)/shard_map/all_gather | solution.py:159
  8.7 181.9 %all-gather.11.cloned.1.call-start = ((), (), s32[]{:S(2)}) async-start(), calls=%async_computation.12 | async-start | bytes 9437184 | tf_op jit(solution)/shard_map/all_gather | solution.py:158
  9.4 237.2 %all-gather.13.cloned.1.call-start = ((), (), s32[]{:S(2)}) async-start(), calls=%async_computation.13 | async-start | bytes 9437184 | tf_op jit(solution)/shard_map/all_gather | solution.py:161
  14.6 59.8 %all-to-all-start = ((bf16[256,8,768]{0,2,1:T(8,128)(2,1)}), bf16[256,8,768]{0,2,1:T(8,128)(2,1)}, u32[]{:S(2)}, u32[]{:S(2)}) async-start(bf16[256,8,768]{0,2,1:T(8,128)(2,1)} %bitcast.205), calls=%async_computation | async-start | bytes 6291456 | tf_op jit(solution)/shard_map/all_to_all | solution.py:163
  74.5 64.9 %all-to-all-start.1 = ((bf16[256,8,768]{0,2,1:T(8,128)(2,1)}), bf16[256,8,768]{0,2,1:T(8,128)(2,1)}, u32[]{:S(2)}, u32[]{:S(2)}) async-start(bf16[256,8,768]{0,2,1:T(8,128)(2,1)} %bitcast.204), calls=%async_computation.1 | async-start | bytes 6291456 | tf_op jit(solution)/shard_map/all_to_all | solution.py:164
  79.1 251.1 %all-gather.15.cloned.1.call-start = ((), (), s32[]{:S(2)}) async-start(), calls=%async_computation.14 | async-start | bytes 14155776 | tf_op jit(solution)/shard_map/all_gather | solution.py:202
  134.5 71.1 %copy-start.24 = (f32[384,128]{0,1:T(8,128)}, f32[384,128]{0,1:T(8,128)S(1)}, u32[]{:S(2)}) copy-start(f32[384,128]{0,1:T(8,128)S(1)} %get-tuple-element.102) | copy-start | bytes 589828
  134.5 120.2 %copy-start.57 = (f32[1,2048]{1,0:T(1,128)}, f32[1,2048]{1,0:T(1,128)S(1)}, u32[]{:S(2)}) copy-start(f32[1,2048]{1,0:T(1,128)S(1)} %get-tuple-element.108) | copy-start | bytes 24580
  258.0 146.5 %all-gather.17.cloned.1.call-start = ((), (), s32[]{:S(2)}) async-start(), calls=%async_computation.15 | async-start | bytes 14155776 | tf_op jit(solution)/shard_map/all_gather | solution.py:215
  265.3 374.1 %reduce-scatter.7.cloned.1.call-start = ((), (), s32[]{:S(2)}) async-start(), calls=%async_computation.16 | async-start | bytes 14155776 | tf_op jit(solution)/shard_map/reduce_scatter | solution.py:226
  480.6 69.3 %all-to-all-start.2 = ((bf16[8,256,768]{1,2,0:T(8,128)(2,1)}), bf16[8,256,768]{1,2,0:T(8,128)(2,1)S(1)}, u32[]{:S(2)}, u32[]{:S(2)}) async-start(bf16[8,256,768]{1,2,0:T(8,128)(2,1)} %copy.181), calls=%async_computation.2 | async-start | bytes 6291456 | tf_op jit(solution)/shard_map/all_to_all | solution.py:236
  484.4 325.0 %reduce-scatter.9.cloned.1.call-start = ((), (), s32[]{:S(2)}) async-start(), calls=%async_computation.17 | async-start | bytes 14155776 | tf_op jit(solution)/shard_map/reduce_scatter | solution.py:210
  549.9 59.2 %all-to-all-start.3 = ((bf16[8,256,768]{1,2,0:T(8,128)(2,1)}), bf16[8,256,768]{1,2,0:T(8,128)(2,1)}, u32[]{:S(2)}, u32[]{:S(2)}) async-start(bf16[8,256,768]{1,2,0:T(8,128)(2,1)} %copy.182), calls=%async_computation.3 | async-start | bytes 6291456 | tf_op jit(solution)/shard_map/all_to_all | solution.py:237
  554.4 469.2 %reduce-scatter.15.cloned.1.call-start = ((), (), s32[]{:S(2)}) async-start(), calls=%async_computation.20 | async-start | bytes 4718592 | tf_op jit(solution)/shard_map/reduce_scatter | solution.py:330
  625.6 41.7 %collective-permute-start.1 = (bf16[96,6144]{1,0:T(8,128)(2,1)}, bf16[96,6144]{1,0:T(8,128)(2,1)}, u32[]{:S(2)}, u32[]{:S(2)}) collective-permute-start(bf16[96,6144]{1,0:T(8,128)(2,1)} %dynamic-slice_bitcast_fusion), channel_id=1, source_target_pairs={{0,3},{1,0},{2,1},{3,2},{4,7},{5,4},{6,5},{7,6},{8,11},{9,8},{10,9... | collective-permute-start | bytes 3538952 | tf_op jit(solution)/shard_map/ppermute | solution.py:92
  638.9 38.6 %collective-permute-start = (bf16[96,6144]{1,0:T(8,128)(2,1)}, bf16[96,6144]{1,0:T(8,128)(2,1)}, u32[]{:S(2)}, u32[]{:S(2)}) collective-permute-start(bf16[96,6144]{1,0:T(8,128)(2,1)} %dynamic-slice_bitcast_fusion.1), channel_id=1, source_target_pairs={{0,1},{1,2},{2,3},{3,0},{4,5},{5,6},{6,7},{7,4},{8,9},{9,10},{10,1... | collective-permute-start | bytes 3538952 | tf_op jit(solution)/shard_map/ppermute | solution.py:91
  680.5 30.0 %collective-permute-start.3 = (bf16[96,6144]{1,0:T(8,128)(2,1)}, bf16[96,6144]{1,0:T(8,128)(2,1)}, u32[]{:S(2)}, u32[]{:S(2)}) collective-permute-start(bf16[96,6144]{1,0:T(8,128)(2,1)} %fusion.33), channel_id=1, source_target_pairs={{0,3},{1,0},{2,1},{3,2},{4,7},{5,4},{6,5},{7,6},{8,11},{9,8},{10,9... | collective-permute-start | bytes 3538952 | tf_op jit(solution)/shard_map/ppermute | solution.py:92
  687.2 48.6 %collective-permute-start.2 = (bf16[96,6144]{1,0:T(8,128)(2,1)}, bf16[96,6144]{1,0:T(8,128)(2,1)}, u32[]{:S(2)}, u32[]{:S(2)}) collective-permute-start(bf16[96,6144]{1,0:T(8,128)(2,1)} %fusion.34), channel_id=1, source_target_pairs={{0,1},{1,2},{2,3},{3,0},{4,5},{5,6},{6,7},{7,4},{8,9},{9,10},{10,1... | collective-permute-start | bytes 3538952 | tf_op jit(solution)/shard_map/ppermute | solution.py:91
  737.7 29.7 %collective-permute-start.5 = (bf16[96,6144]{1,0:T(8,128)(2,1)S(1)}, bf16[96,6144]{1,0:T(8,128)(2,1)S(1)}, u32[]{:S(2)}, u32[]{:S(2)}) collective-permute-start(bf16[96,6144]{1,0:T(8,128)(2,1)S(1)} %fusion.31), channel_id=1, source_target_pairs={{0,3},{1,0},{2,1},{3,2},{4,7},{5,4},{6,5},{7,6},{8,11},{9,8},{10,9... | collective-permute-start | bytes 3538952 | tf_op jit(solution)/shard_map/ppermute | solution.py:92
  743.2 49.6 %collective-permute-start.4 = (bf16[96,6144]{1,0:T(8,128)(2,1)S(1)}, bf16[96,6144]{1,0:T(8,128)(2,1)S(1)}, u32[]{:S(2)}, u32[]{:S(2)}) collective-permute-start(bf16[96,6144]{1,0:T(8,128)(2,1)S(1)} %fusion.32), channel_id=1, source_target_pairs={{0,1},{1,2},{2,3},{3,0},{4,5},{5,6},{6,7},{7,4},{8,9},{9,10},{10,1... | collective-permute-start | bytes 3538952 | tf_op jit(solution)/shard_map/ppermute | solution.py:91
  798.5 225.1 %reduce-scatter.13.cloned.1.call-start = ((), (), s32[]{:S(2)}) async-start(), calls=%async_computation.19 | async-start | bytes 4718592 | tf_op jit(solution)/shard_map/reduce_scatter | solution.py:330
  808.5 215.1 %reduce-scatter.17.cloned.1.call-start = ((), (), s32[]{:S(2)}) async-start(), calls=%async_computation.21 | async-start | bytes 9437184 | tf_op jit(solution)/shard_map/reduce_scatter | solution.py:330
  809.3 248.1 %reduce-scatter.11.cloned.1.call-start = ((), (), s32[]{:S(2)}) async-start(), calls=%async_computation.18 | async-start | bytes 9437184 | tf_op jit(solution)/shard_map/reduce_scatter | solution.py:330
  817.2 87.5 %collective-permute-start.7 = (bf16[96,6144]{1,0:T(8,128)(2,1)}, bf16[96,6144]{1,0:T(8,128)(2,1)}, u32[]{:S(2)}, u32[]{:S(2)}) collective-permute-start(bf16[96,6144]{1,0:T(8,128)(2,1)} %get-tuple-element.84), channel_id=1, source_target_pairs={{0,3},{1,0},{2,1},{3,2},{4,7},{5,4},{6,5},{7,6},{8,11},{9,8},{10,9... | collective-permute-start | bytes 3538952 | tf_op jit(solution)/shard_map/ppermute | solution.py:92
  833.8 347.3 %all-reduce.3.cloned.1.call-start = ((), (), s32[]{:S(2)}) async-start(), calls=%async_computation.22 | async-start | bytes 6291456 | tf_op jit(solution)/shard_map/psum | solution.py:341
  839.8 64.9 %collective-permute-start.6 = (bf16[96,6144]{1,0:T(8,128)(2,1)}, bf16[96,6144]{1,0:T(8,128)(2,1)}, u32[]{:S(2)}, u32[]{:S(2)}) collective-permute-start(bf16[96,6144]{1,0:T(8,128)(2,1)} %get-tuple-element.82), channel_id=1, source_target_pairs={{0,1},{1,2},{2,3},{3,0},{4,5},{5,6},{6,7},{7,4},{8,9},{9,10},{10,1... | collective-permute-start | bytes 3538952 | tf_op jit(solution)/shard_map/ppermute | solution.py:91
  904.7 30.9 %collective-permute-start.8 = (bf16[96,6144]{1,0:T(8,128)(2,1)}, bf16[96,6144]{1,0:T(8,128)(2,1)S(1)}, u32[]{:S(2)}, u32[]{:S(2)}) collective-permute-start(bf16[96,6144]{1,0:T(8,128)(2,1)} %collective-permute-done.6), channel_id=1, source_target_pairs={{0,1},{1,2},{2,3},{3,0},{4,5},{5,6},{6,7},{7,4},{8,9},{9,10},{10,1... | collective-permute-start | bytes 3538952 | tf_op jit(solution)/shard_map/ppermute | solution.py:91
  906.5 52.3 %collective-permute-start.9 = (bf16[96,6144]{1,0:T(8,128)(2,1)}, bf16[96,6144]{1,0:T(8,128)(2,1)S(1)}, u32[]{:S(2)}, u32[]{:S(2)}) collective-permute-start(bf16[96,6144]{1,0:T(8,128)(2,1)} %collective-permute-done.7), channel_id=1, source_target_pairs={{0,3},{1,0},{2,1},{3,2},{4,7},{5,4},{6,5},{7,6},{8,11},{9,8},{10,9... | collective-permute-start | bytes 3538952 | tf_op jit(solution)/shard_map/ppermute | solution.py:92
  958.7 30.6 %collective-permute-start.10 = (bf16[96,6144]{1,0:T(8,128)(2,1)S(1)}, bf16[96,6144]{1,0:T(8,128)(2,1)S(1)}, u32[]{:S(2)}, u32[]{:S(2)}) collective-permute-start(bf16[96,6144]{1,0:T(8,128)(2,1)S(1)} %collective-permute-done.8), channel_id=1, source_target_pairs={{0,1},{1,2},{2,3},{3,0},{4,5},{5,6},{6,7},{7,4},{8,9},{9,10},{10,1... | collective-permute-start | bytes 3538952 | tf_op jit(solution)/shard_map/ppermute | solution.py:91
  959.6 53.3 %collective-permute-start.11 = (bf16[96,6144]{1,0:T(8,128)(2,1)S(1)}, bf16[96,6144]{1,0:T(8,128)(2,1)S(1)}, u32[]{:S(2)}, u32[]{:S(2)}) collective-permute-start(bf16[96,6144]{1,0:T(8,128)(2,1)S(1)} %collective-permute-done.9), channel_id=1, source_target_pairs={{0,3},{1,0},{2,1},{3,2},{4,7},{5,4},{6,5},{7,6},{8,11},{9,8},{10,9... | collective-permute-start | bytes 3538952 | tf_op jit(solution)/shard_map/ppermute | solution.py:92
  (81 other events, 824.1 us)
Sparse Core Ops, SparseCore 0:
  9.9 64.1 all-gather.6
  76.0 59.1 all-gather.8
  137.0 53.5 all-gather.10
  192.4 54.2 all-gather.12
  258.1 71.9 all-gather.14
  332.4 71.9 all-gather.16
  463.2 138.2 reduce-scatter.6
  605.0 100.6 reduce-scatter.8
  798.6 53.5 reduce-scatter.14
  856.0 51.4 reduce-scatter.12
  911.0 71.5 reduce-scatter.16
  985.9 71.4 reduce-scatter.10
  1060.0 121.0 all-reduce.2

commit v8 on v7

--- a/solution.py
+++ b/solution.py
@@ -282,6 +282,7 @@
     grad_query_rot, grad_key_rot, grad_value_low = ring.land(
         (grad_query_rot, grad_key_rot, grad_value_low)
     )
+    ring.issue()
     grad_query_raw, query_gain_terms = rms_backward(
         unrotate(grad_query_rot, cosine, sine), query_normal, query_inverse, gain_query
     )
@@ -295,10 +296,13 @@
     )
     grad_key_low = grad_key_raw.astype(jnp.bfloat16).reshape(row_count, value_heads * head_width)
     value_grad = inner_rows(normed_one_low, grad_value_low)
+    grad_query_low, grad_key_low = ring.land((grad_query_low, grad_key_low))
+    ring.issue()
     query_grad = inner_rows(normed_one_low, grad_query_low)
     key_grad = inner_rows(normed_one_low, grad_key_low)
     grad_normed_one = times_transposed(grad_query_low, attention_set[1])
-    grad_normed_one, down_value = lax.optimization_barrier((grad_normed_one, down_value))
+    grad_normed_one, down_value = ring.land((grad_normed_one, down_value))
+    ring.issue()
     layer_out = ((middle + down_value) * valid_rows).astype(jnp.bfloat16)
     grad_normed_one = (
         grad_normed_one
@@ -308,6 +312,7 @@
     grad_from_one, gain_one_terms = rms_backward(grad_normed_one, normal_one, inverse_one, gain_one)
     attention_gain_grad = jnp.sum(gain_one_terms, axis=0)
     input_grad = grad_middle + grad_from_one
+    input_grad = ring.land(input_grad)
     feed_sum = ring.result()
     feed_rep = (
         feed_sum[: feed_rows[0]],
@@ -331,6 +336,10 @@
 
     attention_parts = (
         None, low_sum(query_grad), low_sum(key_grad), low_sum(value_grad), low_sum(output_grad)
+    )
+    output_rep = lax.psum(attention_parts[4].astype(jnp.bfloat16), "rep")
+    output_rep, *late_parts = lax.optimization_barrier(
+        (output_rep,) + tuple(attention_parts[i].astype(jnp.bfloat16) for i in (1, 2, 3))
     )
     finals = (
         feed_gain_out,
@@ -338,10 +347,10 @@
         feed_rep[1],
         feed_rep[2],
         attention_gain_out,
-        lax.psum(attention_parts[1].astype(jnp.bfloat16), "rep").astype(jnp.float32),
-        lax.psum(attention_parts[2].astype(jnp.bfloat16), "rep").astype(jnp.float32),
-        lax.psum(attention_parts[3].astype(jnp.bfloat16), "rep").astype(jnp.float32),
-        lax.psum(attention_parts[4].astype(jnp.bfloat16), "rep").astype(jnp.float32),
+        lax.psum(late_parts[0], "rep").astype(jnp.float32),
+        lax.psum(late_parts[1], "rep").astype(jnp.float32),
+        lax.psum(late_parts[2], "rep").astype(jnp.float32),
+        output_rep.astype(jnp.float32),
     )
     return (
         layer_out,

time: 1200 us -> 1220 us (1.017)
  blocking collectives: 95 us -> 137 us
  waiting for transfers between devices: 564 us -> 542 us
    ppermute x6, waiting for transfers between devices: 109 us -> 58.1 us  [issue(): lax.ppermute(sends[0], self.axis, self.forward)]
    psum x1, blocking collectives: 42.2 us -> 84.7 us  [per_device(): lax.psum(jnp.concatenate([attention_gain_grad, feed_gain_grad, query_gain...]
    psum x1 -> x2, waiting for transfers between devices: 89.2 us -> 52.6 us  [the longest x1 52.6 us: per_device(): lax.psum(late_parts[0], 'rep').astype(jnp.float32)]
    ppermute x6, waiting for transfers between devices: 72 us -> 108 us  [issue(): lax.ppermute(sends[1], self.axis, self.backward)]
    all_to_all x1, waiting for transfers between devices: 20.5 us -> 45.2 us  [per_device(): lax.all_to_all(up_grad_block.astype(jnp.bfloat16), 'fsdp', 0, 1, tiled=True)]
    reduce_scatter x4, waiting for transfers between devices: 33.8 us -> 53.3 us  [low_sum(): lax.psum_scatter(v.astype(jnp.bfloat16), 'fsdp', scatter_dimension=0, til...]
    all_to_all x1, waiting for transfers between devices: 44.4 us -> 28.5 us  [per_device(): lax.all_to_all(gate_grad_block.astype(jnp.bfloat16), 'fsdp', 0, 1, tiled=...]
    unnamed x172 -> x162, local copies, waits for them, and re-layouts: 29.7 us -> 27.8 us
  transfers between devices with their start and end apart: 29 -> 30, of which waited for: 18 -> 18; matrix products, arithmetic and copies ran while one was open for 32% -> 32% of each run, Pallas kernels for 0% -> 0%
where the time goes in v8:
time: 1220 us; the launch traced here: 1210 us
  waiting for transfers between devices  542 us (44%)
  matrix products  248 us (20%)
  blocking collectives  137 us (11%)
  local copies, waits for them, and re-layouts  126 us (10%)
  other arithmetic  99 us (8%)
  starting transfers between devices  42.5 us (3%)
  between operations  17.2 us (1%)
    ppermute x6, waiting for transfers between devices, issue(): lax.ppermute(sends[1], self.axis, self.backward)  108 us
    psum x1, blocking collectives, per_device(): lax.psum(jnp.concatenate([attention_gain_grad, feed_gain_grad, query_gain...  84.7 us
    dot_general x7, matrix products, times_transposed(): lax.dot_general(left, right, (((1,), (1,)), ((), ())), preferred_element_...  78.5 us
    dot_general x7, matrix products, inner_rows(): lax.dot_general(left, right, (((0,), (0,)), ((), ())), preferred_element_...  71.5 us
    all_gather x1, waiting for transfers between devices, per_device(): lax.all_gather(normed_two_low, 'fsdp', axis=0, tiled=True)  64.8 us
    ppermute x6, waiting for transfers between devices, issue(): lax.ppermute(sends[0], self.axis, self.forward)  58.1 us
    reduce_scatter x4, waiting for transfers between devices, low_sum(): lax.psum_scatter(v.astype(jnp.bfloat16), 'fsdp', scatter_dimension=0, til...  53.3 us
    all_gather x1, blocking collectives, per_device(): lax.all_gather(jnp.stack([attention_gain, feed_gain]), 'fsdp', axis=1, ti...  52.8 us
  transfers between devices with their start and end apart: 30, of which 18 were waited for; matrix products, arithmetic and copies ran while one was open for 32% of the time, Pallas kernels for 0%

profile of v8, /device:TPU:0, one launch (start us, length us, event | category | flops | bytes accessed | tf_op | source)
XLA Modules:
  0.0 1211.9 jit_solution(10612204038523240024)
XLA Ops:
  24.5 50.0 %all-to-all-done = bf16[256,8,768]{0,2,1:T(8,128)(2,1)} async-done(((bf16[256,8,768]{0,2,1:T(8,128)(2,1)}), bf16[256,8,768]{0,2,1:T(8,128)(2,1)}, u32[]{:S(2)}, u32[]{:S(2)}) %all-to-all-start) | async-done | bytes 3145760 | tf_op jit(solution)/shard_map/all_to_all | solution.py:163
  80.2 52.8 %all_gather.21 = bf16[2,2048]{1,0:T(2,128)(2,1)S(1)} all-gather(bf16[2,256]{1,0:T(2,128)(2,1)S(1)} %pad_maximum_fusion.5), channel_id=1, replica_groups=mesh['fsdp'=8,'rep'=4] {'fsdp'}, dimensions={1}, use_global_device_ids=true | all-gather | bytes 9216 | tf_op jit(solution)/shard_map/all_gather | solution.py:155
  167.6 23.0 %all-gather.11.cloned.1.call-done = bf16[2048,2048]{1,0:T(8,128)(2,1)} async-done(((bf16[256,2048]{1,0:T(8,128)(2,1)}), bf16[2048,2048]{1,0:T(8,128)(2,1)}) %all-gather.11.cloned.1.call-update) | async-done | bytes 8388624 | tf_op jit(solution)/shard_map/all_gather | solution.py:158
  217.7 29.0 %all-gather.13.cloned.1.call-done = bf16[2048,2048]{1,0:T(8,128)(2,1)} async-done(((bf16[256,2048]{1,0:T(8,128)(2,1)}), bf16[2048,2048]{1,0:T(8,128)(2,1)}) %all-gather.13.cloned.1.call-update) | async-done | bytes 8388624 | tf_op jit(solution)/shard_map/all_gather | solution.py:161
  265.3 64.8 %all-gather.15.cloned.1.call-done = bf16[3072,2048]{1,0:T(8,128)(2,1)} async-done(((bf16[384,2048]{1,0:T(8,128)(2,1)}), bf16[3072,2048]{1,0:T(8,128)(2,1)}) %all-gather.15.cloned.1.call-update) | async-done | bytes 12582928 | tf_op jit(solution)/shard_map/all_gather | solution.py:202
  330.1 16.4 %fusion.70 = f32[3072,768]{1,0:T(8,128)} fusion(bf16[3072,2048]{1,0:T(8,128)(2,1)} %all-gather.15.cloned.1.call-done, bf16[2048,768]{1,0:T(8,128)(2,1)} %bitcast.210), kind=kOutput, calls=%fused_computation.149 | convolution fusion | flops 9663676416 | bytes 25165824 | tf_op jit(solution)/shard_map/dot_general | solution.py:203
  346.5 17.5 %multiply_convert_fusion.2 = (bf16[3072,768]{1,0:T(8,128)(2,1)S(1)}, f32[3072,768]{1,0:T(8,128)}) fusion(f32[3072,768]{1,0:T(8,128)} %fusion.70, bf16[3072,2048]{1,0:T(8,128)(2,1)} %all-gather.15.cloned.1.call-done, bf16[2048,768]{1,0:T(8,128)(2,1)S(1)} %bitcast.212), kind=kOutput, calls=%fused_computation.13 | convolution fusion | flops 9677832192 | bytes 39321600 | tf_op jit(solution)/shard_map/dot_general | solution.py:204
  366.2 12.3 %fusion.71 = bf16[3072,2048]{1,0:T(8,128)(2,1)} fusion(bf16[3072,768]{1,0:T(8,128)(2,1)S(1)} %get-tuple-element.53, bf16[768,2048]{1,0:T(8,128)(2,1)S(1)} %copy-done), kind=kOutput, calls=%fused_computation.150 | convolution fusion | flops 9663676416 | bytes 20447232 | tf_op jit(solution)/shard_map/dot_general | solution.py:206
  378.5 26.0 %all-gather.17.cloned.1.call-done = bf16[3072,2048]{1,0:T(8,128)(2,1)} async-done(((bf16[384,2048]{1,0:T(8,128)(2,1)}), bf16[3072,2048]{1,0:T(8,128)(2,1)}) %all-gather.17.cloned.1.call-update) | async-done | bytes 12582928 | tf_op jit(solution)/shard_map/all_gather | solution.py:215
  404.4 22.2 %multiply_convert_fusion.1 = (bf16[3072,768]{1,0:T(8,128)(2,1)}, bf16[3072,768]{1,0:T(8,128)(2,1)}) fusion(f32[3072,768]{1,0:T(8,128)} %fusion.70, f32[3072,768]{1,0:T(8,128)} %get-tuple-element.51, bf16[3072,2048]{1,0:T(8,128)(2,1)} %all-gather.17.cloned.1.call-done, bf16[768,2048]{1,0:T(8,128)(2,1)S(1)} %copy-done), kind=kOutput, calls=%fused_computation.11 | convolution fusion | flops 9694347264 | bytes 44040192 | tf_op jit(solution)/shard_map/dot_general | solution.py:52
  426.7 17.7 %fusion.72 = f32[3072,2048]{1,0:T(8,128)} fusion(bf16[3072,768]{1,0:T(8,128)(2,1)} %get-tuple-element.104, bf16[2048,768]{1,0:T(8,128)(2,1)} %bitcast.211), kind=kOutput, calls=%fused_computation.151 | convolution fusion | flops 9663676416 | bytes 33030144 | tf_op jit(solution)/shard_map/dot_general | solution.py:52
  444.4 18.7 %add_convert_fusion = bf16[3072,2048]{1,0:T(8,128)(2,1)} fusion(f32[3072,2048]{1,0:T(8,128)} %fusion.72, bf16[3072,768]{1,0:T(8,128)(2,1)} %get-tuple-element.105, bf16[2048,768]{1,0:T(8,128)(2,1)S(1)} %bitcast.213), kind=kOutput, calls=%fused_computation.1 | convolution fusion | flops 9676259328 | bytes 45613056 | tf_op jit(solution)/shard_map/dot_general | solution.py:52
  463.1 15.0 %convolution_convert_fusion.3 = bf16[2048,768]{1,0:T(8,128)(2,1)S(1)} fusion(bf16[3072,2048]{1,0:T(8,128)(2,1)} %all-gather.15.cloned.1.call-done, bf16[3072,768]{1,0:T(8,128)(2,1)} %get-tuple-element.105), kind=kOutput, calls=%fused_computation.36 | convolution fusion | flops 9665249280 | bytes 20447232 | tf_op jit(solution)/shard_map/dot_general | solution.py:46
  484.5 15.7 %convolution_convert_fusion.4 = bf16[2048,768]{1,0:T(8,128)(2,1)} fusion(bf16[3072,2048]{1,0:T(8,128)(2,1)} %all-gather.15.cloned.1.call-done, bf16[3072,768]{1,0:T(8,128)(2,1)} %get-tuple-element.104), kind=kOutput, calls=%fused_computation.37 | convolution fusion | flops 9665249280 | bytes 20447232 | tf_op jit(solution)/shard_map/dot_general | solution.py:46
  504.8 45.2 %all-to-all-done.3 = bf16[8,256,768]{1,2,0:T(8,128)(2,1)S(1)} async-done(((bf16[8,256,768]{1,2,0:T(8,128)(2,1)}), bf16[8,256,768]{1,2,0:T(8,128)(2,1)S(1)}, u32[]{:S(2)}, u32[]{:S(2)}) %all-to-all-start.3) | async-done | bytes 3145760 | tf_op jit(solution)/shard_map/all_to_all | solution.py:237
  554.6 15.8 %convolution_convert_fusion.5 = bf16[768,2048]{1,0:T(8,128)(2,1)} fusion(bf16[3072,768]{1,0:T(8,128)(2,1)} %copy-done.74, bf16[3072,2048]{1,0:T(8,128)(2,1)} %all-gather.17.cloned.1.call-done), kind=kOutput, calls=%fused_computation.38 | convolution fusion | flops 9665249280 | bytes 20447232 | tf_op jit(solution)/shard_map/dot_general | solution.py:46
  580.7 28.5 %all-to-all-done.2 = bf16[8,256,768]{1,2,0:T(8,128)(2,1)} async-done(((bf16[8,256,768]{1,2,0:T(8,128)(2,1)}), bf16[8,256,768]{1,2,0:T(8,128)(2,1)}, u32[]{:S(2)}, u32[]{:S(2)}) %all-to-all-start.2) | async-done | bytes 3145760 | tf_op jit(solution)/shard_map/all_to_all | solution.py:236
  643.7 10.4 convolution_convert_fusion.6
  665.5 11.9 collective-permute-done.1
  698.2 13.6 %fusion.2 = bf16[8,2,384,384]{2,3,1,0:T(8,128)(2,1)} fusion(f32[8,384,384,2]{2,1,3,0:T(8,128)} %copy-done.2, f32[8,2,384]{2,1,0:T(2,128)S(1)} %bitcast.238, pred[384,384]{0,1:T(8,128)(4,1)S(1)} %copy-done.35, bf16[384,8,2,128]{0,3,2,1:T(8,128)(2,1)S(1)} %copy.190, bf16[384,8,128,1]{2,1,0,3:T(8,128)(2,1)} %bitcast.220), kind=kOutput, calls=%fused_computation.7 | convolution fusion | flops 1226840448 | bytes 16687104 | tf_op jit(solution)/shard_map/sub | solution.py:263
  720.3 24.4 %collective-permute-done.3 = bf16[96,6144]{1,0:T(8,128)(2,1)} collective-permute-done((bf16[96,6144]{1,0:T(8,128)(2,1)}, bf16[96,6144]{1,0:T(8,128)(2,1)}, u32[]{:S(2)}, u32[]{:S(2)}) %collective-permute-start.3) | collective-permute-done | bytes 1179680 | tf_op jit(solution)/shard_map/ppermute | solution.py:92
  758.0 19.5 %collective-permute-done.4 = bf16[96,6144]{1,0:T(8,128)(2,1)} collective-permute-done((bf16[96,6144]{1,0:T(8,128)(2,1)S(1)}, bf16[96,6144]{1,0:T(8,128)(2,1)}, u32[]{:S(2)}, u32[]{:S(2)}) %collective-permute-start.4) | collective-permute-done | bytes 1179680 | tf_op jit(solution)/shard_map/ppermute | solution.py:91
  777.5 24.3 %collective-permute-done.5 = bf16[96,6144]{1,0:T(8,128)(2,1)} collective-permute-done((bf16[96,6144]{1,0:T(8,128)(2,1)S(1)}, bf16[96,6144]{1,0:T(8,128)(2,1)}, u32[]{:S(2)}, u32[]{:S(2)}) %collective-permute-start.5) | collective-permute-done | bytes 1179680 | tf_op jit(solution)/shard_map/ppermute | solution.py:92
  830.9 12.0 collective-permute-done.6
  842.8 24.4 %collective-permute-done.7 = bf16[96,6144]{1,0:T(8,128)(2,1)} collective-permute-done((bf16[96,6144]{1,0:T(8,128)(2,1)S(1)}, bf16[96,6144]{1,0:T(8,128)(2,1)}, u32[]{:S(2)}, u32[]{:S(2)}) %collective-permute-start.7) | collective-permute-done | bytes 1179680 | tf_op jit(solution)/shard_map/ppermute | solution.py:92
  896.4 18.1 %collective-permute-done.8 = bf16[96,6144]{1,0:T(8,128)(2,1)} collective-permute-done((bf16[96,6144]{1,0:T(8,128)(2,1)}, bf16[96,6144]{1,0:T(8,128)(2,1)}, u32[]{:S(2)}, u32[]{:S(2)}) %collective-permute-start.8) | collective-permute-done | bytes 1179680 | tf_op jit(solution)/shard_map/ppermute | solution.py:91
  914.4 22.9 %collective-permute-done.9 = bf16[96,6144]{1,0:T(8,128)(2,1)} collective-permute-done((bf16[96,6144]{1,0:T(8,128)(2,1)}, bf16[96,6144]{1,0:T(8,128)(2,1)}, u32[]{:S(2)}, u32[]{:S(2)}) %collective-permute-start.9) | collective-permute-done | bytes 1179680 | tf_op jit(solution)/shard_map/ppermute | solution.py:92
  945.3 84.7 %psum.35 = f32[4352]{0:T(1024)S(1)} all-reduce(f32[4352]{0:T(1024)S(1)} %pad_maximum_fusion.4), channel_id=1, replica_groups=mesh['fsdp'=8,'rep'=4] {'fsdp','rep'}, use_global_device_ids=true, to_apply=%region_17.18 | all-reduce | flops 4352 | bytes 34816 | tf_op jit(solution)/shard_map/psum | solution.py:324
  1058.1 53.3 %reduce-scatter.13.cloned.1.call-done = bf16[256,2048]{1,0:T(8,128)(2,1)} async-done(((bf16[2048,2048]{1,0:T(8,128)(2,1)}), bf16[256,2048]{1,0:T(8,128)(2,1)}) %reduce-scatter.13.cloned.1.call-update) | async-done | bytes 1048592 | tf_op jit(solution)/shard_map/reduce_scatter | solution.py:335
  1111.4 13.0 %bitcast_convert_fusion = f32[768,6144]{1,0:T(8,128)} fusion(bf16[2,4,96,6144]{3,2,1,0:T(8,128)(2,1)} %pad_maximum_fusion), kind=kLoop, calls=%fused_computation.3 | loop fusion | flops 4718592 | bytes 28311552 | tf_op jit(solution)/shard_map/convert_element_type | solution.py:121
  1124.3 13.9 %fusion.67 = (f32[256,6144]{1,0:T(8,128)}, f32[256,6144]{1,0:T(8,128)}, f32[256,6144]{1,0:T(8,128)}) fusion(f32[768,6144]{1,0:T(8,128)} %bitcast_convert_fusion), kind=kLoop, calls=%fused_computation.146 | loop fusion | bytes 37748736 | tf_op jit(solution)/shard_map/slice | solution.py:320
  1147.4 52.6 %all-reduce.6.cloned.1.call-done = (bf16[256,2048]{1,0:T(8,128)(2,1)}, bf16[256,1024]{1,0:T(8,128)(2,1)}, bf16[256,1024]{1,0:T(8,128)(2,1)}) async-done(((bf16[256,2048]{1,0:T(8,128)(2,1)}, bf16[256,1024]{1,0:T(8,128)(2,1)}, bf16[256,1024]{1,0:T(8,128)(2,1)}), (bf16[256,2048]{1,0:T(8,128)(2,1)}, bf16[256,1024]{1,0:T(8,128)(2,1)}, bf16[256,1024]{1,0:T(8,128)(2,1)})) %all-reduce.6.cloned.1.call-update) | async-done | bytes 2097168 | tf_op jit(solution)/shard_map/psum | solution.py:350
  (323 shorter events, 325.5 us)
Async XLA Ops:
  7.2 359.0 %copy-start = (bf16[768,2048]{1,0:T(8,128)(2,1)S(1)}, bf16[768,2048]{1,0:T(8,128)(2,1)}, u32[]{:S(2)}) copy-start(bf16[768,2048]{1,0:T(8,128)(2,1)} %param.28) | copy-start | bytes 9437188
  7.2 139.6 %all-gather.9.cloned.1.call-start = ((), (), s32[]{:S(2)}) async-start(), calls=%async_computation.11 | async-start | bytes 4718592 | tf_op jit(solution)/shard_map/all_gather | solution.py:159
  7.9 152.1 %all-gather.7.cloned.1.call-start = ((), (), s32[]{:S(2)}) async-start(), calls=%async_computation.10 | async-start | bytes 4718592 | tf_op jit(solution)/shard_map/all_gather | solution.py:160
  8.7 181.9 %all-gather.11.cloned.1.call-start = ((), (), s32[]{:S(2)}) async-start(), calls=%async_computation.12 | async-start | bytes 9437184 | tf_op jit(solution)/shard_map/all_gather | solution.py:158
  9.4 237.2 %all-gather.13.cloned.1.call-start = ((), (), s32[]{:S(2)}) async-start(), calls=%async_computation.13 | async-start | bytes 9437184 | tf_op jit(solution)/shard_map/all_gather | solution.py:161
  14.6 59.8 %all-to-all-start = ((bf16[256,8,768]{0,2,1:T(8,128)(2,1)}), bf16[256,8,768]{0,2,1:T(8,128)(2,1)}, u32[]{:S(2)}, u32[]{:S(2)}) async-start(bf16[256,8,768]{0,2,1:T(8,128)(2,1)} %bitcast.205), calls=%async_computation | async-start | bytes 6291456 | tf_op jit(solution)/shard_map/all_to_all | solution.py:163
  74.5 64.8 %all-to-all-start.1 = ((bf16[256,8,768]{0,2,1:T(8,128)(2,1)}), bf16[256,8,768]{0,2,1:T(8,128)(2,1)}, u32[]{:S(2)}, u32[]{:S(2)}) async-start(bf16[256,8,768]{0,2,1:T(8,128)(2,1)} %bitcast.204), calls=%async_computation.1 | async-start | bytes 6291456 | tf_op jit(solution)/shard_map/all_to_all | solution.py:164
  79.1 251.0 %all-gather.15.cloned.1.call-start = ((), (), s32[]{:S(2)}) async-start(), calls=%async_computation.14 | async-start | bytes 14155776 | tf_op jit(solution)/shard_map/all_gather | solution.py:202
  257.9 146.5 %all-gather.17.cloned.1.call-start = ((), (), s32[]{:S(2)}) async-start(), calls=%async_computation.15 | async-start | bytes 14155776 | tf_op jit(solution)/shard_map/all_gather | solution.py:215
  265.2 373.0 %reduce-scatter.7.cloned.1.call-start = ((), (), s32[]{:S(2)}) async-start(), calls=%async_computation.16 | async-start | bytes 14155776 | tf_op jit(solution)/shard_map/reduce_scatter | solution.py:226
  480.8 69.2 %all-to-all-start.3 = ((bf16[8,256,768]{1,2,0:T(8,128)(2,1)}), bf16[8,256,768]{1,2,0:T(8,128)(2,1)S(1)}, u32[]{:S(2)}, u32[]{:S(2)}) async-start(bf16[8,256,768]{1,2,0:T(8,128)(2,1)} %copy.182), calls=%async_computation.3 | async-start | bytes 6291456 | tf_op jit(solution)/shard_map/all_to_all | solution.py:237
  550.0 59.1 %all-to-all-start.2 = ((bf16[8,256,768]{1,2,0:T(8,128)(2,1)}), bf16[8,256,768]{1,2,0:T(8,128)(2,1)}, u32[]{:S(2)}, u32[]{:S(2)}) async-start(bf16[8,256,768]{1,2,0:T(8,128)(2,1)} %copy.181), calls=%async_computation.2 | async-start | bytes 6291456 | tf_op jit(solution)/shard_map/all_to_all | solution.py:236
  554.5 317.4 %reduce-scatter.11.cloned.1.call-start = ((), (), s32[]{:S(2)}) async-start(), calls=%async_computation.18 | async-start | bytes 9437184 | tf_op jit(solution)/shard_map/reduce_scatter | solution.py:335
  625.3 40.3 %collective-permute-start = (bf16[96,6144]{1,0:T(8,128)(2,1)}, bf16[96,6144]{1,0:T(8,128)(2,1)}, u32[]{:S(2)}, u32[]{:S(2)}) collective-permute-start(bf16[96,6144]{1,0:T(8,128)(2,1)} %dynamic-slice_bitcast_fusion.1), channel_id=1, source_target_pairs={{0,1},{1,2},{2,3},{3,0},{4,5},{5,6},{6,7},{7,4},{8,9},{9,10},{10,1... | collective-permute-start | bytes 3538952 | tf_op jit(solution)/shard_map/ppermute | solution.py:91
  636.0 41.5 %collective-permute-start.1 = (bf16[96,6144]{1,0:T(8,128)(2,1)}, bf16[96,6144]{1,0:T(8,128)(2,1)}, u32[]{:S(2)}, u32[]{:S(2)}) collective-permute-start(bf16[96,6144]{1,0:T(8,128)(2,1)} %dynamic-slice_bitcast_fusion), channel_id=1, source_target_pairs={{0,3},{1,0},{2,1},{3,2},{4,7},{5,4},{6,5},{7,6},{8,11},{9,8},{10,9... | collective-permute-start | bytes 3538952 | tf_op jit(solution)/shard_map/ppermute | solution.py:92
  677.5 202.3 %reduce-scatter.9.cloned.1.call-start = ((), (), s32[]{:S(2)}) async-start(), calls=%async_computation.17 | async-start | bytes 14155776 | tf_op jit(solution)/shard_map/reduce_scatter | solution.py:210
  678.3 379.8 %reduce-scatter.17.cloned.1.call-start = ((), (), s32[]{:S(2)}) async-start(), calls=%async_computation.22 | async-start | bytes 4718592 | tf_op jit(solution)/shard_map/reduce_scatter | solution.py:335
  689.3 31.0 %collective-permute-start.2 = (bf16[96,6144]{1,0:T(8,128)(2,1)}, bf16[96,6144]{1,0:T(8,128)(2,1)}, u32[]{:S(2)}, u32[]{:S(2)}) collective-permute-start(bf16[96,6144]{1,0:T(8,128)(2,1)} %fusion.34), channel_id=1, source_target_pairs={{0,1},{1,2},{2,3},{3,0},{4,5},{5,6},{6,7},{7,4},{8,9},{9,10},{10,1... | collective-permute-start | bytes 3538952 | tf_op jit(solution)/shard_map/ppermute | solution.py:91
  693.1 51.6 %collective-permute-start.3 = (bf16[96,6144]{1,0:T(8,128)(2,1)}, bf16[96,6144]{1,0:T(8,128)(2,1)}, u32[]{:S(2)}, u32[]{:S(2)}) collective-permute-start(bf16[96,6144]{1,0:T(8,128)(2,1)} %fusion.33), channel_id=1, source_target_pairs={{0,3},{1,0},{2,1},{3,2},{4,7},{5,4},{6,5},{7,6},{8,11},{9,8},{10,9... | collective-permute-start | bytes 3538952 | tf_op jit(solution)/shard_map/ppermute | solution.py:92
  746.6 30.8 %collective-permute-start.4 = (bf16[96,6144]{1,0:T(8,128)(2,1)S(1)}, bf16[96,6144]{1,0:T(8,128)(2,1)}, u32[]{:S(2)}, u32[]{:S(2)}) collective-permute-start(bf16[96,6144]{1,0:T(8,128)(2,1)S(1)} %fusion.32), channel_id=1, source_target_pairs={{0,1},{1,2},{2,3},{3,0},{4,5},{5,6},{6,7},{7,4},{8,9},{9,10},{10,1... | collective-permute-start | bytes 3538952 | tf_op jit(solution)/shard_map/ppermute | solution.py:91
  749.3 52.4 %collective-permute-start.5 = (bf16[96,6144]{1,0:T(8,128)(2,1)S(1)}, bf16[96,6144]{1,0:T(8,128)(2,1)}, u32[]{:S(2)}, u32[]{:S(2)}) collective-permute-start(bf16[96,6144]{1,0:T(8,128)(2,1)S(1)} %fusion.31), channel_id=1, source_target_pairs={{0,3},{1,0},{2,1},{3,2},{4,7},{5,4},{6,5},{7,6},{8,11},{9,8},{10,9... | collective-permute-start | bytes 3538952 | tf_op jit(solution)/shard_map/ppermute | solution.py:92
  806.3 251.7 %reduce-scatter.15.cloned.1.call-start = ((), (), s32[]{:S(2)}) async-start(), calls=%async_computation.21 | async-start | bytes 4718592 | tf_op jit(solution)/shard_map/reduce_scatter | solution.py:335
  812.0 30.8 %collective-permute-start.6 = (bf16[96,6144]{1,0:T(8,128)(2,1)S(1)}, bf16[96,6144]{1,0:T(8,128)(2,1)}, u32[]{:S(2)}, u32[]{:S(2)}) collective-permute-start(bf16[96,6144]{1,0:T(8,128)(2,1)S(1)} %get-tuple-element.95), channel_id=1, source_target_pairs={{0,1},{1,2},{2,3},{3,0},{4,5},{5,6},{6,7},{7,4},{8,9},{9,10},{10,1... | collective-permute-start | bytes 3538952 | tf_op jit(solution)/shard_map/ppermute | solution.py:91
  818.4 48.8 %collective-permute-start.7 = (bf16[96,6144]{1,0:T(8,128)(2,1)S(1)}, bf16[96,6144]{1,0:T(8,128)(2,1)}, u32[]{:S(2)}, u32[]{:S(2)}) collective-permute-start(bf16[96,6144]{1,0:T(8,128)(2,1)S(1)} %get-tuple-element.97), channel_id=1, source_target_pairs={{0,3},{1,0},{2,1},{3,2},{4,7},{5,4},{6,5},{7,6},{8,11},{9,8},{10,9... | collective-permute-start | bytes 3538952 | tf_op jit(solution)/shard_map/ppermute | solution.py:92
  871.8 186.2 %all-reduce.4.cloned.1.call-start = ((), (), s32[]{:S(2)}) async-start(), calls=%async_computation.19 | async-start | bytes 2097152 | tf_op jit(solution)/shard_map/psum | solution.py:340
  872.4 238.9 %reduce-scatter.13.cloned.1.call-start = ((), (), s32[]{:S(2)}) async-start(), calls=%async_computation.20 | async-start | bytes 9437184 | tf_op jit(solution)/shard_map/reduce_scatter | solution.py:335
  879.7 320.3 %all-reduce.6.cloned.1.call-start = ((), (), s32[]{:S(2)}) async-start(), calls=%async_computation.23 | async-start | bytes 4194304 | tf_op jit(solution)/shard_map/psum | solution.py:350
  883.4 31.0 %collective-permute-start.8 = (bf16[96,6144]{1,0:T(8,128)(2,1)}, bf16[96,6144]{1,0:T(8,128)(2,1)}, u32[]{:S(2)}, u32[]{:S(2)}) collective-permute-start(bf16[96,6144]{1,0:T(8,128)(2,1)} %collective-permute-done.6), channel_id=1, source_target_pairs={{0,1},{1,2},{2,3},{3,0},{4,5},{5,6},{6,7},{7,4},{8,9},{9,10},{10,1... | collective-permute-start | bytes 3538952 | tf_op jit(solution)/shard_map/ppermute | solution.py:91
  883.9 53.4 %collective-permute-start.9 = (bf16[96,6144]{1,0:T(8,128)(2,1)}, bf16[96,6144]{1,0:T(8,128)(2,1)}, u32[]{:S(2)}, u32[]{:S(2)}) collective-permute-start(bf16[96,6144]{1,0:T(8,128)(2,1)} %collective-permute-done.7), channel_id=1, source_target_pairs={{0,3},{1,0},{2,1},{3,2},{4,7},{5,4},{6,5},{7,6},{8,11},{9,8},{10,9... | collective-permute-start | bytes 3538952 | tf_op jit(solution)/shard_map/ppermute | solution.py:92
  896.4 134.8 %copy-start.7 = (f32[384,2048]{1,0:T(8,128)S(1)}, f32[384,2048]{1,0:T(8,128)}, u32[]{:S(2)}) copy-start(f32[384,2048]{1,0:T(8,128)} %copy-done.5) | copy-start | bytes 9437188
  937.3 106.0 %collective-permute-start.10 = (bf16[96,6144]{1,0:T(8,128)(2,1)}, bf16[96,6144]{1,0:T(8,128)(2,1)}, u32[]{:S(2)}, u32[]{:S(2)}) collective-permute-start(bf16[96,6144]{1,0:T(8,128)(2,1)} %collective-permute-done.8), channel_id=1, source_target_pairs={{0,1},{1,2},{2,3},{3,0},{4,5},{5,6},{6,7},{7,4},{8,9},{9,10},{10,1... | collective-permute-start | bytes 3538952 | tf_op jit(solution)/shard_map/ppermute | solution.py:91
  937.6 105.8 %collective-permute-start.11 = (bf16[96,6144]{1,0:T(8,128)(2,1)}, bf16[96,6144]{1,0:T(8,128)(2,1)}, u32[]{:S(2)}, u32[]{:S(2)}) collective-permute-start(bf16[96,6144]{1,0:T(8,128)(2,1)} %collective-permute-done.9), channel_id=1, source_target_pairs={{0,3},{1,0},{2,1},{3,2},{4,7},{5,4},{6,5},{7,6},{8,11},{9,8},{10,9... | collective-permute-start | bytes 3538952 | tf_op jit(solution)/shard_map/ppermute | solution.py:92
  (77 other events, 1147.2 us)
Sparse Core Ops, SparseCore 0:
  9.9 64.1 all-gather.8
  76.0 59.0 all-gather.6
  137.0 53.5 all-gather.10
  192.4 54.2 all-gather.12
  258.1 71.9 all-gather.14
  332.4 71.9 all-gather.16
  463.2 138.3 reduce-scatter.6
  677.6 71.8 reduce-scatter.10
  753.0 92.2 reduce-scatter.8
  848.6 51.1 reduce-scatter.16
  903.7 51.3 reduce-scatter.14
  957.3 79.7 all-reduce.3
  1040.5 70.8 reduce-scatter.12
  1113.8 86.1 all-reduce.5

commit v9 on v7

--- a/solution.py
+++ b/solution.py
@@ -251,7 +251,7 @@
         .astype(jnp.bfloat16)
         .reshape(row_count, value_heads, group_size, head_width)
     )
-    grad_mixed_low, output_grad = ring.land((grad_mixed_low, output_grad))
+    grad_mixed_low = ring.land(grad_mixed_low)
     ring.issue()
     scores_again = masked_scores(query_low, key_low)
     probs_again = jnp.exp(scores_again - log_total)
@@ -279,9 +279,11 @@
         .astype(jnp.bfloat16)
         .reshape(row_count, value_heads * head_width)
     )
+    value_grad = inner_rows(normed_one_low, grad_value_low)
     grad_query_rot, grad_key_rot, grad_value_low = ring.land(
         (grad_query_rot, grad_key_rot, grad_value_low)
     )
+    ring.issue()
     grad_query_raw, query_gain_terms = rms_backward(
         unrotate(grad_query_rot, cosine, sine), query_normal, query_inverse, gain_query
     )
@@ -294,11 +296,13 @@
         row_count, query_heads * head_width
     )
     grad_key_low = grad_key_raw.astype(jnp.bfloat16).reshape(row_count, value_heads * head_width)
-    value_grad = inner_rows(normed_one_low, grad_value_low)
     query_grad = inner_rows(normed_one_low, grad_query_low)
     key_grad = inner_rows(normed_one_low, grad_key_low)
+    grad_query_low, grad_key_low = ring.land((grad_query_low, grad_key_low))
+    ring.issue()
     grad_normed_one = times_transposed(grad_query_low, attention_set[1])
-    grad_normed_one, down_value = lax.optimization_barrier((grad_normed_one, down_value))
+    grad_normed_one, down_value = ring.land((grad_normed_one, down_value))
+    ring.issue()
     layer_out = ((middle + down_value) * valid_rows).astype(jnp.bfloat16)
     grad_normed_one = (
         grad_normed_one
@@ -308,6 +312,7 @@
     grad_from_one, gain_one_terms = rms_backward(grad_normed_one, normal_one, inverse_one, gain_one)
     attention_gain_grad = jnp.sum(gain_one_terms, axis=0)
     input_grad = grad_middle + grad_from_one
+    input_grad = ring.land(input_grad)
     feed_sum = ring.result()
     feed_rep = (
         feed_sum[: feed_rows[0]],

time: 1200 us -> 1180 us (0.983)
  waiting for transfers between devices: 564 us -> 519 us
  blocking collectives: 95 us -> 120 us
    ppermute x6, waiting for transfers between devices: 109 us -> 51.6 us  [issue(): lax.ppermute(sends[0], self.axis, self.forward)]
    ppermute x6, waiting for transfers between devices: 72 us -> 116 us  [issue(): lax.ppermute(sends[1], self.axis, self.backward)]
    reduce_scatter x4, waiting for transfers between devices: 33.8 us -> 0.02 us  [low_sum(): lax.psum_scatter(v.astype(jnp.bfloat16), 'fsdp', scatter_dimension=0, til...]
    all_to_all x1, waiting for transfers between devices: 20.5 us -> 46.1 us  [per_device(): lax.all_to_all(up_grad_block.astype(jnp.bfloat16), 'fsdp', 0, 1, tiled=True)]
    psum x1, blocking collectives: 42.2 us -> 67.7 us  [per_device(): lax.psum(jnp.concatenate([attention_gain_grad, feed_gain_grad, query_gain...]
    all_to_all x1, waiting for transfers between devices: 44.4 us -> 20.6 us  [per_device(): lax.all_to_all(gate_grad_block.astype(jnp.bfloat16), 'fsdp', 0, 1, tiled=...]
where the time goes in v9:
time: 1180 us
  waiting for transfers between devices  519 us (44%)
  matrix products  247 us (21%)
  local copies, waits for them, and re-layouts  131 us (11%)
  blocking collectives  120 us (10%)
  other arithmetic  98.3 us (8%)
  starting transfers between devices  43 us (4%)
  between operations  17.1 us (1%)
    ppermute x6, waiting for transfers between devices, issue(): lax.ppermute(sends[1], self.axis, self.backward)  116 us
    psum x1, waiting for transfers between devices, per_device(): lax.psum(attention_parts[1].astype(jnp.bfloat16), 'rep').astype(jnp.float32)  88.1 us
    dot_general x7, matrix products, times_transposed(): lax.dot_general(left, right, (((1,), (1,)), ((), ())), preferred_element_...  74.9 us
    dot_general x7, matrix products, inner_rows(): lax.dot_general(left, right, (((0,), (0,)), ((), ())), preferred_element_...  70.6 us
    psum x1, blocking collectives, per_device(): lax.psum(jnp.concatenate([attention_gain_grad, feed_gain_grad, query_gain...  67.7 us
    all_gather x1, waiting for transfers between devices, per_device(): lax.all_gather(normed_two_low, 'fsdp', axis=0, tiled=True)  64.8 us
    all_gather x1, blocking collectives, per_device(): lax.all_gather(jnp.stack([attention_gain, feed_gain]), 'fsdp', axis=1, ti...  52.8 us
    ppermute x6, waiting for transfers between devices, issue(): lax.ppermute(sends[0], self.axis, self.forward)  51.6 us
  transfers between devices with their start and end apart: 29, of which 18 were waited for; matrix products, arithmetic and copies ran while one was open for 32% of the time, Pallas kernels for 0%

profile of v9, /device:TPU:0, one launch (start us, length us, event | category | flops | bytes accessed | tf_op | source)
XLA Modules:
  0.0 1175.9 jit_solution(6824651214492530015)
XLA Ops:
  24.5 50.0 %all-to-all-done = bf16[256,8,768]{0,2,1:T(8,128)(2,1)} async-done(((bf16[256,8,768]{0,2,1:T(8,128)(2,1)}), bf16[256,8,768]{0,2,1:T(8,128)(2,1)}, u32[]{:S(2)}, u32[]{:S(2)}) %all-to-all-start) | async-done | bytes 3145760 | tf_op jit(solution)/shard_map/all_to_all | solution.py:163
  80.2 52.8 %all_gather.21 = bf16[2,2048]{1,0:T(2,128)(2,1)S(1)} all-gather(bf16[2,256]{1,0:T(2,128)(2,1)S(1)} %pad_maximum_fusion.5), channel_id=1, replica_groups=mesh['fsdp'=8,'rep'=4] {'fsdp'}, dimensions={1}, use_global_device_ids=true | all-gather | bytes 9216 | tf_op jit(solution)/shard_map/all_gather | solution.py:155
  167.6 23.0 %all-gather.11.cloned.1.call-done = bf16[2048,2048]{1,0:T(8,128)(2,1)} async-done(((bf16[256,2048]{1,0:T(8,128)(2,1)}), bf16[2048,2048]{1,0:T(8,128)(2,1)}) %all-gather.11.cloned.1.call-update) | async-done | bytes 8388624 | tf_op jit(solution)/shard_map/all_gather | solution.py:158
  190.6 10.2 multiply_reduce_fusion.3
  217.7 29.0 %all-gather.13.cloned.1.call-done = bf16[2048,2048]{1,0:T(8,128)(2,1)} async-done(((bf16[256,2048]{1,0:T(8,128)(2,1)}), bf16[2048,2048]{1,0:T(8,128)(2,1)}) %all-gather.13.cloned.1.call-update) | async-done | bytes 8388624 | tf_op jit(solution)/shard_map/all_gather | solution.py:161
  265.4 64.8 %all-gather.15.cloned.1.call-done = bf16[3072,2048]{1,0:T(8,128)(2,1)} async-done(((bf16[384,2048]{1,0:T(8,128)(2,1)}), bf16[3072,2048]{1,0:T(8,128)(2,1)}) %all-gather.15.cloned.1.call-update) | async-done | bytes 12582928 | tf_op jit(solution)/shard_map/all_gather | solution.py:202
  330.1 16.3 %fusion.69 = f32[3072,768]{1,0:T(8,128)} fusion(bf16[3072,2048]{1,0:T(8,128)(2,1)} %all-gather.15.cloned.1.call-done, bf16[2048,768]{1,0:T(8,128)(2,1)} %bitcast.208), kind=kOutput, calls=%fused_computation.149 | convolution fusion | flops 9663676416 | bytes 25165824 | tf_op jit(solution)/shard_map/dot_general | solution.py:203
  346.5 17.6 %multiply_convert_fusion.2 = (bf16[3072,768]{1,0:T(8,128)(2,1)S(1)}, f32[3072,768]{1,0:T(8,128)}) fusion(f32[3072,768]{1,0:T(8,128)} %fusion.69, bf16[3072,2048]{1,0:T(8,128)(2,1)} %all-gather.15.cloned.1.call-done, bf16[2048,768]{1,0:T(8,128)(2,1)S(1)} %bitcast.210), kind=kOutput, calls=%fused_computation.13 | convolution fusion | flops 9677832192 | bytes 39321600 | tf_op jit(solution)/shard_map/dot_general | solution.py:204
  366.2 12.2 %fusion.70 = bf16[3072,2048]{1,0:T(8,128)(2,1)} fusion(bf16[3072,768]{1,0:T(8,128)(2,1)S(1)} %get-tuple-element.48, bf16[768,2048]{1,0:T(8,128)(2,1)S(1)} %copy-done), kind=kOutput, calls=%fused_computation.150 | convolution fusion | flops 9663676416 | bytes 20447232 | tf_op jit(solution)/shard_map/dot_general | solution.py:206
  378.5 26.0 %all-gather.17.cloned.1.call-done = bf16[3072,2048]{1,0:T(8,128)(2,1)} async-done(((bf16[384,2048]{1,0:T(8,128)(2,1)}), bf16[3072,2048]{1,0:T(8,128)(2,1)}) %all-gather.17.cloned.1.call-update) | async-done | bytes 12582928 | tf_op jit(solution)/shard_map/all_gather | solution.py:215
  404.5 22.2 %multiply_convert_fusion.1 = (bf16[3072,768]{1,0:T(8,128)(2,1)}, bf16[3072,768]{1,0:T(8,128)(2,1)}) fusion(f32[3072,768]{1,0:T(8,128)} %fusion.69, f32[3072,768]{1,0:T(8,128)} %get-tuple-element.46, bf16[3072,2048]{1,0:T(8,128)(2,1)} %all-gather.17.cloned.1.call-done, bf16[768,2048]{1,0:T(8,128)(2,1)S(1)} %copy-done), kind=kOutput, calls=%fused_computation.11 | convolution fusion | flops 9694347264 | bytes 44040192 | tf_op jit(solution)/shard_map/dot_general | solution.py:52
  426.7 17.8 %fusion.71 = f32[3072,2048]{1,0:T(8,128)} fusion(bf16[3072,768]{1,0:T(8,128)(2,1)} %get-tuple-element.95, bf16[2048,768]{1,0:T(8,128)(2,1)} %bitcast.209), kind=kOutput, calls=%fused_computation.151 | convolution fusion | flops 9663676416 | bytes 33030144 | tf_op jit(solution)/shard_map/dot_general | solution.py:52
  444.5 18.5 %add_convert_fusion = bf16[3072,2048]{1,0:T(8,128)(2,1)} fusion(f32[3072,2048]{1,0:T(8,128)} %fusion.71, bf16[3072,768]{1,0:T(8,128)(2,1)} %get-tuple-element.96, bf16[2048,768]{1,0:T(8,128)(2,1)S(1)} %bitcast.211), kind=kOutput, calls=%fused_computation.1 | convolution fusion | flops 9676259328 | bytes 45613056 | tf_op jit(solution)/shard_map/dot_general | solution.py:52
  463.8 15.0 %convolution_convert_fusion.4 = bf16[2048,768]{1,0:T(8,128)(2,1)S(1)} fusion(bf16[3072,2048]{1,0:T(8,128)(2,1)} %all-gather.15.cloned.1.call-done, bf16[3072,768]{1,0:T(8,128)(2,1)} %get-tuple-element.96), kind=kOutput, calls=%fused_computation.37 | convolution fusion | flops 9665249280 | bytes 20447232 | tf_op jit(solution)/shard_map/dot_general | solution.py:46
  485.5 15.7 %convolution_convert_fusion.5 = bf16[2048,768]{1,0:T(8,128)(2,1)} fusion(bf16[3072,2048]{1,0:T(8,128)(2,1)} %all-gather.15.cloned.1.call-done, bf16[3072,768]{1,0:T(8,128)(2,1)} %get-tuple-element.95), kind=kOutput, calls=%fused_computation.38 | convolution fusion | flops 9665249280 | bytes 20447232 | tf_op jit(solution)/shard_map/dot_general | solution.py:46
  505.8 46.1 %all-to-all-done.3 = bf16[8,256,768]{1,2,0:T(8,128)(2,1)S(1)} async-done(((bf16[8,256,768]{1,2,0:T(8,128)(2,1)}), bf16[8,256,768]{1,2,0:T(8,128)(2,1)S(1)}, u32[]{:S(2)}, u32[]{:S(2)}) %all-to-all-start.3) | async-done | bytes 3145760 | tf_op jit(solution)/shard_map/all_to_all | solution.py:237
  564.7 15.5 %convolution_convert_fusion.6 = bf16[768,2048]{1,0:T(8,128)(2,1)} fusion(bf16[3072,768]{1,0:T(8,128)(2,1)} %copy-done.81, bf16[3072,2048]{1,0:T(8,128)(2,1)} %all-gather.17.cloned.1.call-done), kind=kOutput, calls=%fused_computation.39 | convolution fusion | flops 9665249280 | bytes 20447232 | tf_op jit(solution)/shard_map/dot_general | solution.py:46
  590.5 20.6 %all-to-all-done.2 = bf16[8,256,768]{1,2,0:T(8,128)(2,1)} async-done(((bf16[8,256,768]{1,2,0:T(8,128)(2,1)}), bf16[8,256,768]{1,2,0:T(8,128)(2,1)}, u32[]{:S(2)}, u32[]{:S(2)}) %all-to-all-start.2) | async-done | bytes 3145760 | tf_op jit(solution)/shard_map/all_to_all | solution.py:236
  629.1 8.2 copy.185
  658.7 20.8 %collective-permute-done.1 = bf16[96,6144]{1,0:T(8,128)(2,1)} collective-permute-done((bf16[96,6144]{1,0:T(8,128)(2,1)}, bf16[96,6144]{1,0:T(8,128)(2,1)}, u32[]{:S(2)}, u32[]{:S(2)}) %collective-permute-start.1) | collective-permute-done | bytes 1179680 | tf_op jit(solution)/shard_map/ppermute | solution.py:92
  692.2 13.6 %fusion.2 = bf16[8,2,384,384]{2,3,1,0:T(8,128)(2,1)} fusion(f32[8,384,384,2]{2,1,3,0:T(8,128)} %copy-done.2, f32[8,2,384]{2,1,0:T(2,128)S(1)} %bitcast.236, pred[384,384]{0,1:T(8,128)(4,1)S(1)} %copy-done.35, bf16[384,8,2,128]{0,3,2,1:T(8,128)(2,1)S(1)} %copy.190, bf16[384,8,128,1]{2,1,0,3:T(8,128)(2,1)} %bitcast.218), kind=kOutput, calls=%fused_computation.7 | convolution fusion | flops 1226840448 | bytes 16687104 | tf_op jit(solution)/shard_map/sub | solution.py:263
  713.4 24.3 %collective-permute-done.3 = bf16[96,6144]{1,0:T(8,128)(2,1)} collective-permute-done((bf16[96,6144]{1,0:T(8,128)(2,1)}, bf16[96,6144]{1,0:T(8,128)(2,1)}, u32[]{:S(2)}, u32[]{:S(2)}) %collective-permute-start.3) | collective-permute-done | bytes 1179680 | tf_op jit(solution)/shard_map/ppermute | solution.py:92
  759.3 20.3 %collective-permute-done.4 = bf16[96,6144]{1,0:T(8,128)(2,1)S(1)} collective-permute-done((bf16[96,6144]{1,0:T(8,128)(2,1)S(1)}, bf16[96,6144]{1,0:T(8,128)(2,1)S(1)}, u32[]{:S(2)}, u32[]{:S(2)}) %collective-permute-start.4) | collective-permute-done | bytes 1179680 | tf_op jit(solution)/shard_map/ppermute | solution.py:91
  779.6 24.3 %collective-permute-done.5 = bf16[96,6144]{1,0:T(8,128)(2,1)S(1)} collective-permute-done((bf16[96,6144]{1,0:T(8,128)(2,1)S(1)}, bf16[96,6144]{1,0:T(8,128)(2,1)S(1)}, u32[]{:S(2)}, u32[]{:S(2)}) %collective-permute-start.5) | collective-permute-done | bytes 1179680 | tf_op jit(solution)/shard_map/ppermute | solution.py:92
  859.8 24.3 %collective-permute-done.7 = bf16[96,6144]{1,0:T(8,128)(2,1)} collective-permute-done((bf16[96,6144]{1,0:T(8,128)(2,1)}, bf16[96,6144]{1,0:T(8,128)(2,1)}, u32[]{:S(2)}, u32[]{:S(2)}) %collective-permute-start.7) | collective-permute-done | bytes 1179680 | tf_op jit(solution)/shard_map/ppermute | solution.py:92
  898.1 17.0 %collective-permute-done.8 = bf16[96,6144]{1,0:T(8,128)(2,1)} collective-permute-done((bf16[96,6144]{1,0:T(8,128)(2,1)}, bf16[96,6144]{1,0:T(8,128)(2,1)}, u32[]{:S(2)}, u32[]{:S(2)}) %collective-permute-start.8) | collective-permute-done | bytes 1179680 | tf_op jit(solution)/shard_map/ppermute | solution.py:91
  915.1 22.7 %collective-permute-done.9 = bf16[96,6144]{1,0:T(8,128)(2,1)} collective-permute-done((bf16[96,6144]{1,0:T(8,128)(2,1)}, bf16[96,6144]{1,0:T(8,128)(2,1)}, u32[]{:S(2)}, u32[]{:S(2)}) %collective-permute-start.9) | collective-permute-done | bytes 1179680 | tf_op jit(solution)/shard_map/ppermute | solution.py:92
  946.1 67.7 %psum.35 = f32[4352]{0:T(1024)S(1)} all-reduce(f32[4352]{0:T(1024)S(1)} %pad_maximum_fusion.4), channel_id=1, replica_groups=mesh['fsdp'=8,'rep'=4] {'fsdp','rep'}, use_global_device_ids=true, to_apply=%region_17.18 | all-reduce | flops 4352 | bytes 34816 | tf_op jit(solution)/shard_map/psum | solution.py:324
  1031.8 8.2 pad_maximum_fusion
  1040.1 12.9 %bitcast_convert_fusion = f32[768,6144]{1,0:T(8,128)} fusion(bf16[2,4,96,6144]{3,2,1,0:T(8,128)(2,1)} %pad_maximum_fusion), kind=kLoop, calls=%fused_computation.3 | loop fusion | flops 4718592 | bytes 28311552 | tf_op jit(solution)/shard_map/convert_element_type | solution.py:121
  1052.9 13.9 %fusion.66 = (f32[256,6144]{1,0:T(8,128)}, f32[256,6144]{1,0:T(8,128)}, f32[256,6144]{1,0:T(8,128)}) fusion(f32[768,6144]{1,0:T(8,128)} %bitcast_convert_fusion), kind=kLoop, calls=%fused_computation.146 | loop fusion | bytes 37748736 | tf_op jit(solution)/shard_map/slice | solution.py:320
  1074.3 88.1 %all-reduce.3.cloned.1.call-done = (bf16[256,2048]{1,0:T(8,128)(2,1)}, bf16[256,1024]{1,0:T(8,128)(2,1)}, bf16[256,1024]{1,0:T(8,128)(2,1)}, bf16[256,2048]{1,0:T(8,128)(2,1)}) async-done(((bf16[256,2048]{1,0:T(8,128)(2,1)}, bf16[256,1024]{1,0:T(8,128)(2,1)}, bf16[256,1024]{1,0:T(8,128)(2,1)}, bf16[256,2048]{1,0:T(8,128)(2,1)}), (bf16[256,2048]{1,0:T(8,128)(2,1)}, bf16[256,1024]{1,0:T(8,128)(2,1)}, ...) | async-done | bytes 3145744 | tf_op jit(solution)/shard_map/psum | solution.py:346
  (329 shorter events, 319.2 us)
Async XLA Ops:
  7.2 359.0 %copy-start = (bf16[768,2048]{1,0:T(8,128)(2,1)S(1)}, bf16[768,2048]{1,0:T(8,128)(2,1)}, u32[]{:S(2)}) copy-start(bf16[768,2048]{1,0:T(8,128)(2,1)} %param.28) | copy-start | bytes 9437188
  7.2 139.6 %all-gather.9.cloned.1.call-start = ((), (), s32[]{:S(2)}) async-start(), calls=%async_computation.11 | async-start | bytes 4718592 | tf_op jit(solution)/shard_map/all_gather | solution.py:159
  7.9 152.1 %all-gather.7.cloned.1.call-start = ((), (), s32[]{:S(2)}) async-start(), calls=%async_computation.10 | async-start | bytes 4718592 | tf_op jit(solution)/shard_map/all_gather | solution.py:160
  8.7 182.0 %all-gather.11.cloned.1.call-start = ((), (), s32[]{:S(2)}) async-start(), calls=%async_computation.12 | async-start | bytes 9437184 | tf_op jit(solution)/shard_map/all_gather | solution.py:158
  9.4 237.3 %all-gather.13.cloned.1.call-start = ((), (), s32[]{:S(2)}) async-start(), calls=%async_computation.13 | async-start | bytes 9437184 | tf_op jit(solution)/shard_map/all_gather | solution.py:161
  14.6 59.8 %all-to-all-start = ((bf16[256,8,768]{0,2,1:T(8,128)(2,1)}), bf16[256,8,768]{0,2,1:T(8,128)(2,1)}, u32[]{:S(2)}, u32[]{:S(2)}) async-start(bf16[256,8,768]{0,2,1:T(8,128)(2,1)} %bitcast.203), calls=%async_computation | async-start | bytes 6291456 | tf_op jit(solution)/shard_map/all_to_all | solution.py:163
  74.5 64.9 %all-to-all-start.1 = ((bf16[256,8,768]{0,2,1:T(8,128)(2,1)}), bf16[256,8,768]{0,2,1:T(8,128)(2,1)}, u32[]{:S(2)}, u32[]{:S(2)}) async-start(bf16[256,8,768]{0,2,1:T(8,128)(2,1)} %bitcast.202), calls=%async_computation.1 | async-start | bytes 6291456 | tf_op jit(solution)/shard_map/all_to_all | solution.py:164
  79.1 251.1 %all-gather.15.cloned.1.call-start = ((), (), s32[]{:S(2)}) async-start(), calls=%async_computation.14 | async-start | bytes 14155776 | tf_op jit(solution)/shard_map/all_gather | solution.py:202
  134.5 120.3 %copy-start.57 = (f32[1,2048]{1,0:T(1,128)}, f32[1,2048]{1,0:T(1,128)S(1)}, u32[]{:S(2)}) copy-start(f32[1,2048]{1,0:T(1,128)S(1)} %get-tuple-element.113) | copy-start | bytes 24580
  258.0 146.5 %all-gather.17.cloned.1.call-start = ((), (), s32[]{:S(2)}) async-start(), calls=%async_computation.15 | async-start | bytes 14155776 | tf_op jit(solution)/shard_map/all_gather | solution.py:215
  265.3 376.9 %reduce-scatter.7.cloned.1.call-start = ((), (), s32[]{:S(2)}) async-start(), calls=%async_computation.16 | async-start | bytes 14155776 | tf_op jit(solution)/shard_map/reduce_scatter | solution.py:226
  463.1 389.0 %reduce-scatter.9.cloned.1.call-start = ((), (), s32[]{:S(2)}) async-start(), calls=%async_computation.17 | async-start | bytes 14155776 | tf_op jit(solution)/shard_map/reduce_scatter | solution.py:210
  481.6 70.3 %all-to-all-start.3 = ((bf16[8,256,768]{1,2,0:T(8,128)(2,1)}), bf16[8,256,768]{1,2,0:T(8,128)(2,1)S(1)}, u32[]{:S(2)}, u32[]{:S(2)}) async-start(bf16[8,256,768]{1,2,0:T(8,128)(2,1)} %copy.182), calls=%async_computation.3 | async-start | bytes 6291456 | tf_op jit(solution)/shard_map/all_to_all | solution.py:237
  551.9 59.2 %all-to-all-start.2 = ((bf16[8,256,768]{1,2,0:T(8,128)(2,1)}), bf16[8,256,768]{1,2,0:T(8,128)(2,1)}, u32[]{:S(2)}, u32[]{:S(2)}) async-start(bf16[8,256,768]{1,2,0:T(8,128)(2,1)} %copy.181), calls=%async_computation.2 | async-start | bytes 6291456 | tf_op jit(solution)/shard_map/all_to_all | solution.py:236
  556.4 483.6 %reduce-scatter.15.cloned.1.call-start = ((), (), s32[]{:S(2)}) async-start(), calls=%async_computation.20 | async-start | bytes 4718592 | tf_op jit(solution)/shard_map/reduce_scatter | solution.py:335
  627.7 31.0 %collective-permute-start = (bf16[96,6144]{1,0:T(8,128)(2,1)}, bf16[96,6144]{1,0:T(8,128)(2,1)}, u32[]{:S(2)}, u32[]{:S(2)}) collective-permute-start(bf16[96,6144]{1,0:T(8,128)(2,1)} %dynamic-slice_bitcast_fusion.1), channel_id=1, source_target_pairs={{0,1},{1,2},{2,3},{3,0},{4,5},{5,6},{6,7},{7,4},{8,9},{9,10},{10,1... | collective-permute-start | bytes 3538952 | tf_op jit(solution)/shard_map/ppermute | solution.py:91
  639.6 39.9 %collective-permute-start.1 = (bf16[96,6144]{1,0:T(8,128)(2,1)}, bf16[96,6144]{1,0:T(8,128)(2,1)}, u32[]{:S(2)}, u32[]{:S(2)}) collective-permute-start(bf16[96,6144]{1,0:T(8,128)(2,1)} %dynamic-slice_bitcast_fusion), channel_id=1, source_target_pairs={{0,3},{1,0},{2,1},{3,2},{4,7},{5,4},{6,5},{7,6},{8,11},{9,8},{10,9... | collective-permute-start | bytes 3538952 | tf_op jit(solution)/shard_map/ppermute | solution.py:92
  682.4 31.0 %collective-permute-start.2 = (bf16[96,6144]{1,0:T(8,128)(2,1)}, bf16[96,6144]{1,0:T(8,128)(2,1)}, u32[]{:S(2)}, u32[]{:S(2)}) collective-permute-start(bf16[96,6144]{1,0:T(8,128)(2,1)} %fusion.34), channel_id=1, source_target_pairs={{0,1},{1,2},{2,3},{3,0},{4,5},{5,6},{6,7},{7,4},{8,9},{9,10},{10,1... | collective-permute-start | bytes 3538952 | tf_op jit(solution)/shard_map/ppermute | solution.py:91
  686.0 51.8 %collective-permute-start.3 = (bf16[96,6144]{1,0:T(8,128)(2,1)}, bf16[96,6144]{1,0:T(8,128)(2,1)}, u32[]{:S(2)}, u32[]{:S(2)}) collective-permute-start(bf16[96,6144]{1,0:T(8,128)(2,1)} %fusion.33), channel_id=1, source_target_pairs={{0,3},{1,0},{2,1},{3,2},{4,7},{5,4},{6,5},{7,6},{8,11},{9,8},{10,9... | collective-permute-start | bytes 3538952 | tf_op jit(solution)/shard_map/ppermute | solution.py:92
  746.7 293.3 %reduce-scatter.13.cloned.1.call-start = ((), (), s32[]{:S(2)}) async-start(), calls=%async_computation.19 | async-start | bytes 4718592 | tf_op jit(solution)/shard_map/reduce_scatter | solution.py:335
  748.9 30.7 %collective-permute-start.4 = (bf16[96,6144]{1,0:T(8,128)(2,1)S(1)}, bf16[96,6144]{1,0:T(8,128)(2,1)S(1)}, u32[]{:S(2)}, u32[]{:S(2)}) collective-permute-start(bf16[96,6144]{1,0:T(8,128)(2,1)S(1)} %fusion.32), channel_id=1, source_target_pairs={{0,1},{1,2},{2,3},{3,0},{4,5},{5,6},{6,7},{7,4},{8,9},{9,10},{10,1... | collective-permute-start | bytes 3538952 | tf_op jit(solution)/shard_map/ppermute | solution.py:91
  751.4 52.5 %collective-permute-start.5 = (bf16[96,6144]{1,0:T(8,128)(2,1)S(1)}, bf16[96,6144]{1,0:T(8,128)(2,1)S(1)}, u32[]{:S(2)}, u32[]{:S(2)}) collective-permute-start(bf16[96,6144]{1,0:T(8,128)(2,1)S(1)} %fusion.31), channel_id=1, source_target_pairs={{0,3},{1,0},{2,1},{3,2},{4,7},{5,4},{6,5},{7,6},{8,11},{9,8},{10,9... | collective-permute-start | bytes 3538952 | tf_op jit(solution)/shard_map/ppermute | solution.py:92
  812.8 227.2 %reduce-scatter.17.cloned.1.call-start = ((), (), s32[]{:S(2)}) async-start(), calls=%async_computation.21 | async-start | bytes 9437184 | tf_op jit(solution)/shard_map/reduce_scatter | solution.py:335
  822.9 217.1 %reduce-scatter.11.cloned.1.call-start = ((), (), s32[]{:S(2)}) async-start(), calls=%async_computation.18 | async-start | bytes 9437184 | tf_op jit(solution)/shard_map/reduce_scatter | solution.py:335
  828.8 31.0 %collective-permute-start.6 = (bf16[96,6144]{1,0:T(8,128)(2,1)}, bf16[96,6144]{1,0:T(8,128)(2,1)}, u32[]{:S(2)}, u32[]{:S(2)}) collective-permute-start(bf16[96,6144]{1,0:T(8,128)(2,1)} %get-tuple-element.86), channel_id=1, source_target_pairs={{0,1},{1,2},{2,3},{3,0},{4,5},{5,6},{6,7},{7,4},{8,9},{9,10},{10,1... | collective-permute-start | bytes 3538952 | tf_op jit(solution)/shard_map/ppermute | solution.py:91
  835.5 48.7 %collective-permute-start.7 = (bf16[96,6144]{1,0:T(8,128)(2,1)}, bf16[96,6144]{1,0:T(8,128)(2,1)}, u32[]{:S(2)}, u32[]{:S(2)}) collective-permute-start(bf16[96,6144]{1,0:T(8,128)(2,1)} %get-tuple-element.88), channel_id=1, source_target_pairs={{0,3},{1,0},{2,1},{3,2},{4,7},{5,4},{6,5},{7,6},{8,11},{9,8},{10,9... | collective-permute-start | bytes 3538952 | tf_op jit(solution)/shard_map/ppermute | solution.py:92
  852.0 310.5 %all-reduce.3.cloned.1.call-start = ((), (), s32[]{:S(2)}) async-start(), calls=%async_computation.22 | async-start | bytes 6291456 | tf_op jit(solution)/shard_map/psum | solution.py:346
  884.1 31.0 %collective-permute-start.8 = (bf16[96,6144]{1,0:T(8,128)(2,1)}, bf16[96,6144]{1,0:T(8,128)(2,1)}, u32[]{:S(2)}, u32[]{:S(2)}) collective-permute-start(bf16[96,6144]{1,0:T(8,128)(2,1)} %collective-permute-done.6), channel_id=1, source_target_pairs={{0,1},{1,2},{2,3},{3,0},{4,5},{5,6},{6,7},{7,4},{8,9},{9,10},{10,1... | collective-permute-start | bytes 3538952 | tf_op jit(solution)/shard_map/ppermute | solution.py:91
  884.7 53.2 %collective-permute-start.9 = (bf16[96,6144]{1,0:T(8,128)(2,1)}, bf16[96,6144]{1,0:T(8,128)(2,1)}, u32[]{:S(2)}, u32[]{:S(2)}) collective-permute-start(bf16[96,6144]{1,0:T(8,128)(2,1)} %collective-permute-done.7), channel_id=1, source_target_pairs={{0,3},{1,0},{2,1},{3,2},{4,7},{5,4},{6,5},{7,6},{8,11},{9,8},{10,9... | collective-permute-start | bytes 3538952 | tf_op jit(solution)/shard_map/ppermute | solution.py:92
  898.1 116.8 %copy-start.7 = (f32[384,2048]{1,0:T(8,128)S(1)}, f32[384,2048]{1,0:T(8,128)}, u32[]{:S(2)}) copy-start(f32[384,2048]{1,0:T(8,128)} %copy-done.5) | copy-start | bytes 9437188
  937.9 89.2 %collective-permute-start.10 = (bf16[96,6144]{1,0:T(8,128)(2,1)}, bf16[96,6144]{1,0:T(8,128)(2,1)}, u32[]{:S(2)}, u32[]{:S(2)}) collective-permute-start(bf16[96,6144]{1,0:T(8,128)(2,1)} %collective-permute-done.8), channel_id=1, source_target_pairs={{0,1},{1,2},{2,3},{3,0},{4,5},{5,6},{6,7},{7,4},{8,9},{9,10},{10,1... | collective-permute-start | bytes 3538952 | tf_op jit(solution)/shard_map/ppermute | solution.py:91
  938.2 88.9 %collective-permute-start.11 = (bf16[96,6144]{1,0:T(8,128)(2,1)}, bf16[96,6144]{1,0:T(8,128)(2,1)}, u32[]{:S(2)}, u32[]{:S(2)}) collective-permute-start(bf16[96,6144]{1,0:T(8,128)(2,1)} %collective-permute-done.9), channel_id=1, source_target_pairs={{0,3},{1,0},{2,1},{3,2},{4,7},{5,4},{6,5},{7,6},{8,11},{9,8},{10,9... | collective-permute-start | bytes 3538952 | tf_op jit(solution)/shard_map/ppermute | solution.py:92
  (81 other events, 1045.9 us)
Sparse Core Ops, SparseCore 0:
  9.9 64.1 all-gather.8
  76.0 59.1 all-gather.6
  137.0 53.5 all-gather.10
  192.4 54.2 all-gather.12
  258.1 71.9 all-gather.14
  332.5 71.9 all-gather.16
  463.2 140.1 reduce-scatter.6
  606.9 100.7 reduce-scatter.8
  746.8 50.8 reduce-scatter.14
  813.0 50.8 reduce-scatter.12
  867.4 71.4 reduce-scatter.16
  942.2 72.0 reduce-scatter.10
  1040.2 122.2 all-reduce.2

commit v10 on v9

--- a/solution.py
+++ b/solution.py
@@ -320,16 +320,22 @@
         feed_sum[feed_rows[0] + feed_rows[1] :].reshape(feed_parts[3].shape),
     )
     model_width = attention_gain_grad.shape[0]
-    gain_share = model_width // lax.axis_size("fsdp")
-    gain_sums = lax.psum(
-        jnp.concatenate([attention_gain_grad, feed_gain_grad, query_gain_grad, key_gain_grad]),
-        ("fsdp", "rep"),
-    )
-    gain_start = lax.axis_index("fsdp") * gain_share
-    attention_gain_out = lax.dynamic_slice_in_dim(gain_sums, gain_start, gain_share)
-    feed_gain_out = lax.dynamic_slice_in_dim(gain_sums, model_width + gain_start, gain_share)
-    query_gain_out = gain_sums[2 * model_width : 2 * model_width + head_width]
-    key_gain_out = gain_sums[2 * model_width + head_width :]
+    fsdp_count = lax.axis_size("fsdp")
+    gain_share = model_width // fsdp_count
+    head_terms = jnp.concatenate([query_gain_grad, key_gain_grad])
+    head_cols = -(-head_terms.shape[0] // gain_share)
+    head_block = jnp.pad(head_terms, (0, head_cols * gain_share - head_terms.shape[0]))
+    head_block = head_block.reshape(head_cols, gain_share).T
+    gain_cols = jnp.concatenate(
+        [
+            attention_gain_grad[:, None],
+            feed_gain_grad[:, None],
+            jnp.tile(head_block, (fsdp_count, 1)),
+        ],
+        axis=1,
+    )
+    key_width = key_grad.shape[1]
+    key_grad = jnp.concatenate([key_grad, gain_cols], axis=1)
 
     def low_sum(v):
         return lax.psum_scatter(v.astype(jnp.bfloat16), "fsdp", scatter_dimension=0, tiled=True)
@@ -338,27 +344,34 @@
         None, low_sum(query_grad), low_sum(key_grad), low_sum(value_grad), low_sum(output_grad)
     )
     finals = (
-        feed_gain_out,
+        None,
         feed_rep[0],
         feed_rep[1],
         feed_rep[2],
-        attention_gain_out,
+        None,
         lax.psum(attention_parts[1].astype(jnp.bfloat16), "rep").astype(jnp.float32),
         lax.psum(attention_parts[2].astype(jnp.bfloat16), "rep").astype(jnp.float32),
         lax.psum(attention_parts[3].astype(jnp.bfloat16), "rep").astype(jnp.float32),
         lax.psum(attention_parts[4].astype(jnp.bfloat16), "rep").astype(jnp.float32),
     )
+    key_rep = finals[6]
+    gain_rep = key_rep[:, key_width:]
+    attention_gain_out = gain_rep[:, 0]
+    feed_gain_out = gain_rep[:, 1]
+    head_sum = gain_rep[:, 2:].T.reshape(-1)
+    query_gain_out = head_sum[:head_width]
+    key_gain_out = head_sum[head_width : 2 * head_width]
     return (
         layer_out,
         input_grad,
-        finals[4],
+        attention_gain_out,
         finals[5],
-        finals[6],
+        key_rep[:, :key_width],
         finals[7],
         query_gain_out,
         key_gain_out,
         finals[8],
-        finals[0],
+        feed_gain_out,
         finals[1],
         finals[2],
         finals[3],

time: 1180 us -> 1290 us (1.093)
  waiting for transfers between devices: 519 us -> 665 us
  blocking collectives: 120 us -> 52.8 us
  local copies, waits for them, and re-layouts: 131 us -> 151 us
    reduce_scatter x4, waiting for transfers between devices: 0.02 us -> 114 us  [low_sum(): lax.psum_scatter(v.astype(jnp.bfloat16), 'fsdp', scatter_dimension=0, til...]
    psum x1 -> x0, blocking collectives: 67.7 us -> none  [per_device(): lax.psum(jnp.concatenate([attention_gain_grad, feed_gain_grad, query_gain...]
    concatenate x0 -> x1, local copies, waits for them, and re-layouts: none -> 18.5 us  [per_device(): key_grad = jnp.concatenate([key_grad, gain_cols], axis=1)]
    reduce_scatter x1, waiting for transfers between devices: 0.02 us -> 16.9 us  [per_device(): lax.psum_scatter(down_part.astype(jnp.bfloat16), 'fsdp', scatter_dimensio...]
    unnamed x172 -> x159, local copies, waits for them, and re-layouts: 33 us -> 35.6 us
  transfers between devices with their start and end apart: 29 -> 29, of which waited for: 18 -> 22; matrix products, arithmetic and copies ran while one was open for 32% -> 31% of each run, Pallas kernels for 0% -> 0%
where the time goes in v10:
time: 1290 us; the launch traced here: 1280 us
  waiting for transfers between devices  665 us (52%)
  matrix products  251 us (19%)
  local copies, waits for them, and re-layouts  151 us (12%)
  other arithmetic  102 us (8%)
  blocking collectives  52.8 us (4%)
  starting transfers between devices  42.5 us (3%)
  between operations  17.1 us (1%)
    ppermute x6, waiting for transfers between devices, issue(): lax.ppermute(sends[1], self.axis, self.backward)  128 us
    reduce_scatter x4, waiting for transfers between devices, low_sum(): lax.psum_scatter(v.astype(jnp.bfloat16), 'fsdp', scatter_dimension=0, til...  114 us
    psum x1, waiting for transfers between devices, per_device(): lax.psum(attention_parts[2].astype(jnp.bfloat16), 'rep').astype(jnp.float32)  89.6 us
    dot_general x7, matrix products, times_transposed(): lax.dot_general(left, right, (((1,), (1,)), ((), ())), preferred_element_...  77.5 us
    dot_general x7, matrix products, inner_rows(): lax.dot_general(left, right, (((0,), (0,)), ((), ())), preferred_element_...  70.6 us
    all_gather x1, waiting for transfers between devices, per_device(): lax.all_gather(normed_two_low, 'fsdp', axis=0, tiled=True)  64.8 us
    ppermute x6, waiting for transfers between devices, issue(): lax.ppermute(sends[0], self.axis, self.forward)  53.1 us
    all_gather x1, blocking collectives, per_device(): lax.all_gather(jnp.stack([attention_gain, feed_gain]), 'fsdp', axis=1, ti...  52.8 us
  transfers between devices with their start and end apart: 29, of which 22 were waited for; matrix products, arithmetic and copies ran while one was open for 31% of the time, Pallas kernels for 0%

profile of v10, /device:TPU:0, one launch (start us, length us, event | category | flops | bytes accessed | tf_op | source)
XLA Modules:
  0.0 1281.4 jit_solution(9078823386213040214)
XLA Ops:
  24.5 50.0 %all-to-all-done = bf16[256,8,768]{0,2,1:T(8,128)(2,1)} async-done(((bf16[256,8,768]{0,2,1:T(8,128)(2,1)}), bf16[256,8,768]{0,2,1:T(8,128)(2,1)}, u32[]{:S(2)}, u32[]{:S(2)}) %all-to-all-start) | async-done | bytes 3145760 | tf_op jit(solution)/shard_map/all_to_all | solution.py:163
  80.2 52.8 %all_gather.21 = bf16[2,2048]{1,0:T(2,128)(2,1)S(1)} all-gather(bf16[2,256]{1,0:T(2,128)(2,1)S(1)} %pad_maximum_fusion.4), channel_id=1, replica_groups=mesh['fsdp'=8,'rep'=4] {'fsdp'}, dimensions={1}, use_global_device_ids=true | all-gather | bytes 9216 | tf_op jit(solution)/shard_map/all_gather | solution.py:155
  167.6 23.0 %all-gather.11.cloned.1.call-done = bf16[2048,2048]{1,0:T(8,128)(2,1)} async-done(((bf16[256,2048]{1,0:T(8,128)(2,1)}), bf16[2048,2048]{1,0:T(8,128)(2,1)}) %all-gather.11.cloned.1.call-update) | async-done | bytes 8388624 | tf_op jit(solution)/shard_map/all_gather | solution.py:158
  217.7 28.9 %all-gather.13.cloned.1.call-done = bf16[2048,2048]{1,0:T(8,128)(2,1)} async-done(((bf16[256,2048]{1,0:T(8,128)(2,1)}), bf16[2048,2048]{1,0:T(8,128)(2,1)}) %all-gather.13.cloned.1.call-update) | async-done | bytes 8388624 | tf_op jit(solution)/shard_map/all_gather | solution.py:161
  265.3 64.8 %all-gather.15.cloned.1.call-done = bf16[3072,2048]{1,0:T(8,128)(2,1)} async-done(((bf16[384,2048]{1,0:T(8,128)(2,1)}), bf16[3072,2048]{1,0:T(8,128)(2,1)}) %all-gather.15.cloned.1.call-update) | async-done | bytes 12582928 | tf_op jit(solution)/shard_map/all_gather | solution.py:202
  330.1 16.3 %fusion.68 = f32[3072,768]{1,0:T(8,128)} fusion(bf16[3072,2048]{1,0:T(8,128)(2,1)} %all-gather.15.cloned.1.call-done, bf16[2048,768]{1,0:T(8,128)(2,1)} %bitcast.219), kind=kOutput, calls=%fused_computation.151 | convolution fusion | flops 9663676416 | bytes 25165824 | tf_op jit(solution)/shard_map/dot_general | solution.py:203
  346.4 17.6 %multiply_convert_fusion.2 = (bf16[3072,768]{1,0:T(8,128)(2,1)S(1)}, f32[3072,768]{1,0:T(8,128)}) fusion(f32[3072,768]{1,0:T(8,128)} %fusion.68, bf16[3072,2048]{1,0:T(8,128)(2,1)} %all-gather.15.cloned.1.call-done, bf16[2048,768]{1,0:T(8,128)(2,1)S(1)} %bitcast.221), kind=kOutput, calls=%fused_computation.13 | convolution fusion | flops 9677832192 | bytes 39321600 | tf_op jit(solution)/shard_map/dot_general | solution.py:204
  378.4 26.0 %all-gather.17.cloned.1.call-done = bf16[3072,2048]{1,0:T(8,128)(2,1)} async-done(((bf16[384,2048]{1,0:T(8,128)(2,1)}), bf16[3072,2048]{1,0:T(8,128)(2,1)}) %all-gather.17.cloned.1.call-update) | async-done | bytes 12582928 | tf_op jit(solution)/shard_map/all_gather | solution.py:215
  404.4 22.2 %multiply_convert_fusion.1 = (bf16[3072,768]{1,0:T(8,128)(2,1)}, bf16[3072,768]{1,0:T(8,128)(2,1)}) fusion(f32[3072,768]{1,0:T(8,128)} %fusion.68, f32[3072,768]{1,0:T(8,128)} %get-tuple-element.46, bf16[3072,2048]{1,0:T(8,128)(2,1)} %all-gather.17.cloned.1.call-done, bf16[768,2048]{1,0:T(8,128)(2,1)S(1)} %copy-done), kind=kOutput, calls=%fused_computation.11 | convolution fusion | flops 9694347264 | bytes 44040192 | tf_op jit(solution)/shard_map/dot_general | solution.py:52
  426.7 17.7 %fusion.70 = f32[3072,2048]{1,0:T(8,128)} fusion(bf16[3072,768]{1,0:T(8,128)(2,1)} %get-tuple-element.173, bf16[2048,768]{1,0:T(8,128)(2,1)} %bitcast.220), kind=kOutput, calls=%fused_computation.153 | convolution fusion | flops 9663676416 | bytes 33030144 | tf_op jit(solution)/shard_map/dot_general | solution.py:52
  444.3 18.5 %add_convert_fusion = bf16[3072,2048]{1,0:T(8,128)(2,1)} fusion(f32[3072,2048]{1,0:T(8,128)} %fusion.70, bf16[3072,768]{1,0:T(8,128)(2,1)} %get-tuple-element.174, bf16[2048,768]{1,0:T(8,128)(2,1)S(1)} %bitcast.222), kind=kOutput, calls=%fused_computation.1 | convolution fusion | flops 9676259328 | bytes 45613056 | tf_op jit(solution)/shard_map/dot_general | solution.py:52
  463.6 15.0 %convolution_convert_fusion.4 = bf16[2048,768]{1,0:T(8,128)(2,1)S(1)} fusion(bf16[3072,2048]{1,0:T(8,128)(2,1)} %all-gather.15.cloned.1.call-done, bf16[3072,768]{1,0:T(8,128)(2,1)} %get-tuple-element.174), kind=kOutput, calls=%fused_computation.37 | convolution fusion | flops 9665249280 | bytes 20447232 | tf_op jit(solution)/shard_map/dot_general | solution.py:46
  485.4 15.7 %convolution_convert_fusion.5 = bf16[2048,768]{1,0:T(8,128)(2,1)} fusion(bf16[3072,2048]{1,0:T(8,128)(2,1)} %all-gather.15.cloned.1.call-done, bf16[3072,768]{1,0:T(8,128)(2,1)} %get-tuple-element.173), kind=kOutput, calls=%fused_computation.38 | convolution fusion | flops 9665249280 | bytes 20447232 | tf_op jit(solution)/shard_map/dot_general | solution.py:46
  505.7 46.0 %all-to-all-done.3 = bf16[8,256,768]{1,2,0:T(8,128)(2,1)S(1)} async-done(((bf16[8,256,768]{1,2,0:T(8,128)(2,1)}), bf16[8,256,768]{1,2,0:T(8,128)(2,1)S(1)}, u32[]{:S(2)}, u32[]{:S(2)}) %all-to-all-start.3) | async-done | bytes 3145760 | tf_op jit(solution)/shard_map/all_to_all | solution.py:237
  564.4 15.5 %convolution_convert_fusion.6 = bf16[768,2048]{1,0:T(8,128)(2,1)} fusion(bf16[3072,768]{1,0:T(8,128)(2,1)} %copy-done.75, bf16[3072,2048]{1,0:T(8,128)(2,1)} %all-gather.17.cloned.1.call-done), kind=kOutput, calls=%fused_computation.39 | convolution fusion | flops 9665249280 | bytes 20447232 | tf_op jit(solution)/shard_map/dot_general | solution.py:46
  590.3 20.5 %all-to-all-done.2 = bf16[8,256,768]{1,2,0:T(8,128)(2,1)} async-done(((bf16[8,256,768]{1,2,0:T(8,128)(2,1)}), bf16[8,256,768]{1,2,0:T(8,128)(2,1)}, u32[]{:S(2)}, u32[]{:S(2)}) %all-to-all-start.2) | async-done | bytes 3145760 | tf_op jit(solution)/shard_map/all_to_all | solution.py:236
  658.4 20.8 %collective-permute-done.1 = bf16[96,6144]{1,0:T(8,128)(2,1)} collective-permute-done((bf16[96,6144]{1,0:T(8,128)(2,1)}, bf16[96,6144]{1,0:T(8,128)(2,1)}, u32[]{:S(2)}, u32[]{:S(2)}) %collective-permute-start.1) | collective-permute-done | bytes 1179680 | tf_op jit(solution)/shard_map/ppermute | solution.py:92
  690.5 16.9 %reduce-scatter.9.cloned.1.call-done = bf16[384,2048]{1,0:T(8,128)(2,1)} async-done(((bf16[3072,2048]{1,0:T(8,128)(2,1)}), bf16[384,2048]{1,0:T(8,128)(2,1)}) %reduce-scatter.9.cloned.1.call-update) | async-done | bytes 1572880 | tf_op jit(solution)/shard_map/reduce_scatter | solution.py:210
  710.9 13.1 %fusion.2 = bf16[8,2,384,384]{2,3,1,0:T(8,128)(2,1)} fusion(f32[8,384,384,2]{2,1,3,0:T(8,128)} %copy-done.2, f32[8,2,384]{2,1,0:T(2,128)S(1)} %bitcast.247, pred[384,384]{0,1:T(8,128)(4,1)S(1)} %copy-done.32, bf16[384,8,2,128]{0,3,2,1:T(8,128)(2,1)S(1)} %copy.195, bf16[384,8,128,1]{2,1,0,3:T(8,128)(2,1)S(1)} %bitcast.230), kind=kOutput, calls=%fused_computation.7 | convolution fusion | flops 1226840448 | bytes 16687104 | tf_op jit(solution)/shard_map/sub | solution.py:263
  724.0 13.5 %collective-permute-done.3 = bf16[96,6144]{1,0:T(8,128)(2,1)} collective-permute-done((bf16[96,6144]{1,0:T(8,128)(2,1)}, bf16[96,6144]{1,0:T(8,128)(2,1)}, u32[]{:S(2)}, u32[]{:S(2)}) %collective-permute-start.3) | collective-permute-done | bytes 1179680 | tf_op jit(solution)/shard_map/ppermute | solution.py:92
  771.4 24.3 %collective-permute-done.5 = bf16[96,6144]{1,0:T(8,128)(2,1)} collective-permute-done((bf16[96,6144]{1,0:T(8,128)(2,1)}, bf16[96,6144]{1,0:T(8,128)(2,1)}, u32[]{:S(2)}, u32[]{:S(2)}) %collective-permute-start.5) | collective-permute-done | bytes 1179680 | tf_op jit(solution)/shard_map/ppermute | solution.py:92
  832.3 24.4 %collective-permute-done.7 = bf16[96,6144]{1,0:T(8,128)(2,1)S(1)} collective-permute-done((bf16[96,6144]{1,0:T(8,128)(2,1)S(1)}, bf16[96,6144]{1,0:T(8,128)(2,1)S(1)}, u32[]{:S(2)}, u32[]{:S(2)}) %collective-permute-start.7) | collective-permute-done | bytes 1179680 | tf_op jit(solution)/shard_map/ppermute | solution.py:92
  868.8 18.6 %collective-permute-done.8 = bf16[96,6144]{1,0:T(8,128)(2,1)S(1)} collective-permute-done((bf16[96,6144]{1,0:T(8,128)(2,1)S(1)}, bf16[96,6144]{1,0:T(8,128)(2,1)S(1)}, u32[]{:S(2)}, u32[]{:S(2)}) %collective-permute-start.8) | collective-permute-done | bytes 1179680 | tf_op jit(solution)/shard_map/ppermute | solution.py:91
  887.4 22.9 %collective-permute-done.9 = bf16[96,6144]{1,0:T(8,128)(2,1)S(1)} collective-permute-done((bf16[96,6144]{1,0:T(8,128)(2,1)S(1)}, bf16[96,6144]{1,0:T(8,128)(2,1)S(1)}, u32[]{:S(2)}, u32[]{:S(2)}) %collective-permute-start.9) | collective-permute-done | bytes 1179680 | tf_op jit(solution)/shard_map/ppermute | solution.py:92
  914.5 18.5 %concatenate.52 = bf16[2048,1027]{0,1:T(8,128)(2,1)} concatenate(bf16[2048,1024]{0,1:T(8,128)(2,1)} %convolution_convert_fusion.2, bf16[2048,1]{0,1:T(2,128)(2,1)S(1)} %broadcast_in_dim.26, bf16[2048,1]{0,1:T(2,128)(2,1)S(1)} %broadcast_in_dim.27, bf16[2048,1]{0,1:T(2,128)(2,1)S(1)} %bitcast.248), dimensions={1} | concatenate | bytes 8413184 | tf_op jit(solution)/shard_map/concatenate | solution.py:338
  969.6 17.0 %collective-permute-done.10 = bf16[96,6144]{1,0:T(8,128)(2,1)S(1)} collective-permute-done((bf16[96,6144]{1,0:T(8,128)(2,1)S(1)}, bf16[96,6144]{1,0:T(8,128)(2,1)S(1)}, u32[]{:S(2)}, u32[]{:S(2)}) %collective-permute-start.10) | collective-permute-done | bytes 1179680 | tf_op jit(solution)/shard_map/ppermute | solution.py:91
  986.6 22.6 %collective-permute-done.11 = bf16[96,6144]{1,0:T(8,128)(2,1)S(1)} collective-permute-done((bf16[96,6144]{1,0:T(8,128)(2,1)}, bf16[96,6144]{1,0:T(8,128)(2,1)S(1)}, u32[]{:S(2)}, u32[]{:S(2)}) %collective-permute-start.11) | collective-permute-done | bytes 1179680 | tf_op jit(solution)/shard_map/ppermute | solution.py:92
  1020.3 39.3 %reduce-scatter.17.cloned.1.call-done = bf16[256,2048]{1,0:T(8,128)(2,1)} async-done(((bf16[2048,2048]{1,0:T(8,128)(2,1)}), bf16[256,2048]{1,0:T(8,128)(2,1)}) %reduce-scatter.17.cloned.1.call-update) | async-done | bytes 1048592 | tf_op jit(solution)/shard_map/reduce_scatter | solution.py:341
  1059.6 74.9 %reduce-scatter.13.cloned.1.call-done = bf16[256,2048]{1,0:T(8,128)(2,1)} async-done(((bf16[2048,2048]{1,0:T(8,128)(2,1)}), bf16[256,2048]{1,0:T(8,128)(2,1)}) %reduce-scatter.13.cloned.1.call-update) | async-done | bytes 1048592 | tf_op jit(solution)/shard_map/reduce_scatter | solution.py:341
  1134.5 13.2 %bitcast_convert_fusion = f32[768,6144]{1,0:T(8,128)} fusion(bf16[2,4,96,6144]{3,2,1,0:T(8,128)(2,1)} %pad_maximum_fusion), kind=kLoop, calls=%fused_computation.3 | loop fusion | flops 4718592 | bytes 28311552 | tf_op jit(solution)/shard_map/convert_element_type | solution.py:121
  1147.7 13.9 %fusion.66 = (f32[256,6144]{1,0:T(8,128)}, f32[256,6144]{1,0:T(8,128)}, f32[256,6144]{1,0:T(8,128)}) fusion(f32[768,6144]{1,0:T(8,128)} %bitcast_convert_fusion), kind=kLoop, calls=%fused_computation.149 | loop fusion | bytes 37748736 | tf_op jit(solution)/shard_map/slice | solution.py:320
  1169.1 89.6 %all-reduce.3.cloned.1.call-done = (bf16[256,1027]{0,1:T(8,128)(2,1)}, bf16[256,2048]{1,0:T(8,128)(2,1)}, bf16[256,1024]{1,0:T(8,128)(2,1)}, bf16[256,2048]{1,0:T(8,128)(2,1)}) async-done(((bf16[256,1027]{0,1:T(8,128)(2,1)}, bf16[256,2048]{1,0:T(8,128)(2,1)}, bf16[256,1024]{1,0:T(8,128)(2,1)}, bf16[256,2048]{1,0:T(8,128)(2,1)}), (bf16[256,1027]{0,1:T(8,128)(2,1)}, bf16[256,2048]{1,0:T(8,128)(2,1)}, ...) | async-done | bytes 3147280 | tf_op jit(solution)/shard_map/psum | solution.py:353
  (318 shorter events, 370.4 us)
Async XLA Ops:
  7.2 359.0 %copy-start = (bf16[768,2048]{1,0:T(8,128)(2,1)S(1)}, bf16[768,2048]{1,0:T(8,128)(2,1)}, u32[]{:S(2)}) copy-start(bf16[768,2048]{1,0:T(8,128)(2,1)} %param.28) | copy-start | bytes 9437188
  7.2 139.5 %all-gather.9.cloned.1.call-start = ((), (), s32[]{:S(2)}) async-start(), calls=%async_computation.11 | async-start | bytes 4718592 | tf_op jit(solution)/shard_map/all_gather | solution.py:159
  7.9 152.0 %all-gather.7.cloned.1.call-start = ((), (), s32[]{:S(2)}) async-start(), calls=%async_computation.10 | async-start | bytes 4718592 | tf_op jit(solution)/shard_map/all_gather | solution.py:160
  8.7 181.9 %all-gather.11.cloned.1.call-start = ((), (), s32[]{:S(2)}) async-start(), calls=%async_computation.12 | async-start | bytes 9437184 | tf_op jit(solution)/shard_map/all_gather | solution.py:158
  9.4 237.2 %all-gather.13.cloned.1.call-start = ((), (), s32[]{:S(2)}) async-start(), calls=%async_computation.13 | async-start | bytes 9437184 | tf_op jit(solution)/shard_map/all_gather | solution.py:161
  14.6 59.8 %all-to-all-start = ((bf16[256,8,768]{0,2,1:T(8,128)(2,1)}), bf16[256,8,768]{0,2,1:T(8,128)(2,1)}, u32[]{:S(2)}, u32[]{:S(2)}) async-start(bf16[256,8,768]{0,2,1:T(8,128)(2,1)} %bitcast.214), calls=%async_computation | async-start | bytes 6291456 | tf_op jit(solution)/shard_map/all_to_all | solution.py:163
  74.5 64.8 %all-to-all-start.1 = ((bf16[256,8,768]{0,2,1:T(8,128)(2,1)}), bf16[256,8,768]{0,2,1:T(8,128)(2,1)}, u32[]{:S(2)}, u32[]{:S(2)}) async-start(bf16[256,8,768]{0,2,1:T(8,128)(2,1)} %bitcast.213), calls=%async_computation.1 | async-start | bytes 6291456 | tf_op jit(solution)/shard_map/all_to_all | solution.py:164
  79.1 251.0 %all-gather.15.cloned.1.call-start = ((), (), s32[]{:S(2)}) async-start(), calls=%async_computation.14 | async-start | bytes 14155776 | tf_op jit(solution)/shard_map/all_gather | solution.py:202
  134.5 71.1 %copy-start.24 = (f32[384,128]{0,1:T(8,128)}, f32[384,128]{0,1:T(8,128)S(1)}, u32[]{:S(2)}) copy-start(f32[384,128]{0,1:T(8,128)S(1)} %get-tuple-element.189) | copy-start | bytes 589828
  134.5 120.2 %copy-start.53 = (f32[1,2048]{1,0:T(1,128)}, f32[1,2048]{1,0:T(1,128)S(1)}, u32[]{:S(2)}) copy-start(f32[1,2048]{1,0:T(1,128)S(1)} %get-tuple-element.191) | copy-start | bytes 24580
  257.9 146.5 %all-gather.17.cloned.1.call-start = ((), (), s32[]{:S(2)}) async-start(), calls=%async_computation.15 | async-start | bytes 14155776 | tf_op jit(solution)/shard_map/all_gather | solution.py:215
  265.3 376.7 %reduce-scatter.7.cloned.1.call-start = ((), (), s32[]{:S(2)}) async-start(), calls=%async_computation.16 | async-start | bytes 14155776 | tf_op jit(solution)/shard_map/reduce_scatter | solution.py:226
  462.9 244.6 %reduce-scatter.9.cloned.1.call-start = ((), (), s32[]{:S(2)}) async-start(), calls=%async_computation.17 | async-start | bytes 14155776 | tf_op jit(solution)/shard_map/reduce_scatter | solution.py:210
  481.4 70.3 %all-to-all-start.3 = ((bf16[8,256,768]{1,2,0:T(8,128)(2,1)}), bf16[8,256,768]{1,2,0:T(8,128)(2,1)S(1)}, u32[]{:S(2)}, u32[]{:S(2)}) async-start(bf16[8,256,768]{1,2,0:T(8,128)(2,1)} %copy.187), calls=%async_computation.3 | async-start | bytes 6291456 | tf_op jit(solution)/shard_map/all_to_all | solution.py:237
  551.7 59.1 %all-to-all-start.2 = ((bf16[8,256,768]{1,2,0:T(8,128)(2,1)}), bf16[8,256,768]{1,2,0:T(8,128)(2,1)}, u32[]{:S(2)}, u32[]{:S(2)}) async-start(bf16[8,256,768]{1,2,0:T(8,128)(2,1)} %copy.186), calls=%async_computation.2 | async-start | bytes 6291456 | tf_op jit(solution)/shard_map/all_to_all | solution.py:236
  556.1 464.2 %reduce-scatter.15.cloned.1.call-start = ((), (), s32[]{:S(2)}) async-start(), calls=%async_computation.20 | async-start | bytes 4718592 | tf_op jit(solution)/shard_map/reduce_scatter | solution.py:341
  627.4 31.0 %collective-permute-start = (bf16[96,6144]{1,0:T(8,128)(2,1)}, bf16[96,6144]{1,0:T(8,128)(2,1)}, u32[]{:S(2)}, u32[]{:S(2)}) collective-permute-start(bf16[96,6144]{1,0:T(8,128)(2,1)} %dynamic-slice_bitcast_fusion.1), channel_id=1, source_target_pairs={{0,1},{1,2},{2,3},{3,0},{4,5},{5,6},{6,7},{7,4},{8,9},{9,10},{10,1... | collective-permute-start | bytes 3538952 | tf_op jit(solution)/shard_map/ppermute | solution.py:91
  639.4 39.8 %collective-permute-start.1 = (bf16[96,6144]{1,0:T(8,128)(2,1)}, bf16[96,6144]{1,0:T(8,128)(2,1)}, u32[]{:S(2)}, u32[]{:S(2)}) collective-permute-start(bf16[96,6144]{1,0:T(8,128)(2,1)} %dynamic-slice_bitcast_fusion), channel_id=1, source_target_pairs={{0,3},{1,0},{2,1},{3,2},{4,7},{5,4},{6,5},{7,6},{8,11},{9,8},{10,9... | collective-permute-start | bytes 3538952 | tf_op jit(solution)/shard_map/ppermute | solution.py:92
  682.1 41.8 %collective-permute-start.2 = (bf16[96,6144]{1,0:T(8,128)(2,1)}, bf16[96,6144]{1,0:T(8,128)(2,1)}, u32[]{:S(2)}, u32[]{:S(2)}) collective-permute-start(bf16[96,6144]{1,0:T(8,128)(2,1)} %fusion.34), channel_id=1, source_target_pairs={{0,1},{1,2},{2,3},{3,0},{4,5},{5,6},{6,7},{7,4},{8,9},{9,10},{10,1... | collective-permute-start | bytes 3538952 | tf_op jit(solution)/shard_map/ppermute | solution.py:91
  685.6 51.8 %collective-permute-start.3 = (bf16[96,6144]{1,0:T(8,128)(2,1)}, bf16[96,6144]{1,0:T(8,128)(2,1)}, u32[]{:S(2)}, u32[]{:S(2)}) collective-permute-start(bf16[96,6144]{1,0:T(8,128)(2,1)} %fusion.33), channel_id=1, source_target_pairs={{0,3},{1,0},{2,1},{3,2},{4,7},{5,4},{6,5},{7,6},{8,11},{9,8},{10,9... | collective-permute-start | bytes 3538952 | tf_op jit(solution)/shard_map/ppermute | solution.py:92
  740.4 31.0 %collective-permute-start.4 = (bf16[96,6144]{1,0:T(8,128)(2,1)}, bf16[96,6144]{1,0:T(8,128)(2,1)}, u32[]{:S(2)}, u32[]{:S(2)}) collective-permute-start(bf16[96,6144]{1,0:T(8,128)(2,1)} %fusion.32), channel_id=1, source_target_pairs={{0,1},{1,2},{2,3},{3,0},{4,5},{5,6},{6,7},{7,4},{8,9},{9,10},{10,1... | collective-permute-start | bytes 3538952 | tf_op jit(solution)/shard_map/ppermute | solution.py:91
  743.9 51.8 %collective-permute-start.5 = (bf16[96,6144]{1,0:T(8,128)(2,1)}, bf16[96,6144]{1,0:T(8,128)(2,1)}, u32[]{:S(2)}, u32[]{:S(2)}) collective-permute-start(bf16[96,6144]{1,0:T(8,128)(2,1)} %fusion.31), channel_id=1, source_target_pairs={{0,3},{1,0},{2,1},{3,2},{4,7},{5,4},{6,5},{7,6},{8,11},{9,8},{10,9... | collective-permute-start | bytes 3538952 | tf_op jit(solution)/shard_map/ppermute | solution.py:92
  756.9 263.4 %reduce-scatter.11.cloned.1.call-start = ((), (), s32[]{:S(2)}) async-start(), calls=%async_computation.18 | async-start | bytes 4755456 | tf_op jit(solution)/shard_map/reduce_scatter | solution.py:341
  801.6 30.7 %collective-permute-start.6 = (bf16[96,6144]{1,0:T(8,128)(2,1)S(1)}, bf16[96,6144]{1,0:T(8,128)(2,1)S(1)}, u32[]{:S(2)}, u32[]{:S(2)}) collective-permute-start(bf16[96,6144]{1,0:T(8,128)(2,1)S(1)} %get-tuple-element.164), channel_id=1, source_target_pairs={{0,1},{1,2},{2,3},{3,0},{4,5},{5,6},{6,7},{7,4},{8,9},{9,10},{10,1... | collective-permute-start | bytes 3538952 | tf_op jit(solution)/shard_map/ppermute | solution.py:91
  807.6 49.0 %collective-permute-start.7 = (bf16[96,6144]{1,0:T(8,128)(2,1)S(1)}, bf16[96,6144]{1,0:T(8,128)(2,1)S(1)}, u32[]{:S(2)}, u32[]{:S(2)}) collective-permute-start(bf16[96,6144]{1,0:T(8,128)(2,1)S(1)} %get-tuple-element.166), channel_id=1, source_target_pairs={{0,3},{1,0},{2,1},{3,2},{4,7},{5,4},{6,5},{7,6},{8,11},{9,8},{10,9... | collective-permute-start | bytes 3538952 | tf_op jit(solution)/shard_map/ppermute | solution.py:92
  856.7 30.7 %collective-permute-start.8 = (bf16[96,6144]{1,0:T(8,128)(2,1)S(1)}, bf16[96,6144]{1,0:T(8,128)(2,1)S(1)}, u32[]{:S(2)}, u32[]{:S(2)}) collective-permute-start(bf16[96,6144]{1,0:T(8,128)(2,1)S(1)} %collective-permute-done.6), channel_id=1, source_target_pairs={{0,1},{1,2},{2,3},{3,0},{4,5},{5,6},{6,7},{7,4},{8,9},{9,10},{10,1... | collective-permute-start | bytes 3538952 | tf_op jit(solution)/shard_map/ppermute | solution.py:91
  857.2 53.0 %collective-permute-start.9 = (bf16[96,6144]{1,0:T(8,128)(2,1)S(1)}, bf16[96,6144]{1,0:T(8,128)(2,1)S(1)}, u32[]{:S(2)}, u32[]{:S(2)}) collective-permute-start(bf16[96,6144]{1,0:T(8,128)(2,1)S(1)} %collective-permute-done.7), channel_id=1, source_target_pairs={{0,3},{1,0},{2,1},{3,2},{4,7},{5,4},{6,5},{7,6},{8,11},{9,8},{10,9... | collective-permute-start | bytes 3538952 | tf_op jit(solution)/shard_map/ppermute | solution.py:92
  933.0 126.7 %reduce-scatter.17.cloned.1.call-start = ((), (), s32[]{:S(2)}) async-start(), calls=%async_computation.21 | async-start | bytes 9437184 | tf_op jit(solution)/shard_map/reduce_scatter | solution.py:341
  943.1 191.4 %reduce-scatter.13.cloned.1.call-start = ((), (), s32[]{:S(2)}) async-start(), calls=%async_computation.19 | async-start | bytes 9437184 | tf_op jit(solution)/shard_map/reduce_scatter | solution.py:341
  952.4 306.3 %all-reduce.3.cloned.1.call-start = ((), (), s32[]{:S(2)}) async-start(), calls=%async_computation.22 | async-start | bytes 6299648 | tf_op jit(solution)/shard_map/psum | solution.py:353
  955.9 30.7 %collective-permute-start.10 = (bf16[96,6144]{1,0:T(8,128)(2,1)S(1)}, bf16[96,6144]{1,0:T(8,128)(2,1)S(1)}, u32[]{:S(2)}, u32[]{:S(2)}) collective-permute-start(bf16[96,6144]{1,0:T(8,128)(2,1)S(1)} %copy-done.40), channel_id=1, source_target_pairs={{0,1},{1,2},{2,3},{3,0},{4,5},{5,6},{6,7},{7,4},{8,9},{9,10},{10,1... | collective-permute-start | bytes 3538952 | tf_op jit(solution)/shard_map/ppermute | solution.py:91
  956.1 53.1 %collective-permute-start.11 = (bf16[96,6144]{1,0:T(8,128)(2,1)}, bf16[96,6144]{1,0:T(8,128)(2,1)S(1)}, u32[]{:S(2)}, u32[]{:S(2)}) collective-permute-start(bf16[96,6144]{1,0:T(8,128)(2,1)} %copy-done.41), channel_id=1, source_target_pairs={{0,3},{1,0},{2,1},{3,2},{4,7},{5,4},{6,5},{7,6},{8,11},{9,8},{10,9... | collective-permute-start | bytes 3538952 | tf_op jit(solution)/shard_map/ppermute | solution.py:92
  (73 other events, 704.4 us)
Sparse Core Ops, SparseCore 0:
  9.9 64.1 all-gather.8
  76.0 59.0 all-gather.6
  137.0 53.5 all-gather.10
  192.3 54.2 all-gather.12
  258.1 71.9 all-gather.14
  332.4 71.9 all-gather.16
  463.0 140.1 reduce-scatter.6
  606.7 100.7 reduce-scatter.8
  757.0 50.9 reduce-scatter.14
  933.1 51.5 reduce-scatter.10
  988.1 71.4 reduce-scatter.16
  1063.0 71.5 reduce-scatter.12
  1137.2 121.5 all-reduce.2

commit v11 on v10

--- a/solution.py
+++ b/solution.py
@@ -334,44 +334,43 @@
         ],
         axis=1,
     )
-    key_width = key_grad.shape[1]
-    key_grad = jnp.concatenate([key_grad, gain_cols], axis=1)
-
-    def low_sum(v):
-        return lax.psum_scatter(v.astype(jnp.bfloat16), "fsdp", scatter_dimension=0, tiled=True)
-
-    attention_parts = (
-        None, low_sum(query_grad), low_sum(key_grad), low_sum(value_grad), low_sum(output_grad)
-    )
-    finals = (
-        None,
-        feed_rep[0],
-        feed_rep[1],
-        feed_rep[2],
-        None,
-        lax.psum(attention_parts[1].astype(jnp.bfloat16), "rep").astype(jnp.float32),
-        lax.psum(attention_parts[2].astype(jnp.bfloat16), "rep").astype(jnp.float32),
-        lax.psum(attention_parts[3].astype(jnp.bfloat16), "rep").astype(jnp.float32),
-        lax.psum(attention_parts[4].astype(jnp.bfloat16), "rep").astype(jnp.float32),
-    )
-    key_rep = finals[6]
-    gain_rep = key_rep[:, key_width:]
+    gain_parts = lax.all_to_all(gain_cols, "fsdp", 0, 1, tiled=True)
+    gain_part = gain_parts.reshape(gain_share, fsdp_count, gain_cols.shape[1]).sum(axis=1)
+    gain_rep = lax.psum(gain_part.astype(jnp.bfloat16), "rep").astype(jnp.float32)
     attention_gain_out = gain_rep[:, 0]
     feed_gain_out = gain_rep[:, 1]
     head_sum = gain_rep[:, 2:].T.reshape(-1)
     query_gain_out = head_sum[:head_width]
     key_gain_out = head_sum[head_width : 2 * head_width]
+
+    def low_sum(v):
+        return lax.psum_scatter(v.astype(jnp.bfloat16), "fsdp", scatter_dimension=0, tiled=True)
+
+    attention_parts = (
+        None, low_sum(query_grad), low_sum(key_grad), low_sum(value_grad), low_sum(output_grad)
+    )
+    finals = (
+        feed_gain_out,
+        feed_rep[0],
+        feed_rep[1],
+        feed_rep[2],
+        attention_gain_out,
+        lax.psum(attention_parts[1].astype(jnp.bfloat16), "rep").astype(jnp.float32),
+        lax.psum(attention_parts[2].astype(jnp.bfloat16), "rep").astype(jnp.float32),
+        lax.psum(attention_parts[3].astype(jnp.bfloat16), "rep").astype(jnp.float32),
+        lax.psum(attention_parts[4].astype(jnp.bfloat16), "rep").astype(jnp.float32),
+    )
     return (
         layer_out,
         input_grad,
-        attention_gain_out,
+        finals[4],
         finals[5],
-        key_rep[:, :key_width],
+        finals[6],
         finals[7],
         query_gain_out,
         key_gain_out,
         finals[8],
-        feed_gain_out,
+        finals[0],
         finals[1],
         finals[2],
         finals[3],

time: 1290 us -> 1160 us (0.90)
  waiting for transfers between devices: 665 us -> 527 us
  blocking collectives: 52.8 us -> 82.8 us
  local copies, waits for them, and re-layouts: 151 us -> 131 us
    reduce_scatter x4, waiting for transfers between devices: 114 us -> 4.64 us  [low_sum(): lax.psum_scatter(v.astype(jnp.bfloat16), 'fsdp', scatter_dimension=0, til...]
    psum x0 -> x1, blocking collectives: none -> 30 us  [per_device(): lax.psum(gain_part.astype(jnp.bfloat16), 'rep').astype(jnp.float32)]
    concatenate x1 -> x3, local copies, waits for them, and re-layouts: 18.5 us -> 0.64 us  [per_device(): jnp.concatenate([attention_gain_grad[:, None], feed_gain_grad[:, None], j...]
    reduce_scatter x1, waiting for transfers between devices: 16.9 us -> 0.01 us  [per_device(): lax.psum_scatter(down_part.astype(jnp.bfloat16), 'fsdp', scatter_dimensio...]
    unnamed x159 -> x174, local copies, waits for them, and re-layouts: 35.6 us -> 35.3 us
  transfers between devices with their start and end apart: 29 -> 30, of which waited for: 22 -> 19; matrix products, arithmetic and copies ran while one was open for 31% -> 33% of each run, Pallas kernels for 0% -> 0%
where the time goes in v11:
time: 1160 us; the launch traced here: 1150 us
  waiting for transfers between devices  527 us (45%)
  matrix products  247 us (21%)
  local copies, waits for them, and re-layouts  131 us (11%)
  other arithmetic  98.7 us (9%)
  blocking collectives  82.8 us (7%)
  starting transfers between devices  48.2 us (4%)
  between operations  17.1 us (1%)
    ppermute x6, waiting for transfers between devices, issue(): lax.ppermute(sends[1], self.axis, self.backward)  116 us
    psum x1, waiting for transfers between devices, per_device(): lax.psum(attention_parts[1].astype(jnp.bfloat16), 'rep').astype(jnp.float32)  89.2 us
    dot_general x7, matrix products, times_transposed(): lax.dot_general(left, right, (((1,), (1,)), ((), ())), preferred_element_...  74.9 us
    dot_general x7, matrix products, inner_rows(): lax.dot_general(left, right, (((0,), (0,)), ((), ())), preferred_element_...  70.6 us
    all_gather x1, waiting for transfers between devices, per_device(): lax.all_gather(normed_two_low, 'fsdp', axis=0, tiled=True)  64.8 us
    ppermute x6, waiting for transfers between devices, issue(): lax.ppermute(sends[0], self.axis, self.forward)  53.6 us
    all_gather x1, blocking collectives, per_device(): lax.all_gather(jnp.stack([attention_gain, feed_gain]), 'fsdp', axis=1, ti...  52.8 us
    all_to_all x1, waiting for transfers between devices, per_device(): gate_block = lax.all_to_all(gate_weight, 'fsdp', 1, 0, tiled=True)  50 us
  transfers between devices with their start and end apart: 30, of which 19 were waited for; matrix products, arithmetic and copies ran while one was open for 33% of the time, Pallas kernels for 0%

profile of v11, /device:TPU:0, one launch (start us, length us, event | category | flops | bytes accessed | tf_op | source)
XLA Modules:
  0.0 1150.9 jit_solution(11564511782472396171)
XLA Ops:
  24.5 50.0 %all-to-all-done = bf16[256,8,768]{0,2,1:T(8,128)(2,1)} async-done(((bf16[256,8,768]{0,2,1:T(8,128)(2,1)}), bf16[256,8,768]{0,2,1:T(8,128)(2,1)}, u32[]{:S(2)}, u32[]{:S(2)}) %all-to-all-start) | async-done | bytes 3145760 | tf_op jit(solution)/shard_map/all_to_all | solution.py:163
  80.2 52.8 %all_gather.21 = bf16[2,2048]{1,0:T(2,128)(2,1)S(1)} all-gather(bf16[2,256]{1,0:T(2,128)(2,1)S(1)} %pad_maximum_fusion.5), channel_id=1, replica_groups=mesh['fsdp'=8,'rep'=4] {'fsdp'}, dimensions={1}, use_global_device_ids=true | all-gather | bytes 9216 | tf_op jit(solution)/shard_map/all_gather | solution.py:155
  167.6 23.0 %all-gather.11.cloned.1.call-done = bf16[2048,2048]{1,0:T(8,128)(2,1)} async-done(((bf16[256,2048]{1,0:T(8,128)(2,1)}), bf16[2048,2048]{1,0:T(8,128)(2,1)}) %all-gather.11.cloned.1.call-update) | async-done | bytes 8388624 | tf_op jit(solution)/shard_map/all_gather | solution.py:158
  190.6 10.2 multiply_reduce_fusion.3
  217.7 29.0 %all-gather.13.cloned.1.call-done = bf16[2048,2048]{1,0:T(8,128)(2,1)} async-done(((bf16[256,2048]{1,0:T(8,128)(2,1)}), bf16[2048,2048]{1,0:T(8,128)(2,1)}) %all-gather.13.cloned.1.call-update) | async-done | bytes 8388624 | tf_op jit(solution)/shard_map/all_gather | solution.py:161
  265.4 64.8 %all-gather.15.cloned.1.call-done = bf16[3072,2048]{1,0:T(8,128)(2,1)} async-done(((bf16[384,2048]{1,0:T(8,128)(2,1)}), bf16[3072,2048]{1,0:T(8,128)(2,1)}) %all-gather.15.cloned.1.call-update) | async-done | bytes 12582928 | tf_op jit(solution)/shard_map/all_gather | solution.py:202
  330.1 16.3 %fusion.68 = f32[3072,768]{1,0:T(8,128)} fusion(bf16[3072,2048]{1,0:T(8,128)(2,1)} %all-gather.15.cloned.1.call-done, bf16[2048,768]{1,0:T(8,128)(2,1)} %bitcast.214), kind=kOutput, calls=%fused_computation.151 | convolution fusion | flops 9663676416 | bytes 25165824 | tf_op jit(solution)/shard_map/dot_general | solution.py:203
  346.5 17.6 %multiply_convert_fusion.2 = (bf16[3072,768]{1,0:T(8,128)(2,1)S(1)}, f32[3072,768]{1,0:T(8,128)}) fusion(f32[3072,768]{1,0:T(8,128)} %fusion.68, bf16[3072,2048]{1,0:T(8,128)(2,1)} %all-gather.15.cloned.1.call-done, bf16[2048,768]{1,0:T(8,128)(2,1)S(1)} %bitcast.216), kind=kOutput, calls=%fused_computation.13 | convolution fusion | flops 9677832192 | bytes 39321600 | tf_op jit(solution)/shard_map/dot_general | solution.py:204
  366.2 12.2 %fusion.69 = bf16[3072,2048]{1,0:T(8,128)(2,1)} fusion(bf16[3072,768]{1,0:T(8,128)(2,1)S(1)} %get-tuple-element.48, bf16[768,2048]{1,0:T(8,128)(2,1)S(1)} %copy-done), kind=kOutput, calls=%fused_computation.152 | convolution fusion | flops 9663676416 | bytes 20447232 | tf_op jit(solution)/shard_map/dot_general | solution.py:206
  378.5 26.0 %all-gather.17.cloned.1.call-done = bf16[3072,2048]{1,0:T(8,128)(2,1)} async-done(((bf16[384,2048]{1,0:T(8,128)(2,1)}), bf16[3072,2048]{1,0:T(8,128)(2,1)}) %all-gather.17.cloned.1.call-update) | async-done | bytes 12582928 | tf_op jit(solution)/shard_map/all_gather | solution.py:215
  404.5 22.2 %multiply_convert_fusion.1 = (bf16[3072,768]{1,0:T(8,128)(2,1)}, bf16[3072,768]{1,0:T(8,128)(2,1)}) fusion(f32[3072,768]{1,0:T(8,128)} %fusion.68, f32[3072,768]{1,0:T(8,128)} %get-tuple-element.46, bf16[3072,2048]{1,0:T(8,128)(2,1)} %all-gather.17.cloned.1.call-done, bf16[768,2048]{1,0:T(8,128)(2,1)S(1)} %copy-done), kind=kOutput, calls=%fused_computation.11 | convolution fusion | flops 9694347264 | bytes 44040192 | tf_op jit(solution)/shard_map/dot_general | solution.py:52
  426.7 17.8 %fusion.70 = f32[3072,2048]{1,0:T(8,128)} fusion(bf16[3072,768]{1,0:T(8,128)(2,1)} %get-tuple-element.95, bf16[2048,768]{1,0:T(8,128)(2,1)} %bitcast.215), kind=kOutput, calls=%fused_computation.153 | convolution fusion | flops 9663676416 | bytes 33030144 | tf_op jit(solution)/shard_map/dot_general | solution.py:52
  444.5 18.5 %add_convert_fusion = bf16[3072,2048]{1,0:T(8,128)(2,1)} fusion(f32[3072,2048]{1,0:T(8,128)} %fusion.70, bf16[3072,768]{1,0:T(8,128)(2,1)} %get-tuple-element.96, bf16[2048,768]{1,0:T(8,128)(2,1)S(1)} %bitcast.217), kind=kOutput, calls=%fused_computation.1 | convolution fusion | flops 9676259328 | bytes 45613056 | tf_op jit(solution)/shard_map/dot_general | solution.py:52
  463.8 15.0 %convolution_convert_fusion.4 = bf16[2048,768]{1,0:T(8,128)(2,1)S(1)} fusion(bf16[3072,2048]{1,0:T(8,128)(2,1)} %all-gather.15.cloned.1.call-done, bf16[3072,768]{1,0:T(8,128)(2,1)} %get-tuple-element.96), kind=kOutput, calls=%fused_computation.37 | convolution fusion | flops 9665249280 | bytes 20447232 | tf_op jit(solution)/shard_map/dot_general | solution.py:46
  485.5 15.7 %convolution_convert_fusion.5 = bf16[2048,768]{1,0:T(8,128)(2,1)} fusion(bf16[3072,2048]{1,0:T(8,128)(2,1)} %all-gather.15.cloned.1.call-done, bf16[3072,768]{1,0:T(8,128)(2,1)} %get-tuple-element.95), kind=kOutput, calls=%fused_computation.38 | convolution fusion | flops 9665249280 | bytes 20447232 | tf_op jit(solution)/shard_map/dot_general | solution.py:46
  505.8 46.1 %all-to-all-done.3 = bf16[8,256,768]{1,2,0:T(8,128)(2,1)S(1)} async-done(((bf16[8,256,768]{1,2,0:T(8,128)(2,1)}), bf16[8,256,768]{1,2,0:T(8,128)(2,1)S(1)}, u32[]{:S(2)}, u32[]{:S(2)}) %all-to-all-start.3) | async-done | bytes 3145760 | tf_op jit(solution)/shard_map/all_to_all | solution.py:237
  564.7 15.5 %convolution_convert_fusion.6 = bf16[768,2048]{1,0:T(8,128)(2,1)} fusion(bf16[3072,768]{1,0:T(8,128)(2,1)} %copy-done.82, bf16[3072,2048]{1,0:T(8,128)(2,1)} %all-gather.17.cloned.1.call-done), kind=kOutput, calls=%fused_computation.39 | convolution fusion | flops 9665249280 | bytes 20447232 | tf_op jit(solution)/shard_map/dot_general | solution.py:46
  590.5 20.6 %all-to-all-done.2 = bf16[8,256,768]{1,2,0:T(8,128)(2,1)} async-done(((bf16[8,256,768]{1,2,0:T(8,128)(2,1)}), bf16[8,256,768]{1,2,0:T(8,128)(2,1)}, u32[]{:S(2)}, u32[]{:S(2)}) %all-to-all-start.2) | async-done | bytes 3145760 | tf_op jit(solution)/shard_map/all_to_all | solution.py:236
  629.1 8.2 copy.187
  658.7 20.8 %collective-permute-done.1 = bf16[96,6144]{1,0:T(8,128)(2,1)} collective-permute-done((bf16[96,6144]{1,0:T(8,128)(2,1)}, bf16[96,6144]{1,0:T(8,128)(2,1)}, u32[]{:S(2)}, u32[]{:S(2)}) %collective-permute-start.1) | collective-permute-done | bytes 1179680 | tf_op jit(solution)/shard_map/ppermute | solution.py:92
  692.2 13.6 %fusion.2 = bf16[8,2,384,384]{2,3,1,0:T(8,128)(2,1)} fusion(f32[8,384,384,2]{2,1,3,0:T(8,128)} %copy-done.2, f32[8,2,384]{2,1,0:T(2,128)S(1)} %bitcast.242, pred[384,384]{0,1:T(8,128)(4,1)S(1)} %copy-done.36, bf16[384,8,2,128]{0,3,2,1:T(8,128)(2,1)S(1)} %copy.192, bf16[384,8,128,1]{2,1,0,3:T(8,128)(2,1)} %bitcast.224), kind=kOutput, calls=%fused_computation.7 | convolution fusion | flops 1226840448 | bytes 16687104 | tf_op jit(solution)/shard_map/sub | solution.py:263
  713.4 24.3 %collective-permute-done.3 = bf16[96,6144]{1,0:T(8,128)(2,1)} collective-permute-done((bf16[96,6144]{1,0:T(8,128)(2,1)}, bf16[96,6144]{1,0:T(8,128)(2,1)}, u32[]{:S(2)}, u32[]{:S(2)}) %collective-permute-start.3) | collective-permute-done | bytes 1179680 | tf_op jit(solution)/shard_map/ppermute | solution.py:92
  759.3 20.3 %collective-permute-done.4 = bf16[96,6144]{1,0:T(8,128)(2,1)S(1)} collective-permute-done((bf16[96,6144]{1,0:T(8,128)(2,1)S(1)}, bf16[96,6144]{1,0:T(8,128)(2,1)S(1)}, u32[]{:S(2)}, u32[]{:S(2)}) %collective-permute-start.4) | collective-permute-done | bytes 1179680 | tf_op jit(solution)/shard_map/ppermute | solution.py:91
  779.6 24.3 %collective-permute-done.5 = bf16[96,6144]{1,0:T(8,128)(2,1)S(1)} collective-permute-done((bf16[96,6144]{1,0:T(8,128)(2,1)S(1)}, bf16[96,6144]{1,0:T(8,128)(2,1)S(1)}, u32[]{:S(2)}, u32[]{:S(2)}) %collective-permute-start.5) | collective-permute-done | bytes 1179680 | tf_op jit(solution)/shard_map/ppermute | solution.py:92
  860.2 24.3 %collective-permute-done.7 = bf16[96,6144]{1,0:T(8,128)(2,1)} collective-permute-done((bf16[96,6144]{1,0:T(8,128)(2,1)}, bf16[96,6144]{1,0:T(8,128)(2,1)}, u32[]{:S(2)}, u32[]{:S(2)}) %collective-permute-start.7) | collective-permute-done | bytes 1179680 | tf_op jit(solution)/shard_map/ppermute | solution.py:92
  898.4 17.1 %collective-permute-done.8 = bf16[96,6144]{1,0:T(8,128)(2,1)} collective-permute-done((bf16[96,6144]{1,0:T(8,128)(2,1)}, bf16[96,6144]{1,0:T(8,128)(2,1)}, u32[]{:S(2)}, u32[]{:S(2)}) %collective-permute-start.8) | collective-permute-done | bytes 1179680 | tf_op jit(solution)/shard_map/ppermute | solution.py:91
  915.5 22.7 %collective-permute-done.9 = bf16[96,6144]{1,0:T(8,128)(2,1)} collective-permute-done((bf16[96,6144]{1,0:T(8,128)(2,1)}, bf16[96,6144]{1,0:T(8,128)(2,1)}, u32[]{:S(2)}, u32[]{:S(2)}) %collective-permute-start.9) | collective-permute-done | bytes 1179680 | tf_op jit(solution)/shard_map/ppermute | solution.py:92
  964.7 30.0 %psum.35 = bf16[256,3]{0,1:T(4,128)(2,1)S(1)} all-reduce(bf16[256,3]{0,1:T(4,128)(2,1)S(1)} %reduce_sum.149), channel_id=1, replica_groups=mesh['fsdp'=8,'rep'=4] {'rep'}, use_global_device_ids=true, to_apply=%region_18.19 | all-reduce | flops 768 | bytes 3072 | tf_op jit(solution)/shard_map/psum | solution.py:339
  1000.9 8.2 pad_maximum_fusion
  1013.7 13.2 %bitcast_convert_fusion = f32[768,6144]{1,0:T(8,128)} fusion(bf16[2,4,96,6144]{3,2,1,0:T(8,128)(2,1)} %pad_maximum_fusion), kind=kLoop, calls=%fused_computation.3 | loop fusion | flops 4718592 | bytes 28311552 | tf_op jit(solution)/shard_map/convert_element_type | solution.py:121
  1026.9 13.9 %fusion.66 = (f32[256,6144]{1,0:T(8,128)}, f32[256,6144]{1,0:T(8,128)}, f32[256,6144]{1,0:T(8,128)}) fusion(f32[768,6144]{1,0:T(8,128)} %bitcast_convert_fusion), kind=kLoop, calls=%fused_computation.149 | loop fusion | bytes 37748736 | tf_op jit(solution)/shard_map/slice | solution.py:320
  1048.3 89.2 %all-reduce.3.cloned.1.call-done = (bf16[256,2048]{1,0:T(8,128)(2,1)}, bf16[256,1024]{1,0:T(8,128)(2,1)}, bf16[256,1024]{1,0:T(8,128)(2,1)}, bf16[256,2048]{1,0:T(8,128)(2,1)}) async-done(((bf16[256,2048]{1,0:T(8,128)(2,1)}, bf16[256,1024]{1,0:T(8,128)(2,1)}, bf16[256,1024]{1,0:T(8,128)(2,1)}, bf16[256,2048]{1,0:T(8,128)(2,1)}), (bf16[256,2048]{1,0:T(8,128)(2,1)}, bf16[256,1024]{1,0:T(8,128)(2,1)}, ...) | async-done | bytes 3145744 | tf_op jit(solution)/shard_map/psum | solution.py:358
  (340 shorter events, 330.5 us)
Async XLA Ops:
  7.2 359.0 %copy-start = (bf16[768,2048]{1,0:T(8,128)(2,1)S(1)}, bf16[768,2048]{1,0:T(8,128)(2,1)}, u32[]{:S(2)}) copy-start(bf16[768,2048]{1,0:T(8,128)(2,1)} %param.28) | copy-start | bytes 9437188
  7.2 139.6 %all-gather.9.cloned.1.call-start = ((), (), s32[]{:S(2)}) async-start(), calls=%async_computation.12 | async-start | bytes 4718592 | tf_op jit(solution)/shard_map/all_gather | solution.py:159
  7.9 152.1 %all-gather.7.cloned.1.call-start = ((), (), s32[]{:S(2)}) async-start(), calls=%async_computation.11 | async-start | bytes 4718592 | tf_op jit(solution)/shard_map/all_gather | solution.py:160
  8.7 182.0 %all-gather.11.cloned.1.call-start = ((), (), s32[]{:S(2)}) async-start(), calls=%async_computation.13 | async-start | bytes 9437184 | tf_op jit(solution)/shard_map/all_gather | solution.py:158
  9.4 237.3 %all-gather.13.cloned.1.call-start = ((), (), s32[]{:S(2)}) async-start(), calls=%async_computation.14 | async-start | bytes 9437184 | tf_op jit(solution)/shard_map/all_gather | solution.py:161
  14.6 59.8 %all-to-all-start = ((bf16[256,8,768]{0,2,1:T(8,128)(2,1)}), bf16[256,8,768]{0,2,1:T(8,128)(2,1)}, u32[]{:S(2)}, u32[]{:S(2)}) async-start(bf16[256,8,768]{0,2,1:T(8,128)(2,1)} %bitcast.209), calls=%async_computation | async-start | bytes 6291456 | tf_op jit(solution)/shard_map/all_to_all | solution.py:163
  74.5 64.9 %all-to-all-start.1 = ((bf16[256,8,768]{0,2,1:T(8,128)(2,1)}), bf16[256,8,768]{0,2,1:T(8,128)(2,1)}, u32[]{:S(2)}, u32[]{:S(2)}) async-start(bf16[256,8,768]{0,2,1:T(8,128)(2,1)} %bitcast.208), calls=%async_computation.1 | async-start | bytes 6291456 | tf_op jit(solution)/shard_map/all_to_all | solution.py:164
  79.1 251.1 %all-gather.15.cloned.1.call-start = ((), (), s32[]{:S(2)}) async-start(), calls=%async_computation.15 | async-start | bytes 14155776 | tf_op jit(solution)/shard_map/all_gather | solution.py:202
  134.5 120.3 %copy-start.58 = (f32[1,2048]{1,0:T(1,128)}, f32[1,2048]{1,0:T(1,128)S(1)}, u32[]{:S(2)}) copy-start(f32[1,2048]{1,0:T(1,128)S(1)} %get-tuple-element.109) | copy-start | bytes 24580
  258.0 146.5 %all-gather.17.cloned.1.call-start = ((), (), s32[]{:S(2)}) async-start(), calls=%async_computation.16 | async-start | bytes 14155776 | tf_op jit(solution)/shard_map/all_gather | solution.py:215
  265.3 376.9 %reduce-scatter.7.cloned.1.call-start = ((), (), s32[]{:S(2)}) async-start(), calls=%async_computation.17 | async-start | bytes 14155776 | tf_op jit(solution)/shard_map/reduce_scatter | solution.py:226
  463.1 387.4 %reduce-scatter.9.cloned.1.call-start = ((), (), s32[]{:S(2)}) async-start(), calls=%async_computation.18 | async-start | bytes 14155776 | tf_op jit(solution)/shard_map/reduce_scatter | solution.py:210
  481.6 70.3 %all-to-all-start.3 = ((bf16[8,256,768]{1,2,0:T(8,128)(2,1)}), bf16[8,256,768]{1,2,0:T(8,128)(2,1)S(1)}, u32[]{:S(2)}, u32[]{:S(2)}) async-start(bf16[8,256,768]{1,2,0:T(8,128)(2,1)} %copy.184), calls=%async_computation.3 | async-start | bytes 6291456 | tf_op jit(solution)/shard_map/all_to_all | solution.py:237
  551.9 59.2 %all-to-all-start.2 = ((bf16[8,256,768]{1,2,0:T(8,128)(2,1)}), bf16[8,256,768]{1,2,0:T(8,128)(2,1)}, u32[]{:S(2)}, u32[]{:S(2)}) async-start(bf16[8,256,768]{1,2,0:T(8,128)(2,1)} %copy.183), calls=%async_computation.2 | async-start | bytes 6291456 | tf_op jit(solution)/shard_map/all_to_all | solution.py:236
  556.4 452.7 %reduce-scatter.15.cloned.1.call-start = ((), (), s32[]{:S(2)}) async-start(), calls=%async_computation.21 | async-start | bytes 4718592 | tf_op jit(solution)/shard_map/reduce_scatter | solution.py:347
  627.7 31.0 %collective-permute-start = (bf16[96,6144]{1,0:T(8,128)(2,1)}, bf16[96,6144]{1,0:T(8,128)(2,1)}, u32[]{:S(2)}, u32[]{:S(2)}) collective-permute-start(bf16[96,6144]{1,0:T(8,128)(2,1)} %dynamic-slice_bitcast_fusion.1), channel_id=1, source_target_pairs={{0,1},{1,2},{2,3},{3,0},{4,5},{5,6},{6,7},{7,4},{8,9},{9,10},{10,1... | collective-permute-start | bytes 3538952 | tf_op jit(solution)/shard_map/ppermute | solution.py:91
  639.6 39.9 %collective-permute-start.1 = (bf16[96,6144]{1,0:T(8,128)(2,1)}, bf16[96,6144]{1,0:T(8,128)(2,1)}, u32[]{:S(2)}, u32[]{:S(2)}) collective-permute-start(bf16[96,6144]{1,0:T(8,128)(2,1)} %dynamic-slice_bitcast_fusion), channel_id=1, source_target_pairs={{0,3},{1,0},{2,1},{3,2},{4,7},{5,4},{6,5},{7,6},{8,11},{9,8},{10,9... | collective-permute-start | bytes 3538952 | tf_op jit(solution)/shard_map/ppermute | solution.py:92
  682.4 31.0 %collective-permute-start.2 = (bf16[96,6144]{1,0:T(8,128)(2,1)}, bf16[96,6144]{1,0:T(8,128)(2,1)}, u32[]{:S(2)}, u32[]{:S(2)}) collective-permute-start(bf16[96,6144]{1,0:T(8,128)(2,1)} %fusion.34), channel_id=1, source_target_pairs={{0,1},{1,2},{2,3},{3,0},{4,5},{5,6},{6,7},{7,4},{8,9},{9,10},{10,1... | collective-permute-start | bytes 3538952 | tf_op jit(solution)/shard_map/ppermute | solution.py:91
  686.0 51.8 %collective-permute-start.3 = (bf16[96,6144]{1,0:T(8,128)(2,1)}, bf16[96,6144]{1,0:T(8,128)(2,1)}, u32[]{:S(2)}, u32[]{:S(2)}) collective-permute-start(bf16[96,6144]{1,0:T(8,128)(2,1)} %fusion.33), channel_id=1, source_target_pairs={{0,3},{1,0},{2,1},{3,2},{4,7},{5,4},{6,5},{7,6},{8,11},{9,8},{10,9... | collective-permute-start | bytes 3538952 | tf_op jit(solution)/shard_map/ppermute | solution.py:92
  746.7 262.4 %reduce-scatter.13.cloned.1.call-start = ((), (), s32[]{:S(2)}) async-start(), calls=%async_computation.20 | async-start | bytes 4718592 | tf_op jit(solution)/shard_map/reduce_scatter | solution.py:347
  748.9 30.7 %collective-permute-start.4 = (bf16[96,6144]{1,0:T(8,128)(2,1)S(1)}, bf16[96,6144]{1,0:T(8,128)(2,1)S(1)}, u32[]{:S(2)}, u32[]{:S(2)}) collective-permute-start(bf16[96,6144]{1,0:T(8,128)(2,1)S(1)} %fusion.32), channel_id=1, source_target_pairs={{0,1},{1,2},{2,3},{3,0},{4,5},{5,6},{6,7},{7,4},{8,9},{9,10},{10,1... | collective-permute-start | bytes 3538952 | tf_op jit(solution)/shard_map/ppermute | solution.py:91
  751.4 52.5 %collective-permute-start.5 = (bf16[96,6144]{1,0:T(8,128)(2,1)S(1)}, bf16[96,6144]{1,0:T(8,128)(2,1)S(1)}, u32[]{:S(2)}, u32[]{:S(2)}) collective-permute-start(bf16[96,6144]{1,0:T(8,128)(2,1)S(1)} %fusion.31), channel_id=1, source_target_pairs={{0,3},{1,0},{2,1},{3,2},{4,7},{5,4},{6,5},{7,6},{8,11},{9,8},{10,9... | collective-permute-start | bytes 3538952 | tf_op jit(solution)/shard_map/ppermute | solution.py:92
  812.8 196.2 %reduce-scatter.17.cloned.1.call-start = ((), (), s32[]{:S(2)}) async-start(), calls=%async_computation.22 | async-start | bytes 9437184 | tf_op jit(solution)/shard_map/reduce_scatter | solution.py:347
  822.9 190.8 %reduce-scatter.11.cloned.1.call-start = ((), (), s32[]{:S(2)}) async-start(), calls=%async_computation.19 | async-start | bytes 9437184 | tf_op jit(solution)/shard_map/reduce_scatter | solution.py:347
  829.2 31.0 %collective-permute-start.6 = (bf16[96,6144]{1,0:T(8,128)(2,1)}, bf16[96,6144]{1,0:T(8,128)(2,1)}, u32[]{:S(2)}, u32[]{:S(2)}) collective-permute-start(bf16[96,6144]{1,0:T(8,128)(2,1)} %get-tuple-element.86), channel_id=1, source_target_pairs={{0,1},{1,2},{2,3},{3,0},{4,5},{5,6},{6,7},{7,4},{8,9},{9,10},{10,1... | collective-permute-start | bytes 3538952 | tf_op jit(solution)/shard_map/ppermute | solution.py:91
  833.1 51.4 %collective-permute-start.7 = (bf16[96,6144]{1,0:T(8,128)(2,1)}, bf16[96,6144]{1,0:T(8,128)(2,1)}, u32[]{:S(2)}, u32[]{:S(2)}) collective-permute-start(bf16[96,6144]{1,0:T(8,128)(2,1)} %get-tuple-element.88), channel_id=1, source_target_pairs={{0,3},{1,0},{2,1},{3,2},{4,7},{5,4},{6,5},{7,6},{8,11},{9,8},{10,9... | collective-permute-start | bytes 3538952 | tf_op jit(solution)/shard_map/ppermute | solution.py:92
  884.5 31.0 %collective-permute-start.8 = (bf16[96,6144]{1,0:T(8,128)(2,1)}, bf16[96,6144]{1,0:T(8,128)(2,1)}, u32[]{:S(2)}, u32[]{:S(2)}) collective-permute-start(bf16[96,6144]{1,0:T(8,128)(2,1)} %collective-permute-done.6), channel_id=1, source_target_pairs={{0,1},{1,2},{2,3},{3,0},{4,5},{5,6},{6,7},{7,4},{8,9},{9,10},{10,1... | collective-permute-start | bytes 3538952 | tf_op jit(solution)/shard_map/ppermute | solution.py:91
  885.0 53.2 %collective-permute-start.9 = (bf16[96,6144]{1,0:T(8,128)(2,1)}, bf16[96,6144]{1,0:T(8,128)(2,1)}, u32[]{:S(2)}, u32[]{:S(2)}) collective-permute-start(bf16[96,6144]{1,0:T(8,128)(2,1)} %collective-permute-done.7), channel_id=1, source_target_pairs={{0,3},{1,0},{2,1},{3,2},{4,7},{5,4},{6,5},{7,6},{8,11},{9,8},{10,9... | collective-permute-start | bytes 3538952 | tf_op jit(solution)/shard_map/ppermute | solution.py:92
  938.2 57.6 %collective-permute-start.10 = (bf16[96,6144]{1,0:T(8,128)(2,1)}, bf16[96,6144]{1,0:T(8,128)(2,1)}, u32[]{:S(2)}, u32[]{:S(2)}) collective-permute-start(bf16[96,6144]{1,0:T(8,128)(2,1)} %collective-permute-done.8), channel_id=1, source_target_pairs={{0,1},{1,2},{2,3},{3,0},{4,5},{5,6},{6,7},{7,4},{8,9},{9,10},{10,1... | collective-permute-start | bytes 3538952 | tf_op jit(solution)/shard_map/ppermute | solution.py:91
  938.5 57.3 %collective-permute-start.11 = (bf16[96,6144]{1,0:T(8,128)(2,1)}, bf16[96,6144]{1,0:T(8,128)(2,1)}, u32[]{:S(2)}, u32[]{:S(2)}) collective-permute-start(bf16[96,6144]{1,0:T(8,128)(2,1)} %collective-permute-done.9), channel_id=1, source_target_pairs={{0,3},{1,0},{2,1},{3,2},{4,7},{5,4},{6,5},{7,6},{8,11},{9,8},{10,9... | collective-permute-start | bytes 3538952 | tf_op jit(solution)/shard_map/ppermute | solution.py:92
  947.1 17.6 %all-to-all-start.4 = ((f32[8,256,3]{1,2,0:T(4,128)}), f32[8,256,3]{1,2,0:T(4,128)S(1)}, u32[]{:S(2)}, u32[]{:S(2)}) async-start(f32[8,256,3]{1,2,0:T(4,128)} %copy.194), calls=%async_computation.6 | async-start | bytes 65536 | tf_op jit(solution)/shard_map/all_to_all | solution.py:337
  952.2 185.2 %all-reduce.3.cloned.1.call-start = ((), (), s32[]{:S(2)}) async-start(), calls=%async_computation.23 | async-start | bytes 6291456 | tf_op jit(solution)/shard_map/psum | solution.py:358
  (83 other events, 969.0 us)
Sparse Core Ops, SparseCore 0:
  9.9 64.1 all-gather.8
  76.0 59.1 all-gather.6
  137.0 53.5 all-gather.10
  192.4 54.2 all-gather.12
  258.1 71.9 all-gather.14
  332.5 71.9 all-gather.16
  463.2 140.1 reduce-scatter.6
  606.9 100.7 reduce-scatter.8
  746.8 50.8 reduce-scatter.14
  813.0 50.8 reduce-scatter.12
  867.4 71.4 reduce-scatter.16
  942.2 71.4 reduce-scatter.10
  1016.3 121.0 all-reduce.2

commit v12 on v10

--- a/solution.py
+++ b/solution.py
@@ -334,8 +334,8 @@
         ],
         axis=1,
     )
-    key_width = key_grad.shape[1]
-    key_grad = jnp.concatenate([key_grad, gain_cols], axis=1)
+    gain_parts = lax.all_to_all(gain_cols, "fsdp", 0, 1, tiled=True)
+    gain_part = gain_parts.reshape(gain_share, fsdp_count, gain_cols.shape[1]).sum(axis=1)
 
     def low_sum(v):
         return lax.psum_scatter(v.astype(jnp.bfloat16), "fsdp", scatter_dimension=0, tiled=True)
@@ -343,19 +343,13 @@
     attention_parts = (
         None, low_sum(query_grad), low_sum(key_grad), low_sum(value_grad), low_sum(output_grad)
     )
-    finals = (
-        None,
-        feed_rep[0],
-        feed_rep[1],
-        feed_rep[2],
-        None,
-        lax.psum(attention_parts[1].astype(jnp.bfloat16), "rep").astype(jnp.float32),
-        lax.psum(attention_parts[2].astype(jnp.bfloat16), "rep").astype(jnp.float32),
-        lax.psum(attention_parts[3].astype(jnp.bfloat16), "rep").astype(jnp.float32),
-        lax.psum(attention_parts[4].astype(jnp.bfloat16), "rep").astype(jnp.float32),
-    )
-    key_rep = finals[6]
-    gain_rep = key_rep[:, key_width:]
+    finals = (None, feed_rep[0], feed_rep[1], feed_rep[2], None)
+    attention_rep = lax.psum(
+        tuple(attention_parts[i].astype(jnp.bfloat16) for i in (1, 2, 3, 4)), "rep"
+    )
+    gain_part, attention_rep = lax.optimization_barrier((gain_part, attention_rep))
+    finals = finals + tuple(r.astype(jnp.float32) for r in attention_rep)
+    gain_rep = lax.psum(gain_part.astype(jnp.bfloat16), "rep").astype(jnp.float32)
     attention_gain_out = gain_rep[:, 0]
     feed_gain_out = gain_rep[:, 1]
     head_sum = gain_rep[:, 2:].T.reshape(-1)
@@ -366,7 +360,7 @@
         input_grad,
         attention_gain_out,
         finals[5],
-        key_rep[:, :key_width],
+        finals[6],
         finals[7],
         query_gain_out,
         key_gain_out,

time: 1290 us -> 1170 us (0.907)
  waiting for transfers between devices: 665 us -> 557 us
  local copies, waits for them, and re-layouts: 151 us -> 130 us
    reduce_scatter x4, waiting for transfers between devices: 114 us -> 8.35 us  [low_sum(): lax.psum_scatter(v.astype(jnp.bfloat16), 'fsdp', scatter_dimension=0, til...]
    concatenate x1 -> x3, local copies, waits for them, and re-layouts: 18.5 us -> 0.64 us  [per_device(): jnp.concatenate([attention_gain_grad[:, None], feed_gain_grad[:, None], j...]
    reduce_scatter x1, waiting for transfers between devices: 16.9 us -> 0.01 us  [per_device(): lax.psum_scatter(down_part.astype(jnp.bfloat16), 'fsdp', scatter_dimensio...]
    unnamed x159 -> x174, local copies, waits for them, and re-layouts: 35.6 us -> 35.3 us
  transfers between devices with their start and end apart: 29 -> 30, of which waited for: 22 -> 21; matrix products, arithmetic and copies ran while one was open for 31% -> 32% of each run, Pallas kernels for 0% -> 0%
where the time goes in v12:
time: 1170 us; the launch traced here: 1160 us
  waiting for transfers between devices  557 us (48%)
  matrix products  247 us (21%)
  local copies, waits for them, and re-layouts  130 us (11%)
  other arithmetic  99.4 us (8%)
  blocking collectives  62.2 us (5%)
  starting transfers between devices  48.2 us (4%)
  between operations  17.1 us (1%)
    ppermute x6, waiting for transfers between devices, issue(): lax.ppermute(sends[1], self.axis, self.backward)  139 us
    psum x1, waiting for transfers between devices, per_device(): lax.psum(tuple((attention_parts[i].astype(jnp.bfloat16) for i in (1, 2, 3...  89.2 us
    dot_general x7, matrix products, times_transposed(): lax.dot_general(left, right, (((1,), (1,)), ((), ())), preferred_element_...  74.9 us
    dot_general x7, matrix products, inner_rows(): lax.dot_general(left, right, (((0,), (0,)), ((), ())), preferred_element_...  70.6 us
    all_gather x1, waiting for transfers between devices, per_device(): lax.all_gather(normed_two_low, 'fsdp', axis=0, tiled=True)  64.8 us
    ppermute x6, waiting for transfers between devices, issue(): lax.ppermute(sends[0], self.axis, self.forward)  58.2 us
    all_gather x1, blocking collectives, per_device(): lax.all_gather(jnp.stack([attention_gain, feed_gain]), 'fsdp', axis=1, ti...  52.8 us
    all_to_all x1, waiting for transfers between devices, per_device(): gate_block = lax.all_to_all(gate_weight, 'fsdp', 1, 0, tiled=True)  50 us
  transfers between devices with their start and end apart: 30, of which 21 were waited for; matrix products, arithmetic and copies ran while one was open for 32% of the time, Pallas kernels for 0%

profile of v12, /device:TPU:0, one launch (start us, length us, event | category | flops | bytes accessed | tf_op | source)
XLA Modules:
  0.0 1161.4 jit_solution(9063562388134565982)
XLA Ops:
  24.5 50.0 %all-to-all-done = bf16[256,8,768]{0,2,1:T(8,128)(2,1)} async-done(((bf16[256,8,768]{0,2,1:T(8,128)(2,1)}), bf16[256,8,768]{0,2,1:T(8,128)(2,1)}, u32[]{:S(2)}, u32[]{:S(2)}) %all-to-all-start) | async-done | bytes 3145760 | tf_op jit(solution)/shard_map/all_to_all | solution.py:163
  80.2 52.8 %all_gather.21 = bf16[2,2048]{1,0:T(2,128)(2,1)S(1)} all-gather(bf16[2,256]{1,0:T(2,128)(2,1)S(1)} %pad_maximum_fusion.5), channel_id=1, replica_groups=mesh['fsdp'=8,'rep'=4] {'fsdp'}, dimensions={1}, use_global_device_ids=true | all-gather | bytes 9216 | tf_op jit(solution)/shard_map/all_gather | solution.py:155
  167.6 23.0 %all-gather.11.cloned.1.call-done = bf16[2048,2048]{1,0:T(8,128)(2,1)} async-done(((bf16[256,2048]{1,0:T(8,128)(2,1)}), bf16[2048,2048]{1,0:T(8,128)(2,1)}) %all-gather.11.cloned.1.call-update) | async-done | bytes 8388624 | tf_op jit(solution)/shard_map/all_gather | solution.py:158
  190.6 10.2 multiply_reduce_fusion.3
  217.7 29.0 %all-gather.13.cloned.1.call-done = bf16[2048,2048]{1,0:T(8,128)(2,1)} async-done(((bf16[256,2048]{1,0:T(8,128)(2,1)}), bf16[2048,2048]{1,0:T(8,128)(2,1)}) %all-gather.13.cloned.1.call-update) | async-done | bytes 8388624 | tf_op jit(solution)/shard_map/all_gather | solution.py:161
  265.4 64.8 %all-gather.15.cloned.1.call-done = bf16[3072,2048]{1,0:T(8,128)(2,1)} async-done(((bf16[384,2048]{1,0:T(8,128)(2,1)}), bf16[3072,2048]{1,0:T(8,128)(2,1)}) %all-gather.15.cloned.1.call-update) | async-done | bytes 12582928 | tf_op jit(solution)/shard_map/all_gather | solution.py:202
  330.1 16.3 %fusion.68 = f32[3072,768]{1,0:T(8,128)} fusion(bf16[3072,2048]{1,0:T(8,128)(2,1)} %all-gather.15.cloned.1.call-done, bf16[2048,768]{1,0:T(8,128)(2,1)} %bitcast.214), kind=kOutput, calls=%fused_computation.151 | convolution fusion | flops 9663676416 | bytes 25165824 | tf_op jit(solution)/shard_map/dot_general | solution.py:203
  346.5 17.6 %multiply_convert_fusion.2 = (bf16[3072,768]{1,0:T(8,128)(2,1)S(1)}, f32[3072,768]{1,0:T(8,128)}) fusion(f32[3072,768]{1,0:T(8,128)} %fusion.68, bf16[3072,2048]{1,0:T(8,128)(2,1)} %all-gather.15.cloned.1.call-done, bf16[2048,768]{1,0:T(8,128)(2,1)S(1)} %bitcast.216), kind=kOutput, calls=%fused_computation.13 | convolution fusion | flops 9677832192 | bytes 39321600 | tf_op jit(solution)/shard_map/dot_general | solution.py:204
  366.2 12.2 %fusion.69 = bf16[3072,2048]{1,0:T(8,128)(2,1)} fusion(bf16[3072,768]{1,0:T(8,128)(2,1)S(1)} %get-tuple-element.53, bf16[768,2048]{1,0:T(8,128)(2,1)S(1)} %copy-done), kind=kOutput, calls=%fused_computation.152 | convolution fusion | flops 9663676416 | bytes 20447232 | tf_op jit(solution)/shard_map/dot_general | solution.py:206
  378.5 26.0 %all-gather.17.cloned.1.call-done = bf16[3072,2048]{1,0:T(8,128)(2,1)} async-done(((bf16[384,2048]{1,0:T(8,128)(2,1)}), bf16[3072,2048]{1,0:T(8,128)(2,1)}) %all-gather.17.cloned.1.call-update) | async-done | bytes 12582928 | tf_op jit(solution)/shard_map/all_gather | solution.py:215
  404.5 22.2 %multiply_convert_fusion.1 = (bf16[3072,768]{1,0:T(8,128)(2,1)}, bf16[3072,768]{1,0:T(8,128)(2,1)}) fusion(f32[3072,768]{1,0:T(8,128)} %fusion.68, f32[3072,768]{1,0:T(8,128)} %get-tuple-element.51, bf16[3072,2048]{1,0:T(8,128)(2,1)} %all-gather.17.cloned.1.call-done, bf16[768,2048]{1,0:T(8,128)(2,1)S(1)} %copy-done), kind=kOutput, calls=%fused_computation.11 | convolution fusion | flops 9694347264 | bytes 44040192 | tf_op jit(solution)/shard_map/dot_general | solution.py:52
  426.7 17.8 %fusion.70 = f32[3072,2048]{1,0:T(8,128)} fusion(bf16[3072,768]{1,0:T(8,128)(2,1)} %get-tuple-element.105, bf16[2048,768]{1,0:T(8,128)(2,1)} %bitcast.215), kind=kOutput, calls=%fused_computation.153 | convolution fusion | flops 9663676416 | bytes 33030144 | tf_op jit(solution)/shard_map/dot_general | solution.py:52
  444.5 18.5 %add_convert_fusion = bf16[3072,2048]{1,0:T(8,128)(2,1)} fusion(f32[3072,2048]{1,0:T(8,128)} %fusion.70, bf16[3072,768]{1,0:T(8,128)(2,1)} %get-tuple-element.106, bf16[2048,768]{1,0:T(8,128)(2,1)S(1)} %bitcast.217), kind=kOutput, calls=%fused_computation.1 | convolution fusion | flops 9676259328 | bytes 45613056 | tf_op jit(solution)/shard_map/dot_general | solution.py:52
  463.8 15.0 %convolution_convert_fusion.4 = bf16[2048,768]{1,0:T(8,128)(2,1)S(1)} fusion(bf16[3072,2048]{1,0:T(8,128)(2,1)} %all-gather.15.cloned.1.call-done, bf16[3072,768]{1,0:T(8,128)(2,1)} %get-tuple-element.106), kind=kOutput, calls=%fused_computation.37 | convolution fusion | flops 9665249280 | bytes 20447232 | tf_op jit(solution)/shard_map/dot_general | solution.py:46
  485.5 15.7 %convolution_convert_fusion.5 = bf16[2048,768]{1,0:T(8,128)(2,1)} fusion(bf16[3072,2048]{1,0:T(8,128)(2,1)} %all-gather.15.cloned.1.call-done, bf16[3072,768]{1,0:T(8,128)(2,1)} %get-tuple-element.105), kind=kOutput, calls=%fused_computation.38 | convolution fusion | flops 9665249280 | bytes 20447232 | tf_op jit(solution)/shard_map/dot_general | solution.py:46
  505.8 46.1 %all-to-all-done.3 = bf16[8,256,768]{1,2,0:T(8,128)(2,1)S(1)} async-done(((bf16[8,256,768]{1,2,0:T(8,128)(2,1)}), bf16[8,256,768]{1,2,0:T(8,128)(2,1)S(1)}, u32[]{:S(2)}, u32[]{:S(2)}) %all-to-all-start.3) | async-done | bytes 3145760 | tf_op jit(solution)/shard_map/all_to_all | solution.py:237
  564.7 15.5 %convolution_convert_fusion.6 = bf16[768,2048]{1,0:T(8,128)(2,1)} fusion(bf16[3072,768]{1,0:T(8,128)(2,1)} %copy-done.82, bf16[3072,2048]{1,0:T(8,128)(2,1)} %all-gather.17.cloned.1.call-done), kind=kOutput, calls=%fused_computation.39 | convolution fusion | flops 9665249280 | bytes 20447232 | tf_op jit(solution)/shard_map/dot_general | solution.py:46
  590.5 20.6 %all-to-all-done.2 = bf16[8,256,768]{1,2,0:T(8,128)(2,1)} async-done(((bf16[8,256,768]{1,2,0:T(8,128)(2,1)}), bf16[8,256,768]{1,2,0:T(8,128)(2,1)}, u32[]{:S(2)}, u32[]{:S(2)}) %all-to-all-start.2) | async-done | bytes 3145760 | tf_op jit(solution)/shard_map/all_to_all | solution.py:236
  658.7 20.8 %collective-permute-done.1 = bf16[96,6144]{1,0:T(8,128)(2,1)} collective-permute-done((bf16[96,6144]{1,0:T(8,128)(2,1)}, bf16[96,6144]{1,0:T(8,128)(2,1)}, u32[]{:S(2)}, u32[]{:S(2)}) %collective-permute-start.1) | collective-permute-done | bytes 1179680 | tf_op jit(solution)/shard_map/ppermute | solution.py:92
  692.2 13.6 %fusion.2 = bf16[8,2,384,384]{2,3,1,0:T(8,128)(2,1)} fusion(f32[8,384,384,2]{2,1,3,0:T(8,128)} %copy-done.2, f32[8,2,384]{2,1,0:T(2,128)S(1)} %bitcast.242, pred[384,384]{0,1:T(8,128)(4,1)S(1)} %copy-done.36, bf16[384,8,2,128]{0,3,2,1:T(8,128)(2,1)S(1)} %copy.192, bf16[384,8,128,1]{2,1,0,3:T(8,128)(2,1)} %bitcast.224), kind=kOutput, calls=%fused_computation.7 | convolution fusion | flops 1226840448 | bytes 16687104 | tf_op jit(solution)/shard_map/sub | solution.py:263
  713.4 24.3 %collective-permute-done.3 = bf16[96,6144]{1,0:T(8,128)(2,1)} collective-permute-done((bf16[96,6144]{1,0:T(8,128)(2,1)}, bf16[96,6144]{1,0:T(8,128)(2,1)}, u32[]{:S(2)}, u32[]{:S(2)}) %collective-permute-start.3) | collective-permute-done | bytes 1179680 | tf_op jit(solution)/shard_map/ppermute | solution.py:92
  759.3 20.3 %collective-permute-done.4 = bf16[96,6144]{1,0:T(8,128)(2,1)S(1)} collective-permute-done((bf16[96,6144]{1,0:T(8,128)(2,1)S(1)}, bf16[96,6144]{1,0:T(8,128)(2,1)S(1)}, u32[]{:S(2)}, u32[]{:S(2)}) %collective-permute-start.4) | collective-permute-done | bytes 1179680 | tf_op jit(solution)/shard_map/ppermute | solution.py:91
  779.6 24.3 %collective-permute-done.5 = bf16[96,6144]{1,0:T(8,128)(2,1)S(1)} collective-permute-done((bf16[96,6144]{1,0:T(8,128)(2,1)S(1)}, bf16[96,6144]{1,0:T(8,128)(2,1)S(1)}, u32[]{:S(2)}, u32[]{:S(2)}) %collective-permute-start.5) | collective-permute-done | bytes 1179680 | tf_op jit(solution)/shard_map/ppermute | solution.py:92
  860.2 24.3 %collective-permute-done.7 = bf16[96,6144]{1,0:T(8,128)(2,1)} collective-permute-done((bf16[96,6144]{1,0:T(8,128)(2,1)}, bf16[96,6144]{1,0:T(8,128)(2,1)}, u32[]{:S(2)}, u32[]{:S(2)}) %collective-permute-start.7) | collective-permute-done | bytes 1179680 | tf_op jit(solution)/shard_map/ppermute | solution.py:92
  898.4 17.1 %collective-permute-done.8 = bf16[96,6144]{1,0:T(8,128)(2,1)} collective-permute-done((bf16[96,6144]{1,0:T(8,128)(2,1)}, bf16[96,6144]{1,0:T(8,128)(2,1)}, u32[]{:S(2)}, u32[]{:S(2)}) %collective-permute-start.8) | collective-permute-done | bytes 1179680 | tf_op jit(solution)/shard_map/ppermute | solution.py:91
  915.5 22.7 %collective-permute-done.9 = bf16[96,6144]{1,0:T(8,128)(2,1)} collective-permute-done((bf16[96,6144]{1,0:T(8,128)(2,1)}, bf16[96,6144]{1,0:T(8,128)(2,1)}, u32[]{:S(2)}, u32[]{:S(2)}) %collective-permute-start.9) | collective-permute-done | bytes 1179680 | tf_op jit(solution)/shard_map/ppermute | solution.py:92
  969.2 22.5 %collective-permute-done.11 = bf16[96,6144]{1,0:T(8,128)(2,1)} collective-permute-done((bf16[96,6144]{1,0:T(8,128)(2,1)}, bf16[96,6144]{1,0:T(8,128)(2,1)}, u32[]{:S(2)}, u32[]{:S(2)}) %collective-permute-start.11) | collective-permute-done | bytes 1179680 | tf_op jit(solution)/shard_map/ppermute | solution.py:92
  996.5 8.9 pad_maximum_fusion
  1013.7 13.2 %bitcast_convert_fusion = f32[768,6144]{1,0:T(8,128)} fusion(bf16[2,4,96,6144]{3,2,1,0:T(8,128)(2,1)} %pad_maximum_fusion), kind=kLoop, calls=%fused_computation.3 | loop fusion | flops 4718592 | bytes 28311552 | tf_op jit(solution)/shard_map/convert_element_type | solution.py:121
  1026.9 13.9 %fusion.66 = (f32[256,6144]{1,0:T(8,128)}, f32[256,6144]{1,0:T(8,128)}, f32[256,6144]{1,0:T(8,128)}) fusion(f32[768,6144]{1,0:T(8,128)} %bitcast_convert_fusion), kind=kLoop, calls=%fused_computation.149 | loop fusion | bytes 37748736 | tf_op jit(solution)/shard_map/slice | solution.py:320
  1048.3 89.2 %all-reduce.3.cloned.1.call-done = (bf16[256,2048]{1,0:T(8,128)(2,1)}, bf16[256,1024]{1,0:T(8,128)(2,1)}, bf16[256,1024]{1,0:T(8,128)(2,1)}, bf16[256,2048]{1,0:T(8,128)(2,1)}) async-done(((bf16[256,2048]{1,0:T(8,128)(2,1)}, bf16[256,1024]{1,0:T(8,128)(2,1)}, bf16[256,1024]{1,0:T(8,128)(2,1)}, bf16[256,2048]{1,0:T(8,128)(2,1)}), (bf16[256,2048]{1,0:T(8,128)(2,1)}, bf16[256,1024]{1,0:T(8,128)(2,1)}, ...) | async-done | bytes 3145744 | tf_op jit(solution)/shard_map/psum | solution.py:347
  1137.4 9.4 psum.39
  (340 shorter events, 346.6 us)
Async XLA Ops:
  7.2 359.0 %copy-start = (bf16[768,2048]{1,0:T(8,128)(2,1)S(1)}, bf16[768,2048]{1,0:T(8,128)(2,1)}, u32[]{:S(2)}) copy-start(bf16[768,2048]{1,0:T(8,128)(2,1)} %param.28) | copy-start | bytes 9437188
  7.2 139.6 %all-gather.9.cloned.1.call-start = ((), (), s32[]{:S(2)}) async-start(), calls=%async_computation.12 | async-start | bytes 4718592 | tf_op jit(solution)/shard_map/all_gather | solution.py:159
  7.9 152.1 %all-gather.7.cloned.1.call-start = ((), (), s32[]{:S(2)}) async-start(), calls=%async_computation.11 | async-start | bytes 4718592 | tf_op jit(solution)/shard_map/all_gather | solution.py:160
  8.7 182.0 %all-gather.11.cloned.1.call-start = ((), (), s32[]{:S(2)}) async-start(), calls=%async_computation.13 | async-start | bytes 9437184 | tf_op jit(solution)/shard_map/all_gather | solution.py:158
  9.4 237.3 %all-gather.13.cloned.1.call-start = ((), (), s32[]{:S(2)}) async-start(), calls=%async_computation.14 | async-start | bytes 9437184 | tf_op jit(solution)/shard_map/all_gather | solution.py:161
  14.6 59.8 %all-to-all-start = ((bf16[256,8,768]{0,2,1:T(8,128)(2,1)}), bf16[256,8,768]{0,2,1:T(8,128)(2,1)}, u32[]{:S(2)}, u32[]{:S(2)}) async-start(bf16[256,8,768]{0,2,1:T(8,128)(2,1)} %bitcast.209), calls=%async_computation | async-start | bytes 6291456 | tf_op jit(solution)/shard_map/all_to_all | solution.py:163
  74.5 64.9 %all-to-all-start.1 = ((bf16[256,8,768]{0,2,1:T(8,128)(2,1)}), bf16[256,8,768]{0,2,1:T(8,128)(2,1)}, u32[]{:S(2)}, u32[]{:S(2)}) async-start(bf16[256,8,768]{0,2,1:T(8,128)(2,1)} %bitcast.208), calls=%async_computation.1 | async-start | bytes 6291456 | tf_op jit(solution)/shard_map/all_to_all | solution.py:164
  79.1 251.1 %all-gather.15.cloned.1.call-start = ((), (), s32[]{:S(2)}) async-start(), calls=%async_computation.15 | async-start | bytes 14155776 | tf_op jit(solution)/shard_map/all_gather | solution.py:202
  134.5 120.3 %copy-start.58 = (f32[1,2048]{1,0:T(1,128)}, f32[1,2048]{1,0:T(1,128)S(1)}, u32[]{:S(2)}) copy-start(f32[1,2048]{1,0:T(1,128)S(1)} %get-tuple-element.119) | copy-start | bytes 24580
  258.0 146.5 %all-gather.17.cloned.1.call-start = ((), (), s32[]{:S(2)}) async-start(), calls=%async_computation.16 | async-start | bytes 14155776 | tf_op jit(solution)/shard_map/all_gather | solution.py:215
  265.3 376.9 %reduce-scatter.7.cloned.1.call-start = ((), (), s32[]{:S(2)}) async-start(), calls=%async_computation.17 | async-start | bytes 14155776 | tf_op jit(solution)/shard_map/reduce_scatter | solution.py:226
  463.1 387.4 %reduce-scatter.9.cloned.1.call-start = ((), (), s32[]{:S(2)}) async-start(), calls=%async_computation.18 | async-start | bytes 14155776 | tf_op jit(solution)/shard_map/reduce_scatter | solution.py:210
  481.6 70.3 %all-to-all-start.3 = ((bf16[8,256,768]{1,2,0:T(8,128)(2,1)}), bf16[8,256,768]{1,2,0:T(8,128)(2,1)S(1)}, u32[]{:S(2)}, u32[]{:S(2)}) async-start(bf16[8,256,768]{1,2,0:T(8,128)(2,1)} %copy.184), calls=%async_computation.3 | async-start | bytes 6291456 | tf_op jit(solution)/shard_map/all_to_all | solution.py:237
  551.9 59.2 %all-to-all-start.2 = ((bf16[8,256,768]{1,2,0:T(8,128)(2,1)}), bf16[8,256,768]{1,2,0:T(8,128)(2,1)}, u32[]{:S(2)}, u32[]{:S(2)}) async-start(bf16[8,256,768]{1,2,0:T(8,128)(2,1)} %copy.183), calls=%async_computation.2 | async-start | bytes 6291456 | tf_op jit(solution)/shard_map/all_to_all | solution.py:236
  556.4 449.0 %reduce-scatter.15.cloned.1.call-start = ((), (), s32[]{:S(2)}) async-start(), calls=%async_computation.21 | async-start | bytes 4718592 | tf_op jit(solution)/shard_map/reduce_scatter | solution.py:341
  627.7 31.0 %collective-permute-start = (bf16[96,6144]{1,0:T(8,128)(2,1)}, bf16[96,6144]{1,0:T(8,128)(2,1)}, u32[]{:S(2)}, u32[]{:S(2)}) collective-permute-start(bf16[96,6144]{1,0:T(8,128)(2,1)} %dynamic-slice_bitcast_fusion.1), channel_id=1, source_target_pairs={{0,1},{1,2},{2,3},{3,0},{4,5},{5,6},{6,7},{7,4},{8,9},{9,10},{10,1... | collective-permute-start | bytes 3538952 | tf_op jit(solution)/shard_map/ppermute | solution.py:91
  639.6 39.9 %collective-permute-start.1 = (bf16[96,6144]{1,0:T(8,128)(2,1)}, bf16[96,6144]{1,0:T(8,128)(2,1)}, u32[]{:S(2)}, u32[]{:S(2)}) collective-permute-start(bf16[96,6144]{1,0:T(8,128)(2,1)} %dynamic-slice_bitcast_fusion), channel_id=1, source_target_pairs={{0,3},{1,0},{2,1},{3,2},{4,7},{5,4},{6,5},{7,6},{8,11},{9,8},{10,9... | collective-permute-start | bytes 3538952 | tf_op jit(solution)/shard_map/ppermute | solution.py:92
  682.4 31.0 %collective-permute-start.2 = (bf16[96,6144]{1,0:T(8,128)(2,1)}, bf16[96,6144]{1,0:T(8,128)(2,1)}, u32[]{:S(2)}, u32[]{:S(2)}) collective-permute-start(bf16[96,6144]{1,0:T(8,128)(2,1)} %fusion.34), channel_id=1, source_target_pairs={{0,1},{1,2},{2,3},{3,0},{4,5},{5,6},{6,7},{7,4},{8,9},{9,10},{10,1... | collective-permute-start | bytes 3538952 | tf_op jit(solution)/shard_map/ppermute | solution.py:91
  686.0 51.8 %collective-permute-start.3 = (bf16[96,6144]{1,0:T(8,128)(2,1)}, bf16[96,6144]{1,0:T(8,128)(2,1)}, u32[]{:S(2)}, u32[]{:S(2)}) collective-permute-start(bf16[96,6144]{1,0:T(8,128)(2,1)} %fusion.33), channel_id=1, source_target_pairs={{0,3},{1,0},{2,1},{3,2},{4,7},{5,4},{6,5},{7,6},{8,11},{9,8},{10,9... | collective-permute-start | bytes 3538952 | tf_op jit(solution)/shard_map/ppermute | solution.py:92
  746.7 258.7 %reduce-scatter.13.cloned.1.call-start = ((), (), s32[]{:S(2)}) async-start(), calls=%async_computation.20 | async-start | bytes 4718592 | tf_op jit(solution)/shard_map/reduce_scatter | solution.py:341
  748.9 30.7 %collective-permute-start.4 = (bf16[96,6144]{1,0:T(8,128)(2,1)S(1)}, bf16[96,6144]{1,0:T(8,128)(2,1)S(1)}, u32[]{:S(2)}, u32[]{:S(2)}) collective-permute-start(bf16[96,6144]{1,0:T(8,128)(2,1)S(1)} %fusion.32), channel_id=1, source_target_pairs={{0,1},{1,2},{2,3},{3,0},{4,5},{5,6},{6,7},{7,4},{8,9},{9,10},{10,1... | collective-permute-start | bytes 3538952 | tf_op jit(solution)/shard_map/ppermute | solution.py:91
  751.4 52.5 %collective-permute-start.5 = (bf16[96,6144]{1,0:T(8,128)(2,1)S(1)}, bf16[96,6144]{1,0:T(8,128)(2,1)S(1)}, u32[]{:S(2)}, u32[]{:S(2)}) collective-permute-start(bf16[96,6144]{1,0:T(8,128)(2,1)S(1)} %fusion.31), channel_id=1, source_target_pairs={{0,3},{1,0},{2,1},{3,2},{4,7},{5,4},{6,5},{7,6},{8,11},{9,8},{10,9... | collective-permute-start | bytes 3538952 | tf_op jit(solution)/shard_map/ppermute | solution.py:92
  812.8 192.5 %reduce-scatter.17.cloned.1.call-start = ((), (), s32[]{:S(2)}) async-start(), calls=%async_computation.22 | async-start | bytes 9437184 | tf_op jit(solution)/shard_map/reduce_scatter | solution.py:341
  822.9 190.8 %reduce-scatter.11.cloned.1.call-start = ((), (), s32[]{:S(2)}) async-start(), calls=%async_computation.19 | async-start | bytes 9437184 | tf_op jit(solution)/shard_map/reduce_scatter | solution.py:341
  829.2 31.0 %collective-permute-start.6 = (bf16[96,6144]{1,0:T(8,128)(2,1)}, bf16[96,6144]{1,0:T(8,128)(2,1)}, u32[]{:S(2)}, u32[]{:S(2)}) collective-permute-start(bf16[96,6144]{1,0:T(8,128)(2,1)} %get-tuple-element.96), channel_id=1, source_target_pairs={{0,1},{1,2},{2,3},{3,0},{4,5},{5,6},{6,7},{7,4},{8,9},{9,10},{10,1... | collective-permute-start | bytes 3538952 | tf_op jit(solution)/shard_map/ppermute | solution.py:91
  833.1 51.4 %collective-permute-start.7 = (bf16[96,6144]{1,0:T(8,128)(2,1)}, bf16[96,6144]{1,0:T(8,128)(2,1)}, u32[]{:S(2)}, u32[]{:S(2)}) collective-permute-start(bf16[96,6144]{1,0:T(8,128)(2,1)} %get-tuple-element.98), channel_id=1, source_target_pairs={{0,3},{1,0},{2,1},{3,2},{4,7},{5,4},{6,5},{7,6},{8,11},{9,8},{10,9... | collective-permute-start | bytes 3538952 | tf_op jit(solution)/shard_map/ppermute | solution.py:92
  884.5 31.0 %collective-permute-start.8 = (bf16[96,6144]{1,0:T(8,128)(2,1)}, bf16[96,6144]{1,0:T(8,128)(2,1)}, u32[]{:S(2)}, u32[]{:S(2)}) collective-permute-start(bf16[96,6144]{1,0:T(8,128)(2,1)} %collective-permute-done.6), channel_id=1, source_target_pairs={{0,1},{1,2},{2,3},{3,0},{4,5},{5,6},{6,7},{7,4},{8,9},{9,10},{10,1... | collective-permute-start | bytes 3538952 | tf_op jit(solution)/shard_map/ppermute | solution.py:91
  885.0 53.2 %collective-permute-start.9 = (bf16[96,6144]{1,0:T(8,128)(2,1)}, bf16[96,6144]{1,0:T(8,128)(2,1)}, u32[]{:S(2)}, u32[]{:S(2)}) collective-permute-start(bf16[96,6144]{1,0:T(8,128)(2,1)} %collective-permute-done.7), channel_id=1, source_target_pairs={{0,3},{1,0},{2,1},{3,2},{4,7},{5,4},{6,5},{7,6},{8,11},{9,8},{10,9... | collective-permute-start | bytes 3538952 | tf_op jit(solution)/shard_map/ppermute | solution.py:92
  938.2 31.0 %collective-permute-start.10 = (bf16[96,6144]{1,0:T(8,128)(2,1)}, bf16[96,6144]{1,0:T(8,128)(2,1)}, u32[]{:S(2)}, u32[]{:S(2)}) collective-permute-start(bf16[96,6144]{1,0:T(8,128)(2,1)} %collective-permute-done.8), channel_id=1, source_target_pairs={{0,1},{1,2},{2,3},{3,0},{4,5},{5,6},{6,7},{7,4},{8,9},{9,10},{10,1... | collective-permute-start | bytes 3538952 | tf_op jit(solution)/shard_map/ppermute | solution.py:91
  938.5 53.2 %collective-permute-start.11 = (bf16[96,6144]{1,0:T(8,128)(2,1)}, bf16[96,6144]{1,0:T(8,128)(2,1)}, u32[]{:S(2)}, u32[]{:S(2)}) collective-permute-start(bf16[96,6144]{1,0:T(8,128)(2,1)} %collective-permute-done.9), channel_id=1, source_target_pairs={{0,3},{1,0},{2,1},{3,2},{4,7},{5,4},{6,5},{7,6},{8,11},{9,8},{10,9... | collective-permute-start | bytes 3538952 | tf_op jit(solution)/shard_map/ppermute | solution.py:92
  947.1 17.6 %all-to-all-start.4 = ((f32[8,256,3]{1,2,0:T(4,128)}), f32[8,256,3]{1,2,0:T(4,128)S(1)}, u32[]{:S(2)}, u32[]{:S(2)}) async-start(f32[8,256,3]{1,2,0:T(4,128)} %copy.194), calls=%async_computation.6 | async-start | bytes 65536 | tf_op jit(solution)/shard_map/all_to_all | solution.py:337
  952.2 185.2 %all-reduce.3.cloned.1.call-start = ((), (), s32[]{:S(2)}) async-start(), calls=%async_computation.23 | async-start | bytes 6291456 | tf_op jit(solution)/shard_map/psum | solution.py:347
  (83 other events, 974.1 us)
Sparse Core Ops, SparseCore 0:
  9.9 64.1 all-gather.8
  76.0 59.1 all-gather.6
  137.0 53.5 all-gather.10
  192.4 54.2 all-gather.12
  258.1 71.9 all-gather.14
  332.5 71.9 all-gather.16
  463.2 140.1 reduce-scatter.6
  606.9 100.7 reduce-scatter.8
  746.8 50.8 reduce-scatter.14
  813.0 50.8 reduce-scatter.12
  867.4 71.4 reduce-scatter.16
  942.2 71.4 reduce-scatter.10
  1016.3 121.0 all-reduce.2

commit v13 on v11

--- a/solution.py
+++ b/solution.py
@@ -336,7 +336,11 @@
     )
     gain_parts = lax.all_to_all(gain_cols, "fsdp", 0, 1, tiled=True)
     gain_part = gain_parts.reshape(gain_share, fsdp_count, gain_cols.shape[1]).sum(axis=1)
-    gain_rep = lax.psum(gain_part.astype(jnp.bfloat16), "rep").astype(jnp.float32)
+    rep_count = lax.axis_size("rep")
+    rep_share = gain_share // rep_count
+    rep_parts = lax.all_to_all(gain_part, "rep", 0, 1, tiled=True)
+    rep_block = rep_parts.reshape(rep_share, rep_count, gain_part.shape[1]).sum(axis=1)
+    gain_rep = lax.all_to_all(jnp.tile(rep_block, (rep_count, 1)), "rep", 0, 0, tiled=True)
     attention_gain_out = gain_rep[:, 0]
     feed_gain_out = gain_rep[:, 1]
     head_sum = gain_rep[:, 2:].T.reshape(-1)

time: 1160 us -> 1160 us (level)
  blocking collectives: 82.8 us -> 52.8 us
  waiting for transfers between devices: 527 us -> 547 us
    psum x1 -> x0, blocking collectives: 30 us -> none  [per_device(): lax.psum(gain_part.astype(jnp.bfloat16), 'rep').astype(jnp.float32)]
    all_to_all x0 -> x2, waiting for transfers between devices: none -> 26.5 us  [the longest x1 24.3 us: per_device(): rep_parts = lax.all_to_all(gain_part, 'rep', 0, 1, tiled=True)]
    unnamed x174 -> x171, local copies, waits for them, and re-layouts: 35.3 us -> 35.9 us
  transfers between devices with their start and end apart: 30 -> 32, of which waited for: 19 -> 20; matrix products, arithmetic and copies ran while one was open for 33% -> 34% of each run, Pallas kernels for 0% -> 0%
where the time goes in v13:
time: 1160 us
  waiting for transfers between devices  547 us (47%)
  matrix products  252 us (22%)
  local copies, waits for them, and re-layouts  132 us (11%)
  other arithmetic  103 us (9%)
  starting transfers between devices  55 us (5%)
  blocking collectives  52.8 us (5%)
  between operations  17.2 us (1%)
    ppermute x6, waiting for transfers between devices, issue(): lax.ppermute(sends[1], self.axis, self.backward)  116 us
    psum x1, waiting for transfers between devices, per_device(): lax.psum(attention_parts[1].astype(jnp.bfloat16), 'rep').astype(jnp.float32)  88 us
    dot_general x7, matrix products, times_transposed(): lax.dot_general(left, right, (((1,), (1,)), ((), ())), preferred_element_...  80.1 us
    dot_general x7, matrix products, inner_rows(): lax.dot_general(left, right, (((0,), (0,)), ((), ())), preferred_element_...  70.7 us
    all_gather x1, waiting for transfers between devices, per_device(): lax.all_gather(normed_two_low, 'fsdp', axis=0, tiled=True)  64.8 us
    ppermute x6, waiting for transfers between devices, issue(): lax.ppermute(sends[0], self.axis, self.forward)  53.3 us
    all_gather x1, blocking collectives, per_device(): lax.all_gather(jnp.stack([attention_gain, feed_gain]), 'fsdp', axis=1, ti...  52.8 us
    all_to_all x1, waiting for transfers between devices, per_device(): gate_block = lax.all_to_all(gate_weight, 'fsdp', 1, 0, tiled=True)  50 us
  transfers between devices with their start and end apart: 32, of which 20 were waited for; matrix products, arithmetic and copies ran while one was open for 34% of the time, Pallas kernels for 0%

profile of v13, /device:TPU:0, one launch (start us, length us, event | category | flops | bytes accessed | tf_op | source)
XLA Modules:
  0.0 1158.5 jit_solution(7330527631976576897)
XLA Ops:
  24.5 50.0 %all-to-all-done = bf16[256,8,768]{0,2,1:T(8,128)(2,1)} async-done(((bf16[256,8,768]{0,2,1:T(8,128)(2,1)}), bf16[256,8,768]{0,2,1:T(8,128)(2,1)}, u32[]{:S(2)}, u32[]{:S(2)}) %all-to-all-start) | async-done | bytes 3145760 | tf_op jit(solution)/shard_map/all_to_all | solution.py:163
  80.2 52.8 %all_gather.21 = bf16[2,2048]{1,0:T(2,128)(2,1)S(1)} all-gather(bf16[2,256]{1,0:T(2,128)(2,1)S(1)} %pad_maximum_fusion.5), channel_id=1, replica_groups=mesh['fsdp'=8,'rep'=4] {'fsdp'}, dimensions={1}, use_global_device_ids=true | all-gather | bytes 9216 | tf_op jit(solution)/shard_map/all_gather | solution.py:155
  167.6 23.0 %all-gather.11.cloned.1.call-done = bf16[2048,2048]{1,0:T(8,128)(2,1)} async-done(((bf16[256,2048]{1,0:T(8,128)(2,1)}), bf16[2048,2048]{1,0:T(8,128)(2,1)}) %all-gather.11.cloned.1.call-update) | async-done | bytes 8388624 | tf_op jit(solution)/shard_map/all_gather | solution.py:158
  190.6 10.2 multiply_reduce_fusion.3
  217.7 28.9 %all-gather.13.cloned.1.call-done = bf16[2048,2048]{1,0:T(8,128)(2,1)} async-done(((bf16[256,2048]{1,0:T(8,128)(2,1)}), bf16[2048,2048]{1,0:T(8,128)(2,1)}) %all-gather.13.cloned.1.call-update) | async-done | bytes 8388624 | tf_op jit(solution)/shard_map/all_gather | solution.py:161
  265.3 64.8 %all-gather.15.cloned.1.call-done = bf16[3072,2048]{1,0:T(8,128)(2,1)} async-done(((bf16[384,2048]{1,0:T(8,128)(2,1)}), bf16[3072,2048]{1,0:T(8,128)(2,1)}) %all-gather.15.cloned.1.call-update) | async-done | bytes 12582928 | tf_op jit(solution)/shard_map/all_gather | solution.py:202
  330.1 16.3 %fusion.68 = f32[3072,768]{1,0:T(8,128)} fusion(bf16[3072,2048]{1,0:T(8,128)(2,1)} %all-gather.15.cloned.1.call-done, bf16[2048,768]{1,0:T(8,128)(2,1)} %bitcast.226), kind=kOutput, calls=%fused_computation.154 | convolution fusion | flops 9663676416 | bytes 25165824 | tf_op jit(solution)/shard_map/dot_general | solution.py:203
  346.4 17.6 %multiply_convert_fusion.2 = (bf16[3072,768]{1,0:T(8,128)(2,1)S(1)}, f32[3072,768]{1,0:T(8,128)}) fusion(f32[3072,768]{1,0:T(8,128)} %fusion.68, bf16[3072,2048]{1,0:T(8,128)(2,1)} %all-gather.15.cloned.1.call-done, bf16[2048,768]{1,0:T(8,128)(2,1)S(1)} %bitcast.228), kind=kOutput, calls=%fused_computation.13 | convolution fusion | flops 9677832192 | bytes 39321600 | tf_op jit(solution)/shard_map/dot_general | solution.py:204
  366.2 12.3 %fusion.69 = bf16[3072,2048]{1,0:T(8,128)(2,1)} fusion(bf16[3072,768]{1,0:T(8,128)(2,1)S(1)} %get-tuple-element.48, bf16[768,2048]{1,0:T(8,128)(2,1)S(1)} %copy-done), kind=kOutput, calls=%fused_computation.155 | convolution fusion | flops 9663676416 | bytes 20447232 | tf_op jit(solution)/shard_map/dot_general | solution.py:206
  378.5 26.0 %all-gather.17.cloned.1.call-done = bf16[3072,2048]{1,0:T(8,128)(2,1)} async-done(((bf16[384,2048]{1,0:T(8,128)(2,1)}), bf16[3072,2048]{1,0:T(8,128)(2,1)}) %all-gather.17.cloned.1.call-update) | async-done | bytes 12582928 | tf_op jit(solution)/shard_map/all_gather | solution.py:215
  404.5 22.2 %multiply_convert_fusion.1 = (bf16[3072,768]{1,0:T(8,128)(2,1)}, bf16[3072,768]{1,0:T(8,128)(2,1)}) fusion(f32[3072,768]{1,0:T(8,128)} %fusion.68, f32[3072,768]{1,0:T(8,128)} %get-tuple-element.46, bf16[3072,2048]{1,0:T(8,128)(2,1)} %all-gather.17.cloned.1.call-done, bf16[768,2048]{1,0:T(8,128)(2,1)S(1)} %copy-done), kind=kOutput, calls=%fused_computation.11 | convolution fusion | flops 9694347264 | bytes 44040192 | tf_op jit(solution)/shard_map/dot_general | solution.py:52
  426.7 17.8 %fusion.70 = f32[3072,2048]{1,0:T(8,128)} fusion(bf16[3072,768]{1,0:T(8,128)(2,1)} %get-tuple-element.95, bf16[2048,768]{1,0:T(8,128)(2,1)} %bitcast.227), kind=kOutput, calls=%fused_computation.156 | convolution fusion | flops 9663676416 | bytes 33030144 | tf_op jit(solution)/shard_map/dot_general | solution.py:52
  444.5 18.5 %add_convert_fusion = bf16[3072,2048]{1,0:T(8,128)(2,1)} fusion(f32[3072,2048]{1,0:T(8,128)} %fusion.70, bf16[3072,768]{1,0:T(8,128)(2,1)} %get-tuple-element.96, bf16[2048,768]{1,0:T(8,128)(2,1)S(1)} %bitcast.229), kind=kOutput, calls=%fused_computation.1 | convolution fusion | flops 9676259328 | bytes 45613056 | tf_op jit(solution)/shard_map/dot_general | solution.py:52
  463.8 15.0 %convolution_convert_fusion.4 = bf16[2048,768]{1,0:T(8,128)(2,1)S(1)} fusion(bf16[3072,2048]{1,0:T(8,128)(2,1)} %all-gather.15.cloned.1.call-done, bf16[3072,768]{1,0:T(8,128)(2,1)} %get-tuple-element.96), kind=kOutput, calls=%fused_computation.37 | convolution fusion | flops 9665249280 | bytes 20447232 | tf_op jit(solution)/shard_map/dot_general | solution.py:46
  485.5 15.7 %convolution_convert_fusion.5 = bf16[2048,768]{1,0:T(8,128)(2,1)} fusion(bf16[3072,2048]{1,0:T(8,128)(2,1)} %all-gather.15.cloned.1.call-done, bf16[3072,768]{1,0:T(8,128)(2,1)} %get-tuple-element.95), kind=kOutput, calls=%fused_computation.38 | convolution fusion | flops 9665249280 | bytes 20447232 | tf_op jit(solution)/shard_map/dot_general | solution.py:46
  505.8 46.1 %all-to-all-done.3 = bf16[8,256,768]{1,2,0:T(8,128)(2,1)S(1)} async-done(((bf16[8,256,768]{1,2,0:T(8,128)(2,1)}), bf16[8,256,768]{1,2,0:T(8,128)(2,1)S(1)}, u32[]{:S(2)}, u32[]{:S(2)}) %all-to-all-start.3) | async-done | bytes 3145760 | tf_op jit(solution)/shard_map/all_to_all | solution.py:237
  564.6 15.5 %convolution_convert_fusion.6 = bf16[768,2048]{1,0:T(8,128)(2,1)} fusion(bf16[3072,768]{1,0:T(8,128)(2,1)} %copy-done.80, bf16[3072,2048]{1,0:T(8,128)(2,1)} %all-gather.17.cloned.1.call-done), kind=kOutput, calls=%fused_computation.39 | convolution fusion | flops 9665249280 | bytes 20447232 | tf_op jit(solution)/shard_map/dot_general | solution.py:46
  590.5 20.5 %all-to-all-done.2 = bf16[8,256,768]{1,2,0:T(8,128)(2,1)} async-done(((bf16[8,256,768]{1,2,0:T(8,128)(2,1)}), bf16[8,256,768]{1,2,0:T(8,128)(2,1)}, u32[]{:S(2)}, u32[]{:S(2)}) %all-to-all-start.2) | async-done | bytes 3145760 | tf_op jit(solution)/shard_map/all_to_all | solution.py:236
  658.6 20.8 %collective-permute-done.1 = bf16[96,6144]{1,0:T(8,128)(2,1)} collective-permute-done((bf16[96,6144]{1,0:T(8,128)(2,1)}, bf16[96,6144]{1,0:T(8,128)(2,1)}, u32[]{:S(2)}, u32[]{:S(2)}) %collective-permute-start.1) | collective-permute-done | bytes 1179680 | tf_op jit(solution)/shard_map/ppermute | solution.py:92
  692.1 13.6 %fusion.2 = bf16[8,2,384,384]{2,3,1,0:T(8,128)(2,1)} fusion(f32[8,384,384,2]{2,1,3,0:T(8,128)} %copy-done.2, f32[8,2,384]{2,1,0:T(2,128)S(1)} %bitcast.254, pred[384,384]{0,1:T(8,128)(4,1)S(1)} %copy-done.34, bf16[384,8,2,128]{0,3,2,1:T(8,128)(2,1)S(1)} %copy.231, bf16[384,8,128,1]{2,1,0,3:T(8,128)(2,1)} %bitcast.236), kind=kOutput, calls=%fused_computation.7 | convolution fusion | flops 1226840448 | bytes 16687104 | tf_op jit(solution)/shard_map/sub | solution.py:263
  713.4 24.3 %collective-permute-done.3 = bf16[96,6144]{1,0:T(8,128)(2,1)} collective-permute-done((bf16[96,6144]{1,0:T(8,128)(2,1)}, bf16[96,6144]{1,0:T(8,128)(2,1)}, u32[]{:S(2)}, u32[]{:S(2)}) %collective-permute-start.3) | collective-permute-done | bytes 1179680 | tf_op jit(solution)/shard_map/ppermute | solution.py:92
  759.3 20.3 %collective-permute-done.4 = bf16[96,6144]{1,0:T(8,128)(2,1)S(1)} collective-permute-done((bf16[96,6144]{1,0:T(8,128)(2,1)S(1)}, bf16[96,6144]{1,0:T(8,128)(2,1)S(1)}, u32[]{:S(2)}, u32[]{:S(2)}) %collective-permute-start.4) | collective-permute-done | bytes 1179680 | tf_op jit(solution)/shard_map/ppermute | solution.py:91
  779.5 24.3 %collective-permute-done.5 = bf16[96,6144]{1,0:T(8,128)(2,1)S(1)} collective-permute-done((bf16[96,6144]{1,0:T(8,128)(2,1)S(1)}, bf16[96,6144]{1,0:T(8,128)(2,1)S(1)}, u32[]{:S(2)}, u32[]{:S(2)}) %collective-permute-start.5) | collective-permute-done | bytes 1179680 | tf_op jit(solution)/shard_map/ppermute | solution.py:92
  855.4 9.5 collective-permute-done.6
  864.9 24.3 %collective-permute-done.7 = bf16[96,6144]{1,0:T(8,128)(2,1)} collective-permute-done((bf16[96,6144]{1,0:T(8,128)(2,1)}, bf16[96,6144]{1,0:T(8,128)(2,1)}, u32[]{:S(2)}, u32[]{:S(2)}) %collective-permute-start.7) | collective-permute-done | bytes 1179680 | tf_op jit(solution)/shard_map/ppermute | solution.py:92
  906.9 13.4 %collective-permute-done.8 = bf16[96,6144]{1,0:T(8,128)(2,1)} collective-permute-done((bf16[96,6144]{1,0:T(8,128)(2,1)}, bf16[96,6144]{1,0:T(8,128)(2,1)}, u32[]{:S(2)}, u32[]{:S(2)}) %collective-permute-start.8) | collective-permute-done | bytes 1179680 | tf_op jit(solution)/shard_map/ppermute | solution.py:91
  920.3 22.7 %collective-permute-done.9 = bf16[96,6144]{1,0:T(8,128)(2,1)} collective-permute-done((bf16[96,6144]{1,0:T(8,128)(2,1)}, bf16[96,6144]{1,0:T(8,128)(2,1)}, u32[]{:S(2)}, u32[]{:S(2)}) %collective-permute-start.9) | collective-permute-done | bytes 1179680 | tf_op jit(solution)/shard_map/ppermute | solution.py:92
  972.8 24.3 %all-to-all-done.5 = f32[4,1,192]{2,1,0:T(1,128)S(1)} async-done(((f32[4,1,192]{2,1,0:T(1,128)}), f32[4,1,192]{2,1,0:T(1,128)S(1)}, u32[]{:S(2)}, u32[]{:S(2)}) %all-to-all-start.5) | async-done | bytes 3104 | tf_op jit(solution)/shard_map/all_to_all | solution.py:341
  1014.5 8.2 pad_maximum_fusion
  1022.8 12.8 %bitcast_convert_fusion = f32[768,6144]{1,0:T(8,128)} fusion(bf16[2,4,96,6144]{3,2,1,0:T(8,128)(2,1)} %pad_maximum_fusion), kind=kLoop, calls=%fused_computation.3 | loop fusion | flops 4718592 | bytes 28311552 | tf_op jit(solution)/shard_map/convert_element_type | solution.py:121
  1035.6 13.9 %fusion.66 = (f32[256,6144]{1,0:T(8,128)}, f32[256,6144]{1,0:T(8,128)}, f32[256,6144]{1,0:T(8,128)}) fusion(f32[768,6144]{1,0:T(8,128)} %bitcast_convert_fusion), kind=kLoop, calls=%fused_computation.149 | loop fusion | bytes 37748736 | tf_op jit(solution)/shard_map/slice | solution.py:320
  1057.0 88.0 %all-reduce.3.cloned.1.call-done = (bf16[256,2048]{1,0:T(8,128)(2,1)}, bf16[256,1024]{1,0:T(8,128)(2,1)}, bf16[256,1024]{1,0:T(8,128)(2,1)}, bf16[256,2048]{1,0:T(8,128)(2,1)}) async-done(((bf16[256,2048]{1,0:T(8,128)(2,1)}, bf16[256,1024]{1,0:T(8,128)(2,1)}, bf16[256,1024]{1,0:T(8,128)(2,1)}, bf16[256,2048]{1,0:T(8,128)(2,1)}), (bf16[256,2048]{1,0:T(8,128)(2,1)}, bf16[256,1024]{1,0:T(8,128)(2,1)}, ...) | async-done | bytes 3145744 | tf_op jit(solution)/shard_map/psum | solution.py:362
  (346 shorter events, 347.6 us)
Async XLA Ops:
  7.2 139.6 %all-gather.9.cloned.1.call-start = ((), (), s32[]{:S(2)}) async-start(), calls=%async_computation.14 | async-start | bytes 4718592 | tf_op jit(solution)/shard_map/all_gather | solution.py:159
  7.9 152.1 %all-gather.7.cloned.1.call-start = ((), (), s32[]{:S(2)}) async-start(), calls=%async_computation.13 | async-start | bytes 4718592 | tf_op jit(solution)/shard_map/all_gather | solution.py:160
  8.7 181.9 %all-gather.11.cloned.1.call-start = ((), (), s32[]{:S(2)}) async-start(), calls=%async_computation.15 | async-start | bytes 9437184 | tf_op jit(solution)/shard_map/all_gather | solution.py:158
  9.4 237.2 %all-gather.13.cloned.1.call-start = ((), (), s32[]{:S(2)}) async-start(), calls=%async_computation.16 | async-start | bytes 9437184 | tf_op jit(solution)/shard_map/all_gather | solution.py:161
  14.6 59.8 %all-to-all-start = ((bf16[256,8,768]{0,2,1:T(8,128)(2,1)}), bf16[256,8,768]{0,2,1:T(8,128)(2,1)}, u32[]{:S(2)}, u32[]{:S(2)}) async-start(bf16[256,8,768]{0,2,1:T(8,128)(2,1)} %bitcast.221), calls=%async_computation | async-start | bytes 6291456 | tf_op jit(solution)/shard_map/all_to_all | solution.py:163
  74.5 64.8 %all-to-all-start.1 = ((bf16[256,8,768]{0,2,1:T(8,128)(2,1)}), bf16[256,8,768]{0,2,1:T(8,128)(2,1)}, u32[]{:S(2)}, u32[]{:S(2)}) async-start(bf16[256,8,768]{0,2,1:T(8,128)(2,1)} %bitcast.220), calls=%async_computation.1 | async-start | bytes 6291456 | tf_op jit(solution)/shard_map/all_to_all | solution.py:164
  79.1 251.1 %all-gather.15.cloned.1.call-start = ((), (), s32[]{:S(2)}) async-start(), calls=%async_computation.17 | async-start | bytes 14155776 | tf_op jit(solution)/shard_map/all_gather | solution.py:202
  258.0 146.5 %all-gather.17.cloned.1.call-start = ((), (), s32[]{:S(2)}) async-start(), calls=%async_computation.18 | async-start | bytes 14155776 | tf_op jit(solution)/shard_map/all_gather | solution.py:215
  265.3 376.9 %reduce-scatter.7.cloned.1.call-start = ((), (), s32[]{:S(2)}) async-start(), calls=%async_computation.19 | async-start | bytes 14155776 | tf_op jit(solution)/shard_map/reduce_scatter | solution.py:226
  463.0 361.1 %reduce-scatter.9.cloned.1.call-start = ((), (), s32[]{:S(2)}) async-start(), calls=%async_computation.20 | async-start | bytes 14155776 | tf_op jit(solution)/shard_map/reduce_scatter | solution.py:210
  481.6 70.3 %all-to-all-start.3 = ((bf16[8,256,768]{1,2,0:T(8,128)(2,1)}), bf16[8,256,768]{1,2,0:T(8,128)(2,1)S(1)}, u32[]{:S(2)}, u32[]{:S(2)}) async-start(bf16[8,256,768]{1,2,0:T(8,128)(2,1)} %copy.223), calls=%async_computation.3 | async-start | bytes 6291456 | tf_op jit(solution)/shard_map/all_to_all | solution.py:237
  551.9 59.1 %all-to-all-start.2 = ((bf16[8,256,768]{1,2,0:T(8,128)(2,1)}), bf16[8,256,768]{1,2,0:T(8,128)(2,1)}, u32[]{:S(2)}, u32[]{:S(2)}) async-start(bf16[8,256,768]{1,2,0:T(8,128)(2,1)} %copy.222), calls=%async_computation.2 | async-start | bytes 6291456 | tf_op jit(solution)/shard_map/all_to_all | solution.py:236
  556.3 466.4 %reduce-scatter.15.cloned.1.call-start = ((), (), s32[]{:S(2)}) async-start(), calls=%async_computation.23 | async-start | bytes 4718592 | tf_op jit(solution)/shard_map/reduce_scatter | solution.py:351
  627.6 31.0 %collective-permute-start = (bf16[96,6144]{1,0:T(8,128)(2,1)}, bf16[96,6144]{1,0:T(8,128)(2,1)}, u32[]{:S(2)}, u32[]{:S(2)}) collective-permute-start(bf16[96,6144]{1,0:T(8,128)(2,1)} %dynamic-slice_bitcast_fusion.1), channel_id=1, source_target_pairs={{0,1},{1,2},{2,3},{3,0},{4,5},{5,6},{6,7},{7,4},{8,9},{9,10},{10,1... | collective-permute-start | bytes 3538952 | tf_op jit(solution)/shard_map/ppermute | solution.py:91
  639.5 39.9 %collective-permute-start.1 = (bf16[96,6144]{1,0:T(8,128)(2,1)}, bf16[96,6144]{1,0:T(8,128)(2,1)}, u32[]{:S(2)}, u32[]{:S(2)}) collective-permute-start(bf16[96,6144]{1,0:T(8,128)(2,1)} %dynamic-slice_bitcast_fusion), channel_id=1, source_target_pairs={{0,3},{1,0},{2,1},{3,2},{4,7},{5,4},{6,5},{7,6},{8,11},{9,8},{10,9... | collective-permute-start | bytes 3538952 | tf_op jit(solution)/shard_map/ppermute | solution.py:92
  682.4 31.0 %collective-permute-start.2 = (bf16[96,6144]{1,0:T(8,128)(2,1)}, bf16[96,6144]{1,0:T(8,128)(2,1)}, u32[]{:S(2)}, u32[]{:S(2)}) collective-permute-start(bf16[96,6144]{1,0:T(8,128)(2,1)} %fusion.34), channel_id=1, source_target_pairs={{0,1},{1,2},{2,3},{3,0},{4,5},{5,6},{6,7},{7,4},{8,9},{9,10},{10,1... | collective-permute-start | bytes 3538952 | tf_op jit(solution)/shard_map/ppermute | solution.py:91
  685.9 51.8 %collective-permute-start.3 = (bf16[96,6144]{1,0:T(8,128)(2,1)}, bf16[96,6144]{1,0:T(8,128)(2,1)}, u32[]{:S(2)}, u32[]{:S(2)}) collective-permute-start(bf16[96,6144]{1,0:T(8,128)(2,1)} %fusion.33), channel_id=1, source_target_pairs={{0,3},{1,0},{2,1},{3,2},{4,7},{5,4},{6,5},{7,6},{8,11},{9,8},{10,9... | collective-permute-start | bytes 3538952 | tf_op jit(solution)/shard_map/ppermute | solution.py:92
  746.6 276.1 %reduce-scatter.13.cloned.1.call-start = ((), (), s32[]{:S(2)}) async-start(), calls=%async_computation.22 | async-start | bytes 4718592 | tf_op jit(solution)/shard_map/reduce_scatter | solution.py:351
  748.8 30.7 %collective-permute-start.4 = (bf16[96,6144]{1,0:T(8,128)(2,1)S(1)}, bf16[96,6144]{1,0:T(8,128)(2,1)S(1)}, u32[]{:S(2)}, u32[]{:S(2)}) collective-permute-start(bf16[96,6144]{1,0:T(8,128)(2,1)S(1)} %fusion.32), channel_id=1, source_target_pairs={{0,1},{1,2},{2,3},{3,0},{4,5},{5,6},{6,7},{7,4},{8,9},{9,10},{10,1... | collective-permute-start | bytes 3538952 | tf_op jit(solution)/shard_map/ppermute | solution.py:91
  751.3 52.5 %collective-permute-start.5 = (bf16[96,6144]{1,0:T(8,128)(2,1)S(1)}, bf16[96,6144]{1,0:T(8,128)(2,1)S(1)}, u32[]{:S(2)}, u32[]{:S(2)}) collective-permute-start(bf16[96,6144]{1,0:T(8,128)(2,1)S(1)} %fusion.31), channel_id=1, source_target_pairs={{0,3},{1,0},{2,1},{3,2},{4,7},{5,4},{6,5},{7,6},{8,11},{9,8},{10,9... | collective-permute-start | bytes 3538952 | tf_op jit(solution)/shard_map/ppermute | solution.py:92
  812.8 210.0 %reduce-scatter.17.cloned.1.call-start = ((), (), s32[]{:S(2)}) async-start(), calls=%async_computation.24 | async-start | bytes 9437184 | tf_op jit(solution)/shard_map/reduce_scatter | solution.py:351
  822.8 199.9 %reduce-scatter.11.cloned.1.call-start = ((), (), s32[]{:S(2)}) async-start(), calls=%async_computation.21 | async-start | bytes 9437184 | tf_op jit(solution)/shard_map/reduce_scatter | solution.py:351
  833.9 31.0 %collective-permute-start.6 = (bf16[96,6144]{1,0:T(8,128)(2,1)}, bf16[96,6144]{1,0:T(8,128)(2,1)}, u32[]{:S(2)}, u32[]{:S(2)}) collective-permute-start(bf16[96,6144]{1,0:T(8,128)(2,1)} %get-tuple-element.86), channel_id=1, source_target_pairs={{0,1},{1,2},{2,3},{3,0},{4,5},{5,6},{6,7},{7,4},{8,9},{9,10},{10,1... | collective-permute-start | bytes 3538952 | tf_op jit(solution)/shard_map/ppermute | solution.py:91
  837.9 51.3 %collective-permute-start.7 = (bf16[96,6144]{1,0:T(8,128)(2,1)}, bf16[96,6144]{1,0:T(8,128)(2,1)}, u32[]{:S(2)}, u32[]{:S(2)}) collective-permute-start(bf16[96,6144]{1,0:T(8,128)(2,1)} %get-tuple-element.88), channel_id=1, source_target_pairs={{0,3},{1,0},{2,1},{3,2},{4,7},{5,4},{6,5},{7,6},{8,11},{9,8},{10,9... | collective-permute-start | bytes 3538952 | tf_op jit(solution)/shard_map/ppermute | solution.py:92
  889.3 31.0 %collective-permute-start.8 = (bf16[96,6144]{1,0:T(8,128)(2,1)}, bf16[96,6144]{1,0:T(8,128)(2,1)}, u32[]{:S(2)}, u32[]{:S(2)}) collective-permute-start(bf16[96,6144]{1,0:T(8,128)(2,1)} %collective-permute-done.6), channel_id=1, source_target_pairs={{0,1},{1,2},{2,3},{3,0},{4,5},{5,6},{6,7},{7,4},{8,9},{9,10},{10,1... | collective-permute-start | bytes 3538952 | tf_op jit(solution)/shard_map/ppermute | solution.py:91
  889.8 53.2 %collective-permute-start.9 = (bf16[96,6144]{1,0:T(8,128)(2,1)}, bf16[96,6144]{1,0:T(8,128)(2,1)}, u32[]{:S(2)}, u32[]{:S(2)}) collective-permute-start(bf16[96,6144]{1,0:T(8,128)(2,1)} %collective-permute-done.7), channel_id=1, source_target_pairs={{0,3},{1,0},{2,1},{3,2},{4,7},{5,4},{6,5},{7,6},{8,11},{9,8},{10,9... | collective-permute-start | bytes 3538952 | tf_op jit(solution)/shard_map/ppermute | solution.py:92
  943.0 66.8 %collective-permute-start.10 = (bf16[96,6144]{1,0:T(8,128)(2,1)}, bf16[96,6144]{1,0:T(8,128)(2,1)}, u32[]{:S(2)}, u32[]{:S(2)}) collective-permute-start(bf16[96,6144]{1,0:T(8,128)(2,1)} %collective-permute-done.8), channel_id=1, source_target_pairs={{0,1},{1,2},{2,3},{3,0},{4,5},{5,6},{6,7},{7,4},{8,9},{9,10},{10,1... | collective-permute-start | bytes 3538952 | tf_op jit(solution)/shard_map/ppermute | solution.py:91
  943.3 66.6 %collective-permute-start.11 = (bf16[96,6144]{1,0:T(8,128)(2,1)}, bf16[96,6144]{1,0:T(8,128)(2,1)}, u32[]{:S(2)}, u32[]{:S(2)}) collective-permute-start(bf16[96,6144]{1,0:T(8,128)(2,1)} %collective-permute-done.9), channel_id=1, source_target_pairs={{0,3},{1,0},{2,1},{3,2},{4,7},{5,4},{6,5},{7,6},{8,11},{9,8},{10,9... | collective-permute-start | bytes 3538952 | tf_op jit(solution)/shard_map/ppermute | solution.py:92
  952.0 10.1 all-to-all-start.4
  962.9 34.2 %all-to-all-start.5 = ((f32[4,1,192]{2,1,0:T(1,128)}), f32[4,1,192]{2,1,0:T(1,128)S(1)}, u32[]{:S(2)}, u32[]{:S(2)}) async-start(f32[4,1,192]{2,1,0:T(1,128)} %reshape.310), calls=%async_computation.7 | async-start | bytes 8192 | tf_op jit(solution)/shard_map/all_to_all | solution.py:341
  999.1 8.8 all-to-all-start.6
  1002.3 142.7 %all-reduce.3.cloned.1.call-start = ((), (), s32[]{:S(2)}) async-start(), calls=%async_computation.25 | async-start | bytes 6291456 | tf_op jit(solution)/shard_map/psum | solution.py:362
  (81 other events, 1426.1 us)
Sparse Core Ops, SparseCore 0:
  9.9 64.1 all-gather.8
  76.0 59.0 all-gather.6
  137.0 53.5 all-gather.10
  192.4 54.2 all-gather.12
  258.1 71.9 all-gather.14
  332.4 71.9 all-gather.16
  463.2 140.1 reduce-scatter.6
  606.9 100.7 reduce-scatter.8
  746.7 50.9 reduce-scatter.14
  812.9 50.9 reduce-scatter.12
  867.4 71.4 reduce-scatter.16
  942.3 71.4 reduce-scatter.10
  1022.9 122.0 all-reduce.2
